TPU v7x, 256 devices: a whole 4x4x8 slice. The times are simulated.
256 devices in a mesh: nodes: 64 (over x, z, core), heads: 4 (over y).
Axes of the slice: x: 4, y: 4, z: 8, core: 2. Of those that a mesh axis runs over, the one named last changes fastest.
Arguments:
- feats: bfloat16 [65536, 512], P('nodes'), may hold values from -6 to 6
- w_query: bfloat16 [512, 512], P(None, 'heads'), may hold values from -0.25 to 0.25
- w_key: bfloat16 [512, 512], P(None, 'heads'), may hold values from -0.25 to 0.25
- w_value: bfloat16 [512, 512], P(None, 'heads'), may hold values from -0.25 to 0.25
- w_out: bfloat16 [512, 512], P('heads'), may hold values from -6 to 6
- head_scale: float32 [8], P('heads'), may hold values from 2 to 10
- nbr_owner: int32 [512, 4], P('nodes'), may hold values from 0 to 63, all different within a row; in each aligned block of 8 rows (0 to 7, 8 to 15, ...) at most 2 rows name the same one
- nbr_local: int32 [512, 4], P('nodes'), may hold values from 0 to 7
- slot_valid: int32 [512, 4], P('nodes'), may hold values 0 or 1
Outputs:
- mixed: bfloat16 [65536, 512], P('nodes', 'heads')
Inputs may be any that keep to these rules, and one draw needn't show every extreme that they name: `nbr_owner`: the 4 owners listed for one query block are distinct. Among the query blocks of one index of nodes, no owner is listed more than 2 times, and 2 is reached.
All inputs are finite; a program needn't handle non-finite values. No bound on the sum of `slot_valid` on one device may be relied on, other than what follows from the above.
Results may differ from a plain program's by a relative error of at most 0.012.
Values may be sent and summed in bfloat16 or wider, within the bound.
No kernel may reach another device: no remote copies, remote signals or barrier semaphores. Data moves between devices by JAX's collectives and lax.ppermute only.
A program may use at most 128 MiB of HBM per device.

v0:
```python
import functools

import jax
import jax.numpy as jnp
from jax import lax
from jax.experimental import pallas as pl
from jax.experimental.pallas import tpu as pltpu
from jax.sharding import PartitionSpec as P


def unit_rows(values, count):
    shaped = values.reshape(values.shape[0], count, -1)
    total = jnp.sum(shaped * shaped, axis=-1, keepdims=True)
    return (shaped * lax.rsqrt(total + 1e-06)).astype(jnp.bfloat16).reshape(values.shape)


def attend_kernel(
    slot_ref, live_ref, scale_ref, q_ref, own_ref, recv_ref, out_ref, num_scr, den_scr, *, count, slots
):
    b = pl.program_id(0)
    feat, width = q_ref.shape[1], q_ref.shape[2]
    hd = feat // count
    q_t = q_ref[0]
    lane_head = lax.broadcasted_iota(jnp.int32, (width, feat), 1) // hd
    row_head = lax.broadcasted_iota(jnp.int32, (feat, width), 0) // hd
    stack_rows = lax.broadcasted_iota(jnp.int32, (count * width, 1), 0)
    scale_col = jnp.zeros((count * width, 1), jnp.float32)
    for h in range(count):
        inside = (stack_rows >= h * width) & (stack_rows < (h + 1) * width)
        scale_col = jnp.where(inside, scale_ref[h], scale_col)

    def tile(kv):
        keys = kv[:width]
        values_t = kv[width:]
        key_stack = jnp.concatenate(
            [jnp.where(lane_head == h, keys, jnp.zeros_like(keys)) for h in range(count)], axis=0
        )
        value_stack = jnp.concatenate(
            [jnp.where(row_head == h, values_t, jnp.zeros_like(values_t)) for h in range(count)],
            axis=1,
        )
        s = jnp.dot(key_stack, q_t, preferred_element_type=jnp.float32)
        w = jnp.exp(scale_col * (s - 1.0))
        dens = [
            jnp.sum(w[h * width:(h + 1) * width], axis=0, keepdims=True)
            .astype(jnp.bfloat16)
            .astype(jnp.float32)
            for h in range(count)
        ]
        num = jnp.dot(value_stack, w.astype(jnp.bfloat16), preferred_element_type=jnp.float32)
        return num.astype(jnp.bfloat16).astype(jnp.float32), jnp.concatenate(dens, axis=0)

    num, den = tile(own_ref[b])
    num_scr[...] = num
    den_scr[...] = den
    for s in range(slots):
        p = b * slots + s

        @pl.when(live_ref[p] > 0)
        def _():
            num_s, den_s = tile(recv_ref[slot_ref[p]])
            num_scr[...] += num_s
            den_scr[...] += den_s

    den_full = jnp.zeros((feat, width), jnp.float32)
    for h in range(count):
        den_full = jnp.where(row_head == h, den_scr[h:h + 1, :], den_full)
    out_ref[0] = (num_scr[...] / den_full).astype(out_ref.dtype)


def attend(query_t, own_kv, recv_kv, slot_of, live, scales):
    nblocks, feat, width = query_t.shape
    count = scales.shape[0]
    slots = slot_of.shape[0] // nblocks
    tiles = recv_kv.shape[0]
    grid_spec = pltpu.PrefetchScalarGridSpec(
        num_scalar_prefetch=2,
        grid=(nblocks,),
        in_specs=[
            pl.BlockSpec(memory_space=pltpu.SMEM),
            pl.BlockSpec((1, feat, width), lambda b, slot_of, live: (b, 0, 0)),
            pl.BlockSpec((nblocks, 2 * width, feat), lambda b, slot_of, live: (0, 0, 0)),
            pl.BlockSpec((tiles, 2 * width, feat), lambda b, slot_of, live: (0, 0, 0)),
        ],
        out_specs=pl.BlockSpec((1, feat, width), lambda b, slot_of, live: (b, 0, 0)),
        scratch_shapes=[
            pltpu.VMEM((feat, width), jnp.float32),
            pltpu.VMEM((count, width), jnp.float32),
        ],
    )
    return pl.pallas_call(
        functools.partial(attend_kernel, count=count, slots=slots),
        grid_spec=grid_spec,
        out_shape=jax.ShapeDtypeStruct((nblocks, feat, width), jnp.bfloat16),
        compiler_params=pltpu.CompilerParams(vmem_limit_bytes=48 * 1024 * 1024),
    )(slot_of, live, scales, query_t, own_kv, recv_kv)


def body(feats, w_query, w_key, w_value, w_out, head_scale, nbr_owner, nbr_local, slot_valid):
    w_out, feats = lax.optimization_barrier((w_out, feats))
    rows = feats.shape[0]
    feat = w_query.shape[1]
    count = head_scale.shape[0]
    nblocks, slots = nbr_owner.shape
    width = rows // nblocks
    devices = lax.axis_size("nodes")
    capacity = max(2, min(nblocks // 2, 3 * nblocks * slots // (2 * devices)))
    tile_count = devices * capacity
    query_n = unit_rows(jnp.dot(feats, w_query, preferred_element_type=jnp.float32), count)
    key_n = unit_rows(jnp.dot(feats, w_key, preferred_element_type=jnp.float32), count)
    value_b = jnp.dot(feats, w_value, preferred_element_type=jnp.float32).astype(jnp.bfloat16)
    query_t = jnp.swapaxes(query_n.reshape(nblocks, width, feat), 1, 2)
    own_kv = jnp.concatenate(
        [key_n.reshape(nblocks, width, feat), jnp.swapaxes(value_b.reshape(nblocks, width, feat), 1, 2)],
        axis=1,
    )
    owners = nbr_owner.reshape(-1)
    owner_hot = (owners[:, None] == jnp.arange(devices, dtype=jnp.int32)[None, :]).astype(jnp.int32)
    rank = jnp.sum(jnp.cumsum(owner_hot, axis=0) * owner_hot, axis=1) - 1
    target = owners * capacity + rank
    place = (target[:, None] == jnp.arange(tile_count, dtype=jnp.int32)[None, :]).astype(jnp.int32)
    valid = (slot_valid.reshape(-1) > 0).astype(jnp.int32)
    wanted = jnp.where(valid > 0, nbr_local.reshape(-1), -1)
    request = jnp.sum(place * (wanted[:, None] + 1), axis=0) - 1
    asked = lax.all_to_all(
        request.reshape(devices, capacity), "nodes", split_axis=0, concat_axis=0, tiled=True
    ).reshape(-1)
    ask_hot = (asked[:, None] == jnp.arange(nblocks, dtype=jnp.int32)[None, :]).astype(jnp.bfloat16)
    payload = jnp.einsum(
        "cm,mrl->crl", ask_hot, own_kv, preferred_element_type=jnp.float32
    ).astype(jnp.bfloat16)
    recv_kv = lax.all_to_all(
        payload.reshape(devices, capacity * 2 * width, feat),
        "nodes",
        split_axis=0,
        concat_axis=0,
        tiled=True,
    ).reshape(tile_count, 2 * width, feat)
    slot_of = jnp.clip(target, 0, tile_count - 1).astype(jnp.int32)
    attn_t = attend(query_t, own_kv, recv_kv, slot_of, valid, head_scale)
    attn = jnp.swapaxes(attn_t, 1, 2).reshape(rows, feat)
    attn_all = lax.all_gather(attn, "heads", axis=1, tiled=True)
    w_cols = lax.dynamic_slice_in_dim(w_out, lax.axis_index("heads") * feat, feat, axis=1)
    return jnp.dot(attn_all, w_cols, preferred_element_type=jnp.float32).astype(jnp.bfloat16)


def solution(mesh):
    placed = (
        P("nodes", None),
        P(None, "heads"),
        P(None, "heads"),
        P(None, "heads"),
        P(None, None),
        P("heads"),
        P("nodes", None),
        P("nodes", None),
        P("nodes", None),
    )
    return jax.shard_map(
        body, mesh=mesh, in_specs=placed, out_specs=P("nodes", "heads"), check_vma=False
    )
```

profile of v0, /device:TPU:2, one launch (start us, length us, event | category | flops | bytes accessed | tf_op | source)
XLA Modules:
  0.0 305.9 jit_solution(14438164558241066296)
XLA Ops:
  6.5 0.0 copy-start
  6.5 0.8 copy.39
  7.4 0.1 reshape.89
  7.5 0.1 fusion.4
  7.5 0.1 reduce_window_sum.11
  7.6 0.2 select_reduce_fusion.1
  7.8 0.7 compare_convert_fusion
  8.5 0.1 copy.40
  8.6 0.1 reshape.97.live_ref
  8.6 0.8 copy.47
  9.4 0.1 reshape.93
  9.5 0.1 select_reduce_fusion
  9.6 0.8 sub.12
  10.3 12.0 %all-to-all-start = ((s32[64,1,2]{2,1,0:T(1,128)}), s32[64,1,2]{2,1,0:T(1,128)S(1)}, u32[]{:S(2)}, u32[]{:S(2)}) async-start(s32[64,1,2]{2,1,0:T(1,128)} %bitcast.7), calls=%async_computation | async-start | bytes 65536 | tf_op jit(solution)/shard_map/all_to_all | solution.py:125
  22.4 15.2 %all-gather = bf16[512,512]{1,0:T(8,128)(2,1)} all-gather(bf16[128,512]{1,0:T(8,128)(2,1)} %param.13), channel_id=2, replica_groups=mesh['nodes'=64,'heads'=4] {'heads'}, dimensions={0}, use_global_device_ids=true | all-gather | bytes 655360 | tf_op args[4]
  37.6 0.0 copy-done
  37.6 1.3 fusion.11
  39.0 0.2 copy.44
  39.2 0.1 bitcast_reduce_fusion
  39.3 0.1 copy.53
  39.4 0.2 copy.45
  39.6 1.3 convolution_convert_fusion.2
  41.0 0.2 copy.46
  41.2 0.1 multiply_convert_fusion
  41.3 0.0 all-to-all-done
  41.3 0.5 broadcast.80
  41.8 0.7 reduce.3
  42.5 0.1 eq.47
  42.7 5.6 %convolution_convert_fusion = bf16[128,256,128]{2,0,1:T(8,128)(2,1)} fusion(bf16[8,256,128]{2,1,0:T(8,128)(2,1)S(1)} %pad_maximum_fusion.own_ref, s32[128]{0:T(128)S(1)} %eq.47), kind=kOutput, calls=%fused_computation | convolution fusion | flops 71304192 | bytes 8913408 | tf_op jit(solution)/shard_map/cm,mrl->crl/dot_general | solution.py:129
  48.3 12.0 %copy.50 = bf16[128,256,128]{2,1,0:T(8,128)(2,1)} copy(bf16[128,256,128]{2,0,1:T(8,128)(2,1)} %convolution_convert_fusion) | data formatting | bytes 16777216 | tf_op jit(solution)/shard_map/convert_element_type | solution.py:131
  60.3 0.0 copy-start.2
  60.3 0.0 copy-start.1
  60.3 10.6 %all-to-all-start.1 = ((bf16[64,512,128]{2,1,0:T(8,128)(2,1)}), bf16[64,512,128]{2,1,0:T(8,128)(2,1)}, u32[]{:S(2)}, u32[]{:S(2)}) async-start(bf16[64,512,128]{2,1,0:T(8,128)(2,1)} %bitcast.36), calls=%async_computation.1 | async-start | bytes 16777216 | tf_op jit(solution)/shard_map/all_to_all | solution.py:132
  70.9 0.0 all-gather.3.cloned.1.call-start
  70.9 0.0 copy-done.2
  71.0 0.4 fusion.10
  71.4 0.2 copy.41
  71.7 0.1 copy.52
  71.8 0.2 copy.42
  72.0 0.1 fusion.2.q_ref
  72.2 183.1 %all-to-all-done.1 = bf16[64,512,128]{2,1,0:T(8,128)(2,1)} async-done(((bf16[64,512,128]{2,1,0:T(8,128)(2,1)}), bf16[64,512,128]{2,1,0:T(8,128)(2,1)}, u32[]{:S(2)}, u32[]{:S(2)}) %all-to-all-start.1) | async-done | bytes 8388640 | tf_op jit(solution)/shard_map/all_to_all | solution.py:132
  255.2 0.0 copy-done.1
  255.2 14.3 %shard_map.91 = bf16[8,128,128]{2,1,0:T(8,128)(2,1)S(1)} custom-call(s32[32]{0:T(128)S(1)} %get-tuple-element.9.slot_ref, s32[32]{0:T(128)S(1)} %reshape.97.live_ref, f32[2]{0:T(128)S(1)} %copy-done.1, bf16[8,128,128]{2,1,0:T(8,128)(2,1)S(1)} %fusion.2.q_ref, bf16[8,256,128]{2,1,0:T(8,128)(2,1)S(1)} %pad_maximum_fusion.own_ref, ...), custom_call_target="tpu_custom_call" | custom-call | tf_op jit(solution)/shard_map/pallas_call | solution.py:91
  269.6 0.9 copy.51
  270.4 0.0 all-gather.3.cloned.1.call-update
  270.4 26.2 %all-gather.3.cloned.1.call-done = bf16[1024,512]{1,0:T(8,128)(2,1)} async-done(((bf16[1024,128]{1,0:T(8,128)(2,1)}), bf16[1024,512]{1,0:T(8,128)(2,1)}) %all-gather.3.cloned.1.call-update) | async-done | bytes 1048592 | tf_op jit(solution)/shard_map/all_gather | solution.py:142
  296.7 2.4 convolution_convert_fusion.1
  (8 shorter events, 0.2 us)
Async XLA Ops:
  6.5 31.1 %copy-start = (bf16[1024,512]{1,0:T(8,128)(2,1)S(1)}, bf16[1024,512]{1,0:T(8,128)(2,1)}, u32[]{:S(2)}) copy-start(bf16[1024,512]{1,0:T(8,128)(2,1)} %param.9) | copy-start | bytes 3145732
  10.3 30.9 %all-to-all-start = ((s32[64,1,2]{2,1,0:T(1,128)}), s32[64,1,2]{2,1,0:T(1,128)S(1)}, u32[]{:S(2)}, u32[]{:S(2)}) async-start(s32[64,1,2]{2,1,0:T(1,128)} %bitcast.7), calls=%async_computation | async-start | bytes 65536 | tf_op jit(solution)/shard_map/all_to_all | solution.py:125
  60.3 10.7 %copy-start.2 = (bf16[512,128]{1,0:T(8,128)(2,1)S(1)}, bf16[512,128]{1,0:T(8,128)(2,1)}, u32[]{:S(2)}) copy-start(bf16[512,128]{1,0:T(8,128)(2,1)} %param.10) | copy-start | bytes 393220
  60.3 195.0 %copy-start.1 = (f32[2]{0:T(128)S(1)}, f32[2]{0:T(128)}, u32[]{:S(2)}) copy-start(f32[2]{0:T(128)} %scale_ref.1) | copy-start | bytes 28
  60.3 195.0 %all-to-all-start.1 = ((bf16[64,512,128]{2,1,0:T(8,128)(2,1)}), bf16[64,512,128]{2,1,0:T(8,128)(2,1)}, u32[]{:S(2)}, u32[]{:S(2)}) async-start(bf16[64,512,128]{2,1,0:T(8,128)(2,1)} %bitcast.36), calls=%async_computation.1 | async-start | bytes 16777216 | tf_op jit(solution)/shard_map/all_to_all | solution.py:132
  70.9 225.8 %all-gather.3.cloned.1.call-start = ((), (), s32[]{:S(2)}) async-start(), calls=%async_computation.2 | async-start | bytes 1310720 | tf_op jit(solution)/shard_map/all_gather | solution.py:142
Sparse Core Ops, SparseCore 0:
  270.5 26.0 all-gather.2
where the time goes:
time: 306 us
  waiting for transfers between devices  209 us (68%)
  starting transfers between devices  22.7 us (7%)
  local copies, waits for them, and re-layouts  17.5 us (6%)
  blocking collectives  15.2 us (5%)
  Pallas kernels  14.3 us (5%)
  between operations  13.6 us (4%)
  matrix products  11.1 us (4%)
    all_to_all x1, waiting for transfers between devices, body(): lax.all_to_all(payload.reshape(devices, capacity * 2 * width, feat), 'nod...  183 us
    all_gather x1, waiting for transfers between devices, body(): attn_all = lax.all_gather(attn, 'heads', axis=1, tiled=True)  26.2 us
    unnamed x1, blocking collectives  15.2 us
    pallas_call x1, Pallas kernels, attend(): pl.pallas_call(functools.partial(attend_kernel, count=count, slots=slots)...  14.3 us
    all_to_all x1, starting transfers between devices, body(): lax.all_to_all(request.reshape(devices, capacity), 'nodes', split_axis=0,...  12 us
    convert_element_type x1, local copies, waits for them, and re-layouts, body(): payload = jnp.einsum('cm,mrl->crl', ask_hot, own_kv, preferred_element_ty...  12 us
    all_to_all x1, starting transfers between devices, body(): lax.all_to_all(payload.reshape(devices, capacity * 2 * width, feat), 'nod...  10.6 us
  transfers between devices with their start and end apart: 3, of which 2 were waited for; matrix products, arithmetic and copies ran while one was open for 2% of the time, Pallas kernels for 0%

commit v1 on v0

v1 whole, which is shorter than its diff:
```python
import functools

import jax
import jax.numpy as jnp
from jax import lax
from jax.experimental import pallas as pl
from jax.experimental.pallas import tpu as pltpu
from jax.sharding import PartitionSpec as P


def unit_rows(values, count):
    shaped = values.reshape(values.shape[0], count, -1)
    total = jnp.sum(shaped * shaped, axis=-1, keepdims=True)
    return (shaped * lax.rsqrt(total + 1e-06)).astype(jnp.bfloat16).reshape(values.shape)


def attend_kernel(
    slot_ref, live_ref, scale_ref, q_ref, own_ref, recv_ref, out_ref, num_scr, den_scr, *, count, slots
):
    b = pl.program_id(0)
    feat, lanes = q_ref.shape[1], q_ref.shape[2]
    width = lanes // count
    hd = feat // count
    q_stack = q_ref[0]
    row_head = lax.broadcasted_iota(jnp.int32, (feat, width), 0) // hd
    lane_pos = lax.broadcasted_iota(jnp.int32, (1, lanes), 1)
    scale_row = jnp.zeros((1, lanes), jnp.float32)
    for h in range(count):
        inside = (lane_pos >= h * width) & (lane_pos < (h + 1) * width)
        scale_row = jnp.where(inside, scale_ref[h], scale_row)

    def tile(kv):
        keys = kv[:width]
        values_t = kv[width:]
        s = jnp.dot(keys, q_stack, preferred_element_type=jnp.float32)
        w = jnp.exp(scale_row * (s - 1.0))
        den = jnp.sum(w, axis=0, keepdims=True).astype(jnp.bfloat16).astype(jnp.float32)
        w_b = w.astype(jnp.bfloat16)
        num = jnp.zeros((feat, width), jnp.float32)
        for h in range(count):
            part = jnp.dot(values_t, w_b[:, h * width:(h + 1) * width], preferred_element_type=jnp.float32)
            num = jnp.where(row_head == h, part, num)
        return num.astype(jnp.bfloat16).astype(jnp.float32), den

    num, den = tile(own_ref[b])
    num_scr[...] = num
    den_scr[...] = den
    for s in range(slots):
        p = b * slots + s

        @pl.when(live_ref[p] > 0)
        def _():
            num_s, den_s = tile(recv_ref[slot_ref[p]])
            num_scr[...] += num_s
            den_scr[...] += den_s

    den_full = jnp.zeros((feat, width), jnp.float32)
    for h in range(count):
        den_full = jnp.where(row_head == h, den_scr[:, h * width:(h + 1) * width], den_full)
    out_ref[0] = (num_scr[...] / den_full).astype(out_ref.dtype)


def attend(query_stack, own_kv, recv_kv, slot_of, live, scales):
    nblocks, feat, lanes = query_stack.shape
    count = scales.shape[0]
    width = lanes // count
    slots = slot_of.shape[0] // nblocks
    tiles = recv_kv.shape[0]
    grid_spec = pltpu.PrefetchScalarGridSpec(
        num_scalar_prefetch=2,
        grid=(nblocks,),
        in_specs=[
            pl.BlockSpec(memory_space=pltpu.SMEM),
            pl.BlockSpec((1, feat, lanes), lambda b, slot_of, live: (b, 0, 0)),
            pl.BlockSpec((nblocks, 2 * width, feat), lambda b, slot_of, live: (0, 0, 0)),
            pl.BlockSpec((tiles, 2 * width, feat), lambda b, slot_of, live: (0, 0, 0)),
        ],
        out_specs=pl.BlockSpec((1, feat, width), lambda b, slot_of, live: (b, 0, 0)),
        scratch_shapes=[
            pltpu.VMEM((feat, width), jnp.float32),
            pltpu.VMEM((1, lanes), jnp.float32),
        ],
    )
    return pl.pallas_call(
        functools.partial(attend_kernel, count=count, slots=slots),
        grid_spec=grid_spec,
        out_shape=jax.ShapeDtypeStruct((nblocks, feat, width), jnp.bfloat16),
        compiler_params=pltpu.CompilerParams(vmem_limit_bytes=48 * 1024 * 1024),
    )(slot_of, live, scales, query_stack, own_kv, recv_kv)


def gather_kernel(pick_ref, src_ref, out_ref):
    g = pl.program_id(0)
    group = out_ref.shape[0]
    for i in range(group):
        out_ref[i] = src_ref[pick_ref[g * group + i]]


def gather_blocks(blocks, pick):
    nblocks, r, l = blocks.shape
    tiles = pick.shape[0]
    group = 32
    grid_spec = pltpu.PrefetchScalarGridSpec(
        num_scalar_prefetch=1,
        grid=(tiles // group,),
        in_specs=[pl.BlockSpec((nblocks, r, l), lambda g, pick: (0, 0, 0))],
        out_specs=pl.BlockSpec((group, r, l), lambda g, pick: (g, 0, 0)),
    )
    return pl.pallas_call(
        gather_kernel,
        grid_spec=grid_spec,
        out_shape=jax.ShapeDtypeStruct((tiles, r, l), blocks.dtype),
    )(pick, blocks)


def body(feats, w_query, w_key, w_value, w_out, head_scale, nbr_owner, nbr_local, slot_valid):
    rows = feats.shape[0]
    feat = w_query.shape[1]
    count = head_scale.shape[0]
    nblocks, slots = nbr_owner.shape
    width = rows // nblocks
    devices = lax.axis_size("nodes")
    capacity = max(2, min(nblocks // 2, 3 * nblocks * slots // (2 * devices)))
    tile_count = devices * capacity
    query_n = unit_rows(jnp.dot(feats, w_query, preferred_element_type=jnp.float32), count)
    key_n = unit_rows(jnp.dot(feats, w_key, preferred_element_type=jnp.float32), count)
    value_b = jnp.dot(feats, w_value, preferred_element_type=jnp.float32).astype(jnp.bfloat16)
    query_t = jnp.swapaxes(query_n.reshape(nblocks, width, feat), 1, 2)
    head_of = jnp.arange(feat, dtype=jnp.int32) // (feat // count)
    query_stack = jnp.concatenate(
        [jnp.where(head_of[None, :, None] == h, query_t, 0) for h in range(count)], axis=2
    )
    own_kv = jnp.concatenate(
        [key_n.reshape(nblocks, width, feat), jnp.swapaxes(value_b.reshape(nblocks, width, feat), 1, 2)],
        axis=1,
    )
    owners = nbr_owner.reshape(-1)
    owner_hot = (owners[:, None] == jnp.arange(devices, dtype=jnp.int32)[None, :]).astype(jnp.int32)
    rank = jnp.sum(jnp.cumsum(owner_hot, axis=0) * owner_hot, axis=1) - 1
    target = owners * capacity + rank
    place = (target[:, None] == jnp.arange(tile_count, dtype=jnp.int32)[None, :]).astype(jnp.int32)
    valid = (slot_valid.reshape(-1) > 0).astype(jnp.int32)
    wanted = jnp.where(valid > 0, nbr_local.reshape(-1), -1)
    request = jnp.sum(place * (wanted[:, None] + 1), axis=0) - 1
    asked = lax.all_to_all(
        request.reshape(devices, capacity), "nodes", split_axis=0, concat_axis=0, tiled=True
    ).reshape(-1)
    payload = gather_blocks(own_kv, jnp.clip(asked, 0, nblocks - 1).astype(jnp.int32))
    w_out, payload = lax.optimization_barrier((w_out, payload))
    recv_kv = lax.all_to_all(
        payload.reshape(devices, capacity * 2 * width, feat),
        "nodes",
        split_axis=0,
        concat_axis=0,
        tiled=True,
    ).reshape(tile_count, 2 * width, feat)
    slot_of = jnp.clip(target, 0, tile_count - 1).astype(jnp.int32)
    attn_t = attend(query_stack, own_kv, recv_kv, slot_of, valid, head_scale)
    attn = jnp.swapaxes(attn_t, 1, 2).reshape(rows, feat)
    attn_all = lax.all_gather(attn, "heads", axis=1, tiled=True)
    w_cols = lax.dynamic_slice_in_dim(w_out, lax.axis_index("heads") * feat, feat, axis=1)
    return jnp.dot(attn_all, w_cols, preferred_element_type=jnp.float32).astype(jnp.bfloat16)


def solution(mesh):
    placed = (
        P("nodes", None),
        P(None, "heads"),
        P(None, "heads"),
        P(None, "heads"),
        P(None, None),
        P("heads"),
        P("nodes", None),
        P("nodes", None),
        P("nodes", None),
    )
    return jax.shard_map(
        body, mesh=mesh, in_specs=placed, out_specs=P("nodes", "heads"), check_vma=False
    )
```

time: 306 us -> 294 us (0.961)
  local copies, waits for them, and re-layouts: 17.5 us -> 5.5 us
  matrix products: 11.1 us -> 5.48 us
  Pallas kernels: 14.3 us -> 19 us
    convert_element_type x1 -> x0, local copies, waits for them, and re-layouts: 12 us -> none  [body(): payload = jnp.einsum('cm,mrl->crl', ask_hot, own_kv, preferred_element_ty...]
    dot_general x1 -> x0, matrix products: 5.6 us -> none  [body(): jnp.einsum('cm,mrl->crl', ask_hot, own_kv, preferred_element_type=jnp.flo...]
    pallas_call x0 -> x1, Pallas kernels: none -> 5.35 us  [gather_blocks(): pl.pallas_call(gather_kernel, grid_spec=grid_spec, out_shape=jax.ShapeDty...]
where the time goes in v1:
time: 294 us
  waiting for transfers between devices  211 us (72%)
  starting transfers between devices  22.7 us (8%)
  Pallas kernels  19 us (6%)
  blocking collectives  14 us (5%)
  between operations  13.6 us (5%)
  local copies, waits for them, and re-layouts  5.5 us (2%)
  matrix products  5.48 us (2%)
    all_to_all x1, waiting for transfers between devices, body(): lax.all_to_all(payload.reshape(devices, capacity * 2 * width, feat), 'nod...  183 us
    all_gather x1, waiting for transfers between devices, body(): attn_all = lax.all_gather(attn, 'heads', axis=1, tiled=True)  27.9 us
    unnamed x1, blocking collectives  14 us
    pallas_call x1, Pallas kernels, attend(): pl.pallas_call(functools.partial(attend_kernel, count=count, slots=slots)...  13.7 us
    all_to_all x1, starting transfers between devices, body(): lax.all_to_all(request.reshape(devices, capacity), 'nodes', split_axis=0,...  12 us
    all_to_all x1, starting transfers between devices, body(): lax.all_to_all(payload.reshape(devices, capacity * 2 * width, feat), 'nod...  10.6 us
  transfers between devices with their start and end apart: 3, of which 2 were waited for; matrix products, arithmetic and copies ran while one was open for 2% of the time, Pallas kernels for 0%

profile of v1, /device:TPU:2, one launch (start us, length us, event | category | flops | bytes accessed | tf_op | source)
XLA Modules:
  0.0 293.7 jit_solution(170525444847772851)
XLA Ops:
  6.5 0.0 copy-start
  6.5 0.0 copy-start.3
  6.5 0.9 copy.34
  7.4 0.1 reshape.111
  7.5 0.1 fusion.2
  7.5 0.1 reduce_window_sum.11
  7.6 0.2 select_reduce_fusion.1
  7.8 0.7 compare_convert_fusion
  8.5 0.1 copy.35
  8.6 0.1 reshape.119.live_ref
  8.6 0.8 copy.42
  9.4 0.1 reshape.115
  9.5 0.1 select_reduce_fusion
  9.6 0.8 sub.21
  10.4 12.0 %all-to-all-start = ((s32[64,1,2]{2,1,0:T(1,128)}), s32[64,1,2]{2,1,0:T(1,128)S(1)}, u32[]{:S(2)}, u32[]{:S(2)}) async-start(s32[64,1,2]{2,1,0:T(1,128)} %bitcast.8), calls=%async_computation | async-start | bytes 65536 | tf_op jit(solution)/shard_map/all_to_all | solution.py:145
  22.4 0.0 copy-done
  22.4 1.3 fusion.7
  23.7 0.2 copy.39
  23.9 0.1 bitcast_reduce_fusion
  24.1 0.1 copy.46
  24.2 0.2 copy.40
  24.4 1.3 convolution_convert_fusion.1
  25.8 0.2 copy.41
  25.9 0.0 copy-done.3
  26.0 14.0 %all-gather = bf16[512,512]{1,0:T(8,128)(2,1)} all-gather(bf16[128,512]{1,0:T(8,128)(2,1)S(1)} %copy-done.3), channel_id=2, replica_groups=mesh['nodes'=64,'heads'=4] {'heads'}, dimensions={0}, use_global_device_ids=true | all-gather | bytes 655360 | tf_op args[4]
  40.0 0.1 multiply_convert_fusion
  40.1 0.8 pad_maximum_fusion.1.src_ref.own_ref
  40.9 0.0 all-to-all-done
  40.9 0.1 clamp_reduce_fusion
  41.0 0.7 min.22.pick_ref
  41.7 5.3 %shard_map.91 = bf16[128,256,128]{2,1,0:T(8,128)(2,1)} custom-call(s32[128]{0:T(128)} %min.22.pick_ref, bf16[8,256,128]{2,1,0:T(8,128)(2,1)} %pad_maximum_fusion.1.src_ref.own_ref), custom_call_target="tpu_custom_call" | custom-call | tf_op jit(solution)/shard_map/pallas_call | solution.py:109
  47.0 0.0 copy-start.4
  47.0 10.6 %all-to-all-start.1 = ((bf16[64,512,128]{2,1,0:T(8,128)(2,1)}), bf16[64,512,128]{2,1,0:T(8,128)(2,1)}, u32[]{:S(2)}, u32[]{:S(2)}) async-start(bf16[64,512,128]{2,1,0:T(8,128)(2,1)} %bitcast.35), calls=%async_computation.1 | async-start | bytes 16777216 | tf_op jit(solution)/shard_map/all_to_all | solution.py:150
  57.7 0.0 copy-start.1
  57.7 0.0 copy-start.2
  57.7 0.0 all-gather.3.cloned.1.call-start
  57.7 0.0 copy-done.4
  57.7 0.4 fusion.6
  58.2 0.2 copy.36
  58.5 0.1 copy.45
  58.6 0.2 copy.37
  58.8 0.2 select_bitcast_fusion.1
  59.0 0.1 select_bitcast_fusion
  59.1 0.1 pad_maximum_fusion.q_ref
  59.2 182.8 %all-to-all-done.1 = bf16[64,512,128]{2,1,0:T(8,128)(2,1)} async-done(((bf16[64,512,128]{2,1,0:T(8,128)(2,1)}), bf16[64,512,128]{2,1,0:T(8,128)(2,1)}, u32[]{:S(2)}, u32[]{:S(2)}) %all-to-all-start.1) | async-done | bytes 8388640 | tf_op jit(solution)/shard_map/all_to_all | solution.py:150
  242.0 0.0 copy-done.1
  242.0 0.0 copy-done.2
  242.0 13.7 %shard_map.92 = bf16[8,128,128]{2,1,0:T(8,128)(2,1)S(1)} custom-call(s32[32]{0:T(128)S(1)} %get-tuple-element.11.slot_ref, s32[32]{0:T(128)S(1)} %reshape.119.live_ref, f32[2]{0:T(128)S(1)} %copy-done.2, bf16[8,128,256]{2,1,0:T(8,128)(2,1)S(1)} %pad_maximum_fusion.q_ref, bf16[8,256,128]{2,1,0:T(8,128)(2,1)S(1)} %copy-done.1, ...), custom_call_target="tpu_custom_call" | custom-call | tf_op jit(solution)/shard_map/pallas_call | solution.py:84
  255.7 0.9 copy.44
  256.6 0.0 all-gather.3.cloned.1.call-update
  256.6 27.9 %all-gather.3.cloned.1.call-done = bf16[1024,512]{1,0:T(8,128)(2,1)} async-done(((bf16[1024,128]{1,0:T(8,128)(2,1)}), bf16[1024,512]{1,0:T(8,128)(2,1)}) %all-gather.3.cloned.1.call-update) | async-done | bytes 1048592 | tf_op jit(solution)/shard_map/all_gather | solution.py:160
  284.5 2.4 convolution_convert_fusion
  (9 shorter events, 0.2 us)
Async XLA Ops:
  6.5 15.9 %copy-start = (bf16[1024,512]{1,0:T(8,128)(2,1)S(1)}, bf16[1024,512]{1,0:T(8,128)(2,1)}, u32[]{:S(2)}) copy-start(bf16[1024,512]{1,0:T(8,128)(2,1)} %param.9) | copy-start | bytes 3145732
  6.5 19.4 %copy-start.3 = (bf16[128,512]{1,0:T(8,128)(2,1)S(1)}, bf16[128,512]{1,0:T(8,128)(2,1)}, u32[]{:S(2)}) copy-start(bf16[128,512]{1,0:T(8,128)(2,1)} %param.13) | copy-start | bytes 393220
  10.4 30.5 %all-to-all-start = ((s32[64,1,2]{2,1,0:T(1,128)}), s32[64,1,2]{2,1,0:T(1,128)S(1)}, u32[]{:S(2)}, u32[]{:S(2)}) async-start(s32[64,1,2]{2,1,0:T(1,128)} %bitcast.8), calls=%async_computation | async-start | bytes 65536 | tf_op jit(solution)/shard_map/all_to_all | solution.py:145
  47.0 10.7 %copy-start.4 = (bf16[512,128]{1,0:T(8,128)(2,1)S(1)}, bf16[512,128]{1,0:T(8,128)(2,1)}, u32[]{:S(2)}) copy-start(bf16[512,128]{1,0:T(8,128)(2,1)} %param.10) | copy-start | bytes 393220
  47.0 195.0 %all-to-all-start.1 = ((bf16[64,512,128]{2,1,0:T(8,128)(2,1)}), bf16[64,512,128]{2,1,0:T(8,128)(2,1)}, u32[]{:S(2)}, u32[]{:S(2)}) async-start(bf16[64,512,128]{2,1,0:T(8,128)(2,1)} %bitcast.35), calls=%async_computation.1 | async-start | bytes 16777216 | tf_op jit(solution)/shard_map/all_to_all | solution.py:150
  57.7 184.3 %copy-start.1 = (bf16[8,256,128]{2,1,0:T(8,128)(2,1)S(1)}, bf16[8,256,128]{2,1,0:T(8,128)(2,1)}, u32[]{:S(2)}) copy-start(bf16[8,256,128]{2,1,0:T(8,128)(2,1)} %pad_maximum_fusion.1.src_ref.own_ref) | copy-start | bytes 1572868
  57.7 184.3 %copy-start.2 = (f32[2]{0:T(128)S(1)}, f32[2]{0:T(128)}, u32[]{:S(2)}) copy-start(f32[2]{0:T(128)} %scale_ref.1) | copy-start | bytes 28
  57.7 226.8 %all-gather.3.cloned.1.call-start = ((), (), s32[]{:S(2)}) async-start(), calls=%async_computation.2 | async-start | bytes 1310720 | tf_op jit(solution)/shard_map/all_gather | solution.py:160
Sparse Core Ops, SparseCore 0:
  256.7 27.7 all-gather.2

commit v2 on v1

--- a/solution.py
+++ b/solution.py
@@ -15,9 +15,35 @@
 
 
 def attend_kernel(
-    slot_ref, live_ref, scale_ref, q_ref, own_ref, recv_ref, out_ref, num_scr, den_scr, *, count, slots
+    slot_ref,
+    live_ref,
+    scale_ref,
+    q_ref,
+    own_ref,
+    recv_ref,
+    out_ref,
+    num_scr,
+    den_scr,
+    buf,
+    sems,
+    *,
+    count,
+    slots,
 ):
     b = pl.program_id(0)
+    pairs = buf.shape[0]
+
+    def pair_copy(p):
+        return pltpu.make_async_copy(recv_ref.at[slot_ref[p]], buf.at[p], sems.at[p])
+
+    @pl.when(b == 0)
+    def _():
+        for p in range(pairs):
+
+            @pl.when(live_ref[p] > 0)
+            def _():
+                pair_copy(p).start()
+
     feat, lanes = q_ref.shape[1], q_ref.shape[2]
     width = lanes // count
     hd = feat // count
@@ -50,7 +76,8 @@
 
         @pl.when(live_ref[p] > 0)
         def _():
-            num_s, den_s = tile(recv_ref[slot_ref[p]])
+            pair_copy(p).wait()
+            num_s, den_s = tile(buf[p])
             num_scr[...] += num_s
             den_scr[...] += den_s
 
@@ -65,7 +92,6 @@
     count = scales.shape[0]
     width = lanes // count
     slots = slot_of.shape[0] // nblocks
-    tiles = recv_kv.shape[0]
     grid_spec = pltpu.PrefetchScalarGridSpec(
         num_scalar_prefetch=2,
         grid=(nblocks,),
@@ -73,12 +99,14 @@
             pl.BlockSpec(memory_space=pltpu.SMEM),
             pl.BlockSpec((1, feat, lanes), lambda b, slot_of, live: (b, 0, 0)),
             pl.BlockSpec((nblocks, 2 * width, feat), lambda b, slot_of, live: (0, 0, 0)),
-            pl.BlockSpec((tiles, 2 * width, feat), lambda b, slot_of, live: (0, 0, 0)),
+            pl.BlockSpec(memory_space=pl.ANY),
         ],
         out_specs=pl.BlockSpec((1, feat, width), lambda b, slot_of, live: (b, 0, 0)),
         scratch_shapes=[
             pltpu.VMEM((feat, width), jnp.float32),
             pltpu.VMEM((1, lanes), jnp.float32),
+            pltpu.VMEM((nblocks * slots, 2 * width, feat), recv_kv.dtype),
+            pltpu.SemaphoreType.DMA((nblocks * slots,)),
         ],
     )
     return pl.pallas_call(
@@ -147,6 +175,7 @@
     ).reshape(-1)
     payload = gather_blocks(own_kv, jnp.clip(asked, 0, nblocks - 1).astype(jnp.int32))
     w_out, payload = lax.optimization_barrier((w_out, payload))
+    w_out_t = lax.all_gather(w_out.T, "heads", axis=1, tiled=True)
     recv_kv = lax.all_to_all(
         payload.reshape(devices, capacity * 2 * width, feat),
         "nodes",
@@ -154,12 +183,15 @@
         concat_axis=0,
         tiled=True,
     ).reshape(tile_count, 2 * width, feat)
+    recv_kv, w_out_t = lax.optimization_barrier((recv_kv, w_out_t))
     slot_of = jnp.clip(target, 0, tile_count - 1).astype(jnp.int32)
     attn_t = attend(query_stack, own_kv, recv_kv, slot_of, valid, head_scale)
     attn = jnp.swapaxes(attn_t, 1, 2).reshape(rows, feat)
     attn_all = lax.all_gather(attn, "heads", axis=1, tiled=True)
-    w_cols = lax.dynamic_slice_in_dim(w_out, lax.axis_index("heads") * feat, feat, axis=1)
-    return jnp.dot(attn_all, w_cols, preferred_element_type=jnp.float32).astype(jnp.bfloat16)
+    w_rows = lax.dynamic_slice_in_dim(w_out_t, lax.axis_index("heads") * feat, feat, axis=0)
+    return lax.dot_general(
+        attn_all, w_rows, (((1,), (1,)), ((), ())), preferred_element_type=jnp.float32
+    ).astype(jnp.bfloat16)
 
 
 def solution(mesh):
@@ -168,7 +200,7 @@
         P(None, "heads"),
         P(None, "heads"),
         P(None, "heads"),
-        P(None, None),
+        P("heads", None),
         P("heads"),
         P("nodes", None),
         P("nodes", None),

time: 294 us -> 279 us (0.949)
  waiting for transfers between devices: 211 us -> 202 us
  starting transfers between devices: 22.7 us -> 18.8 us
    unnamed x1 -> x0, blocking collectives: 14 us -> none
    all_to_all x1, waiting for transfers between devices: 183 us -> 169 us  [body(): lax.all_to_all(payload.reshape(devices, capacity * 2 * width, feat), 'nod...]
    all_gather x0 -> x1, blocking collectives: none -> 13.3 us  [body(): w_out_t = lax.all_gather(w_out.T, 'heads', axis=1, tiled=True)]
    all_to_all x1, waiting for transfers between devices: 0.01 us -> 4.07 us  [body(): lax.all_to_all(request.reshape(devices, capacity), 'nodes', split_axis=0,...]
    all_to_all x1, starting transfers between devices: 10.6 us -> 6.69 us  [body(): lax.all_to_all(payload.reshape(devices, capacity * 2 * width, feat), 'nod...]
  transfers between devices with their start and end apart: 3 -> 3, of which waited for: 2 -> 3; matrix products, arithmetic and copies ran while one was open for 2% -> 2% of each run, Pallas kernels for 0% -> 0%
where the time goes in v2:
time: 279 us
  waiting for transfers between devices  202 us (72%)
  starting transfers between devices  18.8 us (7%)
  Pallas kernels  17 us (6%)
  between operations  13.6 us (5%)
  blocking collectives  13.3 us (5%)
  local copies, waits for them, and re-layouts  5.49 us (2%)
  matrix products  5.49 us (2%)
    all_to_all x1, waiting for transfers between devices, body(): lax.all_to_all(payload.reshape(devices, capacity * 2 * width, feat), 'nod...  169 us
    all_gather x1, waiting for transfers between devices, body(): attn_all = lax.all_gather(attn, 'heads', axis=1, tiled=True)  28.7 us
    all_gather x1, blocking collectives, body(): w_out_t = lax.all_gather(w_out.T, 'heads', axis=1, tiled=True)  13.3 us
    all_to_all x1, starting transfers between devices, body(): lax.all_to_all(request.reshape(devices, capacity), 'nodes', split_axis=0,...  12 us
    pallas_call x1, Pallas kernels, attend(): pl.pallas_call(functools.partial(attend_kernel, count=count, slots=slots)...  11.6 us
    all_to_all x1, starting transfers between devices, body(): lax.all_to_all(payload.reshape(devices, capacity * 2 * width, feat), 'nod...  6.69 us
  transfers between devices with their start and end apart: 3, of which 3 were waited for; matrix products, arithmetic and copies ran while one was open for 2% of the time, Pallas kernels for 0%

profile of v2, /device:TPU:2, one launch (start us, length us, event | category | flops | bytes accessed | tf_op | source)
XLA Modules:
  0.0 278.5 jit_solution(3263977937757270471)
XLA Ops:
  6.5 0.0 copy-start
  6.5 0.8 copy.34
  7.4 0.1 reshape.111
  7.5 0.1 fusion.2
  7.5 0.1 reduce_window_sum.11
  7.6 0.2 select_reduce_fusion.1
  7.8 0.7 compare_convert_fusion
  8.5 0.1 copy.35
  8.6 0.1 reshape.119.live_ref
  8.6 0.8 copy.42
  9.4 0.1 reshape.115
  9.5 0.1 select_reduce_fusion
  9.6 0.8 sub.21
  10.3 12.0 %all-to-all-start = ((s32[64,1,2]{2,1,0:T(1,128)}), s32[64,1,2]{2,1,0:T(1,128)S(1)}, u32[]{:S(2)}, u32[]{:S(2)}) async-start(s32[64,1,2]{2,1,0:T(1,128)} %bitcast.8), calls=%async_computation | async-start | bytes 65536 | tf_op jit(solution)/shard_map/all_to_all | solution.py:173
  22.4 0.0 copy-done
  22.4 1.3 fusion.7
  23.7 0.2 copy.39
  23.9 0.1 bitcast_reduce_fusion
  24.1 0.1 copy.46
  24.2 0.2 copy.40
  24.4 1.3 convolution_convert_fusion.1
  25.7 0.2 copy.41
  25.9 0.1 multiply_convert_fusion
  26.0 0.8 pad_maximum_fusion.1.src_ref.own_ref
  26.8 4.1 %all-to-all-done = s32[64,1,2]{2,1,0:T(1,128)S(1)} async-done(((s32[64,1,2]{2,1,0:T(1,128)}), s32[64,1,2]{2,1,0:T(1,128)S(1)}, u32[]{:S(2)}, u32[]{:S(2)}) %all-to-all-start) | async-done | bytes 544 | tf_op jit(solution)/shard_map/all_to_all | solution.py:173
  30.9 0.1 clamp_reduce_fusion
  31.0 0.7 min.22.pick_ref
  31.7 5.3 %shard_map.91 = bf16[128,256,128]{2,1,0:T(8,128)(2,1)} custom-call(s32[128]{0:T(128)} %min.22.pick_ref, bf16[8,256,128]{2,1,0:T(8,128)(2,1)} %pad_maximum_fusion.1.src_ref.own_ref), custom_call_target="tpu_custom_call" | custom-call | tf_op jit(solution)/shard_map/pallas_call | solution.py:137
  37.0 0.0 copy-start.3
  37.0 6.7 %all-to-all-start.1 = ((bf16[64,512,128]{2,1,0:T(8,128)(2,1)}), bf16[64,512,128]{2,1,0:T(8,128)(2,1)}, u32[]{:S(2)}, u32[]{:S(2)}) async-start(bf16[64,512,128]{2,1,0:T(8,128)(2,1)} %bitcast.36), calls=%async_computation.1 | async-start | bytes 16777216 | tf_op jit(solution)/shard_map/all_to_all | solution.py:179
  43.7 0.0 copy-start.4
  43.7 0.0 copy-start.1
  43.7 0.0 copy-start.2
  43.8 0.0 all-gather.2.cloned.1.call-start
  43.8 0.0 copy-done.3
  43.8 0.4 fusion.6
  44.2 0.2 copy.36
  44.6 0.1 copy.45
  44.7 0.2 copy.37
  44.9 0.2 select_bitcast_fusion.1
  45.1 0.1 select_bitcast_fusion
  45.2 0.1 pad_maximum_fusion.q_ref
  45.3 0.0 copy-done.4
  45.3 13.3 %all_gather.6 = bf16[512,512]{0,1:T(8,128)(2,1)S(1)} all-gather(bf16[512,128]{0,1:T(8,128)(2,1)S(1)} %bitcast.46), channel_id=1, replica_groups=mesh['nodes'=64,'heads'=4] {'heads'}, dimensions={1}, use_global_device_ids=true | all-gather | bytes 655360 | tf_op jit(solution)/shard_map/all_gather | solution.py:178
  58.6 169.5 %all-to-all-done.1 = bf16[64,512,128]{2,1,0:T(8,128)(2,1)} async-done(((bf16[64,512,128]{2,1,0:T(8,128)(2,1)}), bf16[64,512,128]{2,1,0:T(8,128)(2,1)}, u32[]{:S(2)}, u32[]{:S(2)}) %all-to-all-start.1) | async-done | bytes 8388640 | tf_op jit(solution)/shard_map/all_to_all | solution.py:179
  228.1 0.0 copy-done.1
  228.1 0.0 copy-done.2
  228.1 11.6 %shard_map.92 = bf16[8,128,128]{2,1,0:T(8,128)(2,1)S(1)} custom-call(s32[32]{0:T(128)S(1)} %get-tuple-element.15.slot_ref, s32[32]{0:T(128)S(1)} %reshape.119.live_ref, f32[2]{0:T(128)S(1)} %copy-done.2, bf16[8,128,256]{2,1,0:T(8,128)(2,1)S(1)} %pad_maximum_fusion.q_ref, bf16[8,256,128]{2,1,0:T(8,128)(2,1)S(1)} %copy-done.1, ...), custom_call_target="tpu_custom_call" | custom-call | tf_op jit(solution)/shard_map/pallas_call | solution.py:112
  239.7 0.9 copy.44
  240.6 0.0 all-gather.2.cloned.1.call-update
  240.6 28.7 %all-gather.2.cloned.1.call-done = bf16[1024,512]{1,0:T(8,128)(2,1)} async-done(((bf16[1024,128]{1,0:T(8,128)(2,1)}), bf16[1024,512]{1,0:T(8,128)(2,1)}) %all-gather.2.cloned.1.call-update) | async-done | bytes 1048592 | tf_op jit(solution)/shard_map/all_gather | solution.py:190
  269.3 2.4 convolution_convert_fusion
  (9 shorter events, 0.2 us)
Async XLA Ops:
  6.5 15.8 %copy-start = (bf16[1024,512]{1,0:T(8,128)(2,1)S(1)}, bf16[1024,512]{1,0:T(8,128)(2,1)}, u32[]{:S(2)}) copy-start(bf16[1024,512]{1,0:T(8,128)(2,1)} %param.9) | copy-start | bytes 3145732
  10.3 20.5 %all-to-all-start = ((s32[64,1,2]{2,1,0:T(1,128)}), s32[64,1,2]{2,1,0:T(1,128)S(1)}, u32[]{:S(2)}, u32[]{:S(2)}) async-start(s32[64,1,2]{2,1,0:T(1,128)} %bitcast.8), calls=%async_computation | async-start | bytes 65536 | tf_op jit(solution)/shard_map/all_to_all | solution.py:173
  37.0 6.8 %copy-start.3 = (bf16[512,128]{1,0:T(8,128)(2,1)S(1)}, bf16[512,128]{1,0:T(8,128)(2,1)}, u32[]{:S(2)}) copy-start(bf16[512,128]{1,0:T(8,128)(2,1)} %param.10) | copy-start | bytes 393220
  37.0 191.1 %all-to-all-start.1 = ((bf16[64,512,128]{2,1,0:T(8,128)(2,1)}), bf16[64,512,128]{2,1,0:T(8,128)(2,1)}, u32[]{:S(2)}, u32[]{:S(2)}) async-start(bf16[64,512,128]{2,1,0:T(8,128)(2,1)} %bitcast.36), calls=%async_computation.1 | async-start | bytes 16777216 | tf_op jit(solution)/shard_map/all_to_all | solution.py:179
  43.7 1.6 copy-start.4
  43.7 184.4 %copy-start.1 = (bf16[8,256,128]{2,1,0:T(8,128)(2,1)S(1)}, bf16[8,256,128]{2,1,0:T(8,128)(2,1)}, u32[]{:S(2)}) copy-start(bf16[8,256,128]{2,1,0:T(8,128)(2,1)} %pad_maximum_fusion.1.src_ref.own_ref) | copy-start | bytes 1572868
  43.7 184.3 %copy-start.2 = (f32[2]{0:T(128)S(1)}, f32[2]{0:T(128)}, u32[]{:S(2)}) copy-start(f32[2]{0:T(128)} %scale_ref.1) | copy-start | bytes 28
  43.8 225.5 %all-gather.2.cloned.1.call-start = ((), (), s32[]{:S(2)}) async-start(), calls=%async_computation.2 | async-start | bytes 1310720 | tf_op jit(solution)/shard_map/all_gather | solution.py:190
Sparse Core Ops, SparseCore 0:
  240.7 28.5 all-gather.1

commit v3 on v1

--- a/solution.py
+++ b/solution.py
@@ -14,13 +14,23 @@
     return (shaped * lax.rsqrt(total + 1e-06)).astype(jnp.bfloat16).reshape(values.shape)
 
 
-def attend_kernel(
-    slot_ref, live_ref, scale_ref, q_ref, own_ref, recv_ref, out_ref, num_scr, den_scr, *, count, slots
-):
+def attend_kernel(slot_ref, live_ref, scale_ref, q_ref, own_ref, recv_ref, out_ref, buf, sems, *, count, slots):
     b = pl.program_id(0)
+    pairs = buf.shape[0]
     feat, lanes = q_ref.shape[1], q_ref.shape[2]
     width = lanes // count
     hd = feat // count
+
+    def pair_copy(p):
+        return pltpu.make_async_copy(recv_ref.at[slot_ref[p]], buf.at[p], sems.at[p])
+
+    @pl.when(b == 0)
+    def _():
+        for p in range(pairs):
+            pair_copy(p).start()
+
+    for s in range(slots):
+        pair_copy(b * slots + s).wait()
     q_stack = q_ref[0]
     row_head = lax.broadcasted_iota(jnp.int32, (feat, width), 0) // hd
     lane_pos = lax.broadcasted_iota(jnp.int32, (1, lanes), 1)
@@ -28,36 +38,25 @@
     for h in range(count):
         inside = (lane_pos >= h * width) & (lane_pos < (h + 1) * width)
         scale_row = jnp.where(inside, scale_ref[h], scale_row)
-
-    def tile(kv):
-        keys = kv[:width]
-        values_t = kv[width:]
-        s = jnp.dot(keys, q_stack, preferred_element_type=jnp.float32)
-        w = jnp.exp(scale_row * (s - 1.0))
-        den = jnp.sum(w, axis=0, keepdims=True).astype(jnp.bfloat16).astype(jnp.float32)
-        w_b = w.astype(jnp.bfloat16)
-        num = jnp.zeros((feat, width), jnp.float32)
-        for h in range(count):
-            part = jnp.dot(values_t, w_b[:, h * width:(h + 1) * width], preferred_element_type=jnp.float32)
-            num = jnp.where(row_head == h, part, num)
-        return num.astype(jnp.bfloat16).astype(jnp.float32), den
-
-    num, den = tile(own_ref[b])
-    num_scr[...] = num
-    den_scr[...] = den
+    key_rows = lax.broadcasted_iota(jnp.int32, ((slots + 1) * width, 1), 0)
+    live_col = jnp.ones(((slots + 1) * width, 1), jnp.float32)
     for s in range(slots):
-        p = b * slots + s
-
-        @pl.when(live_ref[p] > 0)
-        def _():
-            num_s, den_s = tile(recv_ref[slot_ref[p]])
-            num_scr[...] += num_s
-            den_scr[...] += den_s
-
+        inside = (key_rows >= (s + 1) * width) & (key_rows < (s + 2) * width)
+        live_col = jnp.where(inside, live_ref[b * slots + s].astype(jnp.float32), live_col)
+    blocks = [own_ref[b]] + [buf[b * slots + s] for s in range(slots)]
+    keys = jnp.concatenate([blk[:width] for blk in blocks], axis=0)
+    values_t = jnp.concatenate([blk[width:] for blk in blocks], axis=1)
+    s_all = jnp.dot(keys, q_stack, preferred_element_type=jnp.float32)
+    w = jnp.exp(scale_row * (s_all - 1.0)) * live_col
+    den = jnp.sum(w, axis=0, keepdims=True)
+    w_b = w.astype(jnp.bfloat16)
+    num = jnp.zeros((feat, width), jnp.float32)
     den_full = jnp.zeros((feat, width), jnp.float32)
     for h in range(count):
-        den_full = jnp.where(row_head == h, den_scr[:, h * width:(h + 1) * width], den_full)
-    out_ref[0] = (num_scr[...] / den_full).astype(out_ref.dtype)
+        part = jnp.dot(values_t, w_b[:, h * width:(h + 1) * width], preferred_element_type=jnp.float32)
+        num = jnp.where(row_head == h, part, num)
+        den_full = jnp.where(row_head == h, den[:, h * width:(h + 1) * width], den_full)
+    out_ref[0] = (num / den_full).astype(out_ref.dtype)
 
 
 def attend(query_stack, own_kv, recv_kv, slot_of, live, scales):
@@ -65,7 +64,6 @@
     count = scales.shape[0]
     width = lanes // count
     slots = slot_of.shape[0] // nblocks
-    tiles = recv_kv.shape[0]
     grid_spec = pltpu.PrefetchScalarGridSpec(
         num_scalar_prefetch=2,
         grid=(nblocks,),
@@ -73,12 +71,12 @@
             pl.BlockSpec(memory_space=pltpu.SMEM),
             pl.BlockSpec((1, feat, lanes), lambda b, slot_of, live: (b, 0, 0)),
             pl.BlockSpec((nblocks, 2 * width, feat), lambda b, slot_of, live: (0, 0, 0)),
-            pl.BlockSpec((tiles, 2 * width, feat), lambda b, slot_of, live: (0, 0, 0)),
+            pl.BlockSpec(memory_space=pl.ANY),
         ],
         out_specs=pl.BlockSpec((1, feat, width), lambda b, slot_of, live: (b, 0, 0)),
         scratch_shapes=[
-            pltpu.VMEM((feat, width), jnp.float32),
-            pltpu.VMEM((1, lanes), jnp.float32),
+            pltpu.VMEM((nblocks * slots, 2 * width, feat), recv_kv.dtype),
+            pltpu.SemaphoreType.DMA((nblocks * slots,)),
         ],
     )
     return pl.pallas_call(
@@ -147,6 +145,7 @@
     ).reshape(-1)
     payload = gather_blocks(own_kv, jnp.clip(asked, 0, nblocks - 1).astype(jnp.int32))
     w_out, payload = lax.optimization_barrier((w_out, payload))
+    w_out_t = lax.all_gather(w_out.T, "heads", axis=1, tiled=True)
     recv_kv = lax.all_to_all(
         payload.reshape(devices, capacity * 2 * width, feat),
         "nodes",
@@ -154,12 +153,24 @@
         concat_axis=0,
         tiled=True,
     ).reshape(tile_count, 2 * width, feat)
+    recv_kv, w_out_t = lax.optimization_barrier((recv_kv, w_out_t))
     slot_of = jnp.clip(target, 0, tile_count - 1).astype(jnp.int32)
     attn_t = attend(query_stack, own_kv, recv_kv, slot_of, valid, head_scale)
     attn = jnp.swapaxes(attn_t, 1, 2).reshape(rows, feat)
-    attn_all = lax.all_gather(attn, "heads", axis=1, tiled=True)
-    w_cols = lax.dynamic_slice_in_dim(w_out, lax.axis_index("heads") * feat, feat, axis=1)
-    return jnp.dot(attn_all, w_cols, preferred_element_type=jnp.float32).astype(jnp.bfloat16)
+    heads = lax.axis_size("heads")
+    me = lax.axis_index("heads")
+
+    def out_part(piece, source):
+        w_part = lax.dynamic_slice(w_out_t, (me * feat, source * feat), (feat, feat))
+        return lax.dot_general(
+            piece, w_part, (((1,), (1,)), ((), ())), preferred_element_type=jnp.float32
+        )
+
+    mixed = out_part(attn, me)
+    for k in range(1, heads):
+        piece = lax.ppermute(attn, "heads", [(j, (j + k) % heads) for j in range(heads)])
+        mixed = mixed + out_part(piece, (me - k) % heads)
+    return mixed.astype(jnp.bfloat16)
 
 
 def solution(mesh):
@@ -168,7 +179,7 @@
         P(None, "heads"),
         P(None, "heads"),
         P(None, "heads"),
-        P(None, None),
+        P("heads", None),
         P("heads"),
         P("nodes", None),
         P("nodes", None),

time: 294 us -> 250 us (0.85)
  waiting for transfers between devices: 211 us -> 187 us
  between operations: 13.6 us -> 0.27 us
  Pallas kernels: 19 us -> 12.1 us
    all_gather x1 -> x0, waiting for transfers between devices: 27.9 us -> none  [body(): attn_all = lax.all_gather(attn, 'heads', axis=1, tiled=True)]
    unnamed x1 -> x0, blocking collectives: 14 us -> none
    all_gather x0 -> x1, blocking collectives: none -> 13.3 us  [body(): w_out_t = lax.all_gather(w_out.T, 'heads', axis=1, tiled=True)]
    all_to_all x1, waiting for transfers between devices: 183 us -> 170 us  [body(): lax.all_to_all(payload.reshape(devices, capacity * 2 * width, feat), 'nod...]
    ppermute x0 -> x3, waiting for transfers between devices: none -> 13.3 us  [body(): lax.ppermute(attn, 'heads', [(j, (j + k) % heads) for j in range(heads)])]
    pallas_call x1, Pallas kernels: 13.7 us -> 6.78 us  [attend(): pl.pallas_call(functools.partial(attend_kernel, count=count, slots=slots)...]
    ppermute x0 -> x3, starting transfers between devices: none -> 5.3 us  [body(): lax.ppermute(attn, 'heads', [(j, (j + k) % heads) for j in range(heads)])]
    all_to_all x1, waiting for transfers between devices: 0.01 us -> 4.08 us  [body(): lax.all_to_all(request.reshape(devices, capacity), 'nodes', split_axis=0,...]
  transfers between devices with their start and end apart: 3 -> 5, of which waited for: 2 -> 4; matrix products, arithmetic and copies ran while one was open for 2% -> 3% of each run, Pallas kernels for 0% -> 0%
where the time goes in v3:
time: 250 us; the launch traced here: 249 us
  waiting for transfers between devices  187 us (75%)
  starting transfers between devices  24 us (10%)
  blocking collectives  13.3 us (5%)
  Pallas kernels  12.1 us (5%)
  local copies, waits for them, and re-layouts  4.83 us (2%)
  matrix products  4.67 us (2%)
  other arithmetic  2.58 us (1%)
    all_to_all x1, waiting for transfers between devices, body(): lax.all_to_all(payload.reshape(devices, capacity * 2 * width, feat), 'nod...  170 us
    all_gather x1, blocking collectives, body(): w_out_t = lax.all_gather(w_out.T, 'heads', axis=1, tiled=True)  13.3 us
    ppermute x3, waiting for transfers between devices, body(): lax.ppermute(attn, 'heads', [(j, (j + k) % heads) for j in range(heads)])  13.3 us
    all_to_all x1, starting transfers between devices, body(): lax.all_to_all(request.reshape(devices, capacity), 'nodes', split_axis=0,...  12 us
    pallas_call x1, Pallas kernels, attend(): pl.pallas_call(functools.partial(attend_kernel, count=count, slots=slots)...  6.78 us
    all_to_all x1, starting transfers between devices, body(): lax.all_to_all(payload.reshape(devices, capacity * 2 * width, feat), 'nod...  6.69 us
    pallas_call x1, Pallas kernels, gather_blocks(): pl.pallas_call(gather_kernel, grid_spec=grid_spec, out_shape=jax.ShapeDty...  5.35 us
    ppermute x3, starting transfers between devices, body(): lax.ppermute(attn, 'heads', [(j, (j + k) % heads) for j in range(heads)])  5.3 us
  transfers between devices with their start and end apart: 5, of which 4 were waited for; matrix products, arithmetic and copies ran while one was open for 3% of the time, Pallas kernels for 0%

profile of v3, /device:TPU:2, one launch (start us, length us, event | category | flops | bytes accessed | tf_op | source)
XLA Modules:
  0.0 248.7 jit_solution(4195344564541747490)
XLA Ops:
  0.0 0.0 copy-start
  0.0 0.8 copy.34
  0.8 0.1 reshape.111
  0.9 0.1 fusion.9
  1.0 0.1 reduce_window_sum.11
  1.1 0.2 select_reduce_fusion.1
  1.2 0.8 copy.42
  2.0 0.1 reshape.115
  2.1 0.7 compare_convert_fusion
  2.8 0.1 copy.35
  2.9 0.1 reshape.119.live_ref
  3.0 0.1 select_reduce_fusion
  3.1 0.8 sub.30
  3.8 12.0 %all-to-all-start = ((s32[64,1,2]{2,1,0:T(1,128)}), s32[64,1,2]{2,1,0:T(1,128)S(1)}, u32[]{:S(2)}, u32[]{:S(2)}) async-start(s32[64,1,2]{2,1,0:T(1,128)} %bitcast.8), calls=%async_computation | async-start | bytes 65536 | tf_op jit(solution)/shard_map/all_to_all | solution.py:143
  15.8 0.0 copy-done
  15.9 1.3 convolution_convert_fusion
  17.2 0.2 copy.41
  17.4 1.3 fusion.13
  18.7 0.2 copy.39
  18.9 0.1 bitcast_reduce_fusion
  19.1 0.1 copy.46
  19.2 0.2 copy.40
  19.4 0.1 multiply_convert_fusion
  19.5 0.8 pad_maximum_fusion.1.src_ref.own_ref
  20.3 4.1 %all-to-all-done = s32[64,1,2]{2,1,0:T(1,128)S(1)} async-done(((s32[64,1,2]{2,1,0:T(1,128)}), s32[64,1,2]{2,1,0:T(1,128)S(1)}, u32[]{:S(2)}, u32[]{:S(2)}) %all-to-all-start) | async-done | bytes 544 | tf_op jit(solution)/shard_map/all_to_all | solution.py:143
  24.4 0.1 clamp_reduce_fusion
  24.5 0.7 min.22.pick_ref
  25.1 5.3 %shard_map.91 = bf16[128,256,128]{2,1,0:T(8,128)(2,1)} custom-call(s32[128]{0:T(128)} %min.22.pick_ref, bf16[8,256,128]{2,1,0:T(8,128)(2,1)} %pad_maximum_fusion.1.src_ref.own_ref), custom_call_target="tpu_custom_call" | custom-call | tf_op jit(solution)/shard_map/pallas_call | solution.py:107
  30.5 0.0 copy-start.3
  30.5 6.7 %all-to-all-start.1 = ((bf16[64,512,128]{2,1,0:T(8,128)(2,1)}), bf16[64,512,128]{2,1,0:T(8,128)(2,1)}, u32[]{:S(2)}, u32[]{:S(2)}) async-start(bf16[64,512,128]{2,1,0:T(8,128)(2,1)} %bitcast.39), calls=%async_computation.1 | async-start | bytes 16777216 | tf_op jit(solution)/shard_map/all_to_all | solution.py:149
  37.2 0.0 copy-done.3
  37.2 0.0 copy-start.4
  37.2 0.0 copy-start.1
  37.2 0.0 copy-start.2
  37.2 0.4 fusion.12
  37.7 0.2 copy.37
  37.9 0.2 copy.36
  38.1 0.1 bitcast_reduce_fusion.1
  38.2 0.1 copy.45
  38.3 0.2 select_bitcast_fusion.1
  38.5 0.1 select_bitcast_fusion
  38.6 0.1 pad_maximum_fusion.q_ref
  38.7 0.0 copy-done.4
  38.7 13.3 %all_gather.3 = bf16[512,512]{0,1:T(8,128)(2,1)S(1)} all-gather(bf16[512,128]{0,1:T(8,128)(2,1)S(1)} %bitcast.52), channel_id=1, replica_groups=mesh['nodes'=64,'heads'=4] {'heads'}, dimensions={1}, use_global_device_ids=true | all-gather | bytes 655360 | tf_op jit(solution)/shard_map/all_gather | solution.py:148
  52.0 169.5 %all-to-all-done.1 = bf16[64,512,128]{2,1,0:T(8,128)(2,1)} async-done(((bf16[64,512,128]{2,1,0:T(8,128)(2,1)}), bf16[64,512,128]{2,1,0:T(8,128)(2,1)}, u32[]{:S(2)}, u32[]{:S(2)}) %all-to-all-start.1) | async-done | bytes 8388640 | tf_op jit(solution)/shard_map/all_to_all | solution.py:149
  221.5 0.0 copy-done.1
  221.5 0.0 copy-done.2
  221.5 6.8 %shard_map.92 = bf16[8,128,128]{2,1,0:T(8,128)(2,1)S(1)} custom-call(s32[32]{0:T(128)S(1)} %get-tuple-element.15.slot_ref, s32[32]{0:T(128)S(1)} %reshape.119.live_ref, f32[2]{0:T(128)S(1)} %copy-done.2, bf16[8,128,256]{2,1,0:T(8,128)(2,1)S(1)} %pad_maximum_fusion.q_ref, bf16[8,256,128]{2,1,0:T(8,128)(2,1)S(1)} %copy-done.1, ...), custom_call_target="tpu_custom_call" | custom-call | tf_op jit(solution)/shard_map/pallas_call | solution.py:82
  228.3 0.2 copy.44
  228.5 3.1 %collective-permute-start.2 = (bf16[1024,128]{1,0:T(8,128)(2,1)S(1)}, bf16[1024,128]{1,0:T(8,128)(2,1)S(1)}, u32[]{:S(2)}, u32[]{:S(2)}) collective-permute-start(bf16[1024,128]{1,0:T(8,128)(2,1)S(1)} %bitcast.46), channel_id=1, source_target_pairs={{0,3},{1,0},{2,1},{3,2},{4,7},{5,4},{6,5},{7,6},{8,11},{9,8},{10,9... | collective-permute-start | bytes 786440 | tf_op jit(solution)/shard_map/ppermute | solution.py:171
  231.6 0.0 collective-permute-start
  231.6 2.2 collective-permute-start.1
  233.8 0.2 fusion.7
  234.0 9.4 %collective-permute-done.2 = bf16[1024,128]{1,0:T(8,128)(2,1)S(1)} collective-permute-done((bf16[1024,128]{1,0:T(8,128)(2,1)S(1)}, bf16[1024,128]{1,0:T(8,128)(2,1)S(1)}, u32[]{:S(2)}, u32[]{:S(2)}) %collective-permute-start.2) | collective-permute-done | bytes 262176 | tf_op jit(solution)/shard_map/ppermute | solution.py:171
  243.5 0.2 fusion.3
  243.7 3.8 %collective-permute-done = bf16[1024,128]{1,0:T(8,128)(2,1)S(1)} collective-permute-done((bf16[1024,128]{1,0:T(8,128)(2,1)S(1)}, bf16[1024,128]{1,0:T(8,128)(2,1)S(1)}, u32[]{:S(2)}, u32[]{:S(2)}) %collective-permute-start) | collective-permute-done | bytes 262176 | tf_op jit(solution)/shard_map/ppermute | solution.py:171
  247.5 0.2 convolution_add_fusion.1
  247.7 0.0 collective-permute-done.1
  247.7 0.9 fusion.1
  (8 shorter events, 0.1 us)
Async XLA Ops:
  0.0 15.8 %copy-start = (bf16[1024,512]{1,0:T(8,128)(2,1)S(1)}, bf16[1024,512]{1,0:T(8,128)(2,1)}, u32[]{:S(2)}) copy-start(bf16[1024,512]{1,0:T(8,128)(2,1)} %param.9) | copy-start | bytes 3145732
  3.8 20.5 %all-to-all-start = ((s32[64,1,2]{2,1,0:T(1,128)}), s32[64,1,2]{2,1,0:T(1,128)S(1)}, u32[]{:S(2)}, u32[]{:S(2)}) async-start(s32[64,1,2]{2,1,0:T(1,128)} %bitcast.8), calls=%async_computation | async-start | bytes 65536 | tf_op jit(solution)/shard_map/all_to_all | solution.py:143
  30.5 6.7 %copy-start.3 = (bf16[512,128]{1,0:T(8,128)(2,1)S(1)}, bf16[512,128]{1,0:T(8,128)(2,1)}, u32[]{:S(2)}) copy-start(bf16[512,128]{1,0:T(8,128)(2,1)} %param.10) | copy-start | bytes 393220
  30.5 191.1 %all-to-all-start.1 = ((bf16[64,512,128]{2,1,0:T(8,128)(2,1)}), bf16[64,512,128]{2,1,0:T(8,128)(2,1)}, u32[]{:S(2)}, u32[]{:S(2)}) async-start(bf16[64,512,128]{2,1,0:T(8,128)(2,1)} %bitcast.39), calls=%async_computation.1 | async-start | bytes 16777216 | tf_op jit(solution)/shard_map/all_to_all | solution.py:149
  37.2 1.5 copy-start.4
  37.2 184.3 %copy-start.1 = (bf16[8,256,128]{2,1,0:T(8,128)(2,1)S(1)}, bf16[8,256,128]{2,1,0:T(8,128)(2,1)}, u32[]{:S(2)}) copy-start(bf16[8,256,128]{2,1,0:T(8,128)(2,1)} %pad_maximum_fusion.1.src_ref.own_ref) | copy-start | bytes 1572868
  37.2 184.3 %copy-start.2 = (f32[2]{0:T(128)S(1)}, f32[2]{0:T(128)}, u32[]{:S(2)}) copy-start(f32[2]{0:T(128)} %scale_ref.1) | copy-start | bytes 28
  228.5 15.0 %collective-permute-start.2 = (bf16[1024,128]{1,0:T(8,128)(2,1)S(1)}, bf16[1024,128]{1,0:T(8,128)(2,1)S(1)}, u32[]{:S(2)}, u32[]{:S(2)}) collective-permute-start(bf16[1024,128]{1,0:T(8,128)(2,1)S(1)} %bitcast.46), channel_id=1, source_target_pairs={{0,3},{1,0},{2,1},{3,2},{4,7},{5,4},{6,5},{7,6},{8,11},{9,8},{10,9... | collective-permute-start | bytes 786440 | tf_op jit(solution)/shard_map/ppermute | solution.py:171
  231.6 15.9 %collective-permute-start = (bf16[1024,128]{1,0:T(8,128)(2,1)S(1)}, bf16[1024,128]{1,0:T(8,128)(2,1)S(1)}, u32[]{:S(2)}, u32[]{:S(2)}) collective-permute-start(bf16[1024,128]{1,0:T(8,128)(2,1)S(1)} %bitcast.47), channel_id=1, source_target_pairs={{0,1},{1,2},{2,3},{3,0},{4,5},{5,6},{6,7},{7,4},{8,9},{9,10},{10,1... | collective-permute-start | bytes 786440 | tf_op jit(solution)/shard_map/ppermute | solution.py:171
  231.6 16.1 %collective-permute-start.1 = (bf16[1024,128]{1,0:T(8,128)(2,1)S(1)}, bf16[1024,128]{1,0:T(8,128)(2,1)S(1)}, u32[]{:S(2)}, u32[]{:S(2)}) collective-permute-start(bf16[1024,128]{1,0:T(8,128)(2,1)S(1)} %bitcast.48), channel_id=1, source_target_pairs={{0,2},{1,3},{2,0},{3,1},{4,6},{5,7},{6,4},{7,5},{8,10},{9,11},{10,... | collective-permute-start | bytes 786440 | tf_op jit(solution)/shard_map/ppermute | solution.py:171

commit v4 on v3

--- a/solution.py
+++ b/solution.py
@@ -27,10 +27,20 @@
     @pl.when(b == 0)
     def _():
         for p in range(pairs):
-            pair_copy(p).start()
+
+            @pl.when(live_ref[p] > 0)
+            def _():
+                pair_copy(p).start()
+
+            @pl.when(live_ref[p] == 0)
+            def _():
+                buf[p] = jnp.zeros(buf.shape[1:], buf.dtype)
 
     for s in range(slots):
-        pair_copy(b * slots + s).wait()
+
+        @pl.when(live_ref[b * slots + s] > 0)
+        def _():
+            pair_copy(b * slots + s).wait()
     q_stack = q_ref[0]
     row_head = lax.broadcasted_iota(jnp.int32, (feat, width), 0) // hd
     lane_pos = lax.broadcasted_iota(jnp.int32, (1, lanes), 1)
@@ -87,27 +97,38 @@
     )(slot_of, live, scales, query_stack, own_kv, recv_kv)
 
 
-def gather_kernel(pick_ref, src_ref, out_ref):
-    g = pl.program_id(0)
-    group = out_ref.shape[0]
-    for i in range(group):
-        out_ref[i] = src_ref[pick_ref[g * group + i]]
+def gather_kernel(pick_ref, src_ref, out_ref, sems):
+    tiles = out_ref.shape[0]
+
+    def slot_copy(c):
+        return pltpu.make_async_copy(src_ref.at[pick_ref[c]], out_ref.at[c], sems.at[c])
+
+    for c in range(tiles):
+
+        @pl.when(pick_ref[c] >= 0)
+        def _():
+            slot_copy(c).start()
+
+    for c in range(tiles):
+
+        @pl.when(pick_ref[c] >= 0)
+        def _():
+            slot_copy(c).wait()
 
 
 def gather_blocks(blocks, pick):
-    nblocks, r, l = blocks.shape
     tiles = pick.shape[0]
-    group = 32
     grid_spec = pltpu.PrefetchScalarGridSpec(
         num_scalar_prefetch=1,
-        grid=(tiles // group,),
-        in_specs=[pl.BlockSpec((nblocks, r, l), lambda g, pick: (0, 0, 0))],
-        out_specs=pl.BlockSpec((group, r, l), lambda g, pick: (g, 0, 0)),
+        grid=(1,),
+        in_specs=[pl.BlockSpec(memory_space=pl.ANY)],
+        out_specs=pl.BlockSpec(memory_space=pl.ANY),
+        scratch_shapes=[pltpu.SemaphoreType.DMA((tiles,))],
     )
     return pl.pallas_call(
         gather_kernel,
         grid_spec=grid_spec,
-        out_shape=jax.ShapeDtypeStruct((tiles, r, l), blocks.dtype),
+        out_shape=jax.ShapeDtypeStruct((tiles,) + blocks.shape[1:], blocks.dtype),
     )(pick, blocks)
 
 
@@ -143,7 +164,7 @@
     asked = lax.all_to_all(
         request.reshape(devices, capacity), "nodes", split_axis=0, concat_axis=0, tiled=True
     ).reshape(-1)
-    payload = gather_blocks(own_kv, jnp.clip(asked, 0, nblocks - 1).astype(jnp.int32))
+    payload = gather_blocks(own_kv, jnp.clip(asked, -1, nblocks - 1).astype(jnp.int32))
     w_out, payload = lax.optimization_barrier((w_out, payload))
     w_out_t = lax.all_gather(w_out.T, "heads", axis=1, tiled=True)
     recv_kv = lax.all_to_all(
@@ -166,10 +187,12 @@
             piece, w_part, (((1,), (1,)), ((), ())), preferred_element_type=jnp.float32
         )
 
-    mixed = out_part(attn, me)
+    pieces = lax.all_to_all(
+        jnp.broadcast_to(attn[None], (heads,) + attn.shape), "heads", 0, 0, tiled=False
+    )
+    mixed = out_part(pieces[0], 0)
     for k in range(1, heads):
-        piece = lax.ppermute(attn, "heads", [(j, (j + k) % heads) for j in range(heads)])
-        mixed = mixed + out_part(piece, (me - k) % heads)
+        mixed = mixed + out_part(pieces[k], k)
     return mixed.astype(jnp.bfloat16)
 
 

time: 250 us -> 446 us (1.78)
  starting transfers between devices: 24 us -> 188 us
  Pallas kernels: 12.1 us -> 43.6 us
    all_to_all x1, starting transfers between devices: 6.69 us -> 171 us  [body(): lax.all_to_all(payload.reshape(devices, capacity * 2 * width, feat), 'nod...]
    pallas_call x1, Pallas kernels: 5.35 us -> 36.7 us  [gather_blocks(): pl.pallas_call(gather_kernel, grid_spec=grid_spec, out_shape=jax.ShapeDty...]
    all_to_all x0 -> x1, waiting for transfers between devices: none -> 16.4 us  [body(): lax.all_to_all(jnp.broadcast_to(attn[None], (heads,) + attn.shape), 'head...]
    ppermute x3 -> x0, waiting for transfers between devices: 13.3 us -> none  [body(): lax.ppermute(attn, 'heads', [(j, (j + k) % heads) for j in range(heads)])]
    ppermute x3 -> x0, starting transfers between devices: 5.3 us -> none  [body(): lax.ppermute(attn, 'heads', [(j, (j + k) % heads) for j in range(heads)])]
    all_to_all x0 -> x1, starting transfers between devices: none -> 4.47 us  [body(): lax.all_to_all(jnp.broadcast_to(attn[None], (heads,) + attn.shape), 'head...]
  transfers between devices with their start and end apart: 5 -> 3, of which waited for: 4 -> 3; matrix products, arithmetic and copies ran while one was open for 3% -> 1% of each run, Pallas kernels for 0% -> 0%
where the time goes in v4:
time: 446 us; the launch traced here: 448 us
  waiting for transfers between devices  190 us (43%)
  starting transfers between devices  188 us (42%)
  Pallas kernels  43.6 us (10%)
  blocking collectives  13.3 us (3%)
  local copies, waits for them, and re-layouts  5.95 us (1%)
  matrix products  4.68 us (1%)
    all_to_all x1, starting transfers between devices, body(): lax.all_to_all(payload.reshape(devices, capacity * 2 * width, feat), 'nod...  171 us
    all_to_all x1, waiting for transfers between devices, body(): lax.all_to_all(payload.reshape(devices, capacity * 2 * width, feat), 'nod...  170 us
    pallas_call x1, Pallas kernels, gather_blocks(): pl.pallas_call(gather_kernel, grid_spec=grid_spec, out_shape=jax.ShapeDty...  36.7 us
    all_to_all x1, waiting for transfers between devices, body(): lax.all_to_all(jnp.broadcast_to(attn[None], (heads,) + attn.shape), 'head...  16.4 us
    all_gather x1, blocking collectives, body(): w_out_t = lax.all_gather(w_out.T, 'heads', axis=1, tiled=True)  13.3 us
    all_to_all x1, starting transfers between devices, body(): lax.all_to_all(request.reshape(devices, capacity), 'nodes', split_axis=0,...  12 us
  transfers between devices with their start and end apart: 3, of which 3 were waited for; matrix products, arithmetic and copies ran while one was open for 1% of the time, Pallas kernels for 0%

profile of v4, /device:TPU:2, one launch (start us, length us, event | category | flops | bytes accessed | tf_op | source)
XLA Modules:
  0.0 448.3 jit_solution(13301612913911710117)
XLA Ops:
  0.0 0.0 copy-start
  0.0 0.8 copy.34
  0.8 0.1 reshape.109
  0.9 0.1 fusion.7
  1.0 0.1 reduce_window_sum.11
  1.1 0.2 select_reduce_fusion.1
  1.2 0.7 compare_convert_fusion
  1.9 0.1 copy.35
  2.0 0.1 reshape.116.live_ref
  2.1 0.8 copy.42
  2.9 0.1 reshape.113
  3.0 0.1 select_reduce_fusion
  3.1 0.8 sub.21
  3.8 12.0 %all-to-all-start = ((s32[64,1,2]{2,1,0:T(1,128)}), s32[64,1,2]{2,1,0:T(1,128)S(1)}, u32[]{:S(2)}, u32[]{:S(2)}) async-start(s32[64,1,2]{2,1,0:T(1,128)} %bitcast.8), calls=%async_computation | async-start | bytes 65536 | tf_op jit(solution)/shard_map/all_to_all | solution.py:164
  15.8 0.0 copy-done
  15.9 1.3 fusion.15
  17.2 0.2 copy.39
  17.4 0.1 bitcast_reduce_fusion
  17.5 0.1 copy.46
  17.6 0.2 copy.40
  17.9 1.3 convolution_convert_fusion
  19.2 0.2 copy.41
  19.4 0.1 multiply_convert_fusion
  19.5 0.8 pad_maximum_fusion.1.src_ref.own_ref
  20.3 4.1 all-to-all-done
  24.4 0.1 clamp_reduce_fusion
  24.5 0.7 min.22.pick_ref
  25.1 36.7 %shard_map.91 = bf16[128,256,128]{2,1,0:T(8,128)(2,1)} custom-call(s32[128]{0:T(128)} %min.22.pick_ref, bf16[8,256,128]{2,1,0:T(8,128)(2,1)} %pad_maximum_fusion.1.src_ref.own_ref), custom_call_target="tpu_custom_call" | custom-call | tf_op jit(solution)/shard_map/pallas_call | solution.py:128
  61.8 0.0 copy-start.3
  61.8 171.5 %all-to-all-start.1 = ((bf16[64,512,128]{2,1,0:T(8,128)(2,1)}), bf16[64,512,128]{2,1,0:T(8,128)(2,1)}, u32[]{:S(2)}, u32[]{:S(2)}) async-start(bf16[64,512,128]{2,1,0:T(8,128)(2,1)} %bitcast.47), calls=%async_computation.1 | async-start | bytes 16777216 | tf_op jit(solution)/shard_map/all_to_all | solution.py:170
  233.3 0.0 copy-done.3
  233.3 0.0 copy-start.4
  233.3 0.0 copy-start.1
  233.3 0.0 copy-start.2
  233.3 0.4 fusion.14
  233.8 0.2 copy.36
  234.1 0.1 copy.45
  234.2 0.2 copy.37
  234.4 0.2 select_bitcast_fusion.1
  234.6 0.1 select_bitcast_fusion
  234.7 0.1 pad_maximum_fusion.q_ref
  234.8 0.0 copy-done.4
  234.8 13.3 %all_gather.3 = bf16[512,512]{0,1:T(8,128)(2,1)S(1)} all-gather(bf16[512,128]{0,1:T(8,128)(2,1)S(1)} %bitcast.57), channel_id=1, replica_groups=mesh['nodes'=64,'heads'=4] {'heads'}, dimensions={1}, use_global_device_ids=true | all-gather | bytes 655360 | tf_op jit(solution)/shard_map/all_gather | solution.py:169
  248.1 169.5 %all-to-all-done.1 = bf16[64,512,128]{2,1,0:T(8,128)(2,1)} async-done(((bf16[64,512,128]{2,1,0:T(8,128)(2,1)}), bf16[64,512,128]{2,1,0:T(8,128)(2,1)}, u32[]{:S(2)}, u32[]{:S(2)}) %all-to-all-start.1) | async-done | bytes 8388640 | tf_op jit(solution)/shard_map/all_to_all | solution.py:170
  417.7 0.0 copy-done.1
  417.7 0.0 copy-done.2
  417.7 6.9 %shard_map.92 = bf16[8,128,128]{2,1,0:T(8,128)(2,1)S(1)} custom-call(s32[32]{0:T(128)S(1)} %get-tuple-element.15.slot_ref, s32[32]{0:T(128)S(1)} %reshape.116.live_ref, f32[2]{0:T(128)S(1)} %copy-done.2, bf16[8,128,256]{2,1,0:T(8,128)(2,1)S(1)} %pad_maximum_fusion.q_ref, bf16[8,256,128]{2,1,0:T(8,128)(2,1)S(1)} %copy-done.1, ...), custom_call_target="tpu_custom_call" | custom-call | tf_op jit(solution)/shard_map/pallas_call | solution.py:92
  424.6 0.2 copy.44
  424.7 1.1 broadcast_in_dim.39
  425.9 4.5 all-to-all-start.2
  430.3 16.4 %all-to-all-done.2 = bf16[4,1024,128]{2,1,0:T(8,128)(2,1)S(1)} async-done(((bf16[4,1024,128]{2,1,0:T(8,128)(2,1)}), bf16[4,1024,128]{2,1,0:T(8,128)(2,1)S(1)}, u32[]{:S(2)}, u32[]{:S(2)}) %all-to-all-start.2) | async-done | bytes 1048608 | tf_op jit(solution)/shard_map/all_to_all | solution.py:190
  446.7 0.2 fusion.2
  446.9 0.2 convolution_add_fusion.2
  447.2 0.2 convolution_add_fusion.1
  447.4 0.9 fusion
  (9 shorter events, 0.2 us)
Async XLA Ops:
  0.0 15.8 %copy-start = (bf16[1024,512]{1,0:T(8,128)(2,1)S(1)}, bf16[1024,512]{1,0:T(8,128)(2,1)}, u32[]{:S(2)}) copy-start(bf16[1024,512]{1,0:T(8,128)(2,1)} %param.9) | copy-start | bytes 3145732
  3.8 20.5 %all-to-all-start = ((s32[64,1,2]{2,1,0:T(1,128)}), s32[64,1,2]{2,1,0:T(1,128)S(1)}, u32[]{:S(2)}, u32[]{:S(2)}) async-start(s32[64,1,2]{2,1,0:T(1,128)} %bitcast.8), calls=%async_computation | async-start | bytes 65536 | tf_op jit(solution)/shard_map/all_to_all | solution.py:164
  61.8 171.5 %copy-start.3 = (bf16[512,128]{1,0:T(8,128)(2,1)S(1)}, bf16[512,128]{1,0:T(8,128)(2,1)}, u32[]{:S(2)}) copy-start(bf16[512,128]{1,0:T(8,128)(2,1)} %param.10) | copy-start | bytes 393220
  61.8 355.8 %all-to-all-start.1 = ((bf16[64,512,128]{2,1,0:T(8,128)(2,1)}), bf16[64,512,128]{2,1,0:T(8,128)(2,1)}, u32[]{:S(2)}, u32[]{:S(2)}) async-start(bf16[64,512,128]{2,1,0:T(8,128)(2,1)} %bitcast.47), calls=%async_computation.1 | async-start | bytes 16777216 | tf_op jit(solution)/shard_map/all_to_all | solution.py:170
  233.3 1.5 copy-start.4
  233.3 184.3 %copy-start.1 = (bf16[8,256,128]{2,1,0:T(8,128)(2,1)S(1)}, bf16[8,256,128]{2,1,0:T(8,128)(2,1)}, u32[]{:S(2)}) copy-start(bf16[8,256,128]{2,1,0:T(8,128)(2,1)} %pad_maximum_fusion.1.src_ref.own_ref) | copy-start | bytes 1572868
  233.3 184.3 %copy-start.2 = (f32[2]{0:T(128)S(1)}, f32[2]{0:T(128)}, u32[]{:S(2)}) copy-start(f32[2]{0:T(128)} %scale_ref.1) | copy-start | bytes 28
  425.9 20.9 %all-to-all-start.2 = ((bf16[4,1024,128]{2,1,0:T(8,128)(2,1)}), bf16[4,1024,128]{2,1,0:T(8,128)(2,1)S(1)}, u32[]{:S(2)}, u32[]{:S(2)}) async-start(bf16[4,1024,128]{2,1,0:T(8,128)(2,1)} %broadcast_in_dim.39), calls=%async_computation.2 | async-start | bytes 2097152 | tf_op jit(solution)/shard_map/all_to_all | solution.py:190

commit v5 on v3

--- a/solution.py
+++ b/solution.py
@@ -132,16 +132,22 @@
         [key_n.reshape(nblocks, width, feat), jnp.swapaxes(value_b.reshape(nblocks, width, feat), 1, 2)],
         axis=1,
     )
+    me = lax.axis_index("nodes")
     owners = nbr_owner.reshape(-1)
-    owner_hot = (owners[:, None] == jnp.arange(devices, dtype=jnp.int32)[None, :]).astype(jnp.int32)
+    valid = (slot_valid.reshape(-1) > 0).astype(jnp.int32)
+    owner_hot = (
+        (owners[:, None] == jnp.arange(devices, dtype=jnp.int32)[None, :]) & (valid[:, None] > 0)
+    ).astype(jnp.int32)
     rank = jnp.sum(jnp.cumsum(owner_hot, axis=0) * owner_hot, axis=1) - 1
-    target = owners * capacity + rank
-    place = (target[:, None] == jnp.arange(tile_count, dtype=jnp.int32)[None, :]).astype(jnp.int32)
-    valid = (slot_valid.reshape(-1) > 0).astype(jnp.int32)
-    wanted = jnp.where(valid > 0, nbr_local.reshape(-1), -1)
-    request = jnp.sum(place * (wanted[:, None] + 1), axis=0) - 1
-    asked = lax.all_to_all(
-        request.reshape(devices, capacity), "nodes", split_axis=0, concat_axis=0, tiled=True
+    target = jnp.where(valid > 0, owners * capacity + rank, 0)
+    code = jnp.where(slot_valid > 0, nbr_owner * nblocks + nbr_local, -1)
+    every = lax.all_gather(code.reshape(1, nblocks * slots), "nodes", axis=0, tiled=True)
+    mine = ((every >= 0) & (every // nblocks == me)).astype(jnp.int32)
+    their_rank = jnp.cumsum(mine, axis=1) - 1
+    local_plus = every - me * nblocks + 1
+    asked = jnp.stack(
+        [jnp.sum(mine * (their_rank == r) * local_plus, axis=1) - 1 for r in range(capacity)],
+        axis=1,
     ).reshape(-1)
     payload = gather_blocks(own_kv, jnp.clip(asked, 0, nblocks - 1).astype(jnp.int32))
     w_out, payload = lax.optimization_barrier((w_out, payload))

time: 250 us -> 274 us (1.096)
  blocking collectives: 13.3 us -> 55.5 us
  starting transfers between devices: 24 us -> 12.8 us
  waiting for transfers between devices: 187 us -> 182 us
    all_gather x0 -> x1, blocking collectives: none -> 42.2 us  [body(): lax.all_gather(code.reshape(1, nblocks * slots), 'nodes', axis=0, tiled=T...]
    all_to_all x1 -> x0, starting transfers between devices: 12 us -> none  [body(): lax.all_to_all(request.reshape(devices, capacity), 'nodes', split_axis=0,...]
    all_to_all x1 -> x0, waiting for transfers between devices: 4.08 us -> none  [body(): lax.all_to_all(request.reshape(devices, capacity), 'nodes', split_axis=0,...]
  transfers between devices with their start and end apart: 5 -> 4, of which waited for: 4 -> 3; matrix products, arithmetic and copies ran while one was open for 3% -> 1% of each run, Pallas kernels for 0% -> 0%
where the time goes in v5:
time: 274 us; the launch traced here: 273 us
  waiting for transfers between devices  182 us (66%)
  blocking collectives  55.5 us (20%)
  starting transfers between devices  12.8 us (5%)
  Pallas kernels  12.1 us (4%)
  matrix products  4.67 us (2%)
  other arithmetic  2.87 us (1%)
    all_to_all x1, waiting for transfers between devices, body(): lax.all_to_all(payload.reshape(devices, capacity * 2 * width, feat), 'nod...  169 us
    all_gather x1, blocking collectives, body(): lax.all_gather(code.reshape(1, nblocks * slots), 'nodes', axis=0, tiled=T...  42.2 us
    all_gather x1, blocking collectives, body(): w_out_t = lax.all_gather(w_out.T, 'heads', axis=1, tiled=True)  13.3 us
    ppermute x3, waiting for transfers between devices, body(): lax.ppermute(attn, 'heads', [(j, (j + k) % heads) for j in range(heads)])  13.3 us
    all_to_all x1, starting transfers between devices, body(): lax.all_to_all(payload.reshape(devices, capacity * 2 * width, feat), 'nod...  7.53 us
    pallas_call x1, Pallas kernels, attend(): pl.pallas_call(functools.partial(attend_kernel, count=count, slots=slots)...  6.75 us
  transfers between devices with their start and end apart: 4, of which 3 were waited for; matrix products, arithmetic and copies ran while one was open for 1% of the time, Pallas kernels for 0%

profile of v5, /device:TPU:2, one launch (start us, length us, event | category | flops | bytes accessed | tf_op | source)
XLA Modules:
  0.0 273.1 jit_solution(5491936806721091434)
XLA Ops:
  0.0 0.0 copy-start
  0.0 0.8 add_select_fusion.1
  0.8 0.1 copy.35
  0.9 0.1 reshape.106
  1.0 42.2 %all-gather = s32[64,1,32]{2,1,0:T(1,128)S(1)} all-gather(s32[1,1,32]{2,1,0:T(1,128)S(1)} %reshape.106), channel_id=1, replica_groups=mesh['nodes'=64,'heads'=4] {'nodes'}, dimensions={0}, use_global_device_ids=true | all-gather | bytes 8320 | tf_op jit(solution)/shard_map/all_gather | solution.py:144
  43.2 0.2 reduce_window_sum.23
  43.4 0.1 multiply_reduce_fusion.1
  43.6 0.1 copy.36
  43.7 0.7 min.22.pick_ref
  44.3 0.0 copy-done
  44.3 1.3 fusion.16
  45.7 0.2 copy.32
  46.0 0.1 copy.39
  46.1 0.2 copy.33
  46.3 1.3 convolution_convert_fusion
  47.7 0.2 copy.34
  47.9 0.1 multiply_convert_fusion
  47.9 0.8 pad_maximum_fusion.1.src_ref.own_ref
  48.8 5.3 %shard_map.91 = bf16[128,256,128]{2,1,0:T(8,128)(2,1)} custom-call(s32[128]{0:T(128)} %min.22.pick_ref, bf16[8,256,128]{2,1,0:T(8,128)(2,1)} %pad_maximum_fusion.1.src_ref.own_ref), custom_call_target="tpu_custom_call" | custom-call | tf_op jit(solution)/shard_map/pallas_call | solution.py:107
  54.1 0.0 copy-start.5
  54.1 0.0 copy-start.3
  54.1 7.5 %all-to-all-start = ((bf16[64,512,128]{2,1,0:T(8,128)(2,1)}), bf16[64,512,128]{2,1,0:T(8,128)(2,1)}, u32[]{:S(2)}, u32[]{:S(2)}) async-start(bf16[64,512,128]{2,1,0:T(8,128)(2,1)} %bitcast.43), calls=%async_computation | async-start | bytes 16777216 | tf_op jit(solution)/shard_map/all_to_all | solution.py:155
  61.6 0.0 copy-done.5
  61.7 0.0 copy-start.4
  61.7 0.0 copy-start.1
  61.7 0.0 copy-start.2
  61.7 0.1 copy.28
  61.8 0.1 copy.27
  61.9 0.1 reshape.105.live_ref
  61.9 0.1 reshape.97
  62.0 0.1 fusion.13
  62.1 0.1 reduce_window_sum.22
  62.2 0.0 copy-done.3
  62.2 0.4 fusion.15
  62.6 0.2 copy.29
  62.8 0.1 bitcast_reduce_fusion.1
  62.9 0.1 copy.38
  63.0 0.2 copy.30
  63.3 0.2 select_reduce_fusion
  63.4 0.2 select_bitcast_fusion.1
  63.6 0.1 select_bitcast_fusion
  63.7 0.1 pad_maximum_fusion.q_ref
  63.8 0.0 copy-done.4
  63.8 13.3 %all_gather.7 = bf16[512,512]{0,1:T(8,128)(2,1)S(1)} all-gather(bf16[512,128]{0,1:T(8,128)(2,1)S(1)} %bitcast.58), channel_id=1, replica_groups=mesh['nodes'=64,'heads'=4] {'heads'}, dimensions={1}, use_global_device_ids=true | all-gather | bytes 655360 | tf_op jit(solution)/shard_map/all_gather | solution.py:154
  77.1 168.9 %all-to-all-done = bf16[64,512,128]{2,1,0:T(8,128)(2,1)} async-done(((bf16[64,512,128]{2,1,0:T(8,128)(2,1)}), bf16[64,512,128]{2,1,0:T(8,128)(2,1)}, u32[]{:S(2)}, u32[]{:S(2)}) %all-to-all-start) | async-done | bytes 8388640 | tf_op jit(solution)/shard_map/all_to_all | solution.py:155
  246.0 0.0 copy-done.1
  246.0 0.0 copy-done.2
  246.0 6.8 %shard_map.92 = bf16[8,128,128]{2,1,0:T(8,128)(2,1)S(1)} custom-call(s32[32]{0:T(128)S(1)} %select_clamp_fusion.slot_ref, s32[32]{0:T(128)S(1)} %reshape.105.live_ref, f32[2]{0:T(128)S(1)} %copy-done.2, bf16[8,128,256]{2,1,0:T(8,128)(2,1)S(1)} %pad_maximum_fusion.q_ref, bf16[8,256,128]{2,1,0:T(8,128)(2,1)S(1)} %copy-done.1, ...), custom_call_target="tpu_custom_call" | custom-call | tf_op jit(solution)/shard_map/pallas_call | solution.py:82
  252.8 0.2 copy.37
  252.9 3.1 %collective-permute-start.2 = (bf16[1024,128]{1,0:T(8,128)(2,1)S(1)}, bf16[1024,128]{1,0:T(8,128)(2,1)S(1)}, u32[]{:S(2)}, u32[]{:S(2)}) collective-permute-start(bf16[1024,128]{1,0:T(8,128)(2,1)S(1)} %bitcast.50), channel_id=1, source_target_pairs={{0,3},{1,0},{2,1},{3,2},{4,7},{5,4},{6,5},{7,6},{8,11},{9,8},{10,9... | collective-permute-start | bytes 786440 | tf_op jit(solution)/shard_map/ppermute | solution.py:177
  256.0 0.0 collective-permute-start
  256.0 2.2 collective-permute-start.1
  258.2 0.2 fusion.9
  258.5 9.4 %collective-permute-done.2 = bf16[1024,128]{1,0:T(8,128)(2,1)S(1)} collective-permute-done((bf16[1024,128]{1,0:T(8,128)(2,1)S(1)}, bf16[1024,128]{1,0:T(8,128)(2,1)S(1)}, u32[]{:S(2)}, u32[]{:S(2)}) %collective-permute-start.2) | collective-permute-done | bytes 262176 | tf_op jit(solution)/shard_map/ppermute | solution.py:177
  267.9 0.2 fusion.5
  268.1 3.8 %collective-permute-done = bf16[1024,128]{1,0:T(8,128)(2,1)S(1)} collective-permute-done((bf16[1024,128]{1,0:T(8,128)(2,1)S(1)}, bf16[1024,128]{1,0:T(8,128)(2,1)S(1)}, u32[]{:S(2)}, u32[]{:S(2)}) %collective-permute-start) | collective-permute-done | bytes 262176 | tf_op jit(solution)/shard_map/ppermute | solution.py:177
  271.9 0.2 convolution_add_fusion.1
  272.2 0.0 collective-permute-done.1
  272.2 0.9 fusion.1
  (13 shorter events, 0.2 us)
Async XLA Ops:
  0.0 44.3 %copy-start = (bf16[1024,512]{1,0:T(8,128)(2,1)S(1)}, bf16[1024,512]{1,0:T(8,128)(2,1)}, u32[]{:S(2)}) copy-start(bf16[1024,512]{1,0:T(8,128)(2,1)} %param.9) | copy-start | bytes 3145732
  54.1 7.5 %copy-start.5 = (s32[8,4]{0,1:T(4,128)S(1)}, s32[8,4]{0,1:T(4,128)}, u32[]{:S(2)}) copy-start(s32[8,4]{0,1:T(4,128)} %param.15) | copy-start | bytes 388
  54.1 8.1 %copy-start.3 = (bf16[512,128]{1,0:T(8,128)(2,1)S(1)}, bf16[512,128]{1,0:T(8,128)(2,1)}, u32[]{:S(2)}) copy-start(bf16[512,128]{1,0:T(8,128)(2,1)} %param.10) | copy-start | bytes 393220
  54.1 191.9 %all-to-all-start = ((bf16[64,512,128]{2,1,0:T(8,128)(2,1)}), bf16[64,512,128]{2,1,0:T(8,128)(2,1)}, u32[]{:S(2)}, u32[]{:S(2)}) async-start(bf16[64,512,128]{2,1,0:T(8,128)(2,1)} %bitcast.43), calls=%async_computation | async-start | bytes 16777216 | tf_op jit(solution)/shard_map/all_to_all | solution.py:155
  61.7 2.2 copy-start.4
  61.7 184.3 %copy-start.1 = (bf16[8,256,128]{2,1,0:T(8,128)(2,1)S(1)}, bf16[8,256,128]{2,1,0:T(8,128)(2,1)}, u32[]{:S(2)}) copy-start(bf16[8,256,128]{2,1,0:T(8,128)(2,1)} %pad_maximum_fusion.1.src_ref.own_ref) | copy-start | bytes 1572868
  61.7 184.3 %copy-start.2 = (f32[2]{0:T(128)S(1)}, f32[2]{0:T(128)}, u32[]{:S(2)}) copy-start(f32[2]{0:T(128)} %scale_ref.1) | copy-start | bytes 28
  252.9 15.0 %collective-permute-start.2 = (bf16[1024,128]{1,0:T(8,128)(2,1)S(1)}, bf16[1024,128]{1,0:T(8,128)(2,1)S(1)}, u32[]{:S(2)}, u32[]{:S(2)}) collective-permute-start(bf16[1024,128]{1,0:T(8,128)(2,1)S(1)} %bitcast.50), channel_id=1, source_target_pairs={{0,3},{1,0},{2,1},{3,2},{4,7},{5,4},{6,5},{7,6},{8,11},{9,8},{10,9... | collective-permute-start | bytes 786440 | tf_op jit(solution)/shard_map/ppermute | solution.py:177
  256.0 15.9 %collective-permute-start = (bf16[1024,128]{1,0:T(8,128)(2,1)S(1)}, bf16[1024,128]{1,0:T(8,128)(2,1)S(1)}, u32[]{:S(2)}, u32[]{:S(2)}) collective-permute-start(bf16[1024,128]{1,0:T(8,128)(2,1)S(1)} %bitcast.51), channel_id=1, source_target_pairs={{0,1},{1,2},{2,3},{3,0},{4,5},{5,6},{6,7},{7,4},{8,9},{9,10},{10,1... | collective-permute-start | bytes 786440 | tf_op jit(solution)/shard_map/ppermute | solution.py:177
  256.0 16.1 %collective-permute-start.1 = (bf16[1024,128]{1,0:T(8,128)(2,1)S(1)}, bf16[1024,128]{1,0:T(8,128)(2,1)S(1)}, u32[]{:S(2)}, u32[]{:S(2)}) collective-permute-start(bf16[1024,128]{1,0:T(8,128)(2,1)S(1)} %bitcast.52), channel_id=1, source_target_pairs={{0,2},{1,3},{2,0},{3,1},{4,6},{5,7},{6,4},{7,5},{8,10},{9,11},{10,... | collective-permute-start | bytes 786440 | tf_op jit(solution)/shard_map/ppermute | solution.py:177

commit v6 on v3

--- a/solution.py
+++ b/solution.py
@@ -15,23 +15,17 @@
 
 
 def attend_kernel(slot_ref, live_ref, scale_ref, q_ref, own_ref, recv_ref, out_ref, buf, sems, *, count, slots):
-    b = pl.program_id(0)
     pairs = buf.shape[0]
-    feat, lanes = q_ref.shape[1], q_ref.shape[2]
+    nblocks, feat, lanes = q_ref.shape
     width = lanes // count
     hd = feat // count
 
     def pair_copy(p):
         return pltpu.make_async_copy(recv_ref.at[slot_ref[p]], buf.at[p], sems.at[p])
 
-    @pl.when(b == 0)
-    def _():
-        for p in range(pairs):
-            pair_copy(p).start()
+    for p in range(pairs):
+        pair_copy(p).start()
 
-    for s in range(slots):
-        pair_copy(b * slots + s).wait()
-    q_stack = q_ref[0]
     row_head = lax.broadcasted_iota(jnp.int32, (feat, width), 0) // hd
     lane_pos = lax.broadcasted_iota(jnp.int32, (1, lanes), 1)
     scale_row = jnp.zeros((1, lanes), jnp.float32)
@@ -39,24 +33,31 @@
         inside = (lane_pos >= h * width) & (lane_pos < (h + 1) * width)
         scale_row = jnp.where(inside, scale_ref[h], scale_row)
     key_rows = lax.broadcasted_iota(jnp.int32, ((slots + 1) * width, 1), 0)
-    live_col = jnp.ones(((slots + 1) * width, 1), jnp.float32)
-    for s in range(slots):
-        inside = (key_rows >= (s + 1) * width) & (key_rows < (s + 2) * width)
-        live_col = jnp.where(inside, live_ref[b * slots + s].astype(jnp.float32), live_col)
-    blocks = [own_ref[b]] + [buf[b * slots + s] for s in range(slots)]
-    keys = jnp.concatenate([blk[:width] for blk in blocks], axis=0)
-    values_t = jnp.concatenate([blk[width:] for blk in blocks], axis=1)
-    s_all = jnp.dot(keys, q_stack, preferred_element_type=jnp.float32)
-    w = jnp.exp(scale_row * (s_all - 1.0)) * live_col
-    den = jnp.sum(w, axis=0, keepdims=True)
-    w_b = w.astype(jnp.bfloat16)
-    num = jnp.zeros((feat, width), jnp.float32)
-    den_full = jnp.zeros((feat, width), jnp.float32)
-    for h in range(count):
-        part = jnp.dot(values_t, w_b[:, h * width:(h + 1) * width], preferred_element_type=jnp.float32)
-        num = jnp.where(row_head == h, part, num)
-        den_full = jnp.where(row_head == h, den[:, h * width:(h + 1) * width], den_full)
-    out_ref[0] = (num / den_full).astype(out_ref.dtype)
+
+    def block(b, carry):
+        for s in range(slots):
+            pair_copy(b * slots + s).wait()
+        live_col = jnp.ones(((slots + 1) * width, 1), jnp.float32)
+        for s in range(slots):
+            inside = (key_rows >= (s + 1) * width) & (key_rows < (s + 2) * width)
+            live_col = jnp.where(inside, live_ref[b * slots + s].astype(jnp.float32), live_col)
+        blocks = [own_ref[b]] + [buf[b * slots + s] for s in range(slots)]
+        keys = jnp.concatenate([blk[:width] for blk in blocks], axis=0)
+        values_t = jnp.concatenate([blk[width:] for blk in blocks], axis=1)
+        s_all = jnp.dot(keys, q_ref[b], preferred_element_type=jnp.float32)
+        w = jnp.exp(scale_row * (s_all - 1.0)) * live_col
+        den = jnp.sum(w, axis=0, keepdims=True)
+        w_b = w.astype(jnp.bfloat16)
+        num = jnp.zeros((feat, width), jnp.float32)
+        den_full = jnp.zeros((feat, width), jnp.float32)
+        for h in range(count):
+            part = jnp.dot(values_t, w_b[:, h * width:(h + 1) * width], preferred_element_type=jnp.float32)
+            num = jnp.where(row_head == h, part, num)
+            den_full = jnp.where(row_head == h, den[:, h * width:(h + 1) * width], den_full)
+        out_ref[b] = (num / den_full).astype(out_ref.dtype)
+        return carry
+
+    lax.fori_loop(0, nblocks, block, 0)
 
 
 def attend(query_stack, own_kv, recv_kv, slot_of, live, scales):
@@ -66,14 +67,14 @@
     slots = slot_of.shape[0] // nblocks
     grid_spec = pltpu.PrefetchScalarGridSpec(
         num_scalar_prefetch=2,
-        grid=(nblocks,),
+        grid=(1,),
         in_specs=[
             pl.BlockSpec(memory_space=pltpu.SMEM),
-            pl.BlockSpec((1, feat, lanes), lambda b, slot_of, live: (b, 0, 0)),
-            pl.BlockSpec((nblocks, 2 * width, feat), lambda b, slot_of, live: (0, 0, 0)),
+            pl.BlockSpec((nblocks, feat, lanes), lambda i, slot_of, live: (0, 0, 0)),
+            pl.BlockSpec((nblocks, 2 * width, feat), lambda i, slot_of, live: (0, 0, 0)),
             pl.BlockSpec(memory_space=pl.ANY),
         ],
-        out_specs=pl.BlockSpec((1, feat, width), lambda b, slot_of, live: (b, 0, 0)),
+        out_specs=pl.BlockSpec((nblocks, feat, width), lambda i, slot_of, live: (0, 0, 0)),
         scratch_shapes=[
             pltpu.VMEM((nblocks * slots, 2 * width, feat), recv_kv.dtype),
             pltpu.SemaphoreType.DMA((nblocks * slots,)),

time: 250 us -> 250 us (level)
  no operation moved by 1% of the time
where the time goes in v6:
time: 250 us; the launch traced here: 249 us
  waiting for transfers between devices  187 us (75%)
  starting transfers between devices  24 us (10%)
  blocking collectives  13.3 us (5%)
  Pallas kernels  12 us (5%)
  local copies, waits for them, and re-layouts  4.83 us (2%)
  matrix products  4.67 us (2%)
  other arithmetic  2.58 us (1%)
    all_to_all x1, waiting for transfers between devices, body(): lax.all_to_all(payload.reshape(devices, capacity * 2 * width, feat), 'nod...  170 us
    all_gather x1, blocking collectives, body(): w_out_t = lax.all_gather(w_out.T, 'heads', axis=1, tiled=True)  13.3 us
    ppermute x3, waiting for transfers between devices, body(): lax.ppermute(attn, 'heads', [(j, (j + k) % heads) for j in range(heads)])  13.3 us
    all_to_all x1, starting transfers between devices, body(): lax.all_to_all(request.reshape(devices, capacity), 'nodes', split_axis=0,...  12 us
    all_to_all x1, starting transfers between devices, body(): lax.all_to_all(payload.reshape(devices, capacity * 2 * width, feat), 'nod...  6.69 us
    pallas_call x1, Pallas kernels, attend(): pl.pallas_call(functools.partial(attend_kernel, count=count, slots=slots)...  6.63 us
    pallas_call x1, Pallas kernels, gather_blocks(): pl.pallas_call(gather_kernel, grid_spec=grid_spec, out_shape=jax.ShapeDty...  5.35 us
    ppermute x3, starting transfers between devices, body(): lax.ppermute(attn, 'heads', [(j, (j + k) % heads) for j in range(heads)])  5.3 us
  transfers between devices with their start and end apart: 5, of which 4 were waited for; matrix products, arithmetic and copies ran while one was open for 3% of the time, Pallas kernels for 0%

profile of v6, /device:TPU:2, one launch (start us, length us, event | category | flops | bytes accessed | tf_op | source)
XLA Modules:
  0.0 248.5 jit_solution(7496993481908391568)
XLA Ops:
  0.0 0.0 copy-start
  0.0 0.8 copy.34
  0.8 0.1 reshape.111
  0.9 0.1 fusion.9
  1.0 0.1 reduce_window_sum.11
  1.1 0.2 select_reduce_fusion.1
  1.2 0.8 copy.42
  2.0 0.1 reshape.115
  2.1 0.7 compare_convert_fusion
  2.8 0.1 copy.35
  2.9 0.1 reshape.119.live_ref
  3.0 0.1 select_reduce_fusion
  3.1 0.8 sub.30
  3.8 12.0 %all-to-all-start = ((s32[64,1,2]{2,1,0:T(1,128)}), s32[64,1,2]{2,1,0:T(1,128)S(1)}, u32[]{:S(2)}, u32[]{:S(2)}) async-start(s32[64,1,2]{2,1,0:T(1,128)} %bitcast.8), calls=%async_computation | async-start | bytes 65536 | tf_op jit(solution)/shard_map/all_to_all | solution.py:144
  15.8 0.0 copy-done
  15.9 1.3 convolution_convert_fusion
  17.2 0.2 copy.41
  17.4 1.3 fusion.13
  18.7 0.2 copy.39
  18.9 0.1 bitcast_reduce_fusion
  19.1 0.1 copy.46
  19.2 0.2 copy.40
  19.4 0.1 multiply_convert_fusion
  19.5 0.8 pad_maximum_fusion.1.src_ref.own_ref
  20.3 4.1 %all-to-all-done = s32[64,1,2]{2,1,0:T(1,128)S(1)} async-done(((s32[64,1,2]{2,1,0:T(1,128)}), s32[64,1,2]{2,1,0:T(1,128)S(1)}, u32[]{:S(2)}, u32[]{:S(2)}) %all-to-all-start) | async-done | bytes 544 | tf_op jit(solution)/shard_map/all_to_all | solution.py:144
  24.4 0.1 clamp_reduce_fusion
  24.5 0.7 min.22.pick_ref
  25.1 5.3 %shard_map.91 = bf16[128,256,128]{2,1,0:T(8,128)(2,1)} custom-call(s32[128]{0:T(128)} %min.22.pick_ref, bf16[8,256,128]{2,1,0:T(8,128)(2,1)} %pad_maximum_fusion.1.src_ref.own_ref), custom_call_target="tpu_custom_call" | custom-call | tf_op jit(solution)/shard_map/pallas_call | solution.py:108
  30.5 0.0 copy-start.3
  30.5 6.7 %all-to-all-start.1 = ((bf16[64,512,128]{2,1,0:T(8,128)(2,1)}), bf16[64,512,128]{2,1,0:T(8,128)(2,1)}, u32[]{:S(2)}, u32[]{:S(2)}) async-start(bf16[64,512,128]{2,1,0:T(8,128)(2,1)} %bitcast.39), calls=%async_computation.1 | async-start | bytes 16777216 | tf_op jit(solution)/shard_map/all_to_all | solution.py:150
  37.2 0.0 copy-done.3
  37.2 0.0 copy-start.4
  37.2 0.0 copy-start.1
  37.2 0.0 copy-start.2
  37.2 0.4 fusion.12
  37.7 0.2 copy.37
  37.9 0.2 copy.36
  38.1 0.1 bitcast_reduce_fusion.1
  38.2 0.1 copy.45
  38.3 0.2 select_bitcast_fusion.1
  38.5 0.1 select_bitcast_fusion
  38.6 0.1 pad_maximum_fusion.q_ref
  38.7 0.0 copy-done.4
  38.7 13.3 %all_gather.3 = bf16[512,512]{0,1:T(8,128)(2,1)S(1)} all-gather(bf16[512,128]{0,1:T(8,128)(2,1)S(1)} %bitcast.52), channel_id=1, replica_groups=mesh['nodes'=64,'heads'=4] {'heads'}, dimensions={1}, use_global_device_ids=true | all-gather | bytes 655360 | tf_op jit(solution)/shard_map/all_gather | solution.py:149
  52.0 169.5 %all-to-all-done.1 = bf16[64,512,128]{2,1,0:T(8,128)(2,1)} async-done(((bf16[64,512,128]{2,1,0:T(8,128)(2,1)}), bf16[64,512,128]{2,1,0:T(8,128)(2,1)}, u32[]{:S(2)}, u32[]{:S(2)}) %all-to-all-start.1) | async-done | bytes 8388640 | tf_op jit(solution)/shard_map/all_to_all | solution.py:150
  221.5 0.0 copy-done.1
  221.5 0.0 copy-done.2
  221.5 6.6 %shard_map.92 = bf16[8,128,128]{2,1,0:T(8,128)(2,1)S(1)} custom-call(s32[32]{0:T(128)S(1)} %get-tuple-element.15.slot_ref, s32[32]{0:T(128)S(1)} %reshape.119.live_ref, f32[2]{0:T(128)S(1)} %copy-done.2, bf16[8,128,256]{2,1,0:T(8,128)(2,1)S(1)} %pad_maximum_fusion.q_ref, bf16[8,256,128]{2,1,0:T(8,128)(2,1)S(1)} %copy-done.1, ...), custom_call_target="tpu_custom_call" | custom-call | tf_op jit(solution)/shard_map/pallas_call | solution.py:83
  228.2 0.2 copy.44
  228.4 3.1 %collective-permute-start.2 = (bf16[1024,128]{1,0:T(8,128)(2,1)S(1)}, bf16[1024,128]{1,0:T(8,128)(2,1)S(1)}, u32[]{:S(2)}, u32[]{:S(2)}) collective-permute-start(bf16[1024,128]{1,0:T(8,128)(2,1)S(1)} %bitcast.46), channel_id=1, source_target_pairs={{0,3},{1,0},{2,1},{3,2},{4,7},{5,4},{6,5},{7,6},{8,11},{9,8},{10,9... | collective-permute-start | bytes 786440 | tf_op jit(solution)/shard_map/ppermute | solution.py:172
  231.5 0.0 collective-permute-start
  231.5 2.2 collective-permute-start.1
  233.7 0.2 fusion.7
  233.9 9.4 %collective-permute-done.2 = bf16[1024,128]{1,0:T(8,128)(2,1)S(1)} collective-permute-done((bf16[1024,128]{1,0:T(8,128)(2,1)S(1)}, bf16[1024,128]{1,0:T(8,128)(2,1)S(1)}, u32[]{:S(2)}, u32[]{:S(2)}) %collective-permute-start.2) | collective-permute-done | bytes 262176 | tf_op jit(solution)/shard_map/ppermute | solution.py:172
  243.3 0.2 fusion.3
  243.5 3.8 %collective-permute-done = bf16[1024,128]{1,0:T(8,128)(2,1)S(1)} collective-permute-done((bf16[1024,128]{1,0:T(8,128)(2,1)S(1)}, bf16[1024,128]{1,0:T(8,128)(2,1)S(1)}, u32[]{:S(2)}, u32[]{:S(2)}) %collective-permute-start) | collective-permute-done | bytes 262176 | tf_op jit(solution)/shard_map/ppermute | solution.py:172
  247.4 0.2 convolution_add_fusion.1
  247.6 0.0 collective-permute-done.1
  247.6 0.9 fusion.1
  (8 shorter events, 0.1 us)
Async XLA Ops:
  0.0 15.8 %copy-start = (bf16[1024,512]{1,0:T(8,128)(2,1)S(1)}, bf16[1024,512]{1,0:T(8,128)(2,1)}, u32[]{:S(2)}) copy-start(bf16[1024,512]{1,0:T(8,128)(2,1)} %param.9) | copy-start | bytes 3145732
  3.8 20.5 %all-to-all-start = ((s32[64,1,2]{2,1,0:T(1,128)}), s32[64,1,2]{2,1,0:T(1,128)S(1)}, u32[]{:S(2)}, u32[]{:S(2)}) async-start(s32[64,1,2]{2,1,0:T(1,128)} %bitcast.8), calls=%async_computation | async-start | bytes 65536 | tf_op jit(solution)/shard_map/all_to_all | solution.py:144
  30.5 6.7 %copy-start.3 = (bf16[512,128]{1,0:T(8,128)(2,1)S(1)}, bf16[512,128]{1,0:T(8,128)(2,1)}, u32[]{:S(2)}) copy-start(bf16[512,128]{1,0:T(8,128)(2,1)} %param.10) | copy-start | bytes 393220
  30.5 191.1 %all-to-all-start.1 = ((bf16[64,512,128]{2,1,0:T(8,128)(2,1)}), bf16[64,512,128]{2,1,0:T(8,128)(2,1)}, u32[]{:S(2)}, u32[]{:S(2)}) async-start(bf16[64,512,128]{2,1,0:T(8,128)(2,1)} %bitcast.39), calls=%async_computation.1 | async-start | bytes 16777216 | tf_op jit(solution)/shard_map/all_to_all | solution.py:150
  37.2 1.5 copy-start.4
  37.2 184.3 %copy-start.1 = (bf16[8,256,128]{2,1,0:T(8,128)(2,1)S(1)}, bf16[8,256,128]{2,1,0:T(8,128)(2,1)}, u32[]{:S(2)}) copy-start(bf16[8,256,128]{2,1,0:T(8,128)(2,1)} %pad_maximum_fusion.1.src_ref.own_ref) | copy-start | bytes 1572868
  37.2 184.3 %copy-start.2 = (f32[2]{0:T(128)S(1)}, f32[2]{0:T(128)}, u32[]{:S(2)}) copy-start(f32[2]{0:T(128)} %scale_ref.1) | copy-start | bytes 28
  228.4 15.0 %collective-permute-start.2 = (bf16[1024,128]{1,0:T(8,128)(2,1)S(1)}, bf16[1024,128]{1,0:T(8,128)(2,1)S(1)}, u32[]{:S(2)}, u32[]{:S(2)}) collective-permute-start(bf16[1024,128]{1,0:T(8,128)(2,1)S(1)} %bitcast.46), channel_id=1, source_target_pairs={{0,3},{1,0},{2,1},{3,2},{4,7},{5,4},{6,5},{7,6},{8,11},{9,8},{10,9... | collective-permute-start | bytes 786440 | tf_op jit(solution)/shard_map/ppermute | solution.py:172
  231.5 15.9 %collective-permute-start = (bf16[1024,128]{1,0:T(8,128)(2,1)S(1)}, bf16[1024,128]{1,0:T(8,128)(2,1)S(1)}, u32[]{:S(2)}, u32[]{:S(2)}) collective-permute-start(bf16[1024,128]{1,0:T(8,128)(2,1)S(1)} %bitcast.47), channel_id=1, source_target_pairs={{0,1},{1,2},{2,3},{3,0},{4,5},{5,6},{6,7},{7,4},{8,9},{9,10},{10,1... | collective-permute-start | bytes 786440 | tf_op jit(solution)/shard_map/ppermute | solution.py:172
  231.5 16.1 %collective-permute-start.1 = (bf16[1024,128]{1,0:T(8,128)(2,1)S(1)}, bf16[1024,128]{1,0:T(8,128)(2,1)S(1)}, u32[]{:S(2)}, u32[]{:S(2)}) collective-permute-start(bf16[1024,128]{1,0:T(8,128)(2,1)S(1)} %bitcast.48), channel_id=1, source_target_pairs={{0,2},{1,3},{2,0},{3,1},{4,6},{5,7},{6,4},{7,5},{8,10},{9,11},{10,... | collective-permute-start | bytes 786440 | tf_op jit(solution)/shard_map/ppermute | solution.py:172

commit v7 on v3

--- a/solution.py
+++ b/solution.py
@@ -143,19 +143,42 @@
     asked = lax.all_to_all(
         request.reshape(devices, capacity), "nodes", split_axis=0, concat_axis=0, tiled=True
     ).reshape(-1)
-    payload = gather_blocks(own_kv, jnp.clip(asked, 0, nblocks - 1).astype(jnp.int32))
+    heads = lax.axis_size("heads")
+    me = lax.axis_index("heads")
+    quarter = width // heads
+    model = feats.shape[1]
+    feats_parts = feats.reshape(nblocks * heads, quarter, model)
+    pick = jnp.clip(asked, 0, nblocks - 1).astype(jnp.int32) * heads + me
+    payload = gather_blocks(feats_parts, pick)
     w_out, payload = lax.optimization_barrier((w_out, payload))
     w_out_t = lax.all_gather(w_out.T, "heads", axis=1, tiled=True)
-    recv_kv = lax.all_to_all(
-        payload.reshape(devices, capacity * 2 * width, feat),
+    recv = lax.all_to_all(
+        payload.reshape(devices, capacity * quarter, model),
         "nodes",
         split_axis=0,
         concat_axis=0,
         tiled=True,
-    ).reshape(tile_count, 2 * width, feat)
-    recv_kv, w_out_t = lax.optimization_barrier((recv_kv, w_out_t))
+    ).reshape(tile_count, quarter, model)
+    recv, w_out_t = lax.optimization_barrier((recv, w_out_t))
     slot_of = jnp.clip(target, 0, tile_count - 1).astype(jnp.int32)
-    attn_t = attend(query_stack, own_kv, recv_kv, slot_of, valid, head_scale)
+    piece = gather_blocks(recv, slot_of)
+    pair_rows = lax.all_gather(piece, "heads", axis=1, tiled=True)
+    pairs = pair_rows.shape[0]
+    pair_k = unit_rows(
+        jnp.dot(pair_rows.reshape(-1, model), w_key, preferred_element_type=jnp.float32), count
+    )
+    pair_v = jnp.dot(
+        pair_rows.reshape(-1, model), w_value, preferred_element_type=jnp.float32
+    ).astype(jnp.bfloat16)
+    pair_kv = jnp.concatenate(
+        [
+            pair_k.reshape(pairs, width, feat),
+            jnp.swapaxes(pair_v.reshape(pairs, width, feat), 1, 2),
+        ],
+        axis=1,
+    )
+    pair_ids = jnp.arange(pairs, dtype=jnp.int32)
+    attn_t = attend(query_stack, own_kv, pair_kv, pair_ids, valid, head_scale)
     attn = jnp.swapaxes(attn_t, 1, 2).reshape(rows, feat)
     heads = lax.axis_size("heads")
     me = lax.axis_index("heads")

time: 250 us -> 237 us (0.948)
  waiting for transfers between devices: 187 us -> 138 us
  between operations: 0.27 us -> 13.7 us
  matrix products: 4.67 us -> 13.7 us
  local copies, waits for them, and re-layouts: 4.83 us -> 11.7 us
  Pallas kernels: 12.1 us -> 16.9 us
    all_to_all x1, waiting for transfers between devices: 170 us -> 80.6 us  [body(): lax.all_to_all(payload.reshape(devices, capacity * quarter, model), 'node...]
    all_gather x0 -> x1, waiting for transfers between devices: none -> 39.4 us  [body(): pair_rows = lax.all_gather(piece, 'heads', axis=1, tiled=True)]
    dot_general x0 -> x2, matrix products: none -> 7.11 us  [the longest x1 3.68 us: body(): jnp.dot(pair_rows.reshape(-1, model), w_key, preferred_element_type=jnp.f...]
    all_to_all x1, waiting for transfers between devices: 4.08 us -> 8.51 us  [body(): lax.all_to_all(request.reshape(devices, capacity), 'nodes', split_axis=0,...]
    ppermute x3, waiting for transfers between devices: 13.3 us -> 9.67 us  [body(): lax.ppermute(attn, 'heads', [(j, (j + k) % heads) for j in range(heads)])]
    dot_general x4, matrix products: 1.56 us -> 4.55 us  [out_part(): lax.dot_general(piece, w_part, (((1,), (1,)), ((), ())), preferred_elemen...]
    pallas_call x1 -> x2, Pallas kernels: 5.35 us -> 8.25 us  [gather_blocks(): pl.pallas_call(gather_kernel, grid_spec=grid_spec, out_shape=jax.ShapeDty...]
  transfers between devices with their start and end apart: 5 -> 6, of which waited for: 4 -> 5; matrix products, arithmetic and copies ran while one was open for 3% -> 5% of each run, Pallas kernels for 0% -> 0%
where the time goes in v7:
time: 237 us; the launch traced here: 236 us
  waiting for transfers between devices  138 us (58%)
  starting transfers between devices  22.8 us (10%)
  Pallas kernels  16.9 us (7%)
  blocking collectives  14.2 us (6%)
  matrix products  13.7 us (6%)
  between operations  13.7 us (6%)
  local copies, waits for them, and re-layouts  11.7 us (5%)
  other arithmetic  4.99 us (2%)
    all_to_all x1, waiting for transfers between devices, body(): lax.all_to_all(payload.reshape(devices, capacity * quarter, model), 'node...  80.6 us
    all_gather x1, waiting for transfers between devices, body(): pair_rows = lax.all_gather(piece, 'heads', axis=1, tiled=True)  39.4 us
    all_gather x1, blocking collectives, body(): w_out_t = lax.all_gather(w_out.T, 'heads', axis=1, tiled=True)  14.2 us
    all_to_all x1, starting transfers between devices, body(): lax.all_to_all(request.reshape(devices, capacity), 'nodes', split_axis=0,...  12 us
    ppermute x3, waiting for transfers between devices, body(): lax.ppermute(attn, 'heads', [(j, (j + k) % heads) for j in range(heads)])  9.67 us
    pallas_call x1, Pallas kernels, attend(): pl.pallas_call(functools.partial(attend_kernel, count=count, slots=slots)...  8.67 us
    all_to_all x1, waiting for transfers between devices, body(): lax.all_to_all(request.reshape(devices, capacity), 'nodes', split_axis=0,...  8.51 us
    pallas_call x2, Pallas kernels, gather_blocks(): pl.pallas_call(gather_kernel, grid_spec=grid_spec, out_shape=jax.ShapeDty...  8.25 us
  transfers between devices with their start and end apart: 6, of which 5 were waited for; matrix products, arithmetic and copies ran while one was open for 5% of the time, Pallas kernels for 0%

profile of v7, /device:TPU:2, one launch (start us, length us, event | category | flops | bytes accessed | tf_op | source)
XLA Modules:
  0.0 236.2 jit_solution(9950969109810441480)
XLA Ops:
  6.5 0.8 copy.49
  7.3 0.1 reshape.136
  7.4 0.1 fusion.9
  7.5 0.1 reduce_window_sum.11
  7.5 0.2 select_reduce_fusion.1
  7.7 0.7 compare_convert_fusion
  8.4 0.1 copy.42
  8.5 0.1 reshape.144.live_ref
  8.6 0.8 copy.50
  9.3 0.1 reshape.137
  9.4 0.6 broadcast_clamp_fusion
  10.0 0.1 select_reduce_fusion
  10.1 0.8 sub.30
  10.9 12.0 %all-to-all-start = ((s32[64,1,2]{2,1,0:T(1,128)}), s32[64,1,2]{2,1,0:T(1,128)S(1)}, u32[]{:S(2)}, u32[]{:S(2)}) async-start(s32[64,1,2]{2,1,0:T(1,128)} %bitcast.8), calls=%async_computation | async-start | bytes 65536 | tf_op jit(solution)/shard_map/all_to_all | solution.py:143
  22.9 8.5 %all-to-all-done = s32[64,1,2]{2,1,0:T(1,128)S(1)} async-done(((s32[64,1,2]{2,1,0:T(1,128)}), s32[64,1,2]{2,1,0:T(1,128)S(1)}, u32[]{:S(2)}, u32[]{:S(2)}) %all-to-all-start) | async-done | bytes 544 | tf_op jit(solution)/shard_map/all_to_all | solution.py:143
  31.4 0.1 add_reduce_fusion
  31.5 0.7 add.121.pick_ref
  32.2 4.4 %shard_map.91 = bf16[128,32,512]{2,1,0:T(8,128)(2,1)} custom-call(s32[128]{0:T(128)} %add.121.pick_ref, bf16[32,32,512]{2,1,0:T(8,128)(2,1)} %bitcast.58), custom_call_target="tpu_custom_call" | custom-call | tf_op jit(solution)/shard_map/pallas_call | solution.py:107
  36.6 6.6 %all-to-all-start.1 = ((bf16[64,64,512]{2,1,0:T(8,128)(2,1)}), bf16[64,64,512]{2,1,0:T(8,128)(2,1)}, u32[]{:S(2)}, u32[]{:S(2)}) async-start(bf16[64,64,512]{2,1,0:T(8,128)(2,1)} %bitcast.57), calls=%async_computation.1 | async-start | bytes 8388608 | tf_op jit(solution)/shard_map/all_to_all | solution.py:155
  43.2 0.0 copy-start.3
  43.2 0.0 copy-start.2
  43.2 0.0 copy-start.5
  43.2 0.0 all-gather.2.cloned.1.call-start
  43.3 14.2 %all_gather.6 = bf16[512,512]{0,1:T(8,128)(2,1)} all-gather(bf16[512,128]{0,1:T(8,128)(2,1)S(1)} %bitcast.77), channel_id=1, replica_groups=mesh['nodes'=64,'heads'=4] {'heads'}, dimensions={1}, use_global_device_ids=true | all-gather | bytes 655360 | tf_op jit(solution)/shard_map/all_gather | solution.py:154
  57.4 80.6 %all-to-all-done.1 = bf16[64,64,512]{2,1,0:T(8,128)(2,1)} async-done(((bf16[64,64,512]{2,1,0:T(8,128)(2,1)}), bf16[64,64,512]{2,1,0:T(8,128)(2,1)}, u32[]{:S(2)}, u32[]{:S(2)}) %all-to-all-start.1) | async-done | bytes 4194336 | tf_op jit(solution)/shard_map/all_to_all | solution.py:155
  138.0 3.9 %shard_map.92 = bf16[32,32,512]{2,1,0:T(8,128)(2,1)} custom-call(s32[32]{0:T(128)} %get-tuple-element.13.pick_ref, bf16[128,32,512]{2,1,0:T(8,128)(2,1)} %bitcast.11.src_ref), custom_call_target="tpu_custom_call" | custom-call | tf_op jit(solution)/shard_map/pallas_call | solution.py:107
  141.9 0.0 all-gather.2.cloned.1.call-update
  142.0 0.8 copy.52
  142.7 0.4 fusion.12
  143.2 0.2 copy.43
  143.5 0.1 copy.56
  143.6 0.2 copy.44
  143.8 0.4 fusion.13
  144.3 1.0 copy.46
  145.3 1.1 bitcast_reduce_fusion
  146.4 0.9 copy.57
  147.3 1.2 copy.47
  148.6 1.1 convolution_convert_fusion.1
  149.7 1.1 copy.48
  150.9 0.2 select_bitcast_fusion.1
  151.0 0.1 select_bitcast_fusion
  151.1 0.1 pad_maximum_fusion.1.q_ref
  151.2 0.1 multiply_convert_fusion.1
  151.3 39.4 %all-gather.2.cloned.1.call-done = bf16[32,128,512]{2,1,0:T(8,128)(2,1)} async-done(((bf16[32,32,512]{2,1,0:T(8,128)(2,1)}), bf16[32,128,512]{2,1,0:T(8,128)(2,1)}) %all-gather.2.cloned.1.call-update) | async-done | bytes 4194320 | tf_op jit(solution)/shard_map/all_gather | solution.py:165
  190.7 3.7 %multiply_reduce_fusion = (f32[4096,2]{0,1:T(2,128)S(1)}, f32[4096,2,64]{0,2,1:T(8,128)S(1)}) fusion(bf16[4096,512,1]{1,0,2:T(8,128)(2,1)} %bitcast.59, bf16[2,64,512]{2,1,0:T(8,128)(2,1)} %bitcast.78), kind=kOutput, calls=%fused_computation.3 | convolution fusion | flops 537911296 | bytes 6455296 | tf_op jit(solution)/shard_map/dot_general | solution.py:168
  194.4 0.2 multiply_convert_fusion
  194.6 0.2 copy.58
  194.8 1.0 copy.54
  195.8 3.4 %convolution_convert_fusion = bf16[4096,128]{1,0:T(8,128)(2,1)S(1)} fusion(bf16[4096,512]{1,0:T(8,128)(2,1)} %bitcast.60, bf16[512,128]{1,0:T(8,128)(2,1)S(1)} %copy-done), kind=kOutput, calls=%fused_computation | convolution fusion | flops 537395200 | bytes 5373952 | tf_op jit(solution)/shard_map/dot_general | solution.py:170
  199.3 0.0 copy-start.1
  199.3 1.3 copy.53
  200.6 1.4 pad_maximum_fusion.recv_ref
  202.0 8.7 %shard_map.93 = bf16[8,128,128]{2,1,0:T(8,128)(2,1)S(1)} custom-call(s32[32]{0:T(128)S(1)} %iota.20.slot_ref, s32[32]{0:T(128)S(1)} %reshape.144.live_ref, f32[2]{0:T(128)S(1)} %copy-done.1, bf16[8,128,256]{2,1,0:T(8,128)(2,1)S(1)} %pad_maximum_fusion.1.q_ref, bf16[8,256,128]{2,1,0:T(8,128)(2,1)S(1)} %pad_maximum_fusion.2.own_ref, ...), custom_call_target="tpu_custom_call" | custom-call | tf_op jit(solution)/shard_map/pallas_call | solution.py:82
  210.7 0.2 copy.55
  210.9 1.2 collective-permute-start.2
  212.1 0.9 collective-permute-start
  213.0 2.1 collective-permute-start.1
  215.1 1.0 fusion.7
  216.0 4.1 %collective-permute-done.2 = bf16[1024,128]{1,0:T(8,128)(2,1)S(1)} collective-permute-done((bf16[1024,128]{1,0:T(8,128)(2,1)S(1)}, bf16[1024,128]{1,0:T(8,128)(2,1)S(1)}, u32[]{:S(2)}, u32[]{:S(2)}) %collective-permute-start.2) | collective-permute-done | bytes 262176 | tf_op jit(solution)/shard_map/ppermute | solution.py:194
  220.2 1.0 fusion.3
  221.1 5.5 %collective-permute-done = bf16[1024,128]{1,0:T(8,128)(2,1)S(1)} collective-permute-done((bf16[1024,128]{1,0:T(8,128)(2,1)S(1)}, bf16[1024,128]{1,0:T(8,128)(2,1)S(1)}, u32[]{:S(2)}, u32[]{:S(2)}) %collective-permute-start) | collective-permute-done | bytes 262176 | tf_op jit(solution)/shard_map/ppermute | solution.py:194
  226.7 1.0 convolution_add_fusion.1
  227.6 0.0 collective-permute-done.1
  227.6 1.7 fusion.1
  (19 shorter events, 0.3 us)
Async XLA Ops:
  6.5 142.0 %copy-start = (bf16[512,128]{1,0:T(8,128)(2,1)S(1)}, bf16[512,128]{1,0:T(8,128)(2,1)}, u32[]{:S(2)}) copy-start(bf16[512,128]{1,0:T(8,128)(2,1)} %param.12) | copy-start | bytes 393220
  10.9 20.5 %all-to-all-start = ((s32[64,1,2]{2,1,0:T(1,128)}), s32[64,1,2]{2,1,0:T(1,128)S(1)}, u32[]{:S(2)}, u32[]{:S(2)}) async-start(s32[64,1,2]{2,1,0:T(1,128)} %bitcast.8), calls=%async_computation | async-start | bytes 65536 | tf_op jit(solution)/shard_map/all_to_all | solution.py:143
  36.6 6.7 %copy-start.4 = (bf16[128,512]{1,0:T(8,128)(2,1)S(1)}, bf16[128,512]{1,0:T(8,128)(2,1)}, u32[]{:S(2)}) copy-start(bf16[128,512]{1,0:T(8,128)(2,1)} %param.13) | copy-start | bytes 393220
  36.6 101.5 %all-to-all-start.1 = ((bf16[64,64,512]{2,1,0:T(8,128)(2,1)}), bf16[64,64,512]{2,1,0:T(8,128)(2,1)}, u32[]{:S(2)}, u32[]{:S(2)}) async-start(bf16[64,64,512]{2,1,0:T(8,128)(2,1)} %bitcast.57), calls=%async_computation.1 | async-start | bytes 8388608 | tf_op jit(solution)/shard_map/all_to_all | solution.py:155
  43.2 98.8 %copy-start.3 = (bf16[512,128]{1,0:T(8,128)(2,1)S(1)}, bf16[512,128]{1,0:T(8,128)(2,1)}, u32[]{:S(2)}) copy-start(bf16[512,128]{1,0:T(8,128)(2,1)} %param.11) | copy-start | bytes 393220
  43.2 99.6 %copy-start.2 = (bf16[1024,512]{1,0:T(8,128)(2,1)S(1)}, bf16[1024,512]{1,0:T(8,128)(2,1)}, u32[]{:S(2)}) copy-start(bf16[1024,512]{1,0:T(8,128)(2,1)} %param.9) | copy-start | bytes 3145732
  43.2 99.6 %copy-start.5 = (bf16[512,128]{1,0:T(8,128)(2,1)S(1)}, bf16[512,128]{1,0:T(8,128)(2,1)}, u32[]{:S(2)}) copy-start(bf16[512,128]{1,0:T(8,128)(2,1)} %param.10) | copy-start | bytes 393220
  43.2 147.5 %all-gather.2.cloned.1.call-start = ((), (), s32[]{:S(2)}) async-start(), calls=%async_computation.2 | async-start | bytes 5242880 | tf_op jit(solution)/shard_map/all_gather | solution.py:165
  199.3 2.8 %copy-start.1 = (f32[2]{0:T(128)S(1)}, f32[2]{0:T(128)}, u32[]{:S(2)}) copy-start(f32[2]{0:T(128)} %scale_ref.1) | copy-start | bytes 28
  210.9 9.3 %collective-permute-start.2 = (bf16[1024,128]{1,0:T(8,128)(2,1)S(1)}, bf16[1024,128]{1,0:T(8,128)(2,1)S(1)}, u32[]{:S(2)}, u32[]{:S(2)}) collective-permute-start(bf16[1024,128]{1,0:T(8,128)(2,1)S(1)} %bitcast.71), channel_id=1, source_target_pairs={{0,3},{1,0},{2,1},{3,2},{4,7},{5,4},{6,5},{7,6},{8,11},{9,8},{10,9... | collective-permute-start | bytes 786440 | tf_op jit(solution)/shard_map/ppermute | solution.py:194
  212.1 14.6 %collective-permute-start = (bf16[1024,128]{1,0:T(8,128)(2,1)S(1)}, bf16[1024,128]{1,0:T(8,128)(2,1)S(1)}, u32[]{:S(2)}, u32[]{:S(2)}) collective-permute-start(bf16[1024,128]{1,0:T(8,128)(2,1)S(1)} %bitcast.72), channel_id=1, source_target_pairs={{0,1},{1,2},{2,3},{3,0},{4,5},{5,6},{6,7},{7,4},{8,9},{9,10},{10,1... | collective-permute-start | bytes 786440 | tf_op jit(solution)/shard_map/ppermute | solution.py:194
  213.0 14.6 %collective-permute-start.1 = (bf16[1024,128]{1,0:T(8,128)(2,1)S(1)}, bf16[1024,128]{1,0:T(8,128)(2,1)S(1)}, u32[]{:S(2)}, u32[]{:S(2)}) collective-permute-start(bf16[1024,128]{1,0:T(8,128)(2,1)S(1)} %bitcast.73), channel_id=1, source_target_pairs={{0,2},{1,3},{2,0},{3,1},{4,6},{5,7},{6,4},{7,5},{8,10},{9,11},{10,... | collective-permute-start | bytes 786440 | tf_op jit(solution)/shard_map/ppermute | solution.py:194
Sparse Core Ops, SparseCore 0:
  142.1 48.5 all-gather.1

commit v8 on v7

--- a/solution.py
+++ b/solution.py
@@ -150,8 +150,11 @@
     feats_parts = feats.reshape(nblocks * heads, quarter, model)
     pick = jnp.clip(asked, 0, nblocks - 1).astype(jnp.int32) * heads + me
     payload = gather_blocks(feats_parts, pick)
-    w_out, payload = lax.optimization_barrier((w_out, payload))
+    w_out, w_key_b, w_value_b, payload = lax.optimization_barrier((w_out, w_key, w_value, payload))
     w_out_t = lax.all_gather(w_out.T, "heads", axis=1, tiled=True)
+    w_key_all = lax.all_gather(w_key_b, "heads", axis=1, tiled=True).reshape(model, heads, feat)
+    w_value_all = lax.all_gather(w_value_b, "heads", axis=1, tiled=True).reshape(model, heads, feat)
+    w_kv_all = jnp.stack([w_key_all, w_value_all], axis=2).reshape(model, heads * 2 * feat)
     recv = lax.all_to_all(
         payload.reshape(devices, capacity * quarter, model),
         "nodes",
@@ -159,24 +162,22 @@
         concat_axis=0,
         tiled=True,
     ).reshape(tile_count, quarter, model)
-    recv, w_out_t = lax.optimization_barrier((recv, w_out_t))
+    recv, w_out_t, w_kv_all = lax.optimization_barrier((recv, w_out_t, w_kv_all))
     slot_of = jnp.clip(target, 0, tile_count - 1).astype(jnp.int32)
     piece = gather_blocks(recv, slot_of)
-    pair_rows = lax.all_gather(piece, "heads", axis=1, tiled=True)
-    pairs = pair_rows.shape[0]
-    pair_k = unit_rows(
-        jnp.dot(pair_rows.reshape(-1, model), w_key, preferred_element_type=jnp.float32), count
-    )
-    pair_v = jnp.dot(
-        pair_rows.reshape(-1, model), w_value, preferred_element_type=jnp.float32
-    ).astype(jnp.bfloat16)
-    pair_kv = jnp.concatenate(
-        [
-            pair_k.reshape(pairs, width, feat),
-            jnp.swapaxes(pair_v.reshape(pairs, width, feat), 1, 2),
-        ],
-        axis=1,
-    )
+    pairs = piece.shape[0]
+    kv_all = jnp.dot(
+        piece.reshape(pairs * quarter, model), w_kv_all, preferred_element_type=jnp.float32
+    ).reshape(pairs * quarter, heads, 2, feat)
+    k_all = unit_rows(kv_all[:, :, 0, :].reshape(pairs * quarter, heads * feat), heads * count)
+    v_all = kv_all[:, :, 1, :].astype(jnp.bfloat16)
+    send = jnp.concatenate(
+        [k_all.reshape(pairs * quarter, heads, feat), v_all], axis=2
+    ).reshape(pairs, quarter, heads, 2 * feat)
+    send = jnp.transpose(send, (2, 0, 1, 3))
+    got = lax.all_to_all(send, "heads", 0, 0, tiled=True)
+    got = jnp.transpose(got, (1, 0, 2, 3)).reshape(pairs, width, 2 * feat)
+    pair_kv = jnp.concatenate([got[:, :, :feat], jnp.swapaxes(got[:, :, feat:], 1, 2)], axis=1)
     pair_ids = jnp.arange(pairs, dtype=jnp.int32)
     attn_t = attend(query_stack, own_kv, pair_kv, pair_ids, valid, head_scale)
     attn = jnp.swapaxes(attn_t, 1, 2).reshape(rows, feat)

time: 237 us -> 229 us (0.966)
  waiting for transfers between devices: 138 us -> 89.3 us
  blocking collectives: 14.2 us -> 41.8 us
  local copies, waits for them, and re-layouts: 11.7 us -> 28.4 us
  between operations: 13.7 us -> 0.35 us
  other arithmetic: 4.99 us -> 15.6 us
  matrix products: 13.7 us -> 9.14 us
  starting transfers between devices: 22.8 us -> 26.1 us
    all_gather x1 -> x0, waiting for transfers between devices: 39.4 us -> none  [body(): pair_rows = lax.all_gather(piece, 'heads', axis=1, tiled=True)]
    all_to_all x1, waiting for transfers between devices: 80.6 us -> 47 us  [body(): lax.all_to_all(payload.reshape(devices, capacity * quarter, model), 'node...]
    all_gather x0 -> x2, blocking collectives: none -> 28.1 us  [the longest x1 14.1 us: body(): lax.all_gather(w_key_b, 'heads', axis=1, tiled=True)]
    all_to_all x0 -> x1, waiting for transfers between devices: none -> 22.8 us  [body(): got = lax.all_to_all(send, 'heads', 0, 0, tiled=True)]
    mul x3 -> x5, local copies, waits for them, and re-layouts: 1.32 us -> 10.6 us  [unit_rows(): shaped * lax.rsqrt(total + 1e-06)]
    dot_general x2 -> x1, matrix products: 7.11 us -> 2.5 us  [body(): jnp.dot(piece.reshape(pairs * quarter, model), w_kv_all, preferred_elemen...]
    all_to_all x0 -> x1, starting transfers between devices: none -> 4.6 us  [body(): got = lax.all_to_all(send, 'heads', 0, 0, tiled=True)]
    convert_element_type x2, other arithmetic: 0.22 us -> 3.68 us  [unit_rows(): (shaped * lax.rsqrt(total + 1e-06)).astype(jnp.bfloat16)]
  transfers between devices with their start and end apart: 6 -> 6, of which waited for: 5 -> 5; matrix products, arithmetic and copies ran while one was open for 5% -> 6% of each run, Pallas kernels for 0% -> 0%
where the time goes in v8:
time: 229 us; the launch traced here: 228 us
  waiting for transfers between devices  89.3 us (39%)
  blocking collectives  41.8 us (18%)
  local copies, waits for them, and re-layouts  28.4 us (12%)
  starting transfers between devices  26.1 us (11%)
  Pallas kernels  16.9 us (7%)
  other arithmetic  15.6 us (7%)
  matrix products  9.14 us (4%)
    all_to_all x1, waiting for transfers between devices, body(): lax.all_to_all(payload.reshape(devices, capacity * quarter, model), 'node...  47 us
    all_to_all x1, waiting for transfers between devices, body(): got = lax.all_to_all(send, 'heads', 0, 0, tiled=True)  22.8 us
    all_gather x1, blocking collectives, body(): lax.all_gather(w_key_b, 'heads', axis=1, tiled=True)  14.1 us
    all_gather x1, blocking collectives, body(): lax.all_gather(w_value_b, 'heads', axis=1, tiled=True)  14 us
    all_gather x1, blocking collectives, body(): w_out_t = lax.all_gather(w_out.T, 'heads', axis=1, tiled=True)  13.7 us
    all_to_all x1, starting transfers between devices, body(): lax.all_to_all(request.reshape(devices, capacity), 'nodes', split_axis=0,...  12 us
    ppermute x3, waiting for transfers between devices, body(): lax.ppermute(attn, 'heads', [(j, (j + k) % heads) for j in range(heads)])  11.1 us
    mul x5, local copies, waits for them, and re-layouts, unit_rows(): shaped * lax.rsqrt(total + 1e-06)  10.6 us
  transfers between devices with their start and end apart: 6, of which 5 were waited for; matrix products, arithmetic and copies ran while one was open for 6% of the time, Pallas kernels for 0%

profile of v8, /device:TPU:2, one launch (start us, length us, event | category | flops | bytes accessed | tf_op | source)
XLA Modules:
  0.0 227.6 jit_solution(7852856774633246646)
XLA Ops:
  0.0 0.7 compare_convert_fusion
  0.7 0.1 copy.53
  0.9 0.8 copy.60
  1.9 0.2 select_reduce_fusion.1
  2.0 0.8 copy.61
  2.9 0.5 broadcast_clamp_fusion
  3.4 0.1 select_reduce_fusion
  3.5 0.8 sub.30
  4.3 12.0 %all-to-all-start = ((s32[64,1,2]{2,1,0:T(1,128)}), s32[64,1,2]{2,1,0:T(1,128)S(1)}, u32[]{:S(2)}, u32[]{:S(2)}) async-start(s32[64,1,2]{2,1,0:T(1,128)} %bitcast.8), calls=%async_computation | async-start | bytes 65536 | tf_op jit(solution)/shard_map/all_to_all | solution.py:143
  16.3 8.5 %all-to-all-done = s32[64,1,2]{2,1,0:T(1,128)S(1)} async-done(((s32[64,1,2]{2,1,0:T(1,128)}), s32[64,1,2]{2,1,0:T(1,128)S(1)}, u32[]{:S(2)}, u32[]{:S(2)}) %all-to-all-start) | async-done | bytes 544 | tf_op jit(solution)/shard_map/all_to_all | solution.py:143
  24.8 0.1 add_reduce_fusion
  25.0 0.7 add.121.pick_ref
  25.6 4.4 %shard_map.91 = bf16[128,32,512]{2,1,0:T(8,128)(2,1)} custom-call(s32[128]{0:T(128)} %add.121.pick_ref, bf16[32,32,512]{2,1,0:T(8,128)(2,1)} %bitcast.63), custom_call_target="tpu_custom_call" | custom-call | tf_op jit(solution)/shard_map/pallas_call | solution.py:107
  30.0 6.6 %all-to-all-start.1 = ((bf16[64,64,512]{2,1,0:T(8,128)(2,1)}), bf16[64,64,512]{2,1,0:T(8,128)(2,1)}, u32[]{:S(2)}, u32[]{:S(2)}) async-start(bf16[64,64,512]{2,1,0:T(8,128)(2,1)} %bitcast.62), calls=%async_computation.1 | async-start | bytes 8388608 | tf_op jit(solution)/shard_map/all_to_all | solution.py:158
  36.6 0.4 fusion.15
  37.1 1.0 copy.55
  38.1 0.2 copy.54
  38.4 0.9 copy.75
  39.3 0.4 convolution_convert_fusion
  39.8 0.2 copy.59
  40.0 1.2 fusion.16
  41.2 1.0 copy.57
  42.2 14.0 %all_gather.11 = bf16[512,512]{1,0:T(8,128)(2,1)S(1)} all-gather(bf16[512,128]{1,0:T(8,128)(2,1)S(1)} %copy-done.8), channel_id=1, replica_groups=mesh['nodes'=64,'heads'=4] {'heads'}, dimensions={1}, use_global_device_ids=true | all-gather | bytes 655360 | tf_op jit(solution)/shard_map/all_gather | solution.py:156
  56.2 0.2 copy.64
  56.4 14.1 %all_gather.10 = bf16[512,512]{1,0:T(8,128)(2,1)S(1)} all-gather(bf16[512,128]{1,0:T(8,128)(2,1)S(1)} %copy-done.7), channel_id=1, replica_groups=mesh['nodes'=64,'heads'=4] {'heads'}, dimensions={1}, use_global_device_ids=true | all-gather | bytes 655360 | tf_op jit(solution)/shard_map/all_gather | solution.py:155
  70.5 0.2 copy.63
  70.7 0.1 pad_maximum_fusion.1
  70.8 13.7 %all_gather.9 = bf16[512,512]{0,1:T(8,128)(2,1)} all-gather(bf16[512,128]{0,1:T(8,128)(2,1)S(1)} %bitcast.85), channel_id=1, replica_groups=mesh['nodes'=64,'heads'=4] {'heads'}, dimensions={1}, use_global_device_ids=true | all-gather | bytes 655360 | tf_op jit(solution)/shard_map/all_gather | solution.py:154
  84.5 47.0 %all-to-all-done.1 = bf16[64,64,512]{2,1,0:T(8,128)(2,1)} async-done(((bf16[64,64,512]{2,1,0:T(8,128)(2,1)}), bf16[64,64,512]{2,1,0:T(8,128)(2,1)}, u32[]{:S(2)}, u32[]{:S(2)}) %all-to-all-start.1) | async-done | bytes 4194336 | tf_op jit(solution)/shard_map/all_to_all | solution.py:158
  131.5 3.9 %shard_map.92 = bf16[32,32,512]{2,1,0:T(8,128)(2,1)} custom-call(s32[32]{0:T(128)} %get-tuple-element.19.pick_ref, bf16[128,32,512]{2,1,0:T(8,128)(2,1)} %bitcast.11.src_ref), custom_call_target="tpu_custom_call" | custom-call | tf_op jit(solution)/shard_map/pallas_call | solution.py:107
  135.4 2.5 %fusion.17 = f32[1024,4,2,128]{3,0,2,1:T(8,128)S(1)} fusion(bf16[1024,512,1,1]{1,0,3,2:T(8,128)(2,1)} %bitcast.70, bf16[4,2,128,512]{3,2,1,0:T(8,128)(2,1)S(1)} %bitcast.68), kind=kOutput, calls=%fused_computation.52 | convolution fusion | flops 1073741824 | bytes 6291456 | tf_op jit(solution)/shard_map/dot_general | solution.py:169
  137.9 0.1 slice.23
  138.0 1.6 fusion.13
  139.6 0.8 copy.68
  140.5 2.9 %copy.65 = f32[1024,4,1,128]{0,3,1,2:T(8,128)} copy(f32[1024,4,1,128]{3,0,2,1:T(8,128)} %get-tuple-element.24) | data formatting | bytes 4194304 | tf_op jit(solution)/shard_map/mul | solution.py:13
  143.4 2.4 %reduce_sum.49 = f32[1024,8]{0,1:T(8,128)} reduce(f32[1024,8,64]{0,2,1:T(8,128)} %bitcast.66, f32[]{:T(128)} %constant.72.clone.1), dimensions={2}, to_apply=%region_5.6 | reduce | flops 516096 | bytes 2129924 | tf_op jit(solution)/shard_map/reduce_sum | solution.py:13
  145.8 1.4 add_rsqrt_fusion
  147.2 1.8 copy.66
  149.0 3.5 %mul.115 = f32[1024,8,64]{2,1,0:T(8,128)} broadcast(f32[1024,8]{1,0:T(8,128)} %copy.66), dimensions={0,1} | broadcast | bytes 2129920 | tf_op jit(solution)/shard_map/mul | solution.py:14
  152.5 4.9 %mul.116 = f32[32,32,4,128]{3,2,1,0:T(4,128)} reshape(f32[1024,8,64]{2,1,0:T(8,128)} %mul.115) | data formatting | bytes 4194304 | tf_op jit(solution)/shard_map/mul | solution.py:14
  157.3 3.6 %fusion = bf16[32,32,4,128]{3,2,1,0:T(4,128)(2,1)S(1)} fusion(f32[32,32,4,128]{3,2,1,0:T(4,128)} %mul.116, f32[32,32,4,128]{3,1,0,2:T(8,128)S(1)} %bitcast.64), kind=kLoop, calls=%fused_computation.4 | loop fusion | flops 1048576 | bytes 5242880 | tf_op jit(solution)/shard_map/convert_element_type | solution.py:14
  161.0 1.5 maximum_bitcast_fusion
  162.5 1.7 copy.69
  164.3 4.6 %all-to-all-start.2 = ((bf16[4,32,32,256]{3,2,1,0:T(8,128)(2,1)}), bf16[4,32,32,256]{3,2,1,0:T(8,128)(2,1)S(1)}, u32[]{:S(2)}, u32[]{:S(2)}) async-start(bf16[4,32,32,256]{3,2,1,0:T(8,128)(2,1)} %copy.69), calls=%async_computation.2 | async-start | bytes 4194304 | tf_op jit(solution)/shard_map/all_to_all | solution.py:178
  169.0 0.9 copy.76
  169.9 2.1 copy.58
  172.0 1.3 select_bitcast_fusion.1
  173.3 0.1 select_bitcast_fusion
  173.6 22.8 %all-to-all-done.2 = bf16[4,32,32,256]{3,2,1,0:T(8,128)(2,1)S(1)} async-done(((bf16[4,32,32,256]{3,2,1,0:T(8,128)(2,1)}), bf16[4,32,32,256]{3,2,1,0:T(8,128)(2,1)S(1)}, u32[]{:S(2)}, u32[]{:S(2)}) %all-to-all-start.2) | async-done | bytes 2097184 | tf_op jit(solution)/shard_map/all_to_all | solution.py:178
  196.4 0.2 copy.70
  196.5 1.6 fusion.14
  198.1 0.7 copy.74
  198.8 1.4 pad_maximum_fusion.recv_ref
  200.2 8.7 %shard_map.93 = bf16[8,128,128]{2,1,0:T(8,128)(2,1)S(1)} custom-call(s32[32]{0:T(128)S(1)} %iota.20.slot_ref, s32[32]{0:T(128)S(1)} %reshape.157.live_ref, f32[2]{0:T(128)S(1)} %copy-done.1, bf16[8,128,256]{2,1,0:T(8,128)(2,1)S(1)} %pad_maximum_fusion.2.q_ref, bf16[8,256,128]{2,1,0:T(8,128)(2,1)S(1)} %pad_maximum_fusion.3.own_ref, ...), custom_call_target="tpu_custom_call" | custom-call | tf_op jit(solution)/shard_map/pallas_call | solution.py:82
  208.9 0.2 copy.72
  209.1 1.2 collective-permute-start.2
  210.3 0.9 collective-permute-start
  211.2 0.8 collective-permute-start.1
  211.9 1.0 fusion.8
  212.9 5.4 %collective-permute-done.2 = bf16[1024,128]{1,0:T(8,128)(2,1)S(1)} collective-permute-done((bf16[1024,128]{1,0:T(8,128)(2,1)S(1)}, bf16[1024,128]{1,0:T(8,128)(2,1)S(1)}, u32[]{:S(2)}, u32[]{:S(2)}) %collective-permute-start.2) | collective-permute-done | bytes 262176 | tf_op jit(solution)/shard_map/ppermute | solution.py:195
  218.3 1.0 fusion.4
  219.3 5.6 %collective-permute-done = bf16[1024,128]{1,0:T(8,128)(2,1)S(1)} collective-permute-done((bf16[1024,128]{1,0:T(8,128)(2,1)S(1)}, bf16[1024,128]{1,0:T(8,128)(2,1)S(1)}, u32[]{:S(2)}, u32[]{:S(2)}) %collective-permute-start) | collective-permute-done | bytes 262176 | tf_op jit(solution)/shard_map/ppermute | solution.py:195
  224.9 1.0 convolution_add_fusion.1
  225.9 1.7 fusion.2
  (39 shorter events, 0.8 us)
Async XLA Ops:
  0.0 36.6 %copy-start = (bf16[512,128]{1,0:T(8,128)(2,1)S(1)}, bf16[512,128]{1,0:T(8,128)(2,1)}, u32[]{:S(2)}) copy-start(bf16[512,128]{1,0:T(8,128)(2,1)} %param.10) | copy-start | bytes 393220
  4.3 20.5 %all-to-all-start = ((s32[64,1,2]{2,1,0:T(1,128)}), s32[64,1,2]{2,1,0:T(1,128)S(1)}, u32[]{:S(2)}, u32[]{:S(2)}) async-start(s32[64,1,2]{2,1,0:T(1,128)} %bitcast.8), calls=%async_computation | async-start | bytes 65536 | tf_op jit(solution)/shard_map/all_to_all | solution.py:143
  30.0 6.6 %copy-start.2 = (bf16[1024,512]{1,0:T(8,128)(2,1)S(1)}, bf16[1024,512]{1,0:T(8,128)(2,1)}, u32[]{:S(2)}) copy-start(bf16[1024,512]{1,0:T(8,128)(2,1)} %param.9) | copy-start | bytes 3145732
  30.0 101.5 %all-to-all-start.1 = ((bf16[64,64,512]{2,1,0:T(8,128)(2,1)}), bf16[64,64,512]{2,1,0:T(8,128)(2,1)}, u32[]{:S(2)}, u32[]{:S(2)}) async-start(bf16[64,64,512]{2,1,0:T(8,128)(2,1)} %bitcast.62), calls=%async_computation.1 | async-start | bytes 8388608 | tf_op jit(solution)/shard_map/all_to_all | solution.py:158
  37.1 2.3 copy-start.8
  38.3 1.6 copy-start.7
  56.4 14.4 %copy-start.9 = (bf16[128,512]{1,0:T(8,128)(2,1)S(1)}, bf16[128,512]{1,0:T(8,128)(2,1)}, u32[]{:S(2)}) copy-start(bf16[128,512]{1,0:T(8,128)(2,1)} %param.13) | copy-start | bytes 393220
  164.3 4.6 %copy-start.5 = (f32[1024,128]{0,1:T(8,128)S(1)}, f32[1024,128]{0,1:T(8,128)}, u32[]{:S(2)}) copy-start(f32[1024,128]{0,1:T(8,128)} %copy.57) | copy-start | bytes 1572868
  164.3 32.1 %all-to-all-start.2 = ((bf16[4,32,32,256]{3,2,1,0:T(8,128)(2,1)}), bf16[4,32,32,256]{3,2,1,0:T(8,128)(2,1)S(1)}, u32[]{:S(2)}, u32[]{:S(2)}) async-start(bf16[4,32,32,256]{3,2,1,0:T(8,128)(2,1)} %copy.69), calls=%async_computation.2 | async-start | bytes 4194304 | tf_op jit(solution)/shard_map/all_to_all | solution.py:178
  168.9 3.1 %copy-start.4 = (f32[8,128,128]{1,2,0:T(8,128)S(1)}, f32[8,128,128]{1,2,0:T(8,128)}, u32[]{:S(2)}) copy-start(f32[8,128,128]{1,2,0:T(8,128)} %copy.55) | copy-start | bytes 1572868
  169.9 3.6 %copy-start.3 = (f32[1024,128]{1,0:T(8,128)S(1)}, f32[1024,128]{1,0:T(8,128)}, u32[]{:S(2)}) copy-start(f32[1024,128]{1,0:T(8,128)} %get-tuple-element.30) | copy-start | bytes 1572868
  172.0 1.5 copy-start.6
  198.7 1.4 copy-start.1
  209.1 9.3 %collective-permute-start.2 = (bf16[1024,128]{1,0:T(8,128)(2,1)S(1)}, bf16[1024,128]{1,0:T(8,128)(2,1)S(1)}, u32[]{:S(2)}, u32[]{:S(2)}) collective-permute-start(bf16[1024,128]{1,0:T(8,128)(2,1)S(1)} %bitcast.79), channel_id=1, source_target_pairs={{0,3},{1,0},{2,1},{3,2},{4,7},{5,4},{6,5},{7,6},{8,11},{9,8},{10,9... | collective-permute-start | bytes 786440 | tf_op jit(solution)/shard_map/ppermute | solution.py:195
  210.3 14.6 %collective-permute-start = (bf16[1024,128]{1,0:T(8,128)(2,1)S(1)}, bf16[1024,128]{1,0:T(8,128)(2,1)S(1)}, u32[]{:S(2)}, u32[]{:S(2)}) collective-permute-start(bf16[1024,128]{1,0:T(8,128)(2,1)S(1)} %bitcast.80), channel_id=1, source_target_pairs={{0,1},{1,2},{2,3},{3,0},{4,5},{5,6},{6,7},{7,4},{8,9},{9,10},{10,1... | collective-permute-start | bytes 786440 | tf_op jit(solution)/shard_map/ppermute | solution.py:195
  211.2 14.7 %collective-permute-start.1 = (bf16[1024,128]{1,0:T(8,128)(2,1)S(1)}, bf16[1024,128]{1,0:T(8,128)(2,1)S(1)}, u32[]{:S(2)}, u32[]{:S(2)}) collective-permute-start(bf16[1024,128]{1,0:T(8,128)(2,1)S(1)} %bitcast.81), channel_id=1, source_target_pairs={{0,2},{1,3},{2,0},{3,1},{4,6},{5,7},{6,4},{7,5},{8,10},{9,11},{10,... | collective-permute-start | bytes 786440 | tf_op jit(solution)/shard_map/ppermute | solution.py:195

commit v9 on v8

--- a/solution.py
+++ b/solution.py
@@ -109,6 +109,36 @@
         grid_spec=grid_spec,
         out_shape=jax.ShapeDtypeStruct((tiles, r, l), blocks.dtype),
     )(pick, blocks)
+
+
+def project_kernel(x_ref, w_ref, out_ref, *, hd):
+    kv = jnp.dot(x_ref[...], w_ref[...], preferred_element_type=jnp.float32)
+    feat = kv.shape[1] // 2
+    keys = kv[:, :feat]
+    lane = lax.broadcasted_iota(jnp.int32, (1, feat), 1)
+    sq = keys * keys
+    scale = jnp.zeros(keys.shape, jnp.float32)
+    for h in range(feat // hd):
+        inside = (lane >= h * hd) & (lane < (h + 1) * hd)
+        total = jnp.sum(jnp.where(inside, sq, 0.0), axis=1, keepdims=True)
+        scale = jnp.where(inside, lax.rsqrt(total + 1e-06), scale)
+    out_ref[0, :, :feat] = (keys * scale).astype(out_ref.dtype)
+    out_ref[0, :, feat:] = kv[:, feat:].astype(out_ref.dtype)
+
+
+def project_all(rows, w_kv, heads, hd):
+    n, model = rows.shape
+    cols = w_kv.shape[1] // heads
+    return pl.pallas_call(
+        functools.partial(project_kernel, hd=hd),
+        grid=(heads,),
+        in_specs=[
+            pl.BlockSpec((n, model), lambda y: (0, 0)),
+            pl.BlockSpec((model, cols), lambda y: (0, y)),
+        ],
+        out_specs=pl.BlockSpec((1, n, cols), lambda y: (y, 0, 0)),
+        out_shape=jax.ShapeDtypeStruct((heads, n, cols), jnp.bfloat16),
+    )(rows, w_kv)
 
 
 def body(feats, w_query, w_key, w_value, w_out, head_scale, nbr_owner, nbr_local, slot_valid):
@@ -166,15 +196,9 @@
     slot_of = jnp.clip(target, 0, tile_count - 1).astype(jnp.int32)
     piece = gather_blocks(recv, slot_of)
     pairs = piece.shape[0]
-    kv_all = jnp.dot(
-        piece.reshape(pairs * quarter, model), w_kv_all, preferred_element_type=jnp.float32
-    ).reshape(pairs * quarter, heads, 2, feat)
-    k_all = unit_rows(kv_all[:, :, 0, :].reshape(pairs * quarter, heads * feat), heads * count)
-    v_all = kv_all[:, :, 1, :].astype(jnp.bfloat16)
-    send = jnp.concatenate(
-        [k_all.reshape(pairs * quarter, heads, feat), v_all], axis=2
-    ).reshape(pairs, quarter, heads, 2 * feat)
-    send = jnp.transpose(send, (2, 0, 1, 3))
+    send = project_all(piece.reshape(pairs * quarter, model), w_kv_all, heads, feat // count).reshape(
+        heads, pairs, quarter, 2 * feat
+    )
     got = lax.all_to_all(send, "heads", 0, 0, tiled=True)
     got = jnp.transpose(got, (1, 0, 2, 3)).reshape(pairs, width, 2 * feat)
     pair_kv = jnp.concatenate([got[:, :, :feat], jnp.swapaxes(got[:, :, feat:], 1, 2)], axis=1)

time: 229 us -> 205 us (0.90)
  local copies, waits for them, and re-layouts: 28.4 us -> 15 us
  other arithmetic: 15.6 us -> 7.64 us
  Pallas kernels: 16.9 us -> 21.9 us
  waiting for transfers between devices: 89.3 us -> 85.5 us
  matrix products: 9.14 us -> 6.64 us
    mul x5 -> x3, local copies, waits for them, and re-layouts: 10.6 us -> 2.19 us  [unit_rows(): shaped * lax.rsqrt(total + 1e-06)]
    pallas_call x0 -> x1, Pallas kernels: none -> 4.93 us  [project_all(): pl.pallas_call(functools.partial(project_kernel, hd=hd), grid=(heads,), i...]
    all_to_all x1, waiting for transfers between devices: 47 us -> 43.2 us  [body(): lax.all_to_all(payload.reshape(devices, capacity * quarter, model), 'node...]
    convert_element_type x2 -> x1, other arithmetic: 3.68 us -> 0.07 us  [unit_rows(): (shaped * lax.rsqrt(total + 1e-06)).astype(jnp.bfloat16)]
    mul x3 -> x2, local copies, waits for them, and re-layouts: 4.1 us -> 1.17 us  [unit_rows(): total = jnp.sum(shaped * shaped, axis=-1, keepdims=True)]
    dot_general x1 -> x0, matrix products: 2.5 us -> none  [body(): jnp.dot(piece.reshape(pairs * quarter, model), w_kv_all, preferred_elemen...]
    reduce_sum x3 -> x2, other arithmetic: 2.54 us -> 0.1 us  [unit_rows(): total = jnp.sum(shaped * shaped, axis=-1, keepdims=True)]
    another operation x1, other arithmetic: 0.1 us -> 2.43 us  [body(): jnp.stack([w_key_all, w_value_all], axis=2).reshape(model, heads * 2 * feat)]
  transfers between devices with their start and end apart: 6 -> 6, of which waited for: 5 -> 5; matrix products, arithmetic and copies ran while one was open for 6% -> 9% of each run, Pallas kernels for 0% -> 0%
where the time goes in v9:
time: 205 us; the launch traced here: 204 us
  waiting for transfers between devices  85.5 us (42%)
  blocking collectives  41.4 us (20%)
  starting transfers between devices  26.1 us (13%)
  Pallas kernels  21.9 us (11%)
  local copies, waits for them, and re-layouts  15 us (7%)
  other arithmetic  7.64 us (4%)
  matrix products  6.64 us (3%)
    all_to_all x1, waiting for transfers between devices, body(): lax.all_to_all(payload.reshape(devices, capacity * quarter, model), 'node...  43.2 us
    all_to_all x1, waiting for transfers between devices, body(): got = lax.all_to_all(send, 'heads', 0, 0, tiled=True)  22.7 us
    all_gather x1, blocking collectives, body(): lax.all_gather(w_value_b, 'heads', axis=1, tiled=True)  14 us
    all_gather x1, blocking collectives, body(): lax.all_gather(w_key_b, 'heads', axis=1, tiled=True)  13.9 us
    all_gather x1, blocking collectives, body(): w_out_t = lax.all_gather(w_out.T, 'heads', axis=1, tiled=True)  13.5 us
    all_to_all x1, starting transfers between devices, body(): lax.all_to_all(request.reshape(devices, capacity), 'nodes', split_axis=0,...  12 us
    ppermute x3, waiting for transfers between devices, body(): lax.ppermute(attn, 'heads', [(j, (j + k) % heads) for j in range(heads)])  11.1 us
    pallas_call x1, Pallas kernels, attend(): pl.pallas_call(functools.partial(attend_kernel, count=count, slots=slots)...  8.67 us
  transfers between devices with their start and end apart: 6, of which 5 were waited for; matrix products, arithmetic and copies ran while one was open for 9% of the time, Pallas kernels for 0%

profile of v9, /device:TPU:2, one launch (start us, length us, event | category | flops | bytes accessed | tf_op | source)
XLA Modules:
  0.0 204.5 jit_solution(10400527477815527561)
XLA Ops:
  0.0 0.7 compare_convert_fusion
  0.7 0.1 copy.46
  0.8 0.1 reshape.143.live_ref
  0.9 0.8 copy.53
  1.6 0.1 reshape.133
  1.7 0.1 fusion.9
  1.8 0.1 reduce_window_sum.11
  1.9 0.2 select_reduce_fusion.1
  2.0 0.8 copy.54
  2.8 0.1 reshape.134
  2.9 0.6 broadcast_clamp_fusion
  3.5 0.1 select_reduce_fusion
  3.6 0.8 sub.30
  4.3 12.0 %all-to-all-start = ((s32[64,1,2]{2,1,0:T(1,128)}), s32[64,1,2]{2,1,0:T(1,128)S(1)}, u32[]{:S(2)}, u32[]{:S(2)}) async-start(s32[64,1,2]{2,1,0:T(1,128)} %bitcast.8), calls=%async_computation | async-start | bytes 65536 | tf_op jit(solution)/shard_map/all_to_all | solution.py:173
  16.4 8.5 %all-to-all-done = s32[64,1,2]{2,1,0:T(1,128)S(1)} async-done(((s32[64,1,2]{2,1,0:T(1,128)}), s32[64,1,2]{2,1,0:T(1,128)S(1)}, u32[]{:S(2)}, u32[]{:S(2)}) %all-to-all-start) | async-done | bytes 544 | tf_op jit(solution)/shard_map/all_to_all | solution.py:173
  24.9 0.1 add_reduce_fusion
  25.0 0.7 add.110.pick_ref
  25.7 4.4 %shard_map.91 = bf16[128,32,512]{2,1,0:T(8,128)(2,1)} custom-call(s32[128]{0:T(128)} %add.110.pick_ref, bf16[32,32,512]{2,1,0:T(8,128)(2,1)} %bitcast.47), custom_call_target="tpu_custom_call" | custom-call | tf_op jit(solution)/shard_map/pallas_call | solution.py:107
  30.0 6.6 %all-to-all-start.1 = ((bf16[64,64,512]{2,1,0:T(8,128)(2,1)}), bf16[64,64,512]{2,1,0:T(8,128)(2,1)}, u32[]{:S(2)}, u32[]{:S(2)}) async-start(bf16[64,64,512]{2,1,0:T(8,128)(2,1)} %bitcast.46), calls=%async_computation.1 | async-start | bytes 8388608 | tf_op jit(solution)/shard_map/all_to_all | solution.py:188
  36.7 0.4 fusion.13
  37.1 0.0 copy-start.8
  37.1 1.0 copy.48
  38.1 0.2 copy.47
  38.3 0.0 copy-start.7
  38.3 0.1 bitcast_reduce_fusion.1
  38.5 0.9 copy.62
  39.4 0.4 convolution_convert_fusion
  39.8 0.2 copy.52
  40.0 1.2 fusion.14
  41.3 1.0 copy.50
  42.2 14.0 %all_gather.11 = bf16[512,512]{1,0:T(8,128)(2,1)S(1)} all-gather(bf16[512,128]{1,0:T(8,128)(2,1)S(1)} %copy-done.8), channel_id=1, replica_groups=mesh['nodes'=64,'heads'=4] {'heads'}, dimensions={1}, use_global_device_ids=true | all-gather | bytes 655360 | tf_op jit(solution)/shard_map/all_gather | solution.py:186
  56.2 0.3 stack_reshape.9
  56.5 13.9 %all_gather.10 = bf16[512,512]{1,0:T(8,128)(2,1)S(1)} all-gather(bf16[512,128]{1,0:T(8,128)(2,1)S(1)} %copy-done.7), channel_id=1, replica_groups=mesh['nodes'=64,'heads'=4] {'heads'}, dimensions={1}, use_global_device_ids=true | all-gather | bytes 655360 | tf_op jit(solution)/shard_map/all_gather | solution.py:185
  70.5 0.3 stack_reshape.8
  70.8 2.4 %pad_maximum_fusion.1 = bf16[512,4,2,128]{3,2,1,0:T(2,128)(2,1)S(1)} fusion(bf16[512,4,1,128]{3,2,1,0:T(2,128)(2,1)S(1)} %stack_reshape.9, bf16[512,4,1,128]{3,2,1,0:T(2,128)(2,1)S(1)} %stack_reshape.8), kind=kLoop, calls=%fused_computation.6 | loop fusion | flops 2097152 | bytes 2097152 | tf_op jit(solution)/shard_map/stack | solution.py:187
  73.2 0.0 copy-start.9
  73.2 1.6 reshape.138.w_ref
  74.8 13.5 %all_gather.9 = bf16[512,512]{0,1:T(8,128)(2,1)} all-gather(bf16[512,128]{0,1:T(8,128)(2,1)S(1)} %bitcast.64), channel_id=1, replica_groups=mesh['nodes'=64,'heads'=4] {'heads'}, dimensions={1}, use_global_device_ids=true | all-gather | bytes 655360 | tf_op jit(solution)/shard_map/all_gather | solution.py:184
  88.3 43.2 %all-to-all-done.1 = bf16[64,64,512]{2,1,0:T(8,128)(2,1)} async-done(((bf16[64,64,512]{2,1,0:T(8,128)(2,1)}), bf16[64,64,512]{2,1,0:T(8,128)(2,1)}, u32[]{:S(2)}, u32[]{:S(2)}) %all-to-all-start.1) | async-done | bytes 4194336 | tf_op jit(solution)/shard_map/all_to_all | solution.py:188
  131.5 3.9 %shard_map.92 = bf16[32,32,512]{2,1,0:T(8,128)(2,1)} custom-call(s32[32]{0:T(128)} %get-tuple-element.19.pick_ref, bf16[128,32,512]{2,1,0:T(8,128)(2,1)} %bitcast.11.src_ref), custom_call_target="tpu_custom_call" | custom-call | tf_op jit(solution)/shard_map/pallas_call | solution.py:107
  135.4 4.9 %shard_map.93 = bf16[4,1024,256]{2,1,0:T(8,128)(2,1)} custom-call(bf16[1024,512]{1,0:T(8,128)(2,1)} %bitcast.51, bf16[512,1024]{1,0:T(8,128)(2,1)} %reshape.138.w_ref), custom_call_target="tpu_custom_call" | custom-call | tf_op jit(solution)/shard_map/pallas_call | solution.py:132
  140.4 4.6 %all-to-all-start.2 = ((bf16[4,32,32,256]{3,2,1,0:T(8,128)(2,1)}), bf16[4,32,32,256]{3,2,1,0:T(8,128)(2,1)S(1)}, u32[]{:S(2)}, u32[]{:S(2)}) async-start(bf16[4,32,32,256]{3,2,1,0:T(8,128)(2,1)} %bitcast.48), calls=%async_computation.2 | async-start | bytes 4194304 | tf_op jit(solution)/shard_map/all_to_all | solution.py:202
  145.1 0.9 copy.63
  146.0 2.1 %copy.51 = f32[8,128,128]{2,1,0:T(8,128)} copy(f32[8,128,128]{1,0,2:T(8,128)} %bitcast.57) | data formatting | bytes 1048576 | tf_op jit(solution)/shard_map/mul | solution.py:14
  148.1 1.3 select_bitcast_fusion.1
  149.4 0.1 select_bitcast_fusion
  149.5 0.1 pad_maximum_fusion.2.q_ref
  149.6 0.1 multiply_convert_fusion
  149.7 22.7 %all-to-all-done.2 = bf16[4,32,32,256]{3,2,1,0:T(8,128)(2,1)S(1)} async-done(((bf16[4,32,32,256]{3,2,1,0:T(8,128)(2,1)}), bf16[4,32,32,256]{3,2,1,0:T(8,128)(2,1)S(1)}, u32[]{:S(2)}, u32[]{:S(2)}) %all-to-all-start.2) | async-done | bytes 2097184 | tf_op jit(solution)/shard_map/all_to_all | solution.py:202
  172.5 0.2 copy.58
  172.7 1.4 fusion.12
  174.0 1.3 copy.61
  175.4 1.7 pad_maximum_fusion.recv_ref
  177.1 8.7 %shard_map.94 = bf16[8,128,128]{2,1,0:T(8,128)(2,1)S(1)} custom-call(s32[32]{0:T(128)S(1)} %iota.20.slot_ref, s32[32]{0:T(128)S(1)} %reshape.143.live_ref, f32[2]{0:T(128)S(1)} %copy-done.1, bf16[8,128,256]{2,1,0:T(8,128)(2,1)S(1)} %pad_maximum_fusion.2.q_ref, bf16[8,256,128]{2,1,0:T(8,128)(2,1)S(1)} %pad_maximum_fusion.3.own_ref, ...), custom_call_target="tpu_custom_call" | custom-call | tf_op jit(solution)/shard_map/pallas_call | solution.py:82
  185.8 0.2 copy.60
  186.0 1.2 collective-permute-start.2
  187.2 0.9 collective-permute-start
  188.1 0.8 collective-permute-start.1
  188.8 1.0 fusion.7
  189.8 5.4 %collective-permute-done.2 = bf16[1024,128]{1,0:T(8,128)(2,1)S(1)} collective-permute-done((bf16[1024,128]{1,0:T(8,128)(2,1)S(1)}, bf16[1024,128]{1,0:T(8,128)(2,1)S(1)}, u32[]{:S(2)}, u32[]{:S(2)}) %collective-permute-start.2) | collective-permute-done | bytes 262176 | tf_op jit(solution)/shard_map/ppermute | solution.py:219
  195.2 1.0 fusion.3
  196.2 5.6 %collective-permute-done = bf16[1024,128]{1,0:T(8,128)(2,1)S(1)} collective-permute-done((bf16[1024,128]{1,0:T(8,128)(2,1)S(1)}, bf16[1024,128]{1,0:T(8,128)(2,1)S(1)}, u32[]{:S(2)}, u32[]{:S(2)}) %collective-permute-start) | collective-permute-done | bytes 262176 | tf_op jit(solution)/shard_map/ppermute | solution.py:219
  201.8 1.0 convolution_add_fusion.1
  202.8 1.7 fusion.1
  (28 shorter events, 0.3 us)
Async XLA Ops:
  0.0 36.7 %copy-start = (bf16[512,128]{1,0:T(8,128)(2,1)S(1)}, bf16[512,128]{1,0:T(8,128)(2,1)}, u32[]{:S(2)}) copy-start(bf16[512,128]{1,0:T(8,128)(2,1)} %param.10) | copy-start | bytes 393220
  4.3 20.5 %all-to-all-start = ((s32[64,1,2]{2,1,0:T(1,128)}), s32[64,1,2]{2,1,0:T(1,128)S(1)}, u32[]{:S(2)}, u32[]{:S(2)}) async-start(s32[64,1,2]{2,1,0:T(1,128)} %bitcast.8), calls=%async_computation | async-start | bytes 65536 | tf_op jit(solution)/shard_map/all_to_all | solution.py:173
  30.0 6.6 %copy-start.2 = (bf16[1024,512]{1,0:T(8,128)(2,1)S(1)}, bf16[1024,512]{1,0:T(8,128)(2,1)}, u32[]{:S(2)}) copy-start(bf16[1024,512]{1,0:T(8,128)(2,1)} %param.9) | copy-start | bytes 3145732
  30.0 101.5 %all-to-all-start.1 = ((bf16[64,64,512]{2,1,0:T(8,128)(2,1)}), bf16[64,64,512]{2,1,0:T(8,128)(2,1)}, u32[]{:S(2)}, u32[]{:S(2)}) async-start(bf16[64,64,512]{2,1,0:T(8,128)(2,1)} %bitcast.46), calls=%async_computation.1 | async-start | bytes 8388608 | tf_op jit(solution)/shard_map/all_to_all | solution.py:188
  37.1 2.3 %copy-start.8 = (bf16[512,128]{1,0:T(8,128)(2,1)S(1)}, bf16[512,128]{1,0:T(8,128)(2,1)}, u32[]{:S(2)}) copy-start(bf16[512,128]{1,0:T(8,128)(2,1)} %param.12) | copy-start | bytes 393220
  38.3 1.7 copy-start.7
  73.2 1.6 copy-start.9
  140.4 4.6 %copy-start.5 = (f32[1024,128]{0,1:T(8,128)S(1)}, f32[1024,128]{0,1:T(8,128)}, u32[]{:S(2)}) copy-start(f32[1024,128]{0,1:T(8,128)} %copy.50) | copy-start | bytes 1572868
  140.4 32.1 %all-to-all-start.2 = ((bf16[4,32,32,256]{3,2,1,0:T(8,128)(2,1)}), bf16[4,32,32,256]{3,2,1,0:T(8,128)(2,1)S(1)}, u32[]{:S(2)}, u32[]{:S(2)}) async-start(bf16[4,32,32,256]{3,2,1,0:T(8,128)(2,1)} %bitcast.48), calls=%async_computation.2 | async-start | bytes 4194304 | tf_op jit(solution)/shard_map/all_to_all | solution.py:202
  145.0 3.2 %copy-start.4 = (f32[8,128,128]{1,2,0:T(8,128)S(1)}, f32[8,128,128]{1,2,0:T(8,128)}, u32[]{:S(2)}) copy-start(f32[8,128,128]{1,2,0:T(8,128)} %copy.48) | copy-start | bytes 1572868
  146.0 3.6 %copy-start.3 = (f32[1024,128]{1,0:T(8,128)S(1)}, f32[1024,128]{1,0:T(8,128)}, u32[]{:S(2)}) copy-start(f32[1024,128]{1,0:T(8,128)} %get-tuple-element.28) | copy-start | bytes 1572868
  148.1 1.5 copy-start.6
  175.4 1.7 copy-start.1
  186.0 9.3 %collective-permute-start.2 = (bf16[1024,128]{1,0:T(8,128)(2,1)S(1)}, bf16[1024,128]{1,0:T(8,128)(2,1)S(1)}, u32[]{:S(2)}, u32[]{:S(2)}) collective-permute-start(bf16[1024,128]{1,0:T(8,128)(2,1)S(1)} %bitcast.58), channel_id=1, source_target_pairs={{0,3},{1,0},{2,1},{3,2},{4,7},{5,4},{6,5},{7,6},{8,11},{9,8},{10,9... | collective-permute-start | bytes 786440 | tf_op jit(solution)/shard_map/ppermute | solution.py:219
  187.2 14.6 %collective-permute-start = (bf16[1024,128]{1,0:T(8,128)(2,1)S(1)}, bf16[1024,128]{1,0:T(8,128)(2,1)S(1)}, u32[]{:S(2)}, u32[]{:S(2)}) collective-permute-start(bf16[1024,128]{1,0:T(8,128)(2,1)S(1)} %bitcast.59), channel_id=1, source_target_pairs={{0,1},{1,2},{2,3},{3,0},{4,5},{5,6},{6,7},{7,4},{8,9},{9,10},{10,1... | collective-permute-start | bytes 786440 | tf_op jit(solution)/shard_map/ppermute | solution.py:219
  188.1 14.7 %collective-permute-start.1 = (bf16[1024,128]{1,0:T(8,128)(2,1)S(1)}, bf16[1024,128]{1,0:T(8,128)(2,1)S(1)}, u32[]{:S(2)}, u32[]{:S(2)}) collective-permute-start(bf16[1024,128]{1,0:T(8,128)(2,1)S(1)} %bitcast.60), channel_id=1, source_target_pairs={{0,2},{1,3},{2,0},{3,1},{4,6},{5,7},{6,4},{7,5},{8,10},{9,11},{10,... | collective-permute-start | bytes 786440 | tf_op jit(solution)/shard_map/ppermute | solution.py:219

commit v10 on v9

--- a/solution.py
+++ b/solution.py
@@ -17,8 +17,8 @@
 def attend_kernel(slot_ref, live_ref, scale_ref, q_ref, own_ref, recv_ref, out_ref, buf, sems, *, count, slots):
     b = pl.program_id(0)
     pairs = buf.shape[0]
-    feat, lanes = q_ref.shape[1], q_ref.shape[2]
-    width = lanes // count
+    stacked, feat = q_ref.shape[1], q_ref.shape[2]
+    width = stacked // count
     hd = feat // count
 
     def pair_copy(p):
@@ -31,58 +31,59 @@
 
     for s in range(slots):
         pair_copy(b * slots + s).wait()
-    q_stack = q_ref[0]
-    row_head = lax.broadcasted_iota(jnp.int32, (feat, width), 0) // hd
-    lane_pos = lax.broadcasted_iota(jnp.int32, (1, lanes), 1)
-    scale_row = jnp.zeros((1, lanes), jnp.float32)
+    lane_head = lax.broadcasted_iota(jnp.int32, (width, feat), 1) // hd
+    stack_rows = lax.broadcasted_iota(jnp.int32, (stacked, 1), 0)
+    scale_col = jnp.zeros((stacked, 1), jnp.float32)
     for h in range(count):
-        inside = (lane_pos >= h * width) & (lane_pos < (h + 1) * width)
-        scale_row = jnp.where(inside, scale_ref[h], scale_row)
-    key_rows = lax.broadcasted_iota(jnp.int32, ((slots + 1) * width, 1), 0)
-    live_col = jnp.ones(((slots + 1) * width, 1), jnp.float32)
+        inside = (stack_rows >= h * width) & (stack_rows < (h + 1) * width)
+        scale_col = jnp.where(inside, scale_ref[h], scale_col)
+    key_lanes = lax.broadcasted_iota(jnp.int32, (1, (slots + 1) * width), 1)
+    live_row = jnp.ones((1, (slots + 1) * width), jnp.float32)
     for s in range(slots):
-        inside = (key_rows >= (s + 1) * width) & (key_rows < (s + 2) * width)
-        live_col = jnp.where(inside, live_ref[b * slots + s].astype(jnp.float32), live_col)
+        inside = (key_lanes >= (s + 1) * width) & (key_lanes < (s + 2) * width)
+        live_row = jnp.where(inside, live_ref[b * slots + s].astype(jnp.float32), live_row)
     blocks = [own_ref[b]] + [buf[b * slots + s] for s in range(slots)]
-    keys = jnp.concatenate([blk[:width] for blk in blocks], axis=0)
-    values_t = jnp.concatenate([blk[width:] for blk in blocks], axis=1)
-    s_all = jnp.dot(keys, q_stack, preferred_element_type=jnp.float32)
-    w = jnp.exp(scale_row * (s_all - 1.0)) * live_col
-    den = jnp.sum(w, axis=0, keepdims=True)
+    keys = jnp.concatenate([blk[:, :feat] for blk in blocks], axis=0)
+    values = jnp.concatenate([blk[:, feat:] for blk in blocks], axis=0)
+    s_all = lax.dot_general(
+        q_ref[0], keys, (((1,), (1,)), ((), ())), preferred_element_type=jnp.float32
+    )
+    w = jnp.exp(scale_col * (s_all - 1.0)) * live_row
+    den = jnp.sum(w, axis=1, keepdims=True)
     w_b = w.astype(jnp.bfloat16)
-    num = jnp.zeros((feat, width), jnp.float32)
-    den_full = jnp.zeros((feat, width), jnp.float32)
+    num = jnp.zeros((width, feat), jnp.float32)
+    den_full = jnp.zeros((width, feat), jnp.float32)
     for h in range(count):
-        part = jnp.dot(values_t, w_b[:, h * width:(h + 1) * width], preferred_element_type=jnp.float32)
-        num = jnp.where(row_head == h, part, num)
-        den_full = jnp.where(row_head == h, den[:, h * width:(h + 1) * width], den_full)
+        part = jnp.dot(w_b[h * width:(h + 1) * width], values, preferred_element_type=jnp.float32)
+        num = jnp.where(lane_head == h, part, num)
+        den_full = jnp.where(lane_head == h, den[h * width:(h + 1) * width], den_full)
     out_ref[0] = (num / den_full).astype(out_ref.dtype)
 
 
 def attend(query_stack, own_kv, recv_kv, slot_of, live, scales):
-    nblocks, feat, lanes = query_stack.shape
+    nblocks, stacked, feat = query_stack.shape
     count = scales.shape[0]
-    width = lanes // count
+    width = stacked // count
     slots = slot_of.shape[0] // nblocks
     grid_spec = pltpu.PrefetchScalarGridSpec(
         num_scalar_prefetch=2,
         grid=(nblocks,),
         in_specs=[
             pl.BlockSpec(memory_space=pltpu.SMEM),
-            pl.BlockSpec((1, feat, lanes), lambda b, slot_of, live: (b, 0, 0)),
-            pl.BlockSpec((nblocks, 2 * width, feat), lambda b, slot_of, live: (0, 0, 0)),
+            pl.BlockSpec((1, stacked, feat), lambda b, slot_of, live: (b, 0, 0)),
+            pl.BlockSpec((nblocks, width, 2 * feat), lambda b, slot_of, live: (0, 0, 0)),
             pl.BlockSpec(memory_space=pl.ANY),
         ],
-        out_specs=pl.BlockSpec((1, feat, width), lambda b, slot_of, live: (b, 0, 0)),
+        out_specs=pl.BlockSpec((1, width, feat), lambda b, slot_of, live: (b, 0, 0)),
         scratch_shapes=[
-            pltpu.VMEM((nblocks * slots, 2 * width, feat), recv_kv.dtype),
+            pltpu.VMEM((nblocks * slots, width, 2 * feat), recv_kv.dtype),
             pltpu.SemaphoreType.DMA((nblocks * slots,)),
         ],
     )
     return pl.pallas_call(
         functools.partial(attend_kernel, count=count, slots=slots),
         grid_spec=grid_spec,
-        out_shape=jax.ShapeDtypeStruct((nblocks, feat, width), jnp.bfloat16),
+        out_shape=jax.ShapeDtypeStruct((nblocks, width, feat), jnp.bfloat16),
         compiler_params=pltpu.CompilerParams(vmem_limit_bytes=48 * 1024 * 1024),
     )(slot_of, live, scales, query_stack, own_kv, recv_kv)
 
@@ -153,15 +154,12 @@
     query_n = unit_rows(jnp.dot(feats, w_query, preferred_element_type=jnp.float32), count)
     key_n = unit_rows(jnp.dot(feats, w_key, preferred_element_type=jnp.float32), count)
     value_b = jnp.dot(feats, w_value, preferred_element_type=jnp.float32).astype(jnp.bfloat16)
-    query_t = jnp.swapaxes(query_n.reshape(nblocks, width, feat), 1, 2)
+    query_blocks = query_n.reshape(nblocks, width, feat)
     head_of = jnp.arange(feat, dtype=jnp.int32) // (feat // count)
     query_stack = jnp.concatenate(
-        [jnp.where(head_of[None, :, None] == h, query_t, 0) for h in range(count)], axis=2
-    )
-    own_kv = jnp.concatenate(
-        [key_n.reshape(nblocks, width, feat), jnp.swapaxes(value_b.reshape(nblocks, width, feat), 1, 2)],
-        axis=1,
-    )
+        [jnp.where(head_of[None, None, :] == h, query_blocks, 0) for h in range(count)], axis=1
+    )
+    own_kv = jnp.concatenate([key_n, value_b], axis=1).reshape(nblocks, width, 2 * feat)
     owners = nbr_owner.reshape(-1)
     owner_hot = (owners[:, None] == jnp.arange(devices, dtype=jnp.int32)[None, :]).astype(jnp.int32)
     rank = jnp.sum(jnp.cumsum(owner_hot, axis=0) * owner_hot, axis=1) - 1
@@ -200,11 +198,10 @@
         heads, pairs, quarter, 2 * feat
     )
     got = lax.all_to_all(send, "heads", 0, 0, tiled=True)
-    got = jnp.transpose(got, (1, 0, 2, 3)).reshape(pairs, width, 2 * feat)
-    pair_kv = jnp.concatenate([got[:, :, :feat], jnp.swapaxes(got[:, :, feat:], 1, 2)], axis=1)
+    pair_kv = jnp.transpose(got, (1, 0, 2, 3)).reshape(pairs, width, 2 * feat)
     pair_ids = jnp.arange(pairs, dtype=jnp.int32)
     attn_t = attend(query_stack, own_kv, pair_kv, pair_ids, valid, head_scale)
-    attn = jnp.swapaxes(attn_t, 1, 2).reshape(rows, feat)
+    attn = attn_t.reshape(rows, feat)
     heads = lax.axis_size("heads")
     me = lax.axis_index("heads")
 

time: 205 us -> 202 us (0.985)
    all_to_all x1, waiting for transfers between devices: 43.2 us -> 39.7 us  [body(): lax.all_to_all(payload.reshape(devices, capacity * quarter, model), 'node...]
    another operation x2, local copies, waits for them, and re-layouts: 0.6 us -> 3.69 us  [body(): jnp.stack([w_key_all, w_value_all], axis=2).reshape(model, heads * 2 * feat)]
    unnamed x25 -> x21, local copies, waits for them, and re-layouts: 4.73 us -> 1.66 us
  transfers between devices with their start and end apart: 6 -> 6, of which waited for: 5 -> 5; matrix products, arithmetic and copies ran while one was open for 9% -> 10% of each run, Pallas kernels for 0% -> 0%
where the time goes in v10:
time: 202 us; the launch traced here: 201 us
  waiting for transfers between devices  83.9 us (42%)
  blocking collectives  42 us (21%)
  starting transfers between devices  26.1 us (13%)
  Pallas kernels  21.3 us (11%)
  local copies, waits for them, and re-layouts  14.3 us (7%)
  matrix products  7.47 us (4%)
  other arithmetic  5.98 us (3%)
    all_to_all x1, waiting for transfers between devices, body(): lax.all_to_all(payload.reshape(devices, capacity * quarter, model), 'node...  39.7 us
    all_to_all x1, waiting for transfers between devices, body(): got = lax.all_to_all(send, 'heads', 0, 0, tiled=True)  24.4 us
    all_gather x1, blocking collectives, body(): lax.all_gather(w_key_b, 'heads', axis=1, tiled=True)  14.5 us
    all_gather x1, blocking collectives, body(): lax.all_gather(w_value_b, 'heads', axis=1, tiled=True)  14 us
    all_gather x1, blocking collectives, body(): w_out_t = lax.all_gather(w_out.T, 'heads', axis=1, tiled=True)  13.5 us
    all_to_all x1, starting transfers between devices, body(): lax.all_to_all(request.reshape(devices, capacity), 'nodes', split_axis=0,...  12 us
    ppermute x3, waiting for transfers between devices, body(): lax.ppermute(attn, 'heads', [(j, (j + k) % heads) for j in range(heads)])  11.3 us
    all_to_all x1, waiting for transfers between devices, body(): lax.all_to_all(request.reshape(devices, capacity), 'nodes', split_axis=0,...  8.51 us
  transfers between devices with their start and end apart: 6, of which 5 were waited for; matrix products, arithmetic and copies ran while one was open for 10% of the time, Pallas kernels for 0%

profile of v10, /device:TPU:2, one launch (start us, length us, event | category | flops | bytes accessed | tf_op | source)
XLA Modules:
  0.0 201.4 jit_solution(14501298669157970032)
XLA Ops:
  0.0 0.0 copy-start
  0.0 0.7 compare_convert_fusion
  0.7 0.1 copy.37
  0.8 0.1 reshape.139.live_ref
  0.9 0.8 copy.42
  1.6 0.1 reshape.129
  1.7 0.1 fusion.8
  1.8 0.1 reduce_window_sum.11
  1.9 0.2 select_reduce_fusion.1
  2.0 0.8 copy.43
  2.8 0.1 reshape.130
  2.9 0.5 broadcast_clamp_fusion
  3.4 0.1 select_reduce_fusion
  3.5 0.8 sub.30
  4.2 12.0 %all-to-all-start = ((s32[64,1,2]{2,1,0:T(1,128)}), s32[64,1,2]{2,1,0:T(1,128)S(1)}, u32[]{:S(2)}, u32[]{:S(2)}) async-start(s32[64,1,2]{2,1,0:T(1,128)} %bitcast.6), calls=%async_computation | async-start | bytes 65536 | tf_op jit(solution)/shard_map/all_to_all | solution.py:171
  16.3 8.5 %all-to-all-done = s32[64,1,2]{2,1,0:T(1,128)S(1)} async-done(((s32[64,1,2]{2,1,0:T(1,128)}), s32[64,1,2]{2,1,0:T(1,128)S(1)}, u32[]{:S(2)}, u32[]{:S(2)}) %all-to-all-start) | async-done | bytes 544 | tf_op jit(solution)/shard_map/all_to_all | solution.py:171
  24.8 0.1 add_reduce_fusion
  24.9 0.7 add.110.pick_ref
  25.6 4.4 %shard_map.91 = bf16[128,32,512]{2,1,0:T(8,128)(2,1)} custom-call(s32[128]{0:T(128)} %add.110.pick_ref, bf16[32,32,512]{2,1,0:T(8,128)(2,1)} %bitcast.39), custom_call_target="tpu_custom_call" | custom-call | tf_op jit(solution)/shard_map/pallas_call | solution.py:108
  29.9 6.6 %all-to-all-start.1 = ((bf16[64,64,512]{2,1,0:T(8,128)(2,1)}), bf16[64,64,512]{2,1,0:T(8,128)(2,1)}, u32[]{:S(2)}, u32[]{:S(2)}) async-start(bf16[64,64,512]{2,1,0:T(8,128)(2,1)} %bitcast.38), calls=%async_computation.1 | async-start | bytes 8388608 | tf_op jit(solution)/shard_map/all_to_all | solution.py:186
  36.6 0.0 copy-done
  36.6 0.0 copy-done.2
  36.6 0.0 copy-start.5
  36.6 1.2 fusion.10
  37.8 0.2 copy.38
  38.0 0.0 copy-start.6
  38.1 1.2 fusion.11
  39.3 0.2 copy.40
  39.6 0.6 add_rsqrt_fusion.1
  40.2 14.0 %all_gather.11 = bf16[512,512]{1,0:T(8,128)(2,1)S(1)} all-gather(bf16[512,128]{1,0:T(8,128)(2,1)S(1)} %copy-done.6), channel_id=1, replica_groups=mesh['nodes'=64,'heads'=4] {'heads'}, dimensions={1}, use_global_device_ids=true | all-gather | bytes 655360 | tf_op jit(solution)/shard_map/all_gather | solution.py:184
  54.2 0.3 stack_reshape.9
  54.5 14.5 %all_gather.10 = bf16[512,512]{1,0:T(8,128)(2,1)} all-gather(bf16[512,128]{1,0:T(8,128)(2,1)S(1)} %copy-done.5), channel_id=1, replica_groups=mesh['nodes'=64,'heads'=4] {'heads'}, dimensions={1}, use_global_device_ids=true | all-gather | bytes 655360 | tf_op jit(solution)/shard_map/all_gather | solution.py:183
  69.0 3.4 %stack_reshape.8 = bf16[512,4,1,128]{3,2,1,0:T(2,128)(2,1)S(1)} reshape(bf16[512,512]{1,0:T(8,128)(2,1)} %all_gather.10) | data formatting | bytes 1048576 | tf_op jit(solution)/shard_map/stack;reshape | solution.py:185
  72.4 0.0 copy-start.7
  72.4 3.2 %pad_maximum_fusion = bf16[512,4,2,128]{3,2,1,0:T(2,128)(2,1)} fusion(bf16[512,4,1,128]{3,2,1,0:T(2,128)(2,1)S(1)} %stack_reshape.9, bf16[512,4,1,128]{3,2,1,0:T(2,128)(2,1)S(1)} %stack_reshape.8), kind=kLoop, calls=%fused_computation.5 | loop fusion | flops 2097152 | bytes 2097152 | tf_op jit(solution)/shard_map/stack | solution.py:185
  75.6 2.6 %reshape.134.w_ref = bf16[512,1024]{1,0:T(8,128)(2,1)} reshape(bf16[512,4,2,128]{3,2,1,0:T(2,128)(2,1)} %pad_maximum_fusion) | data formatting | bytes 2097152 | tf_op jit(solution)/shard_map/reshape | solution.py:185
  78.2 13.5 %all_gather.9 = bf16[512,512]{0,1:T(8,128)(2,1)} all-gather(bf16[512,128]{0,1:T(8,128)(2,1)S(1)} %bitcast.48), channel_id=1, replica_groups=mesh['nodes'=64,'heads'=4] {'heads'}, dimensions={1}, use_global_device_ids=true | all-gather | bytes 655360 | tf_op jit(solution)/shard_map/all_gather | solution.py:182
  91.7 39.7 %all-to-all-done.1 = bf16[64,64,512]{2,1,0:T(8,128)(2,1)} async-done(((bf16[64,64,512]{2,1,0:T(8,128)(2,1)}), bf16[64,64,512]{2,1,0:T(8,128)(2,1)}, u32[]{:S(2)}, u32[]{:S(2)}) %all-to-all-start.1) | async-done | bytes 4194336 | tf_op jit(solution)/shard_map/all_to_all | solution.py:186
  131.4 3.9 %shard_map.92 = bf16[32,32,512]{2,1,0:T(8,128)(2,1)} custom-call(s32[32]{0:T(128)} %get-tuple-element.19.pick_ref, bf16[128,32,512]{2,1,0:T(8,128)(2,1)} %bitcast.9.src_ref), custom_call_target="tpu_custom_call" | custom-call | tf_op jit(solution)/shard_map/pallas_call | solution.py:108
  135.3 4.9 %shard_map.93 = bf16[4,1024,256]{2,1,0:T(8,128)(2,1)} custom-call(bf16[1024,512]{1,0:T(8,128)(2,1)} %bitcast.41, bf16[512,1024]{1,0:T(8,128)(2,1)} %reshape.134.w_ref), custom_call_target="tpu_custom_call" | custom-call | tf_op jit(solution)/shard_map/pallas_call | solution.py:133
  140.2 4.6 %all-to-all-start.2 = ((bf16[4,32,32,256]{3,2,1,0:T(8,128)(2,1)}), bf16[4,32,32,256]{3,2,1,0:T(8,128)(2,1)}, u32[]{:S(2)}, u32[]{:S(2)}) async-start(bf16[4,32,32,256]{3,2,1,0:T(8,128)(2,1)} %bitcast.40), calls=%async_computation.2 | async-start | bytes 4194304 | tf_op jit(solution)/shard_map/all_to_all | solution.py:200
  144.9 0.1 copy.48
  145.0 0.2 copy.39
  145.3 0.8 mul.85
  146.1 1.3 copy.41
  147.4 0.0 copy-done.4
  147.4 0.1 broadcast_select_fusion.1
  147.7 0.1 multiply_convert_fusion
  147.7 0.4 convolution_convert_fusion
  148.1 0.1 pad_maximum_fusion.2.own_ref
  148.2 24.4 %all-to-all-done.2 = bf16[4,32,32,256]{3,2,1,0:T(8,128)(2,1)} async-done(((bf16[4,32,32,256]{3,2,1,0:T(8,128)(2,1)}), bf16[4,32,32,256]{3,2,1,0:T(8,128)(2,1)}, u32[]{:S(2)}, u32[]{:S(2)}) %all-to-all-start.2) | async-done | bytes 2097184 | tf_op jit(solution)/shard_map/all_to_all | solution.py:200
  172.7 1.8 copy.47
  174.5 0.0 copy-done.1
  174.5 8.1 %shard_map.94 = bf16[8,128,128]{2,1,0:T(8,128)(2,1)S(1)} custom-call(s32[32]{0:T(128)S(1)} %iota.20.slot_ref, s32[32]{0:T(128)S(1)} %reshape.139.live_ref, f32[2]{0:T(128)S(1)} %copy-done.1, bf16[8,256,128]{2,1,0:T(8,128)(2,1)S(1)} %pad_maximum_fusion.1.q_ref, bf16[8,128,256]{2,1,0:T(8,128)(2,1)S(1)} %pad_maximum_fusion.2.own_ref, ...), custom_call_target="tpu_custom_call" | custom-call | tf_op jit(solution)/shard_map/pallas_call | solution.py:83
  182.6 1.2 collective-permute-start.2
  183.9 0.9 collective-permute-start
  184.7 0.8 collective-permute-start.1
  185.5 1.0 fusion.6
  186.5 5.4 %collective-permute-done.2 = bf16[1024,128]{1,0:T(8,128)(2,1)S(1)} collective-permute-done((bf16[1024,128]{1,0:T(8,128)(2,1)S(1)}, bf16[1024,128]{1,0:T(8,128)(2,1)S(1)}, u32[]{:S(2)}, u32[]{:S(2)}) %collective-permute-start.2) | collective-permute-done | bytes 262176 | tf_op jit(solution)/shard_map/ppermute | solution.py:216
  191.9 1.0 fusion.2
  192.8 5.9 %collective-permute-done = bf16[1024,128]{1,0:T(8,128)(2,1)S(1)} collective-permute-done((bf16[1024,128]{1,0:T(8,128)(2,1)S(1)}, bf16[1024,128]{1,0:T(8,128)(2,1)S(1)}, u32[]{:S(2)}, u32[]{:S(2)}) %collective-permute-start) | collective-permute-done | bytes 262176 | tf_op jit(solution)/shard_map/ppermute | solution.py:216
  198.7 1.0 convolution_add_fusion.1
  199.7 0.0 collective-permute-done.1
  199.7 1.7 fusion.1
  (20 shorter events, 0.3 us)
Async XLA Ops:
  0.0 36.6 %copy-start = (bf16[512,128]{1,0:T(8,128)(2,1)S(1)}, bf16[512,128]{1,0:T(8,128)(2,1)}, u32[]{:S(2)}) copy-start(bf16[512,128]{1,0:T(8,128)(2,1)} %param.10) | copy-start | bytes 393220
  4.2 20.5 %all-to-all-start = ((s32[64,1,2]{2,1,0:T(1,128)}), s32[64,1,2]{2,1,0:T(1,128)S(1)}, u32[]{:S(2)}, u32[]{:S(2)}) async-start(s32[64,1,2]{2,1,0:T(1,128)} %bitcast.6), calls=%async_computation | async-start | bytes 65536 | tf_op jit(solution)/shard_map/all_to_all | solution.py:171
  29.9 6.6 %copy-start.2 = (bf16[1024,512]{1,0:T(8,128)(2,1)S(1)}, bf16[1024,512]{1,0:T(8,128)(2,1)}, u32[]{:S(2)}) copy-start(bf16[1024,512]{1,0:T(8,128)(2,1)} %param.9) | copy-start | bytes 3145732
  29.9 101.5 %all-to-all-start.1 = ((bf16[64,64,512]{2,1,0:T(8,128)(2,1)}), bf16[64,64,512]{2,1,0:T(8,128)(2,1)}, u32[]{:S(2)}, u32[]{:S(2)}) async-start(bf16[64,64,512]{2,1,0:T(8,128)(2,1)} %bitcast.38), calls=%async_computation.1 | async-start | bytes 8388608 | tf_op jit(solution)/shard_map/all_to_all | solution.py:186
  36.6 1.5 copy-start.5
  38.0 2.2 %copy-start.6 = (bf16[512,128]{1,0:T(8,128)(2,1)S(1)}, bf16[512,128]{1,0:T(8,128)(2,1)}, u32[]{:S(2)}) copy-start(bf16[512,128]{1,0:T(8,128)(2,1)} %param.12) | copy-start | bytes 393220
  72.4 5.8 %copy-start.7 = (bf16[128,512]{1,0:T(8,128)(2,1)S(1)}, bf16[128,512]{1,0:T(8,128)(2,1)}, u32[]{:S(2)}) copy-start(bf16[128,512]{1,0:T(8,128)(2,1)} %param.13) | copy-start | bytes 393220
  140.2 4.6 %copy-start.8 = (f32[1024,2]{0,1:T(2,128)S(1)}, f32[1024,2]{0,1:T(2,128)}, u32[]{:S(2)}) copy-start(f32[1024,2]{0,1:T(2,128)} %add_rsqrt_fusion.1) | copy-start | bytes 24580
  140.2 32.4 %all-to-all-start.2 = ((bf16[4,32,32,256]{3,2,1,0:T(8,128)(2,1)}), bf16[4,32,32,256]{3,2,1,0:T(8,128)(2,1)}, u32[]{:S(2)}, u32[]{:S(2)}) async-start(bf16[4,32,32,256]{3,2,1,0:T(8,128)(2,1)} %bitcast.40), calls=%async_computation.2 | async-start | bytes 4194304 | tf_op jit(solution)/shard_map/all_to_all | solution.py:200
  144.9 2.6 %copy-start.4 = (f32[1024,128]{1,0:T(8,128)S(1)}, f32[1024,128]{1,0:T(8,128)}, u32[]{:S(2)}) copy-start(f32[1024,128]{1,0:T(8,128)} %get-tuple-element.24) | copy-start | bytes 1572868
  146.1 1.5 copy-start.3
  172.7 1.9 copy-start.1
  182.6 9.2 %collective-permute-start.2 = (bf16[1024,128]{1,0:T(8,128)(2,1)S(1)}, bf16[1024,128]{1,0:T(8,128)(2,1)S(1)}, u32[]{:S(2)}, u32[]{:S(2)}) collective-permute-start(bf16[1024,128]{1,0:T(8,128)(2,1)S(1)} %bitcast.34), channel_id=1, source_target_pairs={{0,3},{1,0},{2,1},{3,2},{4,7},{5,4},{6,5},{7,6},{8,11},{9,8},{10,9... | collective-permute-start | bytes 786440 | tf_op jit(solution)/shard_map/ppermute | solution.py:216
  183.9 14.8 %collective-permute-start = (bf16[1024,128]{1,0:T(8,128)(2,1)S(1)}, bf16[1024,128]{1,0:T(8,128)(2,1)S(1)}, u32[]{:S(2)}, u32[]{:S(2)}) collective-permute-start(bf16[1024,128]{1,0:T(8,128)(2,1)S(1)} %bitcast.35), channel_id=1, source_target_pairs={{0,1},{1,2},{2,3},{3,0},{4,5},{5,6},{6,7},{7,4},{8,9},{9,10},{10,1... | collective-permute-start | bytes 786440 | tf_op jit(solution)/shard_map/ppermute | solution.py:216
  184.7 15.0 %collective-permute-start.1 = (bf16[1024,128]{1,0:T(8,128)(2,1)S(1)}, bf16[1024,128]{1,0:T(8,128)(2,1)S(1)}, u32[]{:S(2)}, u32[]{:S(2)}) collective-permute-start(bf16[1024,128]{1,0:T(8,128)(2,1)S(1)} %bitcast.36), channel_id=1, source_target_pairs={{0,2},{1,3},{2,0},{3,1},{4,6},{5,7},{6,4},{7,5},{8,10},{9,11},{10,... | collective-permute-start | bytes 786440 | tf_op jit(solution)/shard_map/ppermute | solution.py:216

commit v11 on v10

--- a/solution.py
+++ b/solution.py
@@ -112,8 +112,24 @@
     )(pick, blocks)
 
 
-def project_kernel(x_ref, w_ref, out_ref, *, hd):
-    kv = jnp.dot(x_ref[...], w_ref[...], preferred_element_type=jnp.float32)
+def project_kernel(slot_ref, recv_ref, w_ref, out_ref, rows_scr, sems, *, hd):
+    y = pl.program_id(0)
+    pairs = sems.shape[0]
+    quarter = recv_ref.shape[1]
+
+    def piece_copy(p):
+        return pltpu.make_async_copy(
+            recv_ref.at[slot_ref[p]], rows_scr.at[pl.ds(p * quarter, quarter)], sems.at[p]
+        )
+
+    @pl.when(y == 0)
+    def _():
+        for p in range(pairs):
+            piece_copy(p).start()
+        for p in range(pairs):
+            piece_copy(p).wait()
+
+    kv = jnp.dot(rows_scr[...], w_ref[...], preferred_element_type=jnp.float32)
     feat = kv.shape[1] // 2
     keys = kv[:, :feat]
     lane = lax.broadcasted_iota(jnp.int32, (1, feat), 1)
@@ -127,19 +143,29 @@
     out_ref[0, :, feat:] = kv[:, feat:].astype(out_ref.dtype)
 
 
-def project_all(rows, w_kv, heads, hd):
-    n, model = rows.shape
+def project_all(recv, slot_of, w_kv, heads, hd):
+    tiles, quarter, model = recv.shape
+    pairs = slot_of.shape[0]
+    n = pairs * quarter
     cols = w_kv.shape[1] // heads
+    grid_spec = pltpu.PrefetchScalarGridSpec(
+        num_scalar_prefetch=1,
+        grid=(heads,),
+        in_specs=[
+            pl.BlockSpec(memory_space=pl.ANY),
+            pl.BlockSpec((model, cols), lambda y, slot_of: (0, y)),
+        ],
+        out_specs=pl.BlockSpec((1, n, cols), lambda y, slot_of: (y, 0, 0)),
+        scratch_shapes=[
+            pltpu.VMEM((n, model), recv.dtype),
+            pltpu.SemaphoreType.DMA((pairs,)),
+        ],
+    )
     return pl.pallas_call(
         functools.partial(project_kernel, hd=hd),
-        grid=(heads,),
-        in_specs=[
-            pl.BlockSpec((n, model), lambda y: (0, 0)),
-            pl.BlockSpec((model, cols), lambda y: (0, y)),
-        ],
-        out_specs=pl.BlockSpec((1, n, cols), lambda y: (y, 0, 0)),
+        grid_spec=grid_spec,
         out_shape=jax.ShapeDtypeStruct((heads, n, cols), jnp.bfloat16),
-    )(rows, w_kv)
+    )(slot_of, recv, w_kv)
 
 
 def body(feats, w_query, w_key, w_value, w_out, head_scale, nbr_owner, nbr_local, slot_valid):
@@ -192,9 +218,8 @@
     ).reshape(tile_count, quarter, model)
     recv, w_out_t, w_kv_all = lax.optimization_barrier((recv, w_out_t, w_kv_all))
     slot_of = jnp.clip(target, 0, tile_count - 1).astype(jnp.int32)
-    piece = gather_blocks(recv, slot_of)
-    pairs = piece.shape[0]
-    send = project_all(piece.reshape(pairs * quarter, model), w_kv_all, heads, feat // count).reshape(
+    pairs = slot_of.shape[0]
+    send = project_all(recv, slot_of, w_kv_all, heads, feat // count).reshape(
         heads, pairs, quarter, 2 * feat
     )
     got = lax.all_to_all(send, "heads", 0, 0, tiled=True)

time: 202 us -> 200 us (0.990)
  Pallas kernels: 21.3 us -> 19.1 us
    pallas_call x2 -> x1, Pallas kernels: 8.26 us -> 4.36 us  [gather_blocks(): pl.pallas_call(gather_kernel, grid_spec=grid_spec, out_shape=jax.ShapeDty...]
where the time goes in v11:
time: 200 us; the launch traced here: 199 us
  waiting for transfers between devices  84 us (42%)
  blocking collectives  42 us (21%)
  starting transfers between devices  26 us (13%)
  Pallas kernels  19.1 us (10%)
  local copies, waits for them, and re-layouts  14.3 us (7%)
  matrix products  7.48 us (4%)
  other arithmetic  5.98 us (3%)
    all_to_all x1, waiting for transfers between devices, body(): lax.all_to_all(payload.reshape(devices, capacity * quarter, model), 'node...  39.7 us
    all_to_all x1, waiting for transfers between devices, body(): got = lax.all_to_all(send, 'heads', 0, 0, tiled=True)  24.5 us
    all_gather x1, blocking collectives, body(): lax.all_gather(w_key_b, 'heads', axis=1, tiled=True)  14.5 us
    all_gather x1, blocking collectives, body(): lax.all_gather(w_value_b, 'heads', axis=1, tiled=True)  14 us
    all_gather x1, blocking collectives, body(): w_out_t = lax.all_gather(w_out.T, 'heads', axis=1, tiled=True)  13.5 us
    all_to_all x1, starting transfers between devices, body(): lax.all_to_all(request.reshape(devices, capacity), 'nodes', split_axis=0,...  12 us
    ppermute x3, waiting for transfers between devices, body(): lax.ppermute(attn, 'heads', [(j, (j + k) % heads) for j in range(heads)])  11.3 us
    all_to_all x1, waiting for transfers between devices, body(): lax.all_to_all(request.reshape(devices, capacity), 'nodes', split_axis=0,...  8.51 us
  transfers between devices with their start and end apart: 6, of which 5 were waited for; matrix products, arithmetic and copies ran while one was open for 10% of the time, Pallas kernels for 0%

profile of v11, /device:TPU:2, one launch (start us, length us, event | category | flops | bytes accessed | tf_op | source)
XLA Modules:
  0.0 199.2 jit_solution(5614397330963196245)
XLA Ops:
  0.0 0.0 copy-start
  0.0 0.7 compare_convert_fusion
  0.7 0.1 copy.37
  0.8 0.1 reshape.135.live_ref
  0.9 0.8 copy.42
  1.6 0.1 reshape.126
  1.7 0.1 fusion.8
  1.8 0.1 reduce_window_sum.11
  1.9 0.2 select_reduce_fusion.1
  2.0 0.8 copy.43
  2.8 0.1 reshape.127
  2.9 0.5 broadcast_clamp_fusion
  3.4 0.1 select_reduce_fusion
  3.5 0.8 sub.30
  4.2 12.0 %all-to-all-start = ((s32[64,1,2]{2,1,0:T(1,128)}), s32[64,1,2]{2,1,0:T(1,128)S(1)}, u32[]{:S(2)}, u32[]{:S(2)}) async-start(s32[64,1,2]{2,1,0:T(1,128)} %bitcast.6), calls=%async_computation | async-start | bytes 65536 | tf_op jit(solution)/shard_map/all_to_all | solution.py:197
  16.3 8.5 %all-to-all-done = s32[64,1,2]{2,1,0:T(1,128)S(1)} async-done(((s32[64,1,2]{2,1,0:T(1,128)}), s32[64,1,2]{2,1,0:T(1,128)S(1)}, u32[]{:S(2)}, u32[]{:S(2)}) %all-to-all-start) | async-done | bytes 544 | tf_op jit(solution)/shard_map/all_to_all | solution.py:197
  24.8 0.1 add_reduce_fusion
  24.9 0.7 add.110.pick_ref
  25.6 4.4 %shard_map.91 = bf16[128,32,512]{2,1,0:T(8,128)(2,1)} custom-call(s32[128]{0:T(128)} %add.110.pick_ref, bf16[32,32,512]{2,1,0:T(8,128)(2,1)} %bitcast.38), custom_call_target="tpu_custom_call" | custom-call | tf_op jit(solution)/shard_map/pallas_call | solution.py:108
  29.9 6.6 %all-to-all-start.1 = ((bf16[64,64,512]{2,1,0:T(8,128)(2,1)}), bf16[64,64,512]{2,1,0:T(8,128)(2,1)}, u32[]{:S(2)}, u32[]{:S(2)}) async-start(bf16[64,64,512]{2,1,0:T(8,128)(2,1)} %bitcast.37), calls=%async_computation.1 | async-start | bytes 8388608 | tf_op jit(solution)/shard_map/all_to_all | solution.py:212
  36.6 0.0 copy-done
  36.6 0.0 copy-done.2
  36.6 0.0 copy-start.5
  36.6 1.2 fusion.10
  37.8 0.2 copy.38
  38.0 0.0 copy-done.5
  38.0 0.0 copy-start.6
  38.1 1.2 fusion.11
  39.3 0.2 copy.40
  39.6 0.6 add_rsqrt_fusion.1
  40.2 14.0 %all_gather.11 = bf16[512,512]{1,0:T(8,128)(2,1)S(1)} all-gather(bf16[512,128]{1,0:T(8,128)(2,1)S(1)} %copy-done.6), channel_id=1, replica_groups=mesh['nodes'=64,'heads'=4] {'heads'}, dimensions={1}, use_global_device_ids=true | all-gather | bytes 655360 | tf_op jit(solution)/shard_map/all_gather | solution.py:210
  54.2 0.3 stack_reshape.9
  54.5 14.5 %all_gather.10 = bf16[512,512]{1,0:T(8,128)(2,1)} all-gather(bf16[512,128]{1,0:T(8,128)(2,1)S(1)} %copy-done.5), channel_id=1, replica_groups=mesh['nodes'=64,'heads'=4] {'heads'}, dimensions={1}, use_global_device_ids=true | all-gather | bytes 655360 | tf_op jit(solution)/shard_map/all_gather | solution.py:209
  69.0 3.4 %stack_reshape.8 = bf16[512,4,1,128]{3,2,1,0:T(2,128)(2,1)S(1)} reshape(bf16[512,512]{1,0:T(8,128)(2,1)} %all_gather.10) | data formatting | bytes 1048576 | tf_op jit(solution)/shard_map/stack;reshape | solution.py:211
  72.4 0.0 copy-start.7
  72.4 3.2 %pad_maximum_fusion = bf16[512,4,2,128]{3,2,1,0:T(2,128)(2,1)} fusion(bf16[512,4,1,128]{3,2,1,0:T(2,128)(2,1)S(1)} %stack_reshape.9, bf16[512,4,1,128]{3,2,1,0:T(2,128)(2,1)S(1)} %stack_reshape.8), kind=kLoop, calls=%fused_computation.5 | loop fusion | flops 2097152 | bytes 2097152 | tf_op jit(solution)/shard_map/stack | solution.py:211
  75.6 2.6 %reshape.131.w_ref = bf16[512,1024]{1,0:T(8,128)(2,1)} reshape(bf16[512,4,2,128]{3,2,1,0:T(2,128)(2,1)} %pad_maximum_fusion) | data formatting | bytes 2097152 | tf_op jit(solution)/shard_map/reshape | solution.py:211
  78.2 13.5 %all_gather.9 = bf16[512,512]{0,1:T(8,128)(2,1)} all-gather(bf16[512,128]{0,1:T(8,128)(2,1)S(1)} %bitcast.46), channel_id=1, replica_groups=mesh['nodes'=64,'heads'=4] {'heads'}, dimensions={1}, use_global_device_ids=true | all-gather | bytes 655360 | tf_op jit(solution)/shard_map/all_gather | solution.py:208
  91.7 39.7 %all-to-all-done.1 = bf16[64,64,512]{2,1,0:T(8,128)(2,1)} async-done(((bf16[64,64,512]{2,1,0:T(8,128)(2,1)}), bf16[64,64,512]{2,1,0:T(8,128)(2,1)}, u32[]{:S(2)}, u32[]{:S(2)}) %all-to-all-start.1) | async-done | bytes 4194336 | tf_op jit(solution)/shard_map/all_to_all | solution.py:212
  131.4 6.7 %shard_map.92 = bf16[4,1024,256]{2,1,0:T(8,128)(2,1)} custom-call(s32[32]{0:T(128)} %get-tuple-element.19.slot_ref, bf16[128,32,512]{2,1,0:T(8,128)(2,1)} %bitcast.9.recv_ref, bf16[512,1024]{1,0:T(8,128)(2,1)} %reshape.131.w_ref), custom_call_target="tpu_custom_call" | custom-call | tf_op jit(solution)/shard_map/pallas_call | solution.py:164
  138.1 0.0 copy-start.8
  138.1 4.5 %all-to-all-start.2 = ((bf16[4,32,32,256]{3,2,1,0:T(8,128)(2,1)}), bf16[4,32,32,256]{3,2,1,0:T(8,128)(2,1)}, u32[]{:S(2)}, u32[]{:S(2)}) async-start(bf16[4,32,32,256]{3,2,1,0:T(8,128)(2,1)} %bitcast.39), calls=%async_computation.2 | async-start | bytes 4194304 | tf_op jit(solution)/shard_map/all_to_all | solution.py:225
  142.7 0.1 copy.48
  142.8 0.2 copy.39
  143.0 0.8 mul.85
  143.9 1.3 copy.41
  145.2 0.0 copy-done.4
  145.2 0.1 broadcast_select_fusion.1
  145.4 0.1 multiply_convert_fusion
  145.5 0.4 convolution_convert_fusion
  145.9 0.1 pad_maximum_fusion.2.own_ref
  146.0 24.5 %all-to-all-done.2 = bf16[4,32,32,256]{3,2,1,0:T(8,128)(2,1)} async-done(((bf16[4,32,32,256]{3,2,1,0:T(8,128)(2,1)}), bf16[4,32,32,256]{3,2,1,0:T(8,128)(2,1)}, u32[]{:S(2)}, u32[]{:S(2)}) %all-to-all-start.2) | async-done | bytes 2097184 | tf_op jit(solution)/shard_map/all_to_all | solution.py:225
  170.4 1.8 copy.47
  172.3 8.1 %shard_map.93 = bf16[8,128,128]{2,1,0:T(8,128)(2,1)S(1)} custom-call(s32[32]{0:T(128)S(1)} %iota.20.slot_ref, s32[32]{0:T(128)S(1)} %reshape.135.live_ref, f32[2]{0:T(128)S(1)} %copy-done.1, bf16[8,256,128]{2,1,0:T(8,128)(2,1)S(1)} %pad_maximum_fusion.1.q_ref, bf16[8,128,256]{2,1,0:T(8,128)(2,1)S(1)} %pad_maximum_fusion.2.own_ref, ...), custom_call_target="tpu_custom_call" | custom-call | tf_op jit(solution)/shard_map/pallas_call | solution.py:83
  180.4 1.2 collective-permute-start.2
  181.7 0.9 collective-permute-start
  182.5 0.8 collective-permute-start.1
  183.3 1.0 fusion.6
  184.3 5.4 %collective-permute-done.2 = bf16[1024,128]{1,0:T(8,128)(2,1)S(1)} collective-permute-done((bf16[1024,128]{1,0:T(8,128)(2,1)S(1)}, bf16[1024,128]{1,0:T(8,128)(2,1)S(1)}, u32[]{:S(2)}, u32[]{:S(2)}) %collective-permute-start.2) | collective-permute-done | bytes 262176 | tf_op jit(solution)/shard_map/ppermute | solution.py:241
  189.7 1.0 fusion.2
  190.6 5.9 %collective-permute-done = bf16[1024,128]{1,0:T(8,128)(2,1)S(1)} collective-permute-done((bf16[1024,128]{1,0:T(8,128)(2,1)S(1)}, bf16[1024,128]{1,0:T(8,128)(2,1)S(1)}, u32[]{:S(2)}, u32[]{:S(2)}) %collective-permute-start) | collective-permute-done | bytes 262176 | tf_op jit(solution)/shard_map/ppermute | solution.py:241
  196.5 1.0 convolution_add_fusion.1
  197.5 0.0 collective-permute-done.1
  197.5 1.7 fusion.1
  (19 shorter events, 0.3 us)
Async XLA Ops:
  0.0 36.6 %copy-start = (bf16[512,128]{1,0:T(8,128)(2,1)S(1)}, bf16[512,128]{1,0:T(8,128)(2,1)}, u32[]{:S(2)}) copy-start(bf16[512,128]{1,0:T(8,128)(2,1)} %param.10) | copy-start | bytes 393220
  4.2 20.5 %all-to-all-start = ((s32[64,1,2]{2,1,0:T(1,128)}), s32[64,1,2]{2,1,0:T(1,128)S(1)}, u32[]{:S(2)}, u32[]{:S(2)}) async-start(s32[64,1,2]{2,1,0:T(1,128)} %bitcast.6), calls=%async_computation | async-start | bytes 65536 | tf_op jit(solution)/shard_map/all_to_all | solution.py:197
  29.9 6.6 %copy-start.2 = (bf16[1024,512]{1,0:T(8,128)(2,1)S(1)}, bf16[1024,512]{1,0:T(8,128)(2,1)}, u32[]{:S(2)}) copy-start(bf16[1024,512]{1,0:T(8,128)(2,1)} %param.9) | copy-start | bytes 3145732
  29.9 101.5 %all-to-all-start.1 = ((bf16[64,64,512]{2,1,0:T(8,128)(2,1)}), bf16[64,64,512]{2,1,0:T(8,128)(2,1)}, u32[]{:S(2)}, u32[]{:S(2)}) async-start(bf16[64,64,512]{2,1,0:T(8,128)(2,1)} %bitcast.37), calls=%async_computation.1 | async-start | bytes 8388608 | tf_op jit(solution)/shard_map/all_to_all | solution.py:212
  36.6 1.5 copy-start.5
  38.0 2.2 %copy-start.6 = (bf16[512,128]{1,0:T(8,128)(2,1)S(1)}, bf16[512,128]{1,0:T(8,128)(2,1)}, u32[]{:S(2)}) copy-start(bf16[512,128]{1,0:T(8,128)(2,1)} %param.12) | copy-start | bytes 393220
  72.4 5.8 %copy-start.7 = (bf16[128,512]{1,0:T(8,128)(2,1)S(1)}, bf16[128,512]{1,0:T(8,128)(2,1)}, u32[]{:S(2)}) copy-start(bf16[128,512]{1,0:T(8,128)(2,1)} %param.13) | copy-start | bytes 393220
  138.1 4.5 %copy-start.8 = (f32[1024,2]{0,1:T(2,128)S(1)}, f32[1024,2]{0,1:T(2,128)}, u32[]{:S(2)}) copy-start(f32[1024,2]{0,1:T(2,128)} %add_rsqrt_fusion.1) | copy-start | bytes 24580
  138.1 32.3 %all-to-all-start.2 = ((bf16[4,32,32,256]{3,2,1,0:T(8,128)(2,1)}), bf16[4,32,32,256]{3,2,1,0:T(8,128)(2,1)}, u32[]{:S(2)}, u32[]{:S(2)}) async-start(bf16[4,32,32,256]{3,2,1,0:T(8,128)(2,1)} %bitcast.39), calls=%async_computation.2 | async-start | bytes 4194304 | tf_op jit(solution)/shard_map/all_to_all | solution.py:225
  142.6 2.6 %copy-start.4 = (f32[1024,128]{1,0:T(8,128)S(1)}, f32[1024,128]{1,0:T(8,128)}, u32[]{:S(2)}) copy-start(f32[1024,128]{1,0:T(8,128)} %get-tuple-element.24) | copy-start | bytes 1572868
  143.9 1.5 copy-start.3
  170.4 1.9 copy-start.1
  180.4 9.2 %collective-permute-start.2 = (bf16[1024,128]{1,0:T(8,128)(2,1)S(1)}, bf16[1024,128]{1,0:T(8,128)(2,1)S(1)}, u32[]{:S(2)}, u32[]{:S(2)}) collective-permute-start(bf16[1024,128]{1,0:T(8,128)(2,1)S(1)} %bitcast.33), channel_id=1, source_target_pairs={{0,3},{1,0},{2,1},{3,2},{4,7},{5,4},{6,5},{7,6},{8,11},{9,8},{10,9... | collective-permute-start | bytes 786440 | tf_op jit(solution)/shard_map/ppermute | solution.py:241
  181.7 14.9 %collective-permute-start = (bf16[1024,128]{1,0:T(8,128)(2,1)S(1)}, bf16[1024,128]{1,0:T(8,128)(2,1)S(1)}, u32[]{:S(2)}, u32[]{:S(2)}) collective-permute-start(bf16[1024,128]{1,0:T(8,128)(2,1)S(1)} %bitcast.34), channel_id=1, source_target_pairs={{0,1},{1,2},{2,3},{3,0},{4,5},{5,6},{6,7},{7,4},{8,9},{9,10},{10,1... | collective-permute-start | bytes 786440 | tf_op jit(solution)/shard_map/ppermute | solution.py:241
  182.5 15.0 %collective-permute-start.1 = (bf16[1024,128]{1,0:T(8,128)(2,1)S(1)}, bf16[1024,128]{1,0:T(8,128)(2,1)S(1)}, u32[]{:S(2)}, u32[]{:S(2)}) collective-permute-start(bf16[1024,128]{1,0:T(8,128)(2,1)S(1)} %bitcast.35), channel_id=1, source_target_pairs={{0,2},{1,3},{2,0},{3,1},{4,6},{5,7},{6,4},{7,5},{8,10},{9,11},{10,... | collective-permute-start | bytes 786440 | tf_op jit(solution)/shard_map/ppermute | solution.py:241

commit v12 on v11

--- a/solution.py
+++ b/solution.py
@@ -225,22 +225,34 @@
     got = lax.all_to_all(send, "heads", 0, 0, tiled=True)
     pair_kv = jnp.transpose(got, (1, 0, 2, 3)).reshape(pairs, width, 2 * feat)
     pair_ids = jnp.arange(pairs, dtype=jnp.int32)
-    attn_t = attend(query_stack, own_kv, pair_kv, pair_ids, valid, head_scale)
-    attn = attn_t.reshape(rows, feat)
-    heads = lax.axis_size("heads")
-    me = lax.axis_index("heads")
+    heads_n = lax.axis_size("heads")
+    me_h = lax.axis_index("heads")
 
     def out_part(piece, source):
-        w_part = lax.dynamic_slice(w_out_t, (me * feat, source * feat), (feat, feat))
+        w_part = lax.dynamic_slice(w_out_t, (me_h * feat, source * feat), (feat, feat))
         return lax.dot_general(
             piece, w_part, (((1,), (1,)), ((), ())), preferred_element_type=jnp.float32
         )
 
-    mixed = out_part(attn, me)
-    for k in range(1, heads):
-        piece = lax.ppermute(attn, "heads", [(j, (j + k) % heads) for j in range(heads)])
-        mixed = mixed + out_part(piece, (me - k) % heads)
-    return mixed.astype(jnp.bfloat16)
+    halves = 2
+    per_half = nblocks // halves
+    outs = []
+    for part in range(halves):
+        lo, hi = part * per_half, (part + 1) * per_half
+        attn_half = attend(
+            query_stack[lo:hi],
+            own_kv[lo:hi],
+            pair_kv,
+            pair_ids[lo * slots:hi * slots],
+            valid[lo * slots:hi * slots],
+            head_scale,
+        ).reshape(per_half * width, feat)
+        mixed = out_part(attn_half, me_h)
+        for k in range(1, heads_n):
+            piece = lax.ppermute(attn_half, "heads", [(j, (j + k) % heads_n) for j in range(heads_n)])
+            mixed = mixed + out_part(piece, (me_h - k) % heads_n)
+        outs.append(mixed.astype(jnp.bfloat16))
+    return jnp.concatenate(outs, axis=0)
 
 
 def solution(mesh):

time: 200 us -> 195 us (0.975)
  waiting for transfers between devices: 84 us -> 73.6 us
  starting transfers between devices: 26 us -> 30.9 us
  matrix products: 7.48 us -> 4.41 us
  other arithmetic: 5.98 us -> 8.93 us
    ppermute x3 -> x6, waiting for transfers between devices: 11.3 us -> 4.78 us  [body(): lax.ppermute(attn_half, 'heads', [(j, (j + k) % heads_n) for j in range(h...]
    ppermute x3 -> x6, starting transfers between devices: 2.87 us -> 7.82 us  [body(): lax.ppermute(attn_half, 'heads', [(j, (j + k) % heads_n) for j in range(h...]
    all_to_all x1, waiting for transfers between devices: 24.5 us -> 20.5 us  [body(): got = lax.all_to_all(send, 'heads', 0, 0, tiled=True)]
    dot_general x4 -> x8, matrix products: 4.57 us -> 1.4 us  [out_part(): lax.dot_general(piece, w_part, (((1,), (1,)), ((), ())), preferred_elemen...]
    pallas_call x1 -> x2, Pallas kernels: 8.1 us -> 9.21 us  [attend(): pl.pallas_call(functools.partial(attend_kernel, count=count, slots=slots)...]
  transfers between devices with their start and end apart: 6 -> 9, of which waited for: 5 -> 4; matrix products, arithmetic and copies ran while one was open for 10% -> 11% of each run, Pallas kernels for 0% -> 2%
where the time goes in v12:
time: 195 us; the launch traced here: 194 us
  waiting for transfers between devices  73.6 us (38%)
  blocking collectives  42 us (22%)
  starting transfers between devices  30.9 us (16%)
  Pallas kernels  20.4 us (10%)
  local copies, waits for them, and re-layouts  13.4 us (7%)
  other arithmetic  8.93 us (5%)
  matrix products  4.41 us (2%)
    all_to_all x1, waiting for transfers between devices, body(): lax.all_to_all(payload.reshape(devices, capacity * quarter, model), 'node...  39.8 us
    all_to_all x1, waiting for transfers between devices, body(): got = lax.all_to_all(send, 'heads', 0, 0, tiled=True)  20.5 us
    all_gather x1, blocking collectives, body(): lax.all_gather(w_key_b, 'heads', axis=1, tiled=True)  14.5 us
    all_gather x1, blocking collectives, body(): lax.all_gather(w_value_b, 'heads', axis=1, tiled=True)  14 us
    all_gather x1, blocking collectives, body(): w_out_t = lax.all_gather(w_out.T, 'heads', axis=1, tiled=True)  13.5 us
    all_to_all x1, starting transfers between devices, body(): lax.all_to_all(request.reshape(devices, capacity), 'nodes', split_axis=0,...  12 us
    pallas_call x2, Pallas kernels, attend(): pl.pallas_call(functools.partial(attend_kernel, count=count, slots=slots)...  9.21 us
    all_to_all x1, waiting for transfers between devices, body(): lax.all_to_all(request.reshape(devices, capacity), 'nodes', split_axis=0,...  8.51 us
  transfers between devices with their start and end apart: 9, of which 4 were waited for; matrix products, arithmetic and copies ran while one was open for 11% of the time, Pallas kernels for 2%

profile of v12, /device:TPU:2, one launch (start us, length us, event | category | flops | bytes accessed | tf_op | source)
XLA Modules:
  0.0 194.1 jit_solution(2587158691266966347)
XLA Ops:
  0.0 0.8 copy.47
  0.8 0.1 reshape.132
  0.9 0.1 fusion.19
  1.0 0.2 select_reduce_fusion.1
  1.2 0.6 broadcast_clamp_fusion
  1.8 0.7 select_add_fusion
  2.5 0.1 copy.48
  2.6 0.1 reshape.142
  2.6 0.1 select_reduce_fusion
  2.7 0.8 sub.33
  3.5 12.0 %all-to-all-start = ((s32[64,1,2]{2,1,0:T(1,128)}), s32[64,1,2]{2,1,0:T(1,128)S(1)}, u32[]{:S(2)}, u32[]{:S(2)}) async-start(s32[64,1,2]{2,1,0:T(1,128)} %bitcast.5), calls=%async_computation | async-start | bytes 65536 | tf_op jit(solution)/shard_map/all_to_all | solution.py:197
  15.5 8.5 %all-to-all-done = s32[64,1,2]{2,1,0:T(1,128)S(1)} async-done(((s32[64,1,2]{2,1,0:T(1,128)}), s32[64,1,2]{2,1,0:T(1,128)S(1)}, u32[]{:S(2)}, u32[]{:S(2)}) %all-to-all-start) | async-done | bytes 544 | tf_op jit(solution)/shard_map/all_to_all | solution.py:197
  24.1 0.1 add_reduce_fusion
  24.2 0.7 add.130.pick_ref
  24.8 4.4 %shard_map.91 = bf16[128,32,512]{2,1,0:T(8,128)(2,1)} custom-call(s32[128]{0:T(128)} %add.130.pick_ref, bf16[32,32,512]{2,1,0:T(8,128)(2,1)} %bitcast.55), custom_call_target="tpu_custom_call" | custom-call | tf_op jit(solution)/shard_map/pallas_call | solution.py:108
  29.2 6.6 %all-to-all-start.1 = ((bf16[64,64,512]{2,1,0:T(8,128)(2,1)}), bf16[64,64,512]{2,1,0:T(8,128)(2,1)}, u32[]{:S(2)}, u32[]{:S(2)}) async-start(bf16[64,64,512]{2,1,0:T(8,128)(2,1)} %bitcast.54), calls=%async_computation.1 | async-start | bytes 8388608 | tf_op jit(solution)/shard_map/all_to_all | solution.py:212
  35.9 1.3 fusion.21
  37.2 0.2 copy.44
  37.4 0.6 add_rsqrt_fusion.1
  38.0 1.3 bitcast_reduce_fusion
  39.3 14.0 %all_gather.11 = bf16[512,512]{1,0:T(8,128)(2,1)S(1)} all-gather(bf16[512,128]{1,0:T(8,128)(2,1)S(1)} %copy-done.5), channel_id=1, replica_groups=mesh['nodes'=64,'heads'=4] {'heads'}, dimensions={1}, use_global_device_ids=true | all-gather | bytes 655360 | tf_op jit(solution)/shard_map/all_gather | solution.py:210
  53.3 0.3 stack_reshape.9
  53.6 14.5 %all_gather.10 = bf16[512,512]{1,0:T(8,128)(2,1)} all-gather(bf16[512,128]{1,0:T(8,128)(2,1)S(1)} %copy-done.4), channel_id=1, replica_groups=mesh['nodes'=64,'heads'=4] {'heads'}, dimensions={1}, use_global_device_ids=true | all-gather | bytes 655360 | tf_op jit(solution)/shard_map/all_gather | solution.py:209
  68.1 3.4 %stack_reshape.8 = bf16[512,4,1,128]{3,2,1,0:T(2,128)(2,1)S(1)} reshape(bf16[512,512]{1,0:T(8,128)(2,1)} %all_gather.10) | data formatting | bytes 1048576 | tf_op jit(solution)/shard_map/stack;reshape | solution.py:211
  71.5 3.2 %pad_maximum_fusion = bf16[512,4,2,128]{3,2,1,0:T(2,128)(2,1)} fusion(bf16[512,4,1,128]{3,2,1,0:T(2,128)(2,1)S(1)} %stack_reshape.9, bf16[512,4,1,128]{3,2,1,0:T(2,128)(2,1)S(1)} %stack_reshape.8), kind=kLoop, calls=%fused_computation.9 | loop fusion | flops 2097152 | bytes 2097152 | tf_op jit(solution)/shard_map/stack | solution.py:211
  74.8 2.6 %reshape.136.w_ref = bf16[512,1024]{1,0:T(8,128)(2,1)} reshape(bf16[512,4,2,128]{3,2,1,0:T(2,128)(2,1)} %pad_maximum_fusion) | data formatting | bytes 2097152 | tf_op jit(solution)/shard_map/reshape | solution.py:211
  77.4 13.5 %all_gather.9 = bf16[512,512]{0,1:T(8,128)(2,1)} all-gather(bf16[512,128]{0,1:T(8,128)(2,1)S(1)} %bitcast.61), channel_id=1, replica_groups=mesh['nodes'=64,'heads'=4] {'heads'}, dimensions={1}, use_global_device_ids=true | all-gather | bytes 655360 | tf_op jit(solution)/shard_map/all_gather | solution.py:208
  90.9 39.8 %all-to-all-done.1 = bf16[64,64,512]{2,1,0:T(8,128)(2,1)} async-done(((bf16[64,64,512]{2,1,0:T(8,128)(2,1)}), bf16[64,64,512]{2,1,0:T(8,128)(2,1)}, u32[]{:S(2)}, u32[]{:S(2)}) %all-to-all-start.1) | async-done | bytes 4194336 | tf_op jit(solution)/shard_map/all_to_all | solution.py:212
  130.7 6.8 %shard_map.92 = bf16[4,1024,256]{2,1,0:T(8,128)(2,1)} custom-call(s32[32]{0:T(128)} %get-tuple-element.19.slot_ref, bf16[128,32,512]{2,1,0:T(8,128)(2,1)} %bitcast.8.recv_ref, bf16[512,1024]{1,0:T(8,128)(2,1)} %reshape.136.w_ref), custom_call_target="tpu_custom_call" | custom-call | tf_op jit(solution)/shard_map/pallas_call | solution.py:164
  137.5 4.5 %all-to-all-start.2 = ((bf16[4,32,32,256]{3,2,1,0:T(8,128)(2,1)}), bf16[4,32,32,256]{3,2,1,0:T(8,128)(2,1)S(1)}, u32[]{:S(2)}, u32[]{:S(2)}) async-start(bf16[4,32,32,256]{3,2,1,0:T(8,128)(2,1)} %bitcast.57), calls=%async_computation.2 | async-start | bytes 4194304 | tf_op jit(solution)/shard_map/all_to_all | solution.py:225
  142.0 0.1 fusion.20
  142.1 0.1 slice.42.slot_ref
  142.2 0.1 copy.53
  142.3 0.1 slice.44.live_ref
  142.4 0.9 copy.55
  143.3 2.0 %copy.45 = f32[8,128,128]{2,1,0:T(8,128)} copy(f32[8,128,128]{1,0,2:T(8,128)} %bitcast.60) | data formatting | bytes 1048576 | tf_op jit(solution)/shard_map/mul | solution.py:14
  145.4 1.1 fusion.4
  146.5 0.5 convolution_convert_fusion
  147.0 0.1 copy.54
  147.1 0.1 copy.43
  147.2 0.1 slice.38.live_ref
  147.3 0.1 copy.46
  147.5 1.3 broadcast_select_fusion.1
  148.9 20.5 %all-to-all-done.2 = bf16[4,32,32,256]{3,2,1,0:T(8,128)(2,1)S(1)} async-done(((bf16[4,32,32,256]{3,2,1,0:T(8,128)(2,1)}), bf16[4,32,32,256]{3,2,1,0:T(8,128)(2,1)S(1)}, u32[]{:S(2)}, u32[]{:S(2)}) %all-to-all-start.2) | async-done | bytes 2097184 | tf_op jit(solution)/shard_map/all_to_all | solution.py:225
  169.4 0.2 copy.52
  169.6 0.4 copy-done.1
  170.0 4.6 %shard_map.94 = bf16[4,128,128]{2,1,0:T(8,128)(2,1)S(1)} custom-call(s32[16]{0:T(128)S(1)} %slice.42.slot_ref, s32[16]{0:T(128)S(1)} %slice.44.live_ref, f32[2]{0:T(128)S(1)} %copy-done.1, bf16[4,256,128]{2,1,0:T(8,128)(2,1)S(1)} %get-tuple-element.26.q_ref, bf16[4,128,256]{2,1,0:T(8,128)(2,1)S(1)} %bitcast.44, bf16[32,128,256]{2,1,0:T(8,128)(2,1)S(1)} %bitcast.41), custom_call_target="tpu_custom_call" | custom-call | tf_op jit(solution)/shard_map/pallas_call | solution.py:83
  174.6 1.2 collective-permute-start.5
  175.9 0.9 collective-permute-start.3
  176.7 0.7 collective-permute-start.4
  177.4 4.6 %shard_map.93 = bf16[4,128,128]{2,1,0:T(8,128)(2,1)S(1)} custom-call(s32[16]{0:T(128)S(1)} %bitcast.53, s32[16]{0:T(128)S(1)} %slice.38.live_ref, f32[2]{0:T(128)S(1)} %copy-done.1, bf16[4,256,128]{2,1,0:T(8,128)(2,1)S(1)} %get-tuple-element.25.q_ref, bf16[4,128,256]{2,1,0:T(8,128)(2,1)S(1)} %bitcast.43, bf16[32,128,256]{2,1,0:T(8,128)(2,1)S(1)} %bitcast.42), custom_call_target="tpu_custom_call" | custom-call | tf_op jit(solution)/shard_map/pallas_call | solution.py:83
  182.1 2.6 %collective-permute-start.2 = (bf16[512,128]{1,0:T(8,128)(2,1)S(1)}, bf16[512,128]{1,0:T(8,128)(2,1)S(1)}, u32[]{:S(2)}, u32[]{:S(2)}) collective-permute-start(bf16[512,128]{1,0:T(8,128)(2,1)S(1)} %bitcast.45), channel_id=1, source_target_pairs={{0,3},{1,0},{2,1},{3,2},{4,7},{5,4},{6,5},{7,6},{8,11},{9,8},{10,9... | collective-permute-start | bytes 393224 | tf_op jit(solution)/shard_map/ppermute | solution.py:252
  184.7 0.1 collective-permute-start
  184.8 0.2 fusion.7
  184.9 0.2 fusion.9
  185.1 2.3 %collective-permute-start.1 = (bf16[512,128]{1,0:T(8,128)(2,1)S(1)}, bf16[512,128]{1,0:T(8,128)(2,1)S(1)}, u32[]{:S(2)}, u32[]{:S(2)}) collective-permute-start(bf16[512,128]{1,0:T(8,128)(2,1)S(1)} %bitcast.48), channel_id=1, source_target_pairs={{0,2},{1,3},{2,0},{3,1},{4,6},{5,7},{6,4},{7,5},{8,10},{9,11},{10,... | collective-permute-start | bytes 393224 | tf_op jit(solution)/shard_map/ppermute | solution.py:252
  187.4 0.2 convolution_add_fusion.1
  187.6 0.2 fusion.11
  187.8 0.2 fusion.3
  188.0 4.8 %collective-permute-done = bf16[512,128]{1,0:T(8,128)(2,1)S(1)} collective-permute-done((bf16[512,128]{1,0:T(8,128)(2,1)S(1)}, bf16[512,128]{1,0:T(8,128)(2,1)S(1)}, u32[]{:S(2)}, u32[]{:S(2)}) %collective-permute-start) | collective-permute-done | bytes 131104 | tf_op jit(solution)/shard_map/ppermute | solution.py:252
  192.8 0.2 convolution_add_fusion.3
  193.0 0.2 fusion.13
  193.2 0.2 fusion.2
  193.4 0.7 pad_maximum_fusion.3
  (35 shorter events, 0.3 us)
Async XLA Ops:
  0.0 35.9 %copy-start = (bf16[512,128]{1,0:T(8,128)(2,1)S(1)}, bf16[512,128]{1,0:T(8,128)(2,1)}, u32[]{:S(2)}) copy-start(bf16[512,128]{1,0:T(8,128)(2,1)} %param.10) | copy-start | bytes 393220
  3.5 20.5 %all-to-all-start = ((s32[64,1,2]{2,1,0:T(1,128)}), s32[64,1,2]{2,1,0:T(1,128)S(1)}, u32[]{:S(2)}, u32[]{:S(2)}) async-start(s32[64,1,2]{2,1,0:T(1,128)} %bitcast.5), calls=%async_computation | async-start | bytes 65536 | tf_op jit(solution)/shard_map/all_to_all | solution.py:197
  29.2 6.6 %copy-start.2 = (bf16[1024,512]{1,0:T(8,128)(2,1)S(1)}, bf16[1024,512]{1,0:T(8,128)(2,1)}, u32[]{:S(2)}) copy-start(bf16[1024,512]{1,0:T(8,128)(2,1)} %param.9) | copy-start | bytes 3145732
  29.2 101.5 %all-to-all-start.1 = ((bf16[64,64,512]{2,1,0:T(8,128)(2,1)}), bf16[64,64,512]{2,1,0:T(8,128)(2,1)}, u32[]{:S(2)}, u32[]{:S(2)}) async-start(bf16[64,64,512]{2,1,0:T(8,128)(2,1)} %bitcast.54), calls=%async_computation.1 | async-start | bytes 8388608 | tf_op jit(solution)/shard_map/all_to_all | solution.py:212
  35.9 1.5 copy-start.8
  35.9 2.2 %copy-start.4 = (bf16[512,128]{1,0:T(8,128)(2,1)S(1)}, bf16[512,128]{1,0:T(8,128)(2,1)}, u32[]{:S(2)}) copy-start(bf16[512,128]{1,0:T(8,128)(2,1)} %param.11) | copy-start | bytes 393220
  37.2 2.2 %copy-start.5 = (bf16[512,128]{1,0:T(8,128)(2,1)S(1)}, bf16[512,128]{1,0:T(8,128)(2,1)}, u32[]{:S(2)}) copy-start(bf16[512,128]{1,0:T(8,128)(2,1)} %param.12) | copy-start | bytes 393220
  71.5 5.9 %copy-start.6 = (bf16[128,512]{1,0:T(8,128)(2,1)S(1)}, bf16[128,512]{1,0:T(8,128)(2,1)}, u32[]{:S(2)}) copy-start(bf16[128,512]{1,0:T(8,128)(2,1)} %param.13) | copy-start | bytes 393220
  137.5 4.8 %copy-start.7 = (f32[1024,2]{0,1:T(2,128)S(1)}, f32[1024,2]{0,1:T(2,128)}, u32[]{:S(2)}) copy-start(f32[1024,2]{0,1:T(2,128)} %add_rsqrt_fusion.1) | copy-start | bytes 24580
  137.5 31.8 %all-to-all-start.2 = ((bf16[4,32,32,256]{3,2,1,0:T(8,128)(2,1)}), bf16[4,32,32,256]{3,2,1,0:T(8,128)(2,1)S(1)}, u32[]{:S(2)}, u32[]{:S(2)}) async-start(bf16[4,32,32,256]{3,2,1,0:T(8,128)(2,1)} %bitcast.57), calls=%async_computation.2 | async-start | bytes 4194304 | tf_op jit(solution)/shard_map/all_to_all | solution.py:225
  169.4 0.7 copy-start.1
  170.0 14.7 %copy-start.3 = (bf16[512,512]{0,1:T(8,128)(2,1)S(1)}, bf16[512,512]{0,1:T(8,128)(2,1)}, u32[]{:S(2)}) copy-start(bf16[512,512]{0,1:T(8,128)(2,1)} %all_gather.9) | copy-start | bytes 1572868
  174.6 13.0 %collective-permute-start.5 = (bf16[512,128]{1,0:T(8,128)(2,1)S(1)}, bf16[512,128]{1,0:T(8,128)(2,1)S(1)}, u32[]{:S(2)}, u32[]{:S(2)}) collective-permute-start(bf16[512,128]{1,0:T(8,128)(2,1)S(1)} %bitcast.49), channel_id=1, source_target_pairs={{0,3},{1,0},{2,1},{3,2},{4,7},{5,4},{6,5},{7,6},{8,11},{9,8},{10,9... | collective-permute-start | bytes 393224 | tf_op jit(solution)/shard_map/ppermute | solution.py:252
  175.9 9.2 %collective-permute-start.3 = (bf16[512,128]{1,0:T(8,128)(2,1)S(1)}, bf16[512,128]{1,0:T(8,128)(2,1)S(1)}, u32[]{:S(2)}, u32[]{:S(2)}) collective-permute-start(bf16[512,128]{1,0:T(8,128)(2,1)S(1)} %bitcast.50), channel_id=1, source_target_pairs={{0,1},{1,2},{2,3},{3,0},{4,5},{5,6},{6,7},{7,4},{8,9},{9,10},{10,1... | collective-permute-start | bytes 393224 | tf_op jit(solution)/shard_map/ppermute | solution.py:252
  176.7 11.1 %collective-permute-start.4 = (bf16[512,128]{1,0:T(8,128)(2,1)S(1)}, bf16[512,128]{1,0:T(8,128)(2,1)S(1)}, u32[]{:S(2)}, u32[]{:S(2)}) collective-permute-start(bf16[512,128]{1,0:T(8,128)(2,1)S(1)} %bitcast.51), channel_id=1, source_target_pairs={{0,2},{1,3},{2,0},{3,1},{4,6},{5,7},{6,4},{7,5},{8,10},{9,11},{10,... | collective-permute-start | bytes 393224 | tf_op jit(solution)/shard_map/ppermute | solution.py:252
  182.1 10.9 %collective-permute-start.2 = (bf16[512,128]{1,0:T(8,128)(2,1)S(1)}, bf16[512,128]{1,0:T(8,128)(2,1)S(1)}, u32[]{:S(2)}, u32[]{:S(2)}) collective-permute-start(bf16[512,128]{1,0:T(8,128)(2,1)S(1)} %bitcast.45), channel_id=1, source_target_pairs={{0,3},{1,0},{2,1},{3,2},{4,7},{5,4},{6,5},{7,6},{8,11},{9,8},{10,9... | collective-permute-start | bytes 393224 | tf_op jit(solution)/shard_map/ppermute | solution.py:252
  184.7 8.1 %collective-permute-start = (bf16[512,128]{1,0:T(8,128)(2,1)S(1)}, bf16[512,128]{1,0:T(8,128)(2,1)S(1)}, u32[]{:S(2)}, u32[]{:S(2)}) collective-permute-start(bf16[512,128]{1,0:T(8,128)(2,1)S(1)} %bitcast.46), channel_id=1, source_target_pairs={{0,1},{1,2},{2,3},{3,0},{4,5},{5,6},{6,7},{7,4},{8,9},{9,10},{10,1... | collective-permute-start | bytes 393224 | tf_op jit(solution)/shard_map/ppermute | solution.py:252
  185.1 8.0 %collective-permute-start.1 = (bf16[512,128]{1,0:T(8,128)(2,1)S(1)}, bf16[512,128]{1,0:T(8,128)(2,1)S(1)}, u32[]{:S(2)}, u32[]{:S(2)}) collective-permute-start(bf16[512,128]{1,0:T(8,128)(2,1)S(1)} %bitcast.48), channel_id=1, source_target_pairs={{0,2},{1,3},{2,0},{3,1},{4,6},{5,7},{6,4},{7,5},{8,10},{9,11},{10,... | collective-permute-start | bytes 393224 | tf_op jit(solution)/shard_map/ppermute | solution.py:252

commit v13 on v12

--- a/solution.py
+++ b/solution.py
@@ -98,7 +98,7 @@
 def gather_blocks(blocks, pick):
     nblocks, r, l = blocks.shape
     tiles = pick.shape[0]
-    group = 32
+    group = 64
     grid_spec = pltpu.PrefetchScalarGridSpec(
         num_scalar_prefetch=1,
         grid=(tiles // group,),

time: 195 us -> 195 us (level)
  no operation moved by 1% of the time
where the time goes in v13:
time: 195 us; the launch traced here: 194 us
  waiting for transfers between devices  73.8 us (38%)
  blocking collectives  42 us (22%)
  starting transfers between devices  30.9 us (16%)
  Pallas kernels  19.9 us (10%)
  local copies, waits for them, and re-layouts  13.4 us (7%)
  other arithmetic  8.93 us (5%)
  matrix products  4.41 us (2%)
    all_to_all x1, waiting for transfers between devices, body(): lax.all_to_all(payload.reshape(devices, capacity * quarter, model), 'node...  39.8 us
    all_to_all x1, waiting for transfers between devices, body(): got = lax.all_to_all(send, 'heads', 0, 0, tiled=True)  20.6 us
    all_gather x1, blocking collectives, body(): lax.all_gather(w_key_b, 'heads', axis=1, tiled=True)  14.5 us
    all_gather x1, blocking collectives, body(): lax.all_gather(w_value_b, 'heads', axis=1, tiled=True)  14 us
    all_gather x1, blocking collectives, body(): w_out_t = lax.all_gather(w_out.T, 'heads', axis=1, tiled=True)  13.5 us
    all_to_all x1, starting transfers between devices, body(): lax.all_to_all(request.reshape(devices, capacity), 'nodes', split_axis=0,...  12 us
    pallas_call x2, Pallas kernels, attend(): pl.pallas_call(functools.partial(attend_kernel, count=count, slots=slots)...  9.21 us
    all_to_all x1, waiting for transfers between devices, body(): lax.all_to_all(request.reshape(devices, capacity), 'nodes', split_axis=0,...  8.51 us
  transfers between devices with their start and end apart: 9, of which 4 were waited for; matrix products, arithmetic and copies ran while one was open for 11% of the time, Pallas kernels for 2%

profile of v13, /device:TPU:2, one launch (start us, length us, event | category | flops | bytes accessed | tf_op | source)
XLA Modules:
  0.0 193.8 jit_solution(7421185433745797190)
XLA Ops:
  0.0 0.8 copy.47
  0.8 0.1 reshape.132
  0.9 0.1 fusion.19
  1.0 0.2 select_reduce_fusion.1
  1.2 0.6 broadcast_clamp_fusion
  1.8 0.7 select_add_fusion
  2.5 0.1 copy.48
  2.6 0.1 reshape.142
  2.6 0.1 select_reduce_fusion
  2.7 0.8 sub.33
  3.5 12.0 %all-to-all-start = ((s32[64,1,2]{2,1,0:T(1,128)}), s32[64,1,2]{2,1,0:T(1,128)S(1)}, u32[]{:S(2)}, u32[]{:S(2)}) async-start(s32[64,1,2]{2,1,0:T(1,128)} %bitcast.5), calls=%async_computation | async-start | bytes 65536 | tf_op jit(solution)/shard_map/all_to_all | solution.py:197
  15.5 8.5 %all-to-all-done = s32[64,1,2]{2,1,0:T(1,128)S(1)} async-done(((s32[64,1,2]{2,1,0:T(1,128)}), s32[64,1,2]{2,1,0:T(1,128)S(1)}, u32[]{:S(2)}, u32[]{:S(2)}) %all-to-all-start) | async-done | bytes 544 | tf_op jit(solution)/shard_map/all_to_all | solution.py:197
  24.1 0.1 add_reduce_fusion
  24.2 0.7 add.130.pick_ref
  24.8 4.0 %shard_map.91 = bf16[128,32,512]{2,1,0:T(8,128)(2,1)} custom-call(s32[128]{0:T(128)} %add.130.pick_ref, bf16[32,32,512]{2,1,0:T(8,128)(2,1)} %bitcast.55), custom_call_target="tpu_custom_call" | custom-call | tf_op jit(solution)/shard_map/pallas_call | solution.py:108
  28.9 6.6 %all-to-all-start.1 = ((bf16[64,64,512]{2,1,0:T(8,128)(2,1)}), bf16[64,64,512]{2,1,0:T(8,128)(2,1)}, u32[]{:S(2)}, u32[]{:S(2)}) async-start(bf16[64,64,512]{2,1,0:T(8,128)(2,1)} %bitcast.54), calls=%async_computation.1 | async-start | bytes 8388608 | tf_op jit(solution)/shard_map/all_to_all | solution.py:212
  35.5 1.2 fusion.21
  36.8 0.2 copy.44
  37.1 0.6 add_rsqrt_fusion.1
  37.7 1.3 bitcast_reduce_fusion
  39.0 14.0 %all_gather.11 = bf16[512,512]{1,0:T(8,128)(2,1)S(1)} all-gather(bf16[512,128]{1,0:T(8,128)(2,1)S(1)} %copy-done.5), channel_id=1, replica_groups=mesh['nodes'=64,'heads'=4] {'heads'}, dimensions={1}, use_global_device_ids=true | all-gather | bytes 655360 | tf_op jit(solution)/shard_map/all_gather | solution.py:210
  52.9 0.3 stack_reshape.9
  53.3 14.5 %all_gather.10 = bf16[512,512]{1,0:T(8,128)(2,1)} all-gather(bf16[512,128]{1,0:T(8,128)(2,1)S(1)} %copy-done.4), channel_id=1, replica_groups=mesh['nodes'=64,'heads'=4] {'heads'}, dimensions={1}, use_global_device_ids=true | all-gather | bytes 655360 | tf_op jit(solution)/shard_map/all_gather | solution.py:209
  67.7 3.4 %stack_reshape.8 = bf16[512,4,1,128]{3,2,1,0:T(2,128)(2,1)S(1)} reshape(bf16[512,512]{1,0:T(8,128)(2,1)} %all_gather.10) | data formatting | bytes 1048576 | tf_op jit(solution)/shard_map/stack;reshape | solution.py:211
  71.2 3.2 %pad_maximum_fusion = bf16[512,4,2,128]{3,2,1,0:T(2,128)(2,1)} fusion(bf16[512,4,1,128]{3,2,1,0:T(2,128)(2,1)S(1)} %stack_reshape.9, bf16[512,4,1,128]{3,2,1,0:T(2,128)(2,1)S(1)} %stack_reshape.8), kind=kLoop, calls=%fused_computation.9 | loop fusion | flops 2097152 | bytes 2097152 | tf_op jit(solution)/shard_map/stack | solution.py:211
  74.4 2.6 %reshape.136.w_ref = bf16[512,1024]{1,0:T(8,128)(2,1)} reshape(bf16[512,4,2,128]{3,2,1,0:T(2,128)(2,1)} %pad_maximum_fusion) | data formatting | bytes 2097152 | tf_op jit(solution)/shard_map/reshape | solution.py:211
  77.0 13.5 %all_gather.9 = bf16[512,512]{0,1:T(8,128)(2,1)} all-gather(bf16[512,128]{0,1:T(8,128)(2,1)S(1)} %bitcast.61), channel_id=1, replica_groups=mesh['nodes'=64,'heads'=4] {'heads'}, dimensions={1}, use_global_device_ids=true | all-gather | bytes 655360 | tf_op jit(solution)/shard_map/all_gather | solution.py:208
  90.5 39.8 %all-to-all-done.1 = bf16[64,64,512]{2,1,0:T(8,128)(2,1)} async-done(((bf16[64,64,512]{2,1,0:T(8,128)(2,1)}), bf16[64,64,512]{2,1,0:T(8,128)(2,1)}, u32[]{:S(2)}, u32[]{:S(2)}) %all-to-all-start.1) | async-done | bytes 4194336 | tf_op jit(solution)/shard_map/all_to_all | solution.py:212
  130.4 6.6 %shard_map.92 = bf16[4,1024,256]{2,1,0:T(8,128)(2,1)} custom-call(s32[32]{0:T(128)} %get-tuple-element.19.slot_ref, bf16[128,32,512]{2,1,0:T(8,128)(2,1)} %bitcast.8.recv_ref, bf16[512,1024]{1,0:T(8,128)(2,1)} %reshape.136.w_ref), custom_call_target="tpu_custom_call" | custom-call | tf_op jit(solution)/shard_map/pallas_call | solution.py:164
  137.0 4.5 %all-to-all-start.2 = ((bf16[4,32,32,256]{3,2,1,0:T(8,128)(2,1)}), bf16[4,32,32,256]{3,2,1,0:T(8,128)(2,1)S(1)}, u32[]{:S(2)}, u32[]{:S(2)}) async-start(bf16[4,32,32,256]{3,2,1,0:T(8,128)(2,1)} %bitcast.57), calls=%async_computation.2 | async-start | bytes 4194304 | tf_op jit(solution)/shard_map/all_to_all | solution.py:225
  141.5 0.1 fusion.20
  141.6 0.1 slice.42.slot_ref
  141.6 0.1 copy.53
  141.7 0.1 slice.44.live_ref
  141.9 0.9 copy.55
  142.8 2.0 %copy.45 = f32[8,128,128]{2,1,0:T(8,128)} copy(f32[8,128,128]{1,0,2:T(8,128)} %bitcast.60) | data formatting | bytes 1048576 | tf_op jit(solution)/shard_map/mul | solution.py:14
  144.9 1.1 fusion.4
  145.9 0.5 convolution_convert_fusion
  146.5 0.1 copy.54
  146.6 0.1 copy.43
  146.7 0.1 slice.38.live_ref
  146.8 0.1 copy.46
  147.0 1.3 broadcast_select_fusion.1
  148.3 20.6 %all-to-all-done.2 = bf16[4,32,32,256]{3,2,1,0:T(8,128)(2,1)S(1)} async-done(((bf16[4,32,32,256]{3,2,1,0:T(8,128)(2,1)}), bf16[4,32,32,256]{3,2,1,0:T(8,128)(2,1)S(1)}, u32[]{:S(2)}, u32[]{:S(2)}) %all-to-all-start.2) | async-done | bytes 2097184 | tf_op jit(solution)/shard_map/all_to_all | solution.py:225
  169.0 0.2 copy.52
  169.2 0.4 copy-done.1
  169.6 4.6 %shard_map.94 = bf16[4,128,128]{2,1,0:T(8,128)(2,1)S(1)} custom-call(s32[16]{0:T(128)S(1)} %slice.42.slot_ref, s32[16]{0:T(128)S(1)} %slice.44.live_ref, f32[2]{0:T(128)S(1)} %copy-done.1, bf16[4,256,128]{2,1,0:T(8,128)(2,1)S(1)} %get-tuple-element.26.q_ref, bf16[4,128,256]{2,1,0:T(8,128)(2,1)S(1)} %bitcast.44, bf16[32,128,256]{2,1,0:T(8,128)(2,1)S(1)} %bitcast.41), custom_call_target="tpu_custom_call" | custom-call | tf_op jit(solution)/shard_map/pallas_call | solution.py:83
  174.3 1.2 collective-permute-start.5
  175.5 0.9 collective-permute-start.3
  176.4 0.7 collective-permute-start.4
  177.1 4.6 %shard_map.93 = bf16[4,128,128]{2,1,0:T(8,128)(2,1)S(1)} custom-call(s32[16]{0:T(128)S(1)} %bitcast.53, s32[16]{0:T(128)S(1)} %slice.38.live_ref, f32[2]{0:T(128)S(1)} %copy-done.1, bf16[4,256,128]{2,1,0:T(8,128)(2,1)S(1)} %get-tuple-element.25.q_ref, bf16[4,128,256]{2,1,0:T(8,128)(2,1)S(1)} %bitcast.43, bf16[32,128,256]{2,1,0:T(8,128)(2,1)S(1)} %bitcast.42), custom_call_target="tpu_custom_call" | custom-call | tf_op jit(solution)/shard_map/pallas_call | solution.py:83
  181.7 2.6 %collective-permute-start.2 = (bf16[512,128]{1,0:T(8,128)(2,1)S(1)}, bf16[512,128]{1,0:T(8,128)(2,1)S(1)}, u32[]{:S(2)}, u32[]{:S(2)}) collective-permute-start(bf16[512,128]{1,0:T(8,128)(2,1)S(1)} %bitcast.45), channel_id=1, source_target_pairs={{0,3},{1,0},{2,1},{3,2},{4,7},{5,4},{6,5},{7,6},{8,11},{9,8},{10,9... | collective-permute-start | bytes 393224 | tf_op jit(solution)/shard_map/ppermute | solution.py:252
  184.3 0.1 collective-permute-start
  184.4 0.2 fusion.7
  184.6 0.2 fusion.9
  184.8 2.3 %collective-permute-start.1 = (bf16[512,128]{1,0:T(8,128)(2,1)S(1)}, bf16[512,128]{1,0:T(8,128)(2,1)S(1)}, u32[]{:S(2)}, u32[]{:S(2)}) collective-permute-start(bf16[512,128]{1,0:T(8,128)(2,1)S(1)} %bitcast.48), channel_id=1, source_target_pairs={{0,2},{1,3},{2,0},{3,1},{4,6},{5,7},{6,4},{7,5},{8,10},{9,11},{10,... | collective-permute-start | bytes 393224 | tf_op jit(solution)/shard_map/ppermute | solution.py:252
  187.1 0.2 convolution_add_fusion.1
  187.3 0.2 fusion.11
  187.5 0.2 fusion.3
  187.6 4.8 %collective-permute-done = bf16[512,128]{1,0:T(8,128)(2,1)S(1)} collective-permute-done((bf16[512,128]{1,0:T(8,128)(2,1)S(1)}, bf16[512,128]{1,0:T(8,128)(2,1)S(1)}, u32[]{:S(2)}, u32[]{:S(2)}) %collective-permute-start) | collective-permute-done | bytes 131104 | tf_op jit(solution)/shard_map/ppermute | solution.py:252
  192.5 0.2 convolution_add_fusion.3
  192.7 0.2 fusion.13
  192.8 0.2 fusion.2
  193.0 0.7 pad_maximum_fusion.3
  (35 shorter events, 0.3 us)
Async XLA Ops:
  0.0 35.5 %copy-start = (bf16[512,128]{1,0:T(8,128)(2,1)S(1)}, bf16[512,128]{1,0:T(8,128)(2,1)}, u32[]{:S(2)}) copy-start(bf16[512,128]{1,0:T(8,128)(2,1)} %param.10) | copy-start | bytes 393220
  3.5 20.5 %all-to-all-start = ((s32[64,1,2]{2,1,0:T(1,128)}), s32[64,1,2]{2,1,0:T(1,128)S(1)}, u32[]{:S(2)}, u32[]{:S(2)}) async-start(s32[64,1,2]{2,1,0:T(1,128)} %bitcast.5), calls=%async_computation | async-start | bytes 65536 | tf_op jit(solution)/shard_map/all_to_all | solution.py:197
  28.9 6.6 %copy-start.2 = (bf16[1024,512]{1,0:T(8,128)(2,1)S(1)}, bf16[1024,512]{1,0:T(8,128)(2,1)}, u32[]{:S(2)}) copy-start(bf16[1024,512]{1,0:T(8,128)(2,1)} %param.9) | copy-start | bytes 3145732
  28.9 101.5 %all-to-all-start.1 = ((bf16[64,64,512]{2,1,0:T(8,128)(2,1)}), bf16[64,64,512]{2,1,0:T(8,128)(2,1)}, u32[]{:S(2)}, u32[]{:S(2)}) async-start(bf16[64,64,512]{2,1,0:T(8,128)(2,1)} %bitcast.54), calls=%async_computation.1 | async-start | bytes 8388608 | tf_op jit(solution)/shard_map/all_to_all | solution.py:212
  35.5 1.5 copy-start.8
  35.5 2.2 %copy-start.4 = (bf16[512,128]{1,0:T(8,128)(2,1)S(1)}, bf16[512,128]{1,0:T(8,128)(2,1)}, u32[]{:S(2)}) copy-start(bf16[512,128]{1,0:T(8,128)(2,1)} %param.11) | copy-start | bytes 393220
  36.8 2.2 %copy-start.5 = (bf16[512,128]{1,0:T(8,128)(2,1)S(1)}, bf16[512,128]{1,0:T(8,128)(2,1)}, u32[]{:S(2)}) copy-start(bf16[512,128]{1,0:T(8,128)(2,1)} %param.12) | copy-start | bytes 393220
  71.1 5.9 %copy-start.6 = (bf16[128,512]{1,0:T(8,128)(2,1)S(1)}, bf16[128,512]{1,0:T(8,128)(2,1)}, u32[]{:S(2)}) copy-start(bf16[128,512]{1,0:T(8,128)(2,1)} %param.13) | copy-start | bytes 393220
  137.0 4.8 %copy-start.7 = (f32[1024,2]{0,1:T(2,128)S(1)}, f32[1024,2]{0,1:T(2,128)}, u32[]{:S(2)}) copy-start(f32[1024,2]{0,1:T(2,128)} %add_rsqrt_fusion.1) | copy-start | bytes 24580
  137.0 32.0 %all-to-all-start.2 = ((bf16[4,32,32,256]{3,2,1,0:T(8,128)(2,1)}), bf16[4,32,32,256]{3,2,1,0:T(8,128)(2,1)S(1)}, u32[]{:S(2)}, u32[]{:S(2)}) async-start(bf16[4,32,32,256]{3,2,1,0:T(8,128)(2,1)} %bitcast.57), calls=%async_computation.2 | async-start | bytes 4194304 | tf_op jit(solution)/shard_map/all_to_all | solution.py:225
  169.0 0.7 copy-start.1
  169.6 14.7 %copy-start.3 = (bf16[512,512]{0,1:T(8,128)(2,1)S(1)}, bf16[512,512]{0,1:T(8,128)(2,1)}, u32[]{:S(2)}) copy-start(bf16[512,512]{0,1:T(8,128)(2,1)} %all_gather.9) | copy-start | bytes 1572868
  174.3 13.0 %collective-permute-start.5 = (bf16[512,128]{1,0:T(8,128)(2,1)S(1)}, bf16[512,128]{1,0:T(8,128)(2,1)S(1)}, u32[]{:S(2)}, u32[]{:S(2)}) collective-permute-start(bf16[512,128]{1,0:T(8,128)(2,1)S(1)} %bitcast.49), channel_id=1, source_target_pairs={{0,3},{1,0},{2,1},{3,2},{4,7},{5,4},{6,5},{7,6},{8,11},{9,8},{10,9... | collective-permute-start | bytes 393224 | tf_op jit(solution)/shard_map/ppermute | solution.py:252
  175.5 9.2 %collective-permute-start.3 = (bf16[512,128]{1,0:T(8,128)(2,1)S(1)}, bf16[512,128]{1,0:T(8,128)(2,1)S(1)}, u32[]{:S(2)}, u32[]{:S(2)}) collective-permute-start(bf16[512,128]{1,0:T(8,128)(2,1)S(1)} %bitcast.50), channel_id=1, source_target_pairs={{0,1},{1,2},{2,3},{3,0},{4,5},{5,6},{6,7},{7,4},{8,9},{9,10},{10,1... | collective-permute-start | bytes 393224 | tf_op jit(solution)/shard_map/ppermute | solution.py:252
  176.4 11.1 %collective-permute-start.4 = (bf16[512,128]{1,0:T(8,128)(2,1)S(1)}, bf16[512,128]{1,0:T(8,128)(2,1)S(1)}, u32[]{:S(2)}, u32[]{:S(2)}) collective-permute-start(bf16[512,128]{1,0:T(8,128)(2,1)S(1)} %bitcast.51), channel_id=1, source_target_pairs={{0,2},{1,3},{2,0},{3,1},{4,6},{5,7},{6,4},{7,5},{8,10},{9,11},{10,... | collective-permute-start | bytes 393224 | tf_op jit(solution)/shard_map/ppermute | solution.py:252
  181.7 11.0 %collective-permute-start.2 = (bf16[512,128]{1,0:T(8,128)(2,1)S(1)}, bf16[512,128]{1,0:T(8,128)(2,1)S(1)}, u32[]{:S(2)}, u32[]{:S(2)}) collective-permute-start(bf16[512,128]{1,0:T(8,128)(2,1)S(1)} %bitcast.45), channel_id=1, source_target_pairs={{0,3},{1,0},{2,1},{3,2},{4,7},{5,4},{6,5},{7,6},{8,11},{9,8},{10,9... | collective-permute-start | bytes 393224 | tf_op jit(solution)/shard_map/ppermute | solution.py:252
  184.3 8.2 %collective-permute-start = (bf16[512,128]{1,0:T(8,128)(2,1)S(1)}, bf16[512,128]{1,0:T(8,128)(2,1)S(1)}, u32[]{:S(2)}, u32[]{:S(2)}) collective-permute-start(bf16[512,128]{1,0:T(8,128)(2,1)S(1)} %bitcast.46), channel_id=1, source_target_pairs={{0,1},{1,2},{2,3},{3,0},{4,5},{5,6},{6,7},{7,4},{8,9},{9,10},{10,1... | collective-permute-start | bytes 393224 | tf_op jit(solution)/shard_map/ppermute | solution.py:252
  184.8 8.1 %collective-permute-start.1 = (bf16[512,128]{1,0:T(8,128)(2,1)S(1)}, bf16[512,128]{1,0:T(8,128)(2,1)S(1)}, u32[]{:S(2)}, u32[]{:S(2)}) collective-permute-start(bf16[512,128]{1,0:T(8,128)(2,1)S(1)} %bitcast.48), channel_id=1, source_target_pairs={{0,2},{1,3},{2,0},{3,1},{4,6},{5,7},{6,4},{7,5},{8,10},{9,11},{10,... | collective-permute-start | bytes 393224 | tf_op jit(solution)/shard_map/ppermute | solution.py:252

commit v14 on v13

--- a/solution.py
+++ b/solution.py
@@ -234,7 +234,7 @@
             piece, w_part, (((1,), (1,)), ((), ())), preferred_element_type=jnp.float32
         )
 
-    halves = 2
+    halves = 4
     per_half = nblocks // halves
     outs = []
     for part in range(halves):

time: 195 us -> 212 us (1.087)
  waiting for transfers between devices: 73.8 us -> 83.7 us
  starting transfers between devices: 30.9 us -> 39.6 us
  Pallas kernels: 19.9 us -> 22.1 us
    ppermute x6 -> x12, starting transfers between devices: 7.82 us -> 16.3 us  [body(): lax.ppermute(attn_half, 'heads', [(j, (j + k) % heads_n) for j in range(h...]
    all_to_all x1, waiting for transfers between devices: 20.6 us -> 25.9 us  [body(): got = lax.all_to_all(send, 'heads', 0, 0, tiled=True)]
    ppermute x6 -> x12, waiting for transfers between devices: 4.83 us -> 8.78 us  [body(): lax.ppermute(attn_half, 'heads', [(j, (j + k) % heads_n) for j in range(h...]
    pallas_call x2 -> x4, Pallas kernels: 9.21 us -> 11.4 us  [attend(): pl.pallas_call(functools.partial(attend_kernel, count=count, slots=slots)...]
  transfers between devices with their start and end apart: 9 -> 15, of which waited for: 4 -> 6; matrix products, arithmetic and copies ran while one was open for 11% -> 8% of each run, Pallas kernels for 2% -> 4%
where the time goes in v14:
time: 212 us; the launch traced here: 211 us
  waiting for transfers between devices  83.7 us (39%)
  blocking collectives  41.3 us (19%)
  starting transfers between devices  39.6 us (19%)
  Pallas kernels  22.1 us (10%)
  local copies, waits for them, and re-layouts  12.6 us (6%)
  other arithmetic  6.85 us (3%)
  matrix products  4.53 us (2%)
    all_to_all x1, waiting for transfers between devices, body(): lax.all_to_all(payload.reshape(devices, capacity * quarter, model), 'node...  40.5 us
    all_to_all x1, waiting for transfers between devices, body(): got = lax.all_to_all(send, 'heads', 0, 0, tiled=True)  25.9 us
    ppermute x12, starting transfers between devices, body(): lax.ppermute(attn_half, 'heads', [(j, (j + k) % heads_n) for j in range(h...  16.3 us
    all_gather x1, blocking collectives, body(): lax.all_gather(w_value_b, 'heads', axis=1, tiled=True)  14.5 us
    all_gather x1, blocking collectives, body(): lax.all_gather(w_key_b, 'heads', axis=1, tiled=True)  14 us
    all_gather x1, blocking collectives, body(): w_out_t = lax.all_gather(w_out.T, 'heads', axis=1, tiled=True)  12.8 us
    all_to_all x1, starting transfers between devices, body(): lax.all_to_all(request.reshape(devices, capacity), 'nodes', split_axis=0,...  12 us
    pallas_call x4, Pallas kernels, attend(): pl.pallas_call(functools.partial(attend_kernel, count=count, slots=slots)...  11.4 us
  transfers between devices with their start and end apart: 15, of which 6 were waited for; matrix products, arithmetic and copies ran while one was open for 8% of the time, Pallas kernels for 4%

profile of v14, /device:TPU:2, one launch (start us, length us, event | category | flops | bytes accessed | tf_op | source)
XLA Modules:
  0.0 211.1 jit_solution(12120373441670841853)
XLA Ops:
  0.0 0.7 select_add_fusion
  0.9 0.8 copy.59
  1.9 0.2 select_reduce_fusion.1
  2.1 0.5 broadcast_clamp_fusion
  2.7 0.8 sub.39
  3.5 12.0 %all-to-all-start = ((s32[64,1,2]{2,1,0:T(1,128)}), s32[64,1,2]{2,1,0:T(1,128)S(1)}, u32[]{:S(2)}, u32[]{:S(2)}) async-start(s32[64,1,2]{2,1,0:T(1,128)} %bitcast.5), calls=%async_computation | async-start | bytes 65536 | tf_op jit(solution)/shard_map/all_to_all | solution.py:197
  15.5 8.5 %all-to-all-done = s32[64,1,2]{2,1,0:T(1,128)S(1)} async-done(((s32[64,1,2]{2,1,0:T(1,128)}), s32[64,1,2]{2,1,0:T(1,128)S(1)}, u32[]{:S(2)}, u32[]{:S(2)}) %all-to-all-start) | async-done | bytes 544 | tf_op jit(solution)/shard_map/all_to_all | solution.py:197
  24.0 0.1 add_reduce_fusion
  24.1 0.7 add.170.pick_ref
  24.8 4.0 %shard_map.91 = bf16[128,32,512]{2,1,0:T(8,128)(2,1)} custom-call(s32[128]{0:T(128)} %add.170.pick_ref, bf16[32,32,512]{2,1,0:T(8,128)(2,1)} %bitcast.79), custom_call_target="tpu_custom_call" | custom-call | tf_op jit(solution)/shard_map/pallas_call | solution.py:108
  28.8 6.6 %all-to-all-start.1 = ((bf16[64,64,512]{2,1,0:T(8,128)(2,1)}), bf16[64,64,512]{2,1,0:T(8,128)(2,1)}, u32[]{:S(2)}, u32[]{:S(2)}) async-start(bf16[64,64,512]{2,1,0:T(8,128)(2,1)} %bitcast.78), calls=%async_computation.1 | async-start | bytes 8388608 | tf_op jit(solution)/shard_map/all_to_all | solution.py:212
  36.6 0.5 bitcast_reduce_fusion
  37.1 0.7 fusion.8
  37.8 1.2 convolution_convert_fusion
  39.1 14.0 %all_gather.10 = bf16[512,512]{1,0:T(8,128)(2,1)S(1)} all-gather(bf16[512,128]{1,0:T(8,128)(2,1)S(1)} %copy-done.5), channel_id=1, replica_groups=mesh['nodes'=64,'heads'=4] {'heads'}, dimensions={1}, use_global_device_ids=true | all-gather | bytes 655360 | tf_op jit(solution)/shard_map/all_gather | solution.py:209
  53.0 0.3 stack_reshape.8
  53.3 14.5 %all_gather.11 = bf16[512,512]{1,0:T(8,128)(2,1)} all-gather(bf16[512,128]{1,0:T(8,128)(2,1)S(1)} %copy-done.6), channel_id=1, replica_groups=mesh['nodes'=64,'heads'=4] {'heads'}, dimensions={1}, use_global_device_ids=true | all-gather | bytes 655360 | tf_op jit(solution)/shard_map/all_gather | solution.py:210
  67.8 3.4 %stack_reshape.9 = bf16[512,4,1,128]{3,2,1,0:T(2,128)(2,1)S(1)} reshape(bf16[512,512]{1,0:T(8,128)(2,1)} %all_gather.11) | data formatting | bytes 1048576 | tf_op jit(solution)/shard_map/stack;reshape | solution.py:211
  71.3 3.2 %pad_maximum_fusion = bf16[512,4,2,128]{3,2,1,0:T(2,128)(2,1)} fusion(bf16[512,4,1,128]{3,2,1,0:T(2,128)(2,1)S(1)} %stack_reshape.9, bf16[512,4,1,128]{3,2,1,0:T(2,128)(2,1)S(1)} %stack_reshape.8), kind=kLoop, calls=%fused_computation.17 | loop fusion | flops 2097152 | bytes 2097152 | tf_op jit(solution)/shard_map/stack | solution.py:211
  74.5 2.6 %reshape.146.w_ref = bf16[512,1024]{1,0:T(8,128)(2,1)} reshape(bf16[512,4,2,128]{3,2,1,0:T(2,128)(2,1)} %pad_maximum_fusion) | data formatting | bytes 2097152 | tf_op jit(solution)/shard_map/reshape | solution.py:211
  77.1 12.8 %all_gather.9 = bf16[512,512]{0,1:T(8,128)(2,1)S(1)} all-gather(bf16[512,128]{0,1:T(8,128)(2,1)S(1)} %bitcast.84), channel_id=1, replica_groups=mesh['nodes'=64,'heads'=4] {'heads'}, dimensions={1}, use_global_device_ids=true | all-gather | bytes 655360 | tf_op jit(solution)/shard_map/all_gather | solution.py:208
  89.9 40.5 %all-to-all-done.1 = bf16[64,64,512]{2,1,0:T(8,128)(2,1)} async-done(((bf16[64,64,512]{2,1,0:T(8,128)(2,1)}), bf16[64,64,512]{2,1,0:T(8,128)(2,1)}, u32[]{:S(2)}, u32[]{:S(2)}) %all-to-all-start.1) | async-done | bytes 4194336 | tf_op jit(solution)/shard_map/all_to_all | solution.py:212
  130.3 6.7 %shard_map.92 = bf16[4,1024,256]{2,1,0:T(8,128)(2,1)} custom-call(s32[32]{0:T(128)} %get-tuple-element.19.slot_ref, bf16[128,32,512]{2,1,0:T(8,128)(2,1)} %bitcast.8.recv_ref, bf16[512,1024]{1,0:T(8,128)(2,1)} %reshape.146.w_ref), custom_call_target="tpu_custom_call" | custom-call | tf_op jit(solution)/shard_map/pallas_call | solution.py:164
  137.1 4.6 %all-to-all-start.2 = ((bf16[4,32,32,256]{3,2,1,0:T(8,128)(2,1)}), bf16[4,32,32,256]{3,2,1,0:T(8,128)(2,1)}, u32[]{:S(2)}, u32[]{:S(2)}) async-start(bf16[4,32,32,256]{3,2,1,0:T(8,128)(2,1)} %bitcast.80), calls=%async_computation.2 | async-start | bytes 4194304 | tf_op jit(solution)/shard_map/all_to_all | solution.py:225
  142.0 0.1 copy.68
  142.2 0.4 fusion.41
  142.6 0.2 copy.56
  143.0 0.2 copy.57
  143.3 0.1 broadcast_select_fusion.1
  143.5 25.9 %all-to-all-done.2 = bf16[4,32,32,256]{3,2,1,0:T(8,128)(2,1)} async-done(((bf16[4,32,32,256]{3,2,1,0:T(8,128)(2,1)}), bf16[4,32,32,256]{3,2,1,0:T(8,128)(2,1)}, u32[]{:S(2)}, u32[]{:S(2)}) %all-to-all-start.2) | async-done | bytes 2097184 | tf_op jit(solution)/shard_map/all_to_all | solution.py:225
  169.5 1.8 copy.64
  171.3 2.9 %shard_map.96 = bf16[2,128,128]{2,1,0:T(8,128)(2,1)S(1)} custom-call(s32[8]{0:T(128)S(1)} %slice.90.slot_ref, s32[8]{0:T(128)S(1)} %slice.92.live_ref, f32[2]{0:T(128)S(1)} %copy-done.1, bf16[2,256,128]{2,1,0:T(8,128)(2,1)S(1)} %get-tuple-element.29.q_ref, bf16[2,128,256]{2,1,0:T(8,128)(2,1)S(1)} %bitcast.60, bf16[32,128,256]{2,1,0:T(8,128)(2,1)S(1)} %bitcast.53), custom_call_target="tpu_custom_call" | custom-call | tf_op jit(solution)/shard_map/pallas_call | solution.py:83
  174.2 1.2 collective-permute-start.11
  175.4 1.5 collective-permute-start.10
  176.9 2.8 %shard_map.95 = bf16[2,128,128]{2,1,0:T(8,128)(2,1)S(1)} custom-call(s32[8]{0:T(128)S(1)} %slice.84.slot_ref, s32[8]{0:T(128)S(1)} %slice.86.live_ref, f32[2]{0:T(128)S(1)} %copy-done.1, bf16[2,256,128]{2,1,0:T(8,128)(2,1)S(1)} %get-tuple-element.30.q_ref, bf16[2,128,256]{2,1,0:T(8,128)(2,1)S(1)} %bitcast.59, bf16[32,128,256]{2,1,0:T(8,128)(2,1)S(1)} %bitcast.54), custom_call_target="tpu_custom_call" | custom-call | tf_op jit(solution)/shard_map/pallas_call | solution.py:83
  179.8 3.5 %collective-permute-start.8 = (bf16[256,128]{1,0:T(8,128)(2,1)S(1)}, bf16[256,128]{1,0:T(8,128)(2,1)S(1)}, u32[]{:S(2)}, u32[]{:S(2)}) collective-permute-start(bf16[256,128]{1,0:T(8,128)(2,1)S(1)} %bitcast.73), channel_id=1, source_target_pairs={{0,3},{1,0},{2,1},{3,2},{4,7},{5,4},{6,5},{7,6},{8,11},{9,8},{10,9... | collective-permute-start | bytes 196616 | tf_op jit(solution)/shard_map/ppermute | solution.py:252
  183.3 0.1 fusion.17
  183.4 0.1 fusion.15
  183.6 2.9 %shard_map.94 = bf16[2,128,128]{2,1,0:T(8,128)(2,1)S(1)} custom-call(s32[8]{0:T(128)S(1)} %slice.78.slot_ref, s32[8]{0:T(128)S(1)} %slice.80.live_ref, f32[2]{0:T(128)S(1)} %copy-done.1, bf16[2,256,128]{2,1,0:T(8,128)(2,1)S(1)} %get-tuple-element.28.q_ref, bf16[2,128,256]{2,1,0:T(8,128)(2,1)S(1)} %bitcast.58, bf16[32,128,256]{2,1,0:T(8,128)(2,1)S(1)} %bitcast.55), custom_call_target="tpu_custom_call" | custom-call | tf_op jit(solution)/shard_map/pallas_call | solution.py:83
  186.4 0.1 fusion.19
  186.6 2.8 %shard_map.93 = bf16[2,128,128]{2,1,0:T(8,128)(2,1)S(1)} custom-call(s32[8]{0:T(128)S(1)} %bitcast.77, s32[8]{0:T(128)S(1)} %slice.74.live_ref, f32[2]{0:T(128)S(1)} %copy-done.1, bf16[2,256,128]{2,1,0:T(8,128)(2,1)S(1)} %get-tuple-element.27.q_ref, bf16[2,128,256]{2,1,0:T(8,128)(2,1)S(1)} %bitcast.57, bf16[32,128,256]{2,1,0:T(8,128)(2,1)S(1)} %bitcast.56), custom_call_target="tpu_custom_call" | custom-call | tf_op jit(solution)/shard_map/pallas_call | solution.py:83
  189.5 0.1 fusion.21
  189.6 2.4 %collective-permute-start.7 = (bf16[256,128]{1,0:T(8,128)(2,1)S(1)}, bf16[256,128]{1,0:T(8,128)(2,1)S(1)}, u32[]{:S(2)}, u32[]{:S(2)}) collective-permute-start(bf16[256,128]{1,0:T(8,128)(2,1)S(1)} %bitcast.76), channel_id=1, source_target_pairs={{0,2},{1,3},{2,0},{3,1},{4,6},{5,7},{6,4},{7,5},{8,10},{9,11},{10,... | collective-permute-start | bytes 196616 | tf_op jit(solution)/shard_map/ppermute | solution.py:252
  192.0 0.2 convolution_add_fusion.3
  192.1 1.2 collective-permute-start.5
  193.4 0.1 fusion.25
  193.5 1.9 collective-permute-done.7
  195.5 2.3 %collective-permute-start.4 = (bf16[256,128]{1,0:T(8,128)(2,1)S(1)}, bf16[256,128]{1,0:T(8,128)(2,1)S(1)}, u32[]{:S(2)}, u32[]{:S(2)}) collective-permute-start(bf16[256,128]{1,0:T(8,128)(2,1)S(1)} %bitcast.71), channel_id=1, source_target_pairs={{0,2},{1,3},{2,0},{3,1},{4,6},{5,7},{6,4},{7,5},{8,10},{9,11},{10,... | collective-permute-start | bytes 196616 | tf_op jit(solution)/shard_map/ppermute | solution.py:252
  197.7 0.2 fusion.6
  197.9 2.0 collective-permute-start.3
  199.9 0.2 convolution_add_fusion.1
  200.0 1.4 collective-permute-start.2
  201.5 0.1 fusion.23
  201.6 0.8 collective-permute-start.1
  202.4 0.2 fusion.7
  202.6 1.8 collective-permute-done.3
  204.4 0.2 convolution_add_fusion.5
  204.6 0.1 fusion.27
  204.8 0.2 fusion.5
  204.9 5.0 %collective-permute-done = bf16[256,128]{1,0:T(8,128)(2,1)S(1)} collective-permute-done((bf16[256,128]{1,0:T(8,128)(2,1)S(1)}, bf16[256,128]{1,0:T(8,128)(2,1)S(1)}, u32[]{:S(2)}, u32[]{:S(2)}) %collective-permute-start) | collective-permute-done | bytes 65568 | tf_op jit(solution)/shard_map/ppermute | solution.py:252
  209.9 0.2 convolution_add_fusion.7
  210.1 0.1 fusion.29
  210.2 0.2 fusion.4
  210.4 0.7 pad_maximum_fusion.1
  (67 shorter events, 2.2 us)
Async XLA Ops:
  0.0 142.2 %copy-start = (bf16[512,128]{1,0:T(8,128)(2,1)S(1)}, bf16[512,128]{1,0:T(8,128)(2,1)}, u32[]{:S(2)}) copy-start(bf16[512,128]{1,0:T(8,128)(2,1)} %param.10) | copy-start | bytes 393220
  3.5 20.5 %all-to-all-start = ((s32[64,1,2]{2,1,0:T(1,128)}), s32[64,1,2]{2,1,0:T(1,128)S(1)}, u32[]{:S(2)}, u32[]{:S(2)}) async-start(s32[64,1,2]{2,1,0:T(1,128)} %bitcast.5), calls=%async_computation | async-start | bytes 65536 | tf_op jit(solution)/shard_map/all_to_all | solution.py:197
  28.8 6.9 %copy-start.8 = (s32[8,4]{0,1:T(4,128)S(1)}, s32[8,4]{0,1:T(4,128)}, u32[]{:S(2)}) copy-start(s32[8,4]{0,1:T(4,128)} %param.17) | copy-start | bytes 388
  28.8 7.7 %copy-start.2 = (bf16[1024,512]{1,0:T(8,128)(2,1)S(1)}, bf16[1024,512]{1,0:T(8,128)(2,1)}, u32[]{:S(2)}) copy-start(bf16[1024,512]{1,0:T(8,128)(2,1)} %param.9) | copy-start | bytes 3145732
  28.8 7.7 %copy-start.5 = (bf16[512,128]{1,0:T(8,128)(2,1)S(1)}, bf16[512,128]{1,0:T(8,128)(2,1)}, u32[]{:S(2)}) copy-start(bf16[512,128]{1,0:T(8,128)(2,1)} %param.11) | copy-start | bytes 393220
  28.8 101.5 %all-to-all-start.1 = ((bf16[64,64,512]{2,1,0:T(8,128)(2,1)}), bf16[64,64,512]{2,1,0:T(8,128)(2,1)}, u32[]{:S(2)}, u32[]{:S(2)}) async-start(bf16[64,64,512]{2,1,0:T(8,128)(2,1)} %bitcast.78), calls=%async_computation.1 | async-start | bytes 8388608 | tf_op jit(solution)/shard_map/all_to_all | solution.py:212
  35.4 2.4 %copy-start.6 = (bf16[512,128]{1,0:T(8,128)(2,1)S(1)}, bf16[512,128]{1,0:T(8,128)(2,1)}, u32[]{:S(2)}) copy-start(bf16[512,128]{1,0:T(8,128)(2,1)} %param.12) | copy-start | bytes 393220
  71.2 5.9 %copy-start.7 = (bf16[128,512]{1,0:T(8,128)(2,1)S(1)}, bf16[128,512]{1,0:T(8,128)(2,1)}, u32[]{:S(2)}) copy-start(bf16[128,512]{1,0:T(8,128)(2,1)} %param.13) | copy-start | bytes 393220
  137.0 4.6 %copy-start.3 = (bf16[1024,128]{0,1:T(8,128)(2,1)S(1)}, bf16[1024,128]{0,1:T(8,128)(2,1)}, u32[]{:S(2)}) copy-start(bf16[1024,128]{0,1:T(8,128)(2,1)} %fusion.8) | copy-start | bytes 786436
  137.1 4.6 %copy-start.4 = (bf16[1024,128]{0,1:T(8,128)(2,1)S(1)}, bf16[1024,128]{0,1:T(8,128)(2,1)}, u32[]{:S(2)}) copy-start(bf16[1024,128]{0,1:T(8,128)(2,1)} %convolution_convert_fusion) | copy-start | bytes 786436
  137.1 32.4 %all-to-all-start.2 = ((bf16[4,32,32,256]{3,2,1,0:T(8,128)(2,1)}), bf16[4,32,32,256]{3,2,1,0:T(8,128)(2,1)}, u32[]{:S(2)}, u32[]{:S(2)}) async-start(bf16[4,32,32,256]{3,2,1,0:T(8,128)(2,1)} %bitcast.80), calls=%async_computation.2 | async-start | bytes 4194304 | tf_op jit(solution)/shard_map/all_to_all | solution.py:225
  169.5 1.9 copy-start.1
  174.2 25.9 %collective-permute-start.11 = (bf16[256,128]{1,0:T(8,128)(2,1)S(1)}, bf16[256,128]{1,0:T(8,128)(2,1)S(1)}, u32[]{:S(2)}, u32[]{:S(2)}) collective-permute-start(bf16[256,128]{1,0:T(8,128)(2,1)S(1)} %bitcast.65), channel_id=1, source_target_pairs={{0,3},{1,0},{2,1},{3,2},{4,7},{5,4},{6,5},{7,6},{8,11},{9,8},{10,9... | collective-permute-start | bytes 196616 | tf_op jit(solution)/shard_map/ppermute | solution.py:252
  175.4 26.2 %collective-permute-start.10 = (bf16[256,128]{1,0:T(8,128)(2,1)S(1)}, bf16[256,128]{1,0:T(8,128)(2,1)S(1)}, u32[]{:S(2)}, u32[]{:S(2)}) collective-permute-start(bf16[256,128]{1,0:T(8,128)(2,1)S(1)} %bitcast.66), channel_id=1, source_target_pairs={{0,2},{1,3},{2,0},{3,1},{4,6},{5,7},{6,4},{7,5},{8,10},{9,11},{10,... | collective-permute-start | bytes 196616 | tf_op jit(solution)/shard_map/ppermute | solution.py:252
  176.9 21.0 %collective-permute-start.9 = (bf16[256,128]{1,0:T(8,128)(2,1)S(1)}, bf16[256,128]{1,0:T(8,128)(2,1)S(1)}, u32[]{:S(2)}, u32[]{:S(2)}) collective-permute-start(bf16[256,128]{1,0:T(8,128)(2,1)S(1)} %bitcast.67), channel_id=1, source_target_pairs={{0,1},{1,2},{2,3},{3,0},{4,5},{5,6},{6,7},{7,4},{8,9},{9,10},{10,1... | collective-permute-start | bytes 196616 | tf_op jit(solution)/shard_map/ppermute | solution.py:252
  179.8 12.3 %collective-permute-start.8 = (bf16[256,128]{1,0:T(8,128)(2,1)S(1)}, bf16[256,128]{1,0:T(8,128)(2,1)S(1)}, u32[]{:S(2)}, u32[]{:S(2)}) collective-permute-start(bf16[256,128]{1,0:T(8,128)(2,1)S(1)} %bitcast.73), channel_id=1, source_target_pairs={{0,3},{1,0},{2,1},{3,2},{4,7},{5,4},{6,5},{7,6},{8,11},{9,8},{10,9... | collective-permute-start | bytes 196616 | tf_op jit(solution)/shard_map/ppermute | solution.py:252
  183.3 6.3 %collective-permute-start.6 = (bf16[256,128]{1,0:T(8,128)(2,1)S(1)}, bf16[256,128]{1,0:T(8,128)(2,1)S(1)}, u32[]{:S(2)}, u32[]{:S(2)}) collective-permute-start(bf16[256,128]{1,0:T(8,128)(2,1)S(1)} %bitcast.74), channel_id=1, source_target_pairs={{0,1},{1,2},{2,3},{3,0},{4,5},{5,6},{6,7},{7,4},{8,9},{9,10},{10,1... | collective-permute-start | bytes 196616 | tf_op jit(solution)/shard_map/ppermute | solution.py:252
  189.6 5.9 %collective-permute-start.7 = (bf16[256,128]{1,0:T(8,128)(2,1)S(1)}, bf16[256,128]{1,0:T(8,128)(2,1)S(1)}, u32[]{:S(2)}, u32[]{:S(2)}) collective-permute-start(bf16[256,128]{1,0:T(8,128)(2,1)S(1)} %bitcast.76), channel_id=1, source_target_pairs={{0,2},{1,3},{2,0},{3,1},{4,6},{5,7},{6,4},{7,5},{8,10},{9,11},{10,... | collective-permute-start | bytes 196616 | tf_op jit(solution)/shard_map/ppermute | solution.py:252
  192.1 12.5 %collective-permute-start.5 = (bf16[256,128]{1,0:T(8,128)(2,1)S(1)}, bf16[256,128]{1,0:T(8,128)(2,1)S(1)}, u32[]{:S(2)}, u32[]{:S(2)}) collective-permute-start(bf16[256,128]{1,0:T(8,128)(2,1)S(1)} %bitcast.70), channel_id=1, source_target_pairs={{0,3},{1,0},{2,1},{3,2},{4,7},{5,4},{6,5},{7,6},{8,11},{9,8},{10,9... | collective-permute-start | bytes 196616 | tf_op jit(solution)/shard_map/ppermute | solution.py:252
  195.5 9.3 %collective-permute-start.4 = (bf16[256,128]{1,0:T(8,128)(2,1)S(1)}, bf16[256,128]{1,0:T(8,128)(2,1)S(1)}, u32[]{:S(2)}, u32[]{:S(2)}) collective-permute-start(bf16[256,128]{1,0:T(8,128)(2,1)S(1)} %bitcast.71), channel_id=1, source_target_pairs={{0,2},{1,3},{2,0},{3,1},{4,6},{5,7},{6,4},{7,5},{8,10},{9,11},{10,... | collective-permute-start | bytes 196616 | tf_op jit(solution)/shard_map/ppermute | solution.py:252
  197.9 6.5 %collective-permute-start.3 = (bf16[256,128]{1,0:T(8,128)(2,1)S(1)}, bf16[256,128]{1,0:T(8,128)(2,1)S(1)}, u32[]{:S(2)}, u32[]{:S(2)}) collective-permute-start(bf16[256,128]{1,0:T(8,128)(2,1)S(1)} %bitcast.72), channel_id=1, source_target_pairs={{0,1},{1,2},{2,3},{3,0},{4,5},{5,6},{6,7},{7,4},{8,9},{9,10},{10,1... | collective-permute-start | bytes 196616 | tf_op jit(solution)/shard_map/ppermute | solution.py:252
  200.0 10.0 %collective-permute-start.2 = (bf16[256,128]{1,0:T(8,128)(2,1)S(1)}, bf16[256,128]{1,0:T(8,128)(2,1)S(1)}, u32[]{:S(2)}, u32[]{:S(2)}) collective-permute-start(bf16[256,128]{1,0:T(8,128)(2,1)S(1)} %bitcast.62), channel_id=1, source_target_pairs={{0,3},{1,0},{2,1},{3,2},{4,7},{5,4},{6,5},{7,6},{8,11},{9,8},{10,9... | collective-permute-start | bytes 196616 | tf_op jit(solution)/shard_map/ppermute | solution.py:252
  201.6 8.6 %collective-permute-start.1 = (bf16[256,128]{1,0:T(8,128)(2,1)S(1)}, bf16[256,128]{1,0:T(8,128)(2,1)S(1)}, u32[]{:S(2)}, u32[]{:S(2)}) collective-permute-start(bf16[256,128]{1,0:T(8,128)(2,1)S(1)} %bitcast.63), channel_id=1, source_target_pairs={{0,2},{1,3},{2,0},{3,1},{4,6},{5,7},{6,4},{7,5},{8,10},{9,11},{10,... | collective-permute-start | bytes 196616 | tf_op jit(solution)/shard_map/ppermute | solution.py:252
  204.4 5.5 %collective-permute-start = (bf16[256,128]{1,0:T(8,128)(2,1)S(1)}, bf16[256,128]{1,0:T(8,128)(2,1)S(1)}, u32[]{:S(2)}, u32[]{:S(2)}) collective-permute-start(bf16[256,128]{1,0:T(8,128)(2,1)S(1)} %bitcast.64), channel_id=1, source_target_pairs={{0,1},{1,2},{2,3},{3,0},{4,5},{5,6},{6,7},{7,4},{8,9},{9,10},{10,1... | collective-permute-start | bytes 196616 | tf_op jit(solution)/shard_map/ppermute | solution.py:252

commit v15 on v13

--- a/solution.py
+++ b/solution.py
@@ -22,7 +22,7 @@
     hd = feat // count
 
     def pair_copy(p):
-        return pltpu.make_async_copy(recv_ref.at[slot_ref[p]], buf.at[p], sems.at[p])
+        return pltpu.make_async_copy(recv_ref.at[:, slot_ref[p]], buf.at[p], sems.at[p])
 
     @pl.when(b == 0)
     def _():
@@ -42,7 +42,7 @@
     for s in range(slots):
         inside = (key_lanes >= (s + 1) * width) & (key_lanes < (s + 2) * width)
         live_row = jnp.where(inside, live_ref[b * slots + s].astype(jnp.float32), live_row)
-    blocks = [own_ref[b]] + [buf[b * slots + s] for s in range(slots)]
+    blocks = [own_ref[b]] + [buf[b * slots + s].reshape(width, 2 * feat) for s in range(slots)]
     keys = jnp.concatenate([blk[:, :feat] for blk in blocks], axis=0)
     values = jnp.concatenate([blk[:, feat:] for blk in blocks], axis=0)
     s_all = lax.dot_general(
@@ -76,7 +76,7 @@
         ],
         out_specs=pl.BlockSpec((1, width, feat), lambda b, slot_of, live: (b, 0, 0)),
         scratch_shapes=[
-            pltpu.VMEM((nblocks * slots, width, 2 * feat), recv_kv.dtype),
+            pltpu.VMEM((nblocks * slots,) + recv_kv.shape[:1] + recv_kv.shape[2:], recv_kv.dtype),
             pltpu.SemaphoreType.DMA((nblocks * slots,)),
         ],
     )
@@ -223,7 +223,7 @@
         heads, pairs, quarter, 2 * feat
     )
     got = lax.all_to_all(send, "heads", 0, 0, tiled=True)
-    pair_kv = jnp.transpose(got, (1, 0, 2, 3)).reshape(pairs, width, 2 * feat)
+    pair_kv = got
     pair_ids = jnp.arange(pairs, dtype=jnp.int32)
     heads_n = lax.axis_size("heads")
     me_h = lax.axis_index("heads")

time: 195 us -> 192 us (0.985)
  Pallas kernels: 19.9 us -> 17.8 us
    pallas_call x2, Pallas kernels: 9.21 us -> 7.19 us  [attend(): pl.pallas_call(functools.partial(attend_kernel, count=count, slots=slots)...]
  transfers between devices with their start and end apart: 9 -> 9, of which waited for: 4 -> 5; matrix products, arithmetic and copies ran while one was open for 11% -> 11% of each run, Pallas kernels for 2% -> 2%
where the time goes in v15:
time: 192 us
  waiting for transfers between devices  74.5 us (39%)
  blocking collectives  42.1 us (22%)
  starting transfers between devices  30.1 us (16%)
  Pallas kernels  17.8 us (9%)
  local copies, waits for them, and re-layouts  12.8 us (7%)
  other arithmetic  9.52 us (5%)
  matrix products  4.38 us (2%)
    all_to_all x1, waiting for transfers between devices, body(): lax.all_to_all(payload.reshape(devices, capacity * quarter, model), 'node...  39.2 us
    all_to_all x1, waiting for transfers between devices, body(): got = lax.all_to_all(send, 'heads', 0, 0, tiled=True)  20.6 us
    all_gather x1, blocking collectives, body(): lax.all_gather(w_key_b, 'heads', axis=1, tiled=True)  14.6 us
    all_gather x1, blocking collectives, body(): lax.all_gather(w_value_b, 'heads', axis=1, tiled=True)  14 us
    all_gather x1, blocking collectives, body(): w_out_t = lax.all_gather(w_out.T, 'heads', axis=1, tiled=True)  13.5 us
    all_to_all x1, starting transfers between devices, body(): lax.all_to_all(request.reshape(devices, capacity), 'nodes', split_axis=0,...  12 us
    all_to_all x1, waiting for transfers between devices, body(): lax.all_to_all(request.reshape(devices, capacity), 'nodes', split_axis=0,...  8.51 us
    pallas_call x2, Pallas kernels, attend(): pl.pallas_call(functools.partial(attend_kernel, count=count, slots=slots)...  7.19 us
  transfers between devices with their start and end apart: 9, of which 5 were waited for; matrix products, arithmetic and copies ran while one was open for 11% of the time, Pallas kernels for 2%

profile of v15, /device:TPU:2, one launch (start us, length us, event | category | flops | bytes accessed | tf_op | source)
XLA Modules:
  0.0 191.6 jit_solution(1426191702983649142)
XLA Ops:
  0.0 0.8 copy.44
  0.8 0.1 reshape.129
  0.9 0.1 fusion.19
  1.0 0.2 select_reduce_fusion.1
  1.2 0.6 broadcast_clamp_fusion
  1.8 0.7 select_add_fusion
  2.5 0.1 copy.45
  2.6 0.1 reshape.138
  2.6 0.1 select_reduce_fusion
  2.7 0.8 sub.33
  3.5 12.0 %all-to-all-start = ((s32[64,1,2]{2,1,0:T(1,128)}), s32[64,1,2]{2,1,0:T(1,128)S(1)}, u32[]{:S(2)}, u32[]{:S(2)}) async-start(s32[64,1,2]{2,1,0:T(1,128)} %bitcast.5), calls=%async_computation | async-start | bytes 65536 | tf_op jit(solution)/shard_map/all_to_all | solution.py:197
  15.5 8.5 %all-to-all-done = s32[64,1,2]{2,1,0:T(1,128)S(1)} async-done(((s32[64,1,2]{2,1,0:T(1,128)}), s32[64,1,2]{2,1,0:T(1,128)S(1)}, u32[]{:S(2)}, u32[]{:S(2)}) %all-to-all-start) | async-done | bytes 544 | tf_op jit(solution)/shard_map/all_to_all | solution.py:197
  24.1 0.1 add_reduce_fusion
  24.2 0.7 add.130.pick_ref
  24.8 4.0 %shard_map.91 = bf16[128,32,512]{2,1,0:T(8,128)(2,1)} custom-call(s32[128]{0:T(128)} %add.130.pick_ref, bf16[32,32,512]{2,1,0:T(8,128)(2,1)} %bitcast.51), custom_call_target="tpu_custom_call" | custom-call | tf_op jit(solution)/shard_map/pallas_call | solution.py:108
  28.9 6.6 %all-to-all-start.1 = ((bf16[64,64,512]{2,1,0:T(8,128)(2,1)}), bf16[64,64,512]{2,1,0:T(8,128)(2,1)}, u32[]{:S(2)}, u32[]{:S(2)}) async-start(bf16[64,64,512]{2,1,0:T(8,128)(2,1)} %bitcast.50), calls=%async_computation.1 | async-start | bytes 8388608 | tf_op jit(solution)/shard_map/all_to_all | solution.py:212
  35.5 1.2 fusion.21
  36.8 0.2 copy.41
  37.0 0.6 compare_convert_fusion
  37.6 0.6 add_rsqrt_fusion.1
  38.2 1.3 bitcast_reduce_fusion
  39.5 14.0 %all_gather.11 = bf16[512,512]{1,0:T(8,128)(2,1)S(1)} all-gather(bf16[512,128]{1,0:T(8,128)(2,1)S(1)} %copy-done.5), channel_id=1, replica_groups=mesh['nodes'=64,'heads'=4] {'heads'}, dimensions={1}, use_global_device_ids=true | all-gather | bytes 655360 | tf_op jit(solution)/shard_map/all_gather | solution.py:210
  53.5 0.3 stack_reshape.9
  53.8 14.6 %all_gather.10 = bf16[512,512]{1,0:T(8,128)(2,1)} all-gather(bf16[512,128]{1,0:T(8,128)(2,1)S(1)} %copy-done.4), channel_id=1, replica_groups=mesh['nodes'=64,'heads'=4] {'heads'}, dimensions={1}, use_global_device_ids=true | all-gather | bytes 655360 | tf_op jit(solution)/shard_map/all_gather | solution.py:209
  68.4 3.4 %stack_reshape.8 = bf16[512,4,1,128]{3,2,1,0:T(2,128)(2,1)S(1)} reshape(bf16[512,512]{1,0:T(8,128)(2,1)} %all_gather.10) | data formatting | bytes 1048576 | tf_op jit(solution)/shard_map/stack;reshape | solution.py:211
  71.8 3.2 %pad_maximum_fusion = bf16[512,4,2,128]{3,2,1,0:T(2,128)(2,1)} fusion(bf16[512,4,1,128]{3,2,1,0:T(2,128)(2,1)S(1)} %stack_reshape.9, bf16[512,4,1,128]{3,2,1,0:T(2,128)(2,1)S(1)} %stack_reshape.8), kind=kLoop, calls=%fused_computation.9 | loop fusion | flops 2097152 | bytes 2097152 | tf_op jit(solution)/shard_map/stack | solution.py:211
  75.0 2.6 %reshape.133.w_ref = bf16[512,1024]{1,0:T(8,128)(2,1)} reshape(bf16[512,4,2,128]{3,2,1,0:T(2,128)(2,1)} %pad_maximum_fusion) | data formatting | bytes 2097152 | tf_op jit(solution)/shard_map/reshape | solution.py:211
  77.6 13.5 %all_gather.9 = bf16[512,512]{0,1:T(8,128)(2,1)} all-gather(bf16[512,128]{0,1:T(8,128)(2,1)S(1)} %bitcast.56), channel_id=1, replica_groups=mesh['nodes'=64,'heads'=4] {'heads'}, dimensions={1}, use_global_device_ids=true | all-gather | bytes 655360 | tf_op jit(solution)/shard_map/all_gather | solution.py:208
  91.1 39.2 %all-to-all-done.1 = bf16[64,64,512]{2,1,0:T(8,128)(2,1)} async-done(((bf16[64,64,512]{2,1,0:T(8,128)(2,1)}), bf16[64,64,512]{2,1,0:T(8,128)(2,1)}, u32[]{:S(2)}, u32[]{:S(2)}) %all-to-all-start.1) | async-done | bytes 4194336 | tf_op jit(solution)/shard_map/all_to_all | solution.py:212
  130.4 6.6 %shard_map.92 = bf16[4,1024,256]{2,1,0:T(8,128)(2,1)} custom-call(s32[32]{0:T(128)} %get-tuple-element.19.slot_ref, bf16[128,32,512]{2,1,0:T(8,128)(2,1)} %bitcast.8.recv_ref, bf16[512,1024]{1,0:T(8,128)(2,1)} %reshape.133.w_ref), custom_call_target="tpu_custom_call" | custom-call | tf_op jit(solution)/shard_map/pallas_call | solution.py:164
  137.0 4.5 %all-to-all-start.2 = ((bf16[4,32,32,256]{3,2,1,0:T(8,128)(2,1)}), bf16[4,32,32,256]{3,2,1,0:T(8,128)(2,1)S(1)}, u32[]{:S(2)}, u32[]{:S(2)}) async-start(bf16[4,32,32,256]{3,2,1,0:T(8,128)(2,1)} %bitcast.52), calls=%async_computation.2 | async-start | bytes 4194304 | tf_op jit(solution)/shard_map/all_to_all | solution.py:225
  141.5 0.1 fusion.20
  141.6 0.1 slice.42.slot_ref
  141.6 0.1 copy.49
  141.7 0.1 slice.44.live_ref
  141.9 0.9 copy.51
  142.8 2.0 %copy.42 = f32[8,128,128]{2,1,0:T(8,128)} copy(f32[8,128,128]{1,0,2:T(8,128)} %bitcast.55) | data formatting | bytes 1048576 | tf_op jit(solution)/shard_map/mul | solution.py:14
  144.8 1.1 fusion.4
  145.9 0.5 convolution_convert_fusion
  146.5 0.1 copy.50
  146.6 0.1 copy.40
  146.7 0.1 slice.38.live_ref
  146.8 0.1 copy.43
  147.0 1.3 broadcast_select_fusion.1
  148.3 20.6 %all-to-all-done.2.recv_ref = bf16[4,32,32,256]{3,2,1,0:T(8,128)(2,1)S(1)} async-done(((bf16[4,32,32,256]{3,2,1,0:T(8,128)(2,1)}), bf16[4,32,32,256]{3,2,1,0:T(8,128)(2,1)S(1)}, u32[]{:S(2)}, u32[]{:S(2)}) %all-to-all-start.2) | async-done | bytes 2097184 | tf_op jit(solution)/shard_map/all_to_all | solution.py:225
  169.0 3.6 %shard_map.94 = bf16[4,128,128]{2,1,0:T(8,128)(2,1)S(1)} custom-call(s32[16]{0:T(128)S(1)} %slice.42.slot_ref, s32[16]{0:T(128)S(1)} %slice.44.live_ref, f32[2]{0:T(128)S(1)} %copy-done.1, bf16[4,256,128]{2,1,0:T(8,128)(2,1)S(1)} %get-tuple-element.26.q_ref, bf16[4,128,256]{2,1,0:T(8,128)(2,1)S(1)} %bitcast.40, ...), custom_call_target="tpu_custom_call" | custom-call | tf_op jit(solution)/shard_map/pallas_call | solution.py:83
  172.6 1.2 collective-permute-start.5
  173.8 0.9 collective-permute-start.3
  174.7 0.7 collective-permute-start.4
  175.4 3.6 %shard_map.93 = bf16[4,128,128]{2,1,0:T(8,128)(2,1)S(1)} custom-call(s32[16]{0:T(128)S(1)} %bitcast.49, s32[16]{0:T(128)S(1)} %slice.38.live_ref, f32[2]{0:T(128)S(1)} %copy-done.1, bf16[4,256,128]{2,1,0:T(8,128)(2,1)S(1)} %get-tuple-element.25.q_ref, bf16[4,128,256]{2,1,0:T(8,128)(2,1)S(1)} %bitcast.39, bf16[4,32,32,256]{3,2,1,0:T(8,128)(2,1)S(1)} %all-to-all-done.2.recv_ref), custom_call_target="tpu_custom_call" | custom-call | tf_op jit(solution)/shard_map/pallas_call | solution.py:83
  179.0 2.6 %collective-permute-start.2 = (bf16[512,128]{1,0:T(8,128)(2,1)S(1)}, bf16[512,128]{1,0:T(8,128)(2,1)S(1)}, u32[]{:S(2)}, u32[]{:S(2)}) collective-permute-start(bf16[512,128]{1,0:T(8,128)(2,1)S(1)} %bitcast.41), channel_id=1, source_target_pairs={{0,3},{1,0},{2,1},{3,2},{4,7},{5,4},{6,5},{7,6},{8,11},{9,8},{10,9... | collective-permute-start | bytes 393224 | tf_op jit(solution)/shard_map/ppermute | solution.py:252
  181.6 0.1 collective-permute-start
  181.7 0.2 fusion.7
  181.9 0.2 fusion.9
  182.1 0.8 collective-permute-done.3
  182.8 1.5 collective-permute-start.1
  184.4 0.2 convolution_add_fusion.1
  184.6 0.2 fusion.11
  184.8 0.2 fusion.3
  184.9 5.3 %collective-permute-done = bf16[512,128]{1,0:T(8,128)(2,1)S(1)} collective-permute-done((bf16[512,128]{1,0:T(8,128)(2,1)S(1)}, bf16[512,128]{1,0:T(8,128)(2,1)S(1)}, u32[]{:S(2)}, u32[]{:S(2)}) %collective-permute-start) | collective-permute-done | bytes 131104 | tf_op jit(solution)/shard_map/ppermute | solution.py:252
  190.3 0.2 convolution_add_fusion.3
  190.5 0.2 fusion.13
  190.7 0.2 fusion.2
  190.9 0.7 pad_maximum_fusion.3
  (36 shorter events, 0.3 us)
Async XLA Ops:
  0.0 35.5 %copy-start = (bf16[512,128]{1,0:T(8,128)(2,1)S(1)}, bf16[512,128]{1,0:T(8,128)(2,1)}, u32[]{:S(2)}) copy-start(bf16[512,128]{1,0:T(8,128)(2,1)} %param.10) | copy-start | bytes 393220
  3.5 20.5 %all-to-all-start = ((s32[64,1,2]{2,1,0:T(1,128)}), s32[64,1,2]{2,1,0:T(1,128)S(1)}, u32[]{:S(2)}, u32[]{:S(2)}) async-start(s32[64,1,2]{2,1,0:T(1,128)} %bitcast.5), calls=%async_computation | async-start | bytes 65536 | tf_op jit(solution)/shard_map/all_to_all | solution.py:197
  28.9 6.6 %copy-start.2 = (bf16[1024,512]{1,0:T(8,128)(2,1)S(1)}, bf16[1024,512]{1,0:T(8,128)(2,1)}, u32[]{:S(2)}) copy-start(bf16[1024,512]{1,0:T(8,128)(2,1)} %param.9) | copy-start | bytes 3145732
  28.9 101.5 %all-to-all-start.1 = ((bf16[64,64,512]{2,1,0:T(8,128)(2,1)}), bf16[64,64,512]{2,1,0:T(8,128)(2,1)}, u32[]{:S(2)}, u32[]{:S(2)}) async-start(bf16[64,64,512]{2,1,0:T(8,128)(2,1)} %bitcast.50), calls=%async_computation.1 | async-start | bytes 8388608 | tf_op jit(solution)/shard_map/all_to_all | solution.py:212
  35.5 1.5 copy-start.9
  35.5 2.7 %copy-start.4 = (bf16[512,128]{1,0:T(8,128)(2,1)S(1)}, bf16[512,128]{1,0:T(8,128)(2,1)}, u32[]{:S(2)}) copy-start(bf16[512,128]{1,0:T(8,128)(2,1)} %param.11) | copy-start | bytes 393220
  36.8 2.7 %copy-start.5 = (bf16[512,128]{1,0:T(8,128)(2,1)S(1)}, bf16[512,128]{1,0:T(8,128)(2,1)}, u32[]{:S(2)}) copy-start(bf16[512,128]{1,0:T(8,128)(2,1)} %param.12) | copy-start | bytes 393220
  71.8 5.8 %copy-start.6 = (bf16[128,512]{1,0:T(8,128)(2,1)S(1)}, bf16[128,512]{1,0:T(8,128)(2,1)}, u32[]{:S(2)}) copy-start(bf16[128,512]{1,0:T(8,128)(2,1)} %param.13) | copy-start | bytes 393220
  137.0 4.5 %copy-start.8 = (s32[8,4]{0,1:T(4,128)S(1)}, s32[8,4]{0,1:T(4,128)}, u32[]{:S(2)}) copy-start(s32[8,4]{0,1:T(4,128)} %compare_convert_fusion) | copy-start | bytes 388
  137.0 4.8 %copy-start.7 = (f32[1024,2]{0,1:T(2,128)S(1)}, f32[1024,2]{0,1:T(2,128)}, u32[]{:S(2)}) copy-start(f32[1024,2]{0,1:T(2,128)} %add_rsqrt_fusion.1) | copy-start | bytes 24580
  137.0 32.0 %all-to-all-start.2 = ((bf16[4,32,32,256]{3,2,1,0:T(8,128)(2,1)}), bf16[4,32,32,256]{3,2,1,0:T(8,128)(2,1)S(1)}, u32[]{:S(2)}, u32[]{:S(2)}) async-start(bf16[4,32,32,256]{3,2,1,0:T(8,128)(2,1)} %bitcast.52), calls=%async_computation.2 | async-start | bytes 4194304 | tf_op jit(solution)/shard_map/all_to_all | solution.py:225
  146.5 22.5 %copy-start.1 = (f32[2]{0:T(128)S(1)}, f32[2]{0:T(128)}, u32[]{:S(2)}) copy-start(f32[2]{0:T(128)} %scale_ref.3) | copy-start | bytes 28
  169.0 12.7 %copy-start.3 = (bf16[512,512]{0,1:T(8,128)(2,1)S(1)}, bf16[512,512]{0,1:T(8,128)(2,1)}, u32[]{:S(2)}) copy-start(bf16[512,512]{0,1:T(8,128)(2,1)} %all_gather.9) | copy-start | bytes 1572868
  172.6 12.0 %collective-permute-start.5 = (bf16[512,128]{1,0:T(8,128)(2,1)S(1)}, bf16[512,128]{1,0:T(8,128)(2,1)S(1)}, u32[]{:S(2)}, u32[]{:S(2)}) collective-permute-start(bf16[512,128]{1,0:T(8,128)(2,1)S(1)} %bitcast.45), channel_id=1, source_target_pairs={{0,3},{1,0},{2,1},{3,2},{4,7},{5,4},{6,5},{7,6},{8,11},{9,8},{10,9... | collective-permute-start | bytes 393224 | tf_op jit(solution)/shard_map/ppermute | solution.py:252
  173.8 9.0 %collective-permute-start.3 = (bf16[512,128]{1,0:T(8,128)(2,1)S(1)}, bf16[512,128]{1,0:T(8,128)(2,1)S(1)}, u32[]{:S(2)}, u32[]{:S(2)}) collective-permute-start(bf16[512,128]{1,0:T(8,128)(2,1)S(1)} %bitcast.46), channel_id=1, source_target_pairs={{0,1},{1,2},{2,3},{3,0},{4,5},{5,6},{6,7},{7,4},{8,9},{9,10},{10,1... | collective-permute-start | bytes 393224 | tf_op jit(solution)/shard_map/ppermute | solution.py:252
  174.7 10.1 %collective-permute-start.4 = (bf16[512,128]{1,0:T(8,128)(2,1)S(1)}, bf16[512,128]{1,0:T(8,128)(2,1)S(1)}, u32[]{:S(2)}, u32[]{:S(2)}) collective-permute-start(bf16[512,128]{1,0:T(8,128)(2,1)S(1)} %bitcast.47), channel_id=1, source_target_pairs={{0,2},{1,3},{2,0},{3,1},{4,6},{5,7},{6,4},{7,5},{8,10},{9,11},{10,... | collective-permute-start | bytes 393224 | tf_op jit(solution)/shard_map/ppermute | solution.py:252
  179.0 11.5 %collective-permute-start.2 = (bf16[512,128]{1,0:T(8,128)(2,1)S(1)}, bf16[512,128]{1,0:T(8,128)(2,1)S(1)}, u32[]{:S(2)}, u32[]{:S(2)}) collective-permute-start(bf16[512,128]{1,0:T(8,128)(2,1)S(1)} %bitcast.41), channel_id=1, source_target_pairs={{0,3},{1,0},{2,1},{3,2},{4,7},{5,4},{6,5},{7,6},{8,11},{9,8},{10,9... | collective-permute-start | bytes 393224 | tf_op jit(solution)/shard_map/ppermute | solution.py:252
  181.6 8.7 %collective-permute-start = (bf16[512,128]{1,0:T(8,128)(2,1)S(1)}, bf16[512,128]{1,0:T(8,128)(2,1)S(1)}, u32[]{:S(2)}, u32[]{:S(2)}) collective-permute-start(bf16[512,128]{1,0:T(8,128)(2,1)S(1)} %bitcast.42), channel_id=1, source_target_pairs={{0,1},{1,2},{2,3},{3,0},{4,5},{5,6},{6,7},{7,4},{8,9},{9,10},{10,1... | collective-permute-start | bytes 393224 | tf_op jit(solution)/shard_map/ppermute | solution.py:252
  182.8 7.8 %collective-permute-start.1 = (bf16[512,128]{1,0:T(8,128)(2,1)S(1)}, bf16[512,128]{1,0:T(8,128)(2,1)S(1)}, u32[]{:S(2)}, u32[]{:S(2)}) collective-permute-start(bf16[512,128]{1,0:T(8,128)(2,1)S(1)} %bitcast.44), channel_id=1, source_target_pairs={{0,2},{1,3},{2,0},{3,1},{4,6},{5,7},{6,4},{7,5},{8,10},{9,11},{10,... | collective-permute-start | bytes 393224 | tf_op jit(solution)/shard_map/ppermute | solution.py:252

commit v16 on v15

--- a/solution.py
+++ b/solution.py
@@ -98,7 +98,7 @@
 def gather_blocks(blocks, pick):
     nblocks, r, l = blocks.shape
     tiles = pick.shape[0]
-    group = 64
+    group = 128
     grid_spec = pltpu.PrefetchScalarGridSpec(
         num_scalar_prefetch=1,
         grid=(tiles // group,),

time: 192 us -> 193 us (level)
  no operation moved by 1% of the time
where the time goes in v16:
time: 193 us; the launch traced here: 192 us
  waiting for transfers between devices  74.5 us (39%)
  blocking collectives  42.1 us (22%)
  starting transfers between devices  30.1 us (16%)
  Pallas kernels  17.9 us (9%)
  local copies, waits for them, and re-layouts  12.8 us (7%)
  other arithmetic  9.52 us (5%)
  matrix products  4.38 us (2%)
    all_to_all x1, waiting for transfers between devices, body(): lax.all_to_all(payload.reshape(devices, capacity * quarter, model), 'node...  39.2 us
    all_to_all x1, waiting for transfers between devices, body(): got = lax.all_to_all(send, 'heads', 0, 0, tiled=True)  20.6 us
    all_gather x1, blocking collectives, body(): lax.all_gather(w_key_b, 'heads', axis=1, tiled=True)  14.6 us
    all_gather x1, blocking collectives, body(): lax.all_gather(w_value_b, 'heads', axis=1, tiled=True)  14 us
    all_gather x1, blocking collectives, body(): w_out_t = lax.all_gather(w_out.T, 'heads', axis=1, tiled=True)  13.5 us
    all_to_all x1, starting transfers between devices, body(): lax.all_to_all(request.reshape(devices, capacity), 'nodes', split_axis=0,...  12 us
    all_to_all x1, waiting for transfers between devices, body(): lax.all_to_all(request.reshape(devices, capacity), 'nodes', split_axis=0,...  8.51 us
    pallas_call x2, Pallas kernels, attend(): pl.pallas_call(functools.partial(attend_kernel, count=count, slots=slots)...  7.19 us
  transfers between devices with their start and end apart: 9, of which 5 were waited for; matrix products, arithmetic and copies ran while one was open for 11% of the time, Pallas kernels for 2%

profile of v16, /device:TPU:2, one launch (start us, length us, event | category | flops | bytes accessed | tf_op | source)
XLA Modules:
  0.0 191.7 jit_solution(6081447660099701276)
XLA Ops:
  0.0 0.8 copy.44
  0.8 0.1 reshape.129
  0.9 0.1 fusion.19
  1.0 0.2 select_reduce_fusion.1
  1.2 0.6 broadcast_clamp_fusion
  1.8 0.7 select_add_fusion
  2.5 0.1 copy.45
  2.6 0.1 reshape.138
  2.6 0.1 select_reduce_fusion
  2.7 0.8 sub.33
  3.5 12.0 %all-to-all-start = ((s32[64,1,2]{2,1,0:T(1,128)}), s32[64,1,2]{2,1,0:T(1,128)S(1)}, u32[]{:S(2)}, u32[]{:S(2)}) async-start(s32[64,1,2]{2,1,0:T(1,128)} %bitcast.5), calls=%async_computation | async-start | bytes 65536 | tf_op jit(solution)/shard_map/all_to_all | solution.py:197
  15.5 8.5 %all-to-all-done = s32[64,1,2]{2,1,0:T(1,128)S(1)} async-done(((s32[64,1,2]{2,1,0:T(1,128)}), s32[64,1,2]{2,1,0:T(1,128)S(1)}, u32[]{:S(2)}, u32[]{:S(2)}) %all-to-all-start) | async-done | bytes 544 | tf_op jit(solution)/shard_map/all_to_all | solution.py:197
  24.1 0.1 add_reduce_fusion
  24.2 0.7 add.130.pick_ref
  24.8 4.1 %shard_map.91 = bf16[128,32,512]{2,1,0:T(8,128)(2,1)} custom-call(s32[128]{0:T(128)} %add.130.pick_ref, bf16[32,32,512]{2,1,0:T(8,128)(2,1)} %bitcast.51), custom_call_target="tpu_custom_call" | custom-call | tf_op jit(solution)/shard_map/pallas_call | solution.py:108
  29.0 6.6 %all-to-all-start.1 = ((bf16[64,64,512]{2,1,0:T(8,128)(2,1)}), bf16[64,64,512]{2,1,0:T(8,128)(2,1)}, u32[]{:S(2)}, u32[]{:S(2)}) async-start(bf16[64,64,512]{2,1,0:T(8,128)(2,1)} %bitcast.50), calls=%async_computation.1 | async-start | bytes 8388608 | tf_op jit(solution)/shard_map/all_to_all | solution.py:212
  35.6 1.2 fusion.21
  36.9 0.2 copy.41
  37.1 0.6 compare_convert_fusion
  37.7 0.6 add_rsqrt_fusion.1
  38.3 1.3 bitcast_reduce_fusion
  39.6 14.0 %all_gather.11 = bf16[512,512]{1,0:T(8,128)(2,1)S(1)} all-gather(bf16[512,128]{1,0:T(8,128)(2,1)S(1)} %copy-done.5), channel_id=1, replica_groups=mesh['nodes'=64,'heads'=4] {'heads'}, dimensions={1}, use_global_device_ids=true | all-gather | bytes 655360 | tf_op jit(solution)/shard_map/all_gather | solution.py:210
  53.6 0.3 stack_reshape.9
  53.9 14.6 %all_gather.10 = bf16[512,512]{1,0:T(8,128)(2,1)} all-gather(bf16[512,128]{1,0:T(8,128)(2,1)S(1)} %copy-done.4), channel_id=1, replica_groups=mesh['nodes'=64,'heads'=4] {'heads'}, dimensions={1}, use_global_device_ids=true | all-gather | bytes 655360 | tf_op jit(solution)/shard_map/all_gather | solution.py:209
  68.5 3.4 %stack_reshape.8 = bf16[512,4,1,128]{3,2,1,0:T(2,128)(2,1)S(1)} reshape(bf16[512,512]{1,0:T(8,128)(2,1)} %all_gather.10) | data formatting | bytes 1048576 | tf_op jit(solution)/shard_map/stack;reshape | solution.py:211
  71.9 3.2 %pad_maximum_fusion = bf16[512,4,2,128]{3,2,1,0:T(2,128)(2,1)} fusion(bf16[512,4,1,128]{3,2,1,0:T(2,128)(2,1)S(1)} %stack_reshape.9, bf16[512,4,1,128]{3,2,1,0:T(2,128)(2,1)S(1)} %stack_reshape.8), kind=kLoop, calls=%fused_computation.9 | loop fusion | flops 2097152 | bytes 2097152 | tf_op jit(solution)/shard_map/stack | solution.py:211
  75.1 2.6 %reshape.133.w_ref = bf16[512,1024]{1,0:T(8,128)(2,1)} reshape(bf16[512,4,2,128]{3,2,1,0:T(2,128)(2,1)} %pad_maximum_fusion) | data formatting | bytes 2097152 | tf_op jit(solution)/shard_map/reshape | solution.py:211
  77.7 13.5 %all_gather.9 = bf16[512,512]{0,1:T(8,128)(2,1)} all-gather(bf16[512,128]{0,1:T(8,128)(2,1)S(1)} %bitcast.56), channel_id=1, replica_groups=mesh['nodes'=64,'heads'=4] {'heads'}, dimensions={1}, use_global_device_ids=true | all-gather | bytes 655360 | tf_op jit(solution)/shard_map/all_gather | solution.py:208
  91.2 39.2 %all-to-all-done.1 = bf16[64,64,512]{2,1,0:T(8,128)(2,1)} async-done(((bf16[64,64,512]{2,1,0:T(8,128)(2,1)}), bf16[64,64,512]{2,1,0:T(8,128)(2,1)}, u32[]{:S(2)}, u32[]{:S(2)}) %all-to-all-start.1) | async-done | bytes 4194336 | tf_op jit(solution)/shard_map/all_to_all | solution.py:212
  130.5 6.6 %shard_map.92 = bf16[4,1024,256]{2,1,0:T(8,128)(2,1)} custom-call(s32[32]{0:T(128)} %get-tuple-element.19.slot_ref, bf16[128,32,512]{2,1,0:T(8,128)(2,1)} %bitcast.8.recv_ref, bf16[512,1024]{1,0:T(8,128)(2,1)} %reshape.133.w_ref), custom_call_target="tpu_custom_call" | custom-call | tf_op jit(solution)/shard_map/pallas_call | solution.py:164
  137.1 4.5 %all-to-all-start.2 = ((bf16[4,32,32,256]{3,2,1,0:T(8,128)(2,1)}), bf16[4,32,32,256]{3,2,1,0:T(8,128)(2,1)S(1)}, u32[]{:S(2)}, u32[]{:S(2)}) async-start(bf16[4,32,32,256]{3,2,1,0:T(8,128)(2,1)} %bitcast.52), calls=%async_computation.2 | async-start | bytes 4194304 | tf_op jit(solution)/shard_map/all_to_all | solution.py:225
  141.6 0.1 fusion.20
  141.7 0.1 slice.42.slot_ref
  141.7 0.1 copy.49
  141.8 0.1 slice.44.live_ref
  142.0 0.9 copy.51
  142.9 2.0 %copy.42 = f32[8,128,128]{2,1,0:T(8,128)} copy(f32[8,128,128]{1,0,2:T(8,128)} %bitcast.55) | data formatting | bytes 1048576 | tf_op jit(solution)/shard_map/mul | solution.py:14
  144.9 1.1 fusion.4
  146.0 0.5 convolution_convert_fusion
  146.6 0.1 copy.50
  146.7 0.1 copy.40
  146.8 0.1 slice.38.live_ref
  146.9 0.1 copy.43
  147.1 1.3 broadcast_select_fusion.1
  148.5 20.6 %all-to-all-done.2.recv_ref = bf16[4,32,32,256]{3,2,1,0:T(8,128)(2,1)S(1)} async-done(((bf16[4,32,32,256]{3,2,1,0:T(8,128)(2,1)}), bf16[4,32,32,256]{3,2,1,0:T(8,128)(2,1)S(1)}, u32[]{:S(2)}, u32[]{:S(2)}) %all-to-all-start.2) | async-done | bytes 2097184 | tf_op jit(solution)/shard_map/all_to_all | solution.py:225
  169.1 3.6 %shard_map.94 = bf16[4,128,128]{2,1,0:T(8,128)(2,1)S(1)} custom-call(s32[16]{0:T(128)S(1)} %slice.42.slot_ref, s32[16]{0:T(128)S(1)} %slice.44.live_ref, f32[2]{0:T(128)S(1)} %copy-done.1, bf16[4,256,128]{2,1,0:T(8,128)(2,1)S(1)} %get-tuple-element.26.q_ref, bf16[4,128,256]{2,1,0:T(8,128)(2,1)S(1)} %bitcast.40, ...), custom_call_target="tpu_custom_call" | custom-call | tf_op jit(solution)/shard_map/pallas_call | solution.py:83
  172.7 1.2 collective-permute-start.5
  173.9 0.9 collective-permute-start.3
  174.8 0.7 collective-permute-start.4
  175.5 3.6 %shard_map.93 = bf16[4,128,128]{2,1,0:T(8,128)(2,1)S(1)} custom-call(s32[16]{0:T(128)S(1)} %bitcast.49, s32[16]{0:T(128)S(1)} %slice.38.live_ref, f32[2]{0:T(128)S(1)} %copy-done.1, bf16[4,256,128]{2,1,0:T(8,128)(2,1)S(1)} %get-tuple-element.25.q_ref, bf16[4,128,256]{2,1,0:T(8,128)(2,1)S(1)} %bitcast.39, bf16[4,32,32,256]{3,2,1,0:T(8,128)(2,1)S(1)} %all-to-all-done.2.recv_ref), custom_call_target="tpu_custom_call" | custom-call | tf_op jit(solution)/shard_map/pallas_call | solution.py:83
  179.1 2.6 %collective-permute-start.2 = (bf16[512,128]{1,0:T(8,128)(2,1)S(1)}, bf16[512,128]{1,0:T(8,128)(2,1)S(1)}, u32[]{:S(2)}, u32[]{:S(2)}) collective-permute-start(bf16[512,128]{1,0:T(8,128)(2,1)S(1)} %bitcast.41), channel_id=1, source_target_pairs={{0,3},{1,0},{2,1},{3,2},{4,7},{5,4},{6,5},{7,6},{8,11},{9,8},{10,9... | collective-permute-start | bytes 393224 | tf_op jit(solution)/shard_map/ppermute | solution.py:252
  181.7 0.1 collective-permute-start
  181.8 0.2 fusion.7
  182.0 0.2 fusion.9
  182.2 0.8 collective-permute-done.3
  182.9 1.5 collective-permute-start.1
  184.5 0.2 convolution_add_fusion.1
  184.7 0.2 fusion.11
  184.9 0.2 fusion.3
  185.1 5.3 %collective-permute-done = bf16[512,128]{1,0:T(8,128)(2,1)S(1)} collective-permute-done((bf16[512,128]{1,0:T(8,128)(2,1)S(1)}, bf16[512,128]{1,0:T(8,128)(2,1)S(1)}, u32[]{:S(2)}, u32[]{:S(2)}) %collective-permute-start) | collective-permute-done | bytes 131104 | tf_op jit(solution)/shard_map/ppermute | solution.py:252
  190.4 0.2 convolution_add_fusion.3
  190.6 0.2 fusion.13
  190.8 0.2 fusion.2
  191.0 0.7 pad_maximum_fusion.3
  (36 shorter events, 0.3 us)
Async XLA Ops:
  0.0 35.6 %copy-start = (bf16[512,128]{1,0:T(8,128)(2,1)S(1)}, bf16[512,128]{1,0:T(8,128)(2,1)}, u32[]{:S(2)}) copy-start(bf16[512,128]{1,0:T(8,128)(2,1)} %param.10) | copy-start | bytes 393220
  3.5 20.5 %all-to-all-start = ((s32[64,1,2]{2,1,0:T(1,128)}), s32[64,1,2]{2,1,0:T(1,128)S(1)}, u32[]{:S(2)}, u32[]{:S(2)}) async-start(s32[64,1,2]{2,1,0:T(1,128)} %bitcast.5), calls=%async_computation | async-start | bytes 65536 | tf_op jit(solution)/shard_map/all_to_all | solution.py:197
  29.0 6.6 %copy-start.2 = (bf16[1024,512]{1,0:T(8,128)(2,1)S(1)}, bf16[1024,512]{1,0:T(8,128)(2,1)}, u32[]{:S(2)}) copy-start(bf16[1024,512]{1,0:T(8,128)(2,1)} %param.9) | copy-start | bytes 3145732
  29.0 101.5 %all-to-all-start.1 = ((bf16[64,64,512]{2,1,0:T(8,128)(2,1)}), bf16[64,64,512]{2,1,0:T(8,128)(2,1)}, u32[]{:S(2)}, u32[]{:S(2)}) async-start(bf16[64,64,512]{2,1,0:T(8,128)(2,1)} %bitcast.50), calls=%async_computation.1 | async-start | bytes 8388608 | tf_op jit(solution)/shard_map/all_to_all | solution.py:212
  35.6 1.5 copy-start.9
  35.6 2.7 %copy-start.4 = (bf16[512,128]{1,0:T(8,128)(2,1)S(1)}, bf16[512,128]{1,0:T(8,128)(2,1)}, u32[]{:S(2)}) copy-start(bf16[512,128]{1,0:T(8,128)(2,1)} %param.11) | copy-start | bytes 393220
  36.9 2.7 %copy-start.5 = (bf16[512,128]{1,0:T(8,128)(2,1)S(1)}, bf16[512,128]{1,0:T(8,128)(2,1)}, u32[]{:S(2)}) copy-start(bf16[512,128]{1,0:T(8,128)(2,1)} %param.12) | copy-start | bytes 393220
  71.9 5.8 %copy-start.6 = (bf16[128,512]{1,0:T(8,128)(2,1)S(1)}, bf16[128,512]{1,0:T(8,128)(2,1)}, u32[]{:S(2)}) copy-start(bf16[128,512]{1,0:T(8,128)(2,1)} %param.13) | copy-start | bytes 393220
  137.1 4.5 %copy-start.8 = (s32[8,4]{0,1:T(4,128)S(1)}, s32[8,4]{0,1:T(4,128)}, u32[]{:S(2)}) copy-start(s32[8,4]{0,1:T(4,128)} %compare_convert_fusion) | copy-start | bytes 388
  137.1 4.8 %copy-start.7 = (f32[1024,2]{0,1:T(2,128)S(1)}, f32[1024,2]{0,1:T(2,128)}, u32[]{:S(2)}) copy-start(f32[1024,2]{0,1:T(2,128)} %add_rsqrt_fusion.1) | copy-start | bytes 24580
  137.1 32.0 %all-to-all-start.2 = ((bf16[4,32,32,256]{3,2,1,0:T(8,128)(2,1)}), bf16[4,32,32,256]{3,2,1,0:T(8,128)(2,1)S(1)}, u32[]{:S(2)}, u32[]{:S(2)}) async-start(bf16[4,32,32,256]{3,2,1,0:T(8,128)(2,1)} %bitcast.52), calls=%async_computation.2 | async-start | bytes 4194304 | tf_op jit(solution)/shard_map/all_to_all | solution.py:225
  146.6 22.5 %copy-start.1 = (f32[2]{0:T(128)S(1)}, f32[2]{0:T(128)}, u32[]{:S(2)}) copy-start(f32[2]{0:T(128)} %scale_ref.3) | copy-start | bytes 28
  169.1 12.7 %copy-start.3 = (bf16[512,512]{0,1:T(8,128)(2,1)S(1)}, bf16[512,512]{0,1:T(8,128)(2,1)}, u32[]{:S(2)}) copy-start(bf16[512,512]{0,1:T(8,128)(2,1)} %all_gather.9) | copy-start | bytes 1572868
  172.7 12.0 %collective-permute-start.5 = (bf16[512,128]{1,0:T(8,128)(2,1)S(1)}, bf16[512,128]{1,0:T(8,128)(2,1)S(1)}, u32[]{:S(2)}, u32[]{:S(2)}) collective-permute-start(bf16[512,128]{1,0:T(8,128)(2,1)S(1)} %bitcast.45), channel_id=1, source_target_pairs={{0,3},{1,0},{2,1},{3,2},{4,7},{5,4},{6,5},{7,6},{8,11},{9,8},{10,9... | collective-permute-start | bytes 393224 | tf_op jit(solution)/shard_map/ppermute | solution.py:252
  173.9 9.0 %collective-permute-start.3 = (bf16[512,128]{1,0:T(8,128)(2,1)S(1)}, bf16[512,128]{1,0:T(8,128)(2,1)S(1)}, u32[]{:S(2)}, u32[]{:S(2)}) collective-permute-start(bf16[512,128]{1,0:T(8,128)(2,1)S(1)} %bitcast.46), channel_id=1, source_target_pairs={{0,1},{1,2},{2,3},{3,0},{4,5},{5,6},{6,7},{7,4},{8,9},{9,10},{10,1... | collective-permute-start | bytes 393224 | tf_op jit(solution)/shard_map/ppermute | solution.py:252
  174.8 10.1 %collective-permute-start.4 = (bf16[512,128]{1,0:T(8,128)(2,1)S(1)}, bf16[512,128]{1,0:T(8,128)(2,1)S(1)}, u32[]{:S(2)}, u32[]{:S(2)}) collective-permute-start(bf16[512,128]{1,0:T(8,128)(2,1)S(1)} %bitcast.47), channel_id=1, source_target_pairs={{0,2},{1,3},{2,0},{3,1},{4,6},{5,7},{6,4},{7,5},{8,10},{9,11},{10,... | collective-permute-start | bytes 393224 | tf_op jit(solution)/shard_map/ppermute | solution.py:252
  179.1 11.5 %collective-permute-start.2 = (bf16[512,128]{1,0:T(8,128)(2,1)S(1)}, bf16[512,128]{1,0:T(8,128)(2,1)S(1)}, u32[]{:S(2)}, u32[]{:S(2)}) collective-permute-start(bf16[512,128]{1,0:T(8,128)(2,1)S(1)} %bitcast.41), channel_id=1, source_target_pairs={{0,3},{1,0},{2,1},{3,2},{4,7},{5,4},{6,5},{7,6},{8,11},{9,8},{10,9... | collective-permute-start | bytes 393224 | tf_op jit(solution)/shard_map/ppermute | solution.py:252
  181.7 8.7 %collective-permute-start = (bf16[512,128]{1,0:T(8,128)(2,1)S(1)}, bf16[512,128]{1,0:T(8,128)(2,1)S(1)}, u32[]{:S(2)}, u32[]{:S(2)}) collective-permute-start(bf16[512,128]{1,0:T(8,128)(2,1)S(1)} %bitcast.42), channel_id=1, source_target_pairs={{0,1},{1,2},{2,3},{3,0},{4,5},{5,6},{6,7},{7,4},{8,9},{9,10},{10,1... | collective-permute-start | bytes 393224 | tf_op jit(solution)/shard_map/ppermute | solution.py:252
  182.9 7.8 %collective-permute-start.1 = (bf16[512,128]{1,0:T(8,128)(2,1)S(1)}, bf16[512,128]{1,0:T(8,128)(2,1)S(1)}, u32[]{:S(2)}, u32[]{:S(2)}) collective-permute-start(bf16[512,128]{1,0:T(8,128)(2,1)S(1)} %bitcast.44), channel_id=1, source_target_pairs={{0,2},{1,3},{2,0},{3,1},{4,6},{5,7},{6,4},{7,5},{8,10},{9,11},{10,... | collective-permute-start | bytes 393224 | tf_op jit(solution)/shard_map/ppermute | solution.py:252

commit v17 on v16

--- a/solution.py
+++ b/solution.py
@@ -113,34 +113,34 @@
 
 
 def project_kernel(slot_ref, recv_ref, w_ref, out_ref, rows_scr, sems, *, hd):
-    y = pl.program_id(0)
     pairs = sems.shape[0]
     quarter = recv_ref.shape[1]
+    planes = out_ref.shape[0]
+    cols = out_ref.shape[2]
 
     def piece_copy(p):
         return pltpu.make_async_copy(
             recv_ref.at[slot_ref[p]], rows_scr.at[pl.ds(p * quarter, quarter)], sems.at[p]
         )
 
-    @pl.when(y == 0)
-    def _():
-        for p in range(pairs):
-            piece_copy(p).start()
-        for p in range(pairs):
-            piece_copy(p).wait()
-
-    kv = jnp.dot(rows_scr[...], w_ref[...], preferred_element_type=jnp.float32)
-    feat = kv.shape[1] // 2
-    keys = kv[:, :feat]
+    for p in range(pairs):
+        piece_copy(p).start()
+    for p in range(pairs):
+        piece_copy(p).wait()
+    rows = rows_scr[...]
+    feat = cols // 2
     lane = lax.broadcasted_iota(jnp.int32, (1, feat), 1)
-    sq = keys * keys
-    scale = jnp.zeros(keys.shape, jnp.float32)
-    for h in range(feat // hd):
-        inside = (lane >= h * hd) & (lane < (h + 1) * hd)
-        total = jnp.sum(jnp.where(inside, sq, 0.0), axis=1, keepdims=True)
-        scale = jnp.where(inside, lax.rsqrt(total + 1e-06), scale)
-    out_ref[0, :, :feat] = (keys * scale).astype(out_ref.dtype)
-    out_ref[0, :, feat:] = kv[:, feat:].astype(out_ref.dtype)
+    for y in range(planes):
+        kv = jnp.dot(rows, w_ref[:, y * cols:(y + 1) * cols], preferred_element_type=jnp.float32)
+        keys = kv[:, :feat]
+        sq = keys * keys
+        scale = jnp.zeros(keys.shape, jnp.float32)
+        for h in range(feat // hd):
+            inside = (lane >= h * hd) & (lane < (h + 1) * hd)
+            total = jnp.sum(jnp.where(inside, sq, 0.0), axis=1, keepdims=True)
+            scale = jnp.where(inside, lax.rsqrt(total + 1e-06), scale)
+        out_ref[y, :, :feat] = (keys * scale).astype(out_ref.dtype)
+        out_ref[y, :, feat:] = kv[:, feat:].astype(out_ref.dtype)
 
 
 def project_all(recv, slot_of, w_kv, heads, hd):
@@ -150,12 +150,12 @@
     cols = w_kv.shape[1] // heads
     grid_spec = pltpu.PrefetchScalarGridSpec(
         num_scalar_prefetch=1,
-        grid=(heads,),
+        grid=(1,),
         in_specs=[
             pl.BlockSpec(memory_space=pl.ANY),
-            pl.BlockSpec((model, cols), lambda y, slot_of: (0, y)),
-        ],
-        out_specs=pl.BlockSpec((1, n, cols), lambda y, slot_of: (y, 0, 0)),
+            pl.BlockSpec((model, heads * cols), lambda i, slot_of: (0, 0)),
+        ],
+        out_specs=pl.BlockSpec((heads, n, cols), lambda i, slot_of: (0, 0, 0)),
         scratch_shapes=[
             pltpu.VMEM((n, model), recv.dtype),
             pltpu.SemaphoreType.DMA((pairs,)),

time: 193 us -> 192 us (level)
  no operation moved by 1% of the time
where the time goes in v17:
time: 192 us; the launch traced here: 191 us
  waiting for transfers between devices  74.5 us (39%)
  blocking collectives  42.1 us (22%)
  starting transfers between devices  30.1 us (16%)
  Pallas kernels  17.6 us (9%)
  local copies, waits for them, and re-layouts  12.8 us (7%)
  other arithmetic  9.52 us (5%)
  matrix products  4.37 us (2%)
    all_to_all x1, waiting for transfers between devices, body(): lax.all_to_all(payload.reshape(devices, capacity * quarter, model), 'node...  39.2 us
    all_to_all x1, waiting for transfers between devices, body(): got = lax.all_to_all(send, 'heads', 0, 0, tiled=True)  20.6 us
    all_gather x1, blocking collectives, body(): lax.all_gather(w_key_b, 'heads', axis=1, tiled=True)  14.6 us
    all_gather x1, blocking collectives, body(): lax.all_gather(w_value_b, 'heads', axis=1, tiled=True)  14 us
    all_gather x1, blocking collectives, body(): w_out_t = lax.all_gather(w_out.T, 'heads', axis=1, tiled=True)  13.5 us
    all_to_all x1, starting transfers between devices, body(): lax.all_to_all(request.reshape(devices, capacity), 'nodes', split_axis=0,...  12 us
    all_to_all x1, waiting for transfers between devices, body(): lax.all_to_all(request.reshape(devices, capacity), 'nodes', split_axis=0,...  8.51 us
    pallas_call x2, Pallas kernels, attend(): pl.pallas_call(functools.partial(attend_kernel, count=count, slots=slots)...  7.18 us
  transfers between devices with their start and end apart: 9, of which 5 were waited for; matrix products, arithmetic and copies ran while one was open for 11% of the time, Pallas kernels for 2%

profile of v17, /device:TPU:2, one launch (start us, length us, event | category | flops | bytes accessed | tf_op | source)
XLA Modules:
  0.0 191.3 jit_solution(10059638418603898662)
XLA Ops:
  0.0 0.8 copy.44
  0.8 0.1 reshape.129
  0.9 0.1 fusion.19
  1.0 0.2 select_reduce_fusion.1
  1.2 0.6 broadcast_clamp_fusion
  1.8 0.7 select_add_fusion
  2.5 0.1 copy.45
  2.6 0.1 reshape.138
  2.6 0.1 select_reduce_fusion
  2.7 0.8 sub.33
  3.5 12.0 %all-to-all-start = ((s32[64,1,2]{2,1,0:T(1,128)}), s32[64,1,2]{2,1,0:T(1,128)S(1)}, u32[]{:S(2)}, u32[]{:S(2)}) async-start(s32[64,1,2]{2,1,0:T(1,128)} %bitcast.5), calls=%async_computation | async-start | bytes 65536 | tf_op jit(solution)/shard_map/all_to_all | solution.py:197
  15.5 8.5 %all-to-all-done = s32[64,1,2]{2,1,0:T(1,128)S(1)} async-done(((s32[64,1,2]{2,1,0:T(1,128)}), s32[64,1,2]{2,1,0:T(1,128)S(1)}, u32[]{:S(2)}, u32[]{:S(2)}) %all-to-all-start) | async-done | bytes 544 | tf_op jit(solution)/shard_map/all_to_all | solution.py:197
  24.1 0.1 add_reduce_fusion
  24.2 0.7 add.130.pick_ref
  24.8 4.1 %shard_map.91 = bf16[128,32,512]{2,1,0:T(8,128)(2,1)} custom-call(s32[128]{0:T(128)} %add.130.pick_ref, bf16[32,32,512]{2,1,0:T(8,128)(2,1)} %bitcast.51), custom_call_target="tpu_custom_call" | custom-call | tf_op jit(solution)/shard_map/pallas_call | solution.py:108
  29.0 6.6 %all-to-all-start.1 = ((bf16[64,64,512]{2,1,0:T(8,128)(2,1)}), bf16[64,64,512]{2,1,0:T(8,128)(2,1)}, u32[]{:S(2)}, u32[]{:S(2)}) async-start(bf16[64,64,512]{2,1,0:T(8,128)(2,1)} %bitcast.50), calls=%async_computation.1 | async-start | bytes 8388608 | tf_op jit(solution)/shard_map/all_to_all | solution.py:212
  35.6 1.2 fusion.21
  36.9 0.2 copy.41
  37.1 0.6 compare_convert_fusion
  37.7 0.6 add_rsqrt_fusion.1
  38.3 1.3 bitcast_reduce_fusion
  39.6 14.0 %all_gather.11 = bf16[512,512]{1,0:T(8,128)(2,1)S(1)} all-gather(bf16[512,128]{1,0:T(8,128)(2,1)S(1)} %copy-done.5), channel_id=1, replica_groups=mesh['nodes'=64,'heads'=4] {'heads'}, dimensions={1}, use_global_device_ids=true | all-gather | bytes 655360 | tf_op jit(solution)/shard_map/all_gather | solution.py:210
  53.6 0.3 stack_reshape.9
  53.9 14.6 %all_gather.10 = bf16[512,512]{1,0:T(8,128)(2,1)} all-gather(bf16[512,128]{1,0:T(8,128)(2,1)S(1)} %copy-done.4), channel_id=1, replica_groups=mesh['nodes'=64,'heads'=4] {'heads'}, dimensions={1}, use_global_device_ids=true | all-gather | bytes 655360 | tf_op jit(solution)/shard_map/all_gather | solution.py:209
  68.5 3.4 %stack_reshape.8 = bf16[512,4,1,128]{3,2,1,0:T(2,128)(2,1)S(1)} reshape(bf16[512,512]{1,0:T(8,128)(2,1)} %all_gather.10) | data formatting | bytes 1048576 | tf_op jit(solution)/shard_map/stack;reshape | solution.py:211
  71.9 3.2 %pad_maximum_fusion = bf16[512,4,2,128]{3,2,1,0:T(2,128)(2,1)} fusion(bf16[512,4,1,128]{3,2,1,0:T(2,128)(2,1)S(1)} %stack_reshape.9, bf16[512,4,1,128]{3,2,1,0:T(2,128)(2,1)S(1)} %stack_reshape.8), kind=kLoop, calls=%fused_computation.9 | loop fusion | flops 2097152 | bytes 2097152 | tf_op jit(solution)/shard_map/stack | solution.py:211
  75.1 2.6 %reshape.133.w_ref = bf16[512,1024]{1,0:T(8,128)(2,1)} reshape(bf16[512,4,2,128]{3,2,1,0:T(2,128)(2,1)} %pad_maximum_fusion) | data formatting | bytes 2097152 | tf_op jit(solution)/shard_map/reshape | solution.py:211
  77.7 13.5 %all_gather.9 = bf16[512,512]{0,1:T(8,128)(2,1)} all-gather(bf16[512,128]{0,1:T(8,128)(2,1)S(1)} %bitcast.56), channel_id=1, replica_groups=mesh['nodes'=64,'heads'=4] {'heads'}, dimensions={1}, use_global_device_ids=true | all-gather | bytes 655360 | tf_op jit(solution)/shard_map/all_gather | solution.py:208
  91.2 39.2 %all-to-all-done.1 = bf16[64,64,512]{2,1,0:T(8,128)(2,1)} async-done(((bf16[64,64,512]{2,1,0:T(8,128)(2,1)}), bf16[64,64,512]{2,1,0:T(8,128)(2,1)}, u32[]{:S(2)}, u32[]{:S(2)}) %all-to-all-start.1) | async-done | bytes 4194336 | tf_op jit(solution)/shard_map/all_to_all | solution.py:212
  130.5 6.3 %shard_map.92 = bf16[4,1024,256]{2,1,0:T(8,128)(2,1)} custom-call(s32[32]{0:T(128)} %get-tuple-element.19.slot_ref, bf16[128,32,512]{2,1,0:T(8,128)(2,1)} %bitcast.8.recv_ref, bf16[512,1024]{1,0:T(8,128)(2,1)} %reshape.133.w_ref), custom_call_target="tpu_custom_call" | custom-call | tf_op jit(solution)/shard_map/pallas_call | solution.py:164
  136.8 4.5 %all-to-all-start.2 = ((bf16[4,32,32,256]{3,2,1,0:T(8,128)(2,1)}), bf16[4,32,32,256]{3,2,1,0:T(8,128)(2,1)S(1)}, u32[]{:S(2)}, u32[]{:S(2)}) async-start(bf16[4,32,32,256]{3,2,1,0:T(8,128)(2,1)} %bitcast.52), calls=%async_computation.2 | async-start | bytes 4194304 | tf_op jit(solution)/shard_map/all_to_all | solution.py:225
  141.2 0.1 fusion.20
  141.3 0.1 slice.42.slot_ref
  141.4 0.1 copy.49
  141.5 0.1 slice.44.live_ref
  141.6 0.9 copy.51
  142.5 2.0 %copy.42 = f32[8,128,128]{2,1,0:T(8,128)} copy(f32[8,128,128]{1,0,2:T(8,128)} %bitcast.55) | data formatting | bytes 1048576 | tf_op jit(solution)/shard_map/mul | solution.py:14
  144.6 1.1 fusion.4
  145.7 0.5 convolution_convert_fusion
  146.2 0.1 copy.50
  146.4 0.1 copy.40
  146.5 0.1 slice.38.live_ref
  146.5 0.1 copy.43
  146.7 1.3 broadcast_select_fusion.1
  148.1 20.6 %all-to-all-done.2.recv_ref = bf16[4,32,32,256]{3,2,1,0:T(8,128)(2,1)S(1)} async-done(((bf16[4,32,32,256]{3,2,1,0:T(8,128)(2,1)}), bf16[4,32,32,256]{3,2,1,0:T(8,128)(2,1)S(1)}, u32[]{:S(2)}, u32[]{:S(2)}) %all-to-all-start.2) | async-done | bytes 2097184 | tf_op jit(solution)/shard_map/all_to_all | solution.py:225
  168.7 3.6 %shard_map.94 = bf16[4,128,128]{2,1,0:T(8,128)(2,1)S(1)} custom-call(s32[16]{0:T(128)S(1)} %slice.42.slot_ref, s32[16]{0:T(128)S(1)} %slice.44.live_ref, f32[2]{0:T(128)S(1)} %copy-done.1, bf16[4,256,128]{2,1,0:T(8,128)(2,1)S(1)} %get-tuple-element.26.q_ref, bf16[4,128,256]{2,1,0:T(8,128)(2,1)S(1)} %bitcast.40, ...), custom_call_target="tpu_custom_call" | custom-call | tf_op jit(solution)/shard_map/pallas_call | solution.py:83
  172.3 1.2 collective-permute-start.5
  173.6 0.9 collective-permute-start.3
  174.4 0.7 collective-permute-start.4
  175.1 3.6 %shard_map.93 = bf16[4,128,128]{2,1,0:T(8,128)(2,1)S(1)} custom-call(s32[16]{0:T(128)S(1)} %bitcast.49, s32[16]{0:T(128)S(1)} %slice.38.live_ref, f32[2]{0:T(128)S(1)} %copy-done.1, bf16[4,256,128]{2,1,0:T(8,128)(2,1)S(1)} %get-tuple-element.25.q_ref, bf16[4,128,256]{2,1,0:T(8,128)(2,1)S(1)} %bitcast.39, bf16[4,32,32,256]{3,2,1,0:T(8,128)(2,1)S(1)} %all-to-all-done.2.recv_ref), custom_call_target="tpu_custom_call" | custom-call | tf_op jit(solution)/shard_map/pallas_call | solution.py:83
  178.7 2.6 %collective-permute-start.2 = (bf16[512,128]{1,0:T(8,128)(2,1)S(1)}, bf16[512,128]{1,0:T(8,128)(2,1)S(1)}, u32[]{:S(2)}, u32[]{:S(2)}) collective-permute-start(bf16[512,128]{1,0:T(8,128)(2,1)S(1)} %bitcast.41), channel_id=1, source_target_pairs={{0,3},{1,0},{2,1},{3,2},{4,7},{5,4},{6,5},{7,6},{8,11},{9,8},{10,9... | collective-permute-start | bytes 393224 | tf_op jit(solution)/shard_map/ppermute | solution.py:252
  181.4 0.1 collective-permute-start
  181.5 0.2 fusion.7
  181.6 0.2 fusion.9
  181.8 0.8 collective-permute-done.3
  182.6 1.5 collective-permute-start.1
  184.1 0.2 convolution_add_fusion.1
  184.3 0.2 fusion.11
  184.5 0.2 fusion.3
  184.7 5.3 %collective-permute-done = bf16[512,128]{1,0:T(8,128)(2,1)S(1)} collective-permute-done((bf16[512,128]{1,0:T(8,128)(2,1)S(1)}, bf16[512,128]{1,0:T(8,128)(2,1)S(1)}, u32[]{:S(2)}, u32[]{:S(2)}) %collective-permute-start) | collective-permute-done | bytes 131104 | tf_op jit(solution)/shard_map/ppermute | solution.py:252
  190.0 0.2 convolution_add_fusion.3
  190.2 0.2 fusion.13
  190.4 0.2 fusion.2
  190.6 0.7 pad_maximum_fusion.3
  (36 shorter events, 0.3 us)
Async XLA Ops:
  0.0 35.6 %copy-start = (bf16[512,128]{1,0:T(8,128)(2,1)S(1)}, bf16[512,128]{1,0:T(8,128)(2,1)}, u32[]{:S(2)}) copy-start(bf16[512,128]{1,0:T(8,128)(2,1)} %param.10) | copy-start | bytes 393220
  3.5 20.5 %all-to-all-start = ((s32[64,1,2]{2,1,0:T(1,128)}), s32[64,1,2]{2,1,0:T(1,128)S(1)}, u32[]{:S(2)}, u32[]{:S(2)}) async-start(s32[64,1,2]{2,1,0:T(1,128)} %bitcast.5), calls=%async_computation | async-start | bytes 65536 | tf_op jit(solution)/shard_map/all_to_all | solution.py:197
  29.0 6.6 %copy-start.2 = (bf16[1024,512]{1,0:T(8,128)(2,1)S(1)}, bf16[1024,512]{1,0:T(8,128)(2,1)}, u32[]{:S(2)}) copy-start(bf16[1024,512]{1,0:T(8,128)(2,1)} %param.9) | copy-start | bytes 3145732
  29.0 101.5 %all-to-all-start.1 = ((bf16[64,64,512]{2,1,0:T(8,128)(2,1)}), bf16[64,64,512]{2,1,0:T(8,128)(2,1)}, u32[]{:S(2)}, u32[]{:S(2)}) async-start(bf16[64,64,512]{2,1,0:T(8,128)(2,1)} %bitcast.50), calls=%async_computation.1 | async-start | bytes 8388608 | tf_op jit(solution)/shard_map/all_to_all | solution.py:212
  35.6 1.5 copy-start.9
  35.6 2.7 %copy-start.4 = (bf16[512,128]{1,0:T(8,128)(2,1)S(1)}, bf16[512,128]{1,0:T(8,128)(2,1)}, u32[]{:S(2)}) copy-start(bf16[512,128]{1,0:T(8,128)(2,1)} %param.11) | copy-start | bytes 393220
  36.9 2.7 %copy-start.5 = (bf16[512,128]{1,0:T(8,128)(2,1)S(1)}, bf16[512,128]{1,0:T(8,128)(2,1)}, u32[]{:S(2)}) copy-start(bf16[512,128]{1,0:T(8,128)(2,1)} %param.12) | copy-start | bytes 393220
  71.9 5.8 %copy-start.6 = (bf16[128,512]{1,0:T(8,128)(2,1)S(1)}, bf16[128,512]{1,0:T(8,128)(2,1)}, u32[]{:S(2)}) copy-start(bf16[128,512]{1,0:T(8,128)(2,1)} %param.13) | copy-start | bytes 393220
  136.7 4.5 %copy-start.8 = (s32[8,4]{0,1:T(4,128)S(1)}, s32[8,4]{0,1:T(4,128)}, u32[]{:S(2)}) copy-start(s32[8,4]{0,1:T(4,128)} %compare_convert_fusion) | copy-start | bytes 388
  136.7 4.8 %copy-start.7 = (f32[1024,2]{0,1:T(2,128)S(1)}, f32[1024,2]{0,1:T(2,128)}, u32[]{:S(2)}) copy-start(f32[1024,2]{0,1:T(2,128)} %add_rsqrt_fusion.1) | copy-start | bytes 24580
  136.8 32.0 %all-to-all-start.2 = ((bf16[4,32,32,256]{3,2,1,0:T(8,128)(2,1)}), bf16[4,32,32,256]{3,2,1,0:T(8,128)(2,1)S(1)}, u32[]{:S(2)}, u32[]{:S(2)}) async-start(bf16[4,32,32,256]{3,2,1,0:T(8,128)(2,1)} %bitcast.52), calls=%async_computation.2 | async-start | bytes 4194304 | tf_op jit(solution)/shard_map/all_to_all | solution.py:225
  146.2 22.5 %copy-start.1 = (f32[2]{0:T(128)S(1)}, f32[2]{0:T(128)}, u32[]{:S(2)}) copy-start(f32[2]{0:T(128)} %scale_ref.3) | copy-start | bytes 28
  168.7 12.7 %copy-start.3 = (bf16[512,512]{0,1:T(8,128)(2,1)S(1)}, bf16[512,512]{0,1:T(8,128)(2,1)}, u32[]{:S(2)}) copy-start(bf16[512,512]{0,1:T(8,128)(2,1)} %all_gather.9) | copy-start | bytes 1572868
  172.3 12.0 %collective-permute-start.5 = (bf16[512,128]{1,0:T(8,128)(2,1)S(1)}, bf16[512,128]{1,0:T(8,128)(2,1)S(1)}, u32[]{:S(2)}, u32[]{:S(2)}) collective-permute-start(bf16[512,128]{1,0:T(8,128)(2,1)S(1)} %bitcast.45), channel_id=1, source_target_pairs={{0,3},{1,0},{2,1},{3,2},{4,7},{5,4},{6,5},{7,6},{8,11},{9,8},{10,9... | collective-permute-start | bytes 393224 | tf_op jit(solution)/shard_map/ppermute | solution.py:252
  173.6 9.0 %collective-permute-start.3 = (bf16[512,128]{1,0:T(8,128)(2,1)S(1)}, bf16[512,128]{1,0:T(8,128)(2,1)S(1)}, u32[]{:S(2)}, u32[]{:S(2)}) collective-permute-start(bf16[512,128]{1,0:T(8,128)(2,1)S(1)} %bitcast.46), channel_id=1, source_target_pairs={{0,1},{1,2},{2,3},{3,0},{4,5},{5,6},{6,7},{7,4},{8,9},{9,10},{10,1... | collective-permute-start | bytes 393224 | tf_op jit(solution)/shard_map/ppermute | solution.py:252
  174.4 10.1 %collective-permute-start.4 = (bf16[512,128]{1,0:T(8,128)(2,1)S(1)}, bf16[512,128]{1,0:T(8,128)(2,1)S(1)}, u32[]{:S(2)}, u32[]{:S(2)}) collective-permute-start(bf16[512,128]{1,0:T(8,128)(2,1)S(1)} %bitcast.47), channel_id=1, source_target_pairs={{0,2},{1,3},{2,0},{3,1},{4,6},{5,7},{6,4},{7,5},{8,10},{9,11},{10,... | collective-permute-start | bytes 393224 | tf_op jit(solution)/shard_map/ppermute | solution.py:252
  178.7 11.5 %collective-permute-start.2 = (bf16[512,128]{1,0:T(8,128)(2,1)S(1)}, bf16[512,128]{1,0:T(8,128)(2,1)S(1)}, u32[]{:S(2)}, u32[]{:S(2)}) collective-permute-start(bf16[512,128]{1,0:T(8,128)(2,1)S(1)} %bitcast.41), channel_id=1, source_target_pairs={{0,3},{1,0},{2,1},{3,2},{4,7},{5,4},{6,5},{7,6},{8,11},{9,8},{10,9... | collective-permute-start | bytes 393224 | tf_op jit(solution)/shard_map/ppermute | solution.py:252
  181.4 8.7 %collective-permute-start = (bf16[512,128]{1,0:T(8,128)(2,1)S(1)}, bf16[512,128]{1,0:T(8,128)(2,1)S(1)}, u32[]{:S(2)}, u32[]{:S(2)}) collective-permute-start(bf16[512,128]{1,0:T(8,128)(2,1)S(1)} %bitcast.42), channel_id=1, source_target_pairs={{0,1},{1,2},{2,3},{3,0},{4,5},{5,6},{6,7},{7,4},{8,9},{9,10},{10,1... | collective-permute-start | bytes 393224 | tf_op jit(solution)/shard_map/ppermute | solution.py:252
  182.6 7.8 %collective-permute-start.1 = (bf16[512,128]{1,0:T(8,128)(2,1)S(1)}, bf16[512,128]{1,0:T(8,128)(2,1)S(1)}, u32[]{:S(2)}, u32[]{:S(2)}) collective-permute-start(bf16[512,128]{1,0:T(8,128)(2,1)S(1)} %bitcast.44), channel_id=1, source_target_pairs={{0,2},{1,3},{2,0},{3,1},{4,6},{5,7},{6,4},{7,5},{8,10},{9,11},{10,... | collective-permute-start | bytes 393224 | tf_op jit(solution)/shard_map/ppermute | solution.py:252

commit v18 on v16

--- a/solution.py
+++ b/solution.py
@@ -222,7 +222,14 @@
     send = project_all(recv, slot_of, w_kv_all, heads, feat // count).reshape(
         heads, pairs, quarter, 2 * feat
     )
-    got = lax.all_to_all(send, "heads", 0, 0, tiled=True)
+    me_plane = lax.axis_index("heads")
+    received = [lax.dynamic_index_in_dim(send, me_plane, 0, keepdims=False)]
+    for k in range(1, heads):
+        outgoing = lax.dynamic_index_in_dim(send, (me_plane + k) % heads, 0, keepdims=False)
+        received.append(
+            lax.ppermute(outgoing, "heads", [(j, (j + k) % heads) for j in range(heads)])
+        )
+    got = jnp.stack(received, axis=0)
     pair_kv = got
     pair_ids = jnp.arange(pairs, dtype=jnp.int32)
     heads_n = lax.axis_size("heads")

time: 193 us -> 193 us (level)
  waiting for transfers between devices: 74.5 us -> 78 us
  other arithmetic: 9.52 us -> 6.34 us
    ppermute x0 -> x3, waiting for transfers between devices: none -> 25.5 us  [body(): lax.ppermute(outgoing, 'heads', [(j, (j + k) % heads) for j in range(head...]
    all_to_all x1 -> x0, waiting for transfers between devices: 20.6 us -> none  [body(): got = lax.all_to_all(send, 'heads', 0, 0, tiled=True)]
    ppermute x0 -> x3, starting transfers between devices: none -> 4.69 us  [body(): lax.ppermute(outgoing, 'heads', [(j, (j + k) % heads) for j in range(head...]
    all_to_all x1 -> x0, starting transfers between devices: 4.48 us -> none  [body(): got = lax.all_to_all(send, 'heads', 0, 0, tiled=True)]
  transfers between devices with their start and end apart: 9 -> 11, of which waited for: 5 -> 6; matrix products, arithmetic and copies ran while one was open for 11% -> 8% of each run, Pallas kernels for 2% -> 2%
where the time goes in v18:
time: 193 us; the launch traced here: 192 us
  waiting for transfers between devices  78 us (40%)
  blocking collectives  41.5 us (22%)
  starting transfers between devices  31.3 us (16%)
  Pallas kernels  17.9 us (9%)
  local copies, waits for them, and re-layouts  13.1 us (7%)
  other arithmetic  6.34 us (3%)
  matrix products  3.61 us (2%)
    all_to_all x1, waiting for transfers between devices, body(): lax.all_to_all(payload.reshape(devices, capacity * quarter, model), 'node...  39.1 us
    ppermute x3, waiting for transfers between devices, body(): lax.ppermute(outgoing, 'heads', [(j, (j + k) % heads) for j in range(head...  25.5 us
    all_gather x1, blocking collectives, body(): lax.all_gather(w_key_b, 'heads', axis=1, tiled=True)  14.7 us
    all_gather x1, blocking collectives, body(): lax.all_gather(w_value_b, 'heads', axis=1, tiled=True)  14 us
    all_gather x1, blocking collectives, body(): w_out_t = lax.all_gather(w_out.T, 'heads', axis=1, tiled=True)  12.8 us
    all_to_all x1, starting transfers between devices, body(): lax.all_to_all(request.reshape(devices, capacity), 'nodes', split_axis=0,...  12 us
    all_to_all x1, waiting for transfers between devices, body(): lax.all_to_all(request.reshape(devices, capacity), 'nodes', split_axis=0,...  8.51 us
    ppermute x6, starting transfers between devices, body(): lax.ppermute(attn_half, 'heads', [(j, (j + k) % heads_n) for j in range(h...  8 us
  transfers between devices with their start and end apart: 11, of which 6 were waited for; matrix products, arithmetic and copies ran while one was open for 8% of the time, Pallas kernels for 2%

profile of v18, /device:TPU:2, one launch (start us, length us, event | category | flops | bytes accessed | tf_op | source)
XLA Modules:
  0.0 192.2 jit_solution(14055376940128603123)
XLA Ops:
  0.0 0.8 copy.44
  0.8 0.1 reshape.129
  1.0 0.2 select_reduce_fusion.1
  1.2 0.6 broadcast_clamp_fusion
  1.8 0.7 select_add_fusion
  2.5 0.1 copy.45
  2.6 0.1 reshape.138
  2.6 0.1 select_reduce_fusion
  2.7 0.8 sub.33
  3.5 12.0 %all-to-all-start = ((s32[64,1,2]{2,1,0:T(1,128)}), s32[64,1,2]{2,1,0:T(1,128)S(1)}, u32[]{:S(2)}, u32[]{:S(2)}) async-start(s32[64,1,2]{2,1,0:T(1,128)} %bitcast.5), calls=%async_computation | async-start | bytes 65536 | tf_op jit(solution)/shard_map/all_to_all | solution.py:197
  15.5 8.5 %all-to-all-done = s32[64,1,2]{2,1,0:T(1,128)S(1)} async-done(((s32[64,1,2]{2,1,0:T(1,128)}), s32[64,1,2]{2,1,0:T(1,128)S(1)}, u32[]{:S(2)}, u32[]{:S(2)}) %all-to-all-start) | async-done | bytes 544 | tf_op jit(solution)/shard_map/all_to_all | solution.py:197
  24.0 0.1 add_reduce_fusion
  24.2 0.7 add.161.pick_ref
  24.8 4.1 %shard_map.91 = bf16[128,32,512]{2,1,0:T(8,128)(2,1)} custom-call(s32[128]{0:T(128)} %add.161.pick_ref, bf16[32,32,512]{2,1,0:T(8,128)(2,1)} %bitcast.60), custom_call_target="tpu_custom_call" | custom-call | tf_op jit(solution)/shard_map/pallas_call | solution.py:108
  29.0 6.6 %all-to-all-start.1 = ((bf16[64,64,512]{2,1,0:T(8,128)(2,1)}), bf16[64,64,512]{2,1,0:T(8,128)(2,1)}, u32[]{:S(2)}, u32[]{:S(2)}) async-start(bf16[64,64,512]{2,1,0:T(8,128)(2,1)} %bitcast.59), calls=%async_computation.1 | async-start | bytes 8388608 | tf_op jit(solution)/shard_map/all_to_all | solution.py:212
  35.9 0.1 copy.49
  36.0 0.1 slice.44.live_ref
  36.0 1.2 fusion.23
  37.3 0.2 copy.41
  37.6 0.1 copy.51
  37.7 1.0 copy.42
  38.8 0.5 bitcast_reduce_fusion
  39.3 0.5 convolution_convert_fusion
  39.9 0.1 copy.50
  40.0 0.1 copy.40
  40.1 0.1 slice.38.live_ref
  40.2 0.1 copy.43
  40.4 14.0 %all_gather.11 = bf16[512,512]{1,0:T(8,128)(2,1)S(1)} all-gather(bf16[512,128]{1,0:T(8,128)(2,1)S(1)} %copy-done.5), channel_id=1, replica_groups=mesh['nodes'=64,'heads'=4] {'heads'}, dimensions={1}, use_global_device_ids=true | all-gather | bytes 655360 | tf_op jit(solution)/shard_map/all_gather | solution.py:210
  54.4 0.3 stack_reshape.9
  54.7 14.7 %all_gather.10 = bf16[512,512]{1,0:T(8,128)(2,1)} all-gather(bf16[512,128]{1,0:T(8,128)(2,1)S(1)} %copy-done.6), channel_id=1, replica_groups=mesh['nodes'=64,'heads'=4] {'heads'}, dimensions={1}, use_global_device_ids=true | all-gather | bytes 655360 | tf_op jit(solution)/shard_map/all_gather | solution.py:209
  69.4 3.4 %stack_reshape.8 = bf16[512,4,1,128]{3,2,1,0:T(2,128)(2,1)S(1)} reshape(bf16[512,512]{1,0:T(8,128)(2,1)} %all_gather.10) | data formatting | bytes 1048576 | tf_op jit(solution)/shard_map/stack;reshape | solution.py:211
  72.8 3.2 %pad_maximum_fusion.1 = bf16[512,4,2,128]{3,2,1,0:T(2,128)(2,1)} fusion(bf16[512,4,1,128]{3,2,1,0:T(2,128)(2,1)S(1)} %stack_reshape.9, bf16[512,4,1,128]{3,2,1,0:T(2,128)(2,1)S(1)} %stack_reshape.8), kind=kLoop, calls=%fused_computation.8 | loop fusion | flops 2097152 | bytes 2097152 | tf_op jit(solution)/shard_map/stack | solution.py:211
  76.0 2.6 %reshape.133.w_ref = bf16[512,1024]{1,0:T(8,128)(2,1)} reshape(bf16[512,4,2,128]{3,2,1,0:T(2,128)(2,1)} %pad_maximum_fusion.1) | data formatting | bytes 2097152 | tf_op jit(solution)/shard_map/reshape | solution.py:211
  78.6 12.8 %all_gather.9 = bf16[512,512]{0,1:T(8,128)(2,1)S(1)} all-gather(bf16[512,128]{0,1:T(8,128)(2,1)S(1)} %bitcast.68), channel_id=1, replica_groups=mesh['nodes'=64,'heads'=4] {'heads'}, dimensions={1}, use_global_device_ids=true | all-gather | bytes 655360 | tf_op jit(solution)/shard_map/all_gather | solution.py:208
  91.4 39.1 %all-to-all-done.1 = bf16[64,64,512]{2,1,0:T(8,128)(2,1)} async-done(((bf16[64,64,512]{2,1,0:T(8,128)(2,1)}), bf16[64,64,512]{2,1,0:T(8,128)(2,1)}, u32[]{:S(2)}, u32[]{:S(2)}) %all-to-all-start.1) | async-done | bytes 4194336 | tf_op jit(solution)/shard_map/all_to_all | solution.py:212
  130.5 6.6 %shard_map.92 = bf16[4,1024,256]{2,1,0:T(8,128)(2,1)} custom-call(s32[32]{0:T(128)} %get-tuple-element.19.slot_ref, bf16[128,32,512]{2,1,0:T(8,128)(2,1)} %bitcast.8.recv_ref, bf16[512,1024]{1,0:T(8,128)(2,1)} %reshape.133.w_ref), custom_call_target="tpu_custom_call" | custom-call | tf_op jit(solution)/shard_map/pallas_call | solution.py:164
  137.1 1.8 constant_dynamic-slice_fusion
  138.9 3.1 %collective-permute-start.2 = (bf16[32,32,256]{2,1,0:T(8,128)(2,1)S(1)}, bf16[32,32,256]{2,1,0:T(8,128)(2,1)S(1)}, u32[]{:S(2)}, u32[]{:S(2)}) collective-permute-start(bf16[32,32,256]{2,1,0:T(8,128)(2,1)S(1)} %get-tuple-element.24), channel_id=1, source_target_pairs={{0,3},{1,0},{2,1},{3,2},{4,7},{5,4},{6,5},{7,6},{8,11},{9,8},{10,9... | collective-permute-start | bytes 1572872 | tf_op jit(solution)/shard_map/ppermute | solution.py:230
  142.0 0.6 collective-permute-start.1
  142.6 1.0 collective-permute-start
  143.6 0.1 broadcast_select_fusion.1
  143.8 21.8 %collective-permute-done.2 = bf16[32,32,256]{2,1,0:T(8,128)(2,1)S(1)} collective-permute-done((bf16[32,32,256]{2,1,0:T(8,128)(2,1)S(1)}, bf16[32,32,256]{2,1,0:T(8,128)(2,1)S(1)}, u32[]{:S(2)}, u32[]{:S(2)}) %collective-permute-start.2) | collective-permute-done | bytes 524320 | tf_op jit(solution)/shard_map/ppermute | solution.py:230
  165.5 3.8 %collective-permute-done = bf16[32,32,256]{2,1,0:T(8,128)(2,1)S(1)} collective-permute-done((bf16[32,32,256]{2,1,0:T(8,128)(2,1)S(1)}, bf16[32,32,256]{2,1,0:T(8,128)(2,1)S(1)}, u32[]{:S(2)}, u32[]{:S(2)}) %collective-permute-start) | collective-permute-done | bytes 524320 | tf_op jit(solution)/shard_map/ppermute | solution.py:230
  169.3 0.3 pad_maximum_fusion.recv_ref
  169.6 0.4 copy-done.1
  169.9 3.6 %shard_map.94 = bf16[4,128,128]{2,1,0:T(8,128)(2,1)S(1)} custom-call(s32[16]{0:T(128)S(1)} %slice.42.slot_ref, s32[16]{0:T(128)S(1)} %slice.44.live_ref, f32[2]{0:T(128)S(1)} %copy-done.1, bf16[4,256,128]{2,1,0:T(8,128)(2,1)S(1)} %get-tuple-element.30.q_ref, bf16[4,128,256]{2,1,0:T(8,128)(2,1)S(1)} %bitcast.49, ...), custom_call_target="tpu_custom_call" | custom-call | tf_op jit(solution)/shard_map/pallas_call | solution.py:83
  173.5 0.9 collective-permute-start.8
  174.4 0.6 collective-permute-start.7
  175.0 0.8 collective-permute-start.6
  175.9 3.6 %shard_map.93 = bf16[4,128,128]{2,1,0:T(8,128)(2,1)S(1)} custom-call(s32[16]{0:T(128)S(1)} %bitcast.58, s32[16]{0:T(128)S(1)} %slice.38.live_ref, f32[2]{0:T(128)S(1)} %copy-done.1, bf16[4,256,128]{2,1,0:T(8,128)(2,1)S(1)} %get-tuple-element.29.q_ref, bf16[4,128,256]{2,1,0:T(8,128)(2,1)S(1)} %bitcast.48, bf16[4,32,32,256]{3,2,1,0:T(8,128)(2,1)S(1)} %pad_maximum_fusion.recv_ref), custom_call_target="tpu_custom_call" | custom-call | tf_op jit(solution)/shard_map/pallas_call | solution.py:83
  179.5 2.7 %collective-permute-start.5 = (bf16[512,128]{1,0:T(8,128)(2,1)S(1)}, bf16[512,128]{1,0:T(8,128)(2,1)S(1)}, u32[]{:S(2)}, u32[]{:S(2)}) collective-permute-start(bf16[512,128]{1,0:T(8,128)(2,1)S(1)} %bitcast.50), channel_id=1, source_target_pairs={{0,3},{1,0},{2,1},{3,2},{4,7},{5,4},{6,5},{7,6},{8,11},{9,8},{10,9... | collective-permute-start | bytes 393224 | tf_op jit(solution)/shard_map/ppermute | solution.py:259
  182.2 1.6 collective-permute-start.4
  183.7 0.2 fusion.7
  183.9 0.2 fusion.9
  184.1 1.4 collective-permute-start.3
  185.5 0.2 fusion.11
  185.7 0.2 fusion.17
  185.9 0.2 fusion.3
  186.1 1.4 collective-permute-done.5
  187.5 0.2 fusion.13
  187.7 3.5 %collective-permute-done.3 = bf16[512,128]{1,0:T(8,128)(2,1)S(1)} collective-permute-done((bf16[512,128]{1,0:T(8,128)(2,1)S(1)}, bf16[512,128]{1,0:T(8,128)(2,1)S(1)}, u32[]{:S(2)}, u32[]{:S(2)}) %collective-permute-start.3) | collective-permute-done | bytes 131104 | tf_op jit(solution)/shard_map/ppermute | solution.py:259
  191.1 0.2 fusion.19
  191.3 0.2 fusion.2
  191.5 0.7 pad_maximum_fusion.4
  (39 shorter events, 0.6 us)
Async XLA Ops:
  0.0 36.0 %copy-start = (bf16[512,128]{1,0:T(8,128)(2,1)S(1)}, bf16[512,128]{1,0:T(8,128)(2,1)}, u32[]{:S(2)}) copy-start(bf16[512,128]{1,0:T(8,128)(2,1)} %param.10) | copy-start | bytes 393220
  3.5 20.5 %all-to-all-start = ((s32[64,1,2]{2,1,0:T(1,128)}), s32[64,1,2]{2,1,0:T(1,128)S(1)}, u32[]{:S(2)}, u32[]{:S(2)}) async-start(s32[64,1,2]{2,1,0:T(1,128)} %bitcast.5), calls=%async_computation | async-start | bytes 65536 | tf_op jit(solution)/shard_map/all_to_all | solution.py:197
  29.0 6.8 %copy-start.8 = (s32[8,4]{0,1:T(4,128)S(1)}, s32[8,4]{0,1:T(4,128)}, u32[]{:S(2)}) copy-start(s32[8,4]{0,1:T(4,128)} %param.17) | copy-start | bytes 388
  29.0 7.1 %copy-start.2 = (bf16[1024,512]{1,0:T(8,128)(2,1)S(1)}, bf16[1024,512]{1,0:T(8,128)(2,1)}, u32[]{:S(2)}) copy-start(bf16[1024,512]{1,0:T(8,128)(2,1)} %param.9) | copy-start | bytes 3145732
  29.0 101.5 %all-to-all-start.1 = ((bf16[64,64,512]{2,1,0:T(8,128)(2,1)}), bf16[64,64,512]{2,1,0:T(8,128)(2,1)}, u32[]{:S(2)}, u32[]{:S(2)}) async-start(bf16[64,64,512]{2,1,0:T(8,128)(2,1)} %bitcast.59), calls=%async_computation.1 | async-start | bytes 8388608 | tf_op jit(solution)/shard_map/all_to_all | solution.py:212
  37.3 1.5 copy-start.6
  37.6 1.7 copy-start.5
  72.8 5.8 %copy-start.7 = (bf16[128,512]{1,0:T(8,128)(2,1)S(1)}, bf16[128,512]{1,0:T(8,128)(2,1)}, u32[]{:S(2)}) copy-start(bf16[128,512]{1,0:T(8,128)(2,1)} %param.13) | copy-start | bytes 393220
  137.1 6.5 %copy-start.3 = (f32[1024,128]{1,0:T(8,128)S(1)}, f32[1024,128]{1,0:T(8,128)}, u32[]{:S(2)}) copy-start(f32[1024,128]{1,0:T(8,128)} %get-tuple-element.34) | copy-start | bytes 1572868
  137.1 6.5 %copy-start.4 = (f32[8,128,128]{2,1,0:T(8,128)S(1)}, f32[8,128,128]{2,1,0:T(8,128)}, u32[]{:S(2)}) copy-start(f32[8,128,128]{2,1,0:T(8,128)} %copy.42) | copy-start | bytes 1572868
  138.9 26.6 %collective-permute-start.2 = (bf16[32,32,256]{2,1,0:T(8,128)(2,1)S(1)}, bf16[32,32,256]{2,1,0:T(8,128)(2,1)S(1)}, u32[]{:S(2)}, u32[]{:S(2)}) collective-permute-start(bf16[32,32,256]{2,1,0:T(8,128)(2,1)S(1)} %get-tuple-element.24), channel_id=1, source_target_pairs={{0,3},{1,0},{2,1},{3,2},{4,7},{5,4},{6,5},{7,6},{8,11},{9,8},{10,9... | collective-permute-start | bytes 1572872 | tf_op jit(solution)/shard_map/ppermute | solution.py:230
  142.0 23.5 %collective-permute-start.1 = (bf16[32,32,256]{2,1,0:T(8,128)(2,1)S(1)}, bf16[32,32,256]{2,1,0:T(8,128)(2,1)S(1)}, u32[]{:S(2)}, u32[]{:S(2)}) collective-permute-start(bf16[32,32,256]{2,1,0:T(8,128)(2,1)S(1)} %get-tuple-element.25), channel_id=1, source_target_pairs={{0,2},{1,3},{2,0},{3,1},{4,6},{5,7},{6,4},{7,5},{8,10},{9,11},{10,... | collective-permute-start | bytes 1572872 | tf_op jit(solution)/shard_map/ppermute | solution.py:230
  142.6 26.6 %collective-permute-start = (bf16[32,32,256]{2,1,0:T(8,128)(2,1)S(1)}, bf16[32,32,256]{2,1,0:T(8,128)(2,1)S(1)}, u32[]{:S(2)}, u32[]{:S(2)}) collective-permute-start(bf16[32,32,256]{2,1,0:T(8,128)(2,1)S(1)} %get-tuple-element.26), channel_id=1, source_target_pairs={{0,1},{1,2},{2,3},{3,0},{4,5},{5,6},{6,7},{7,4},{8,9},{9,10},{10,1... | collective-permute-start | bytes 1572872 | tf_op jit(solution)/shard_map/ppermute | solution.py:230
  169.3 0.7 copy-start.1
  173.5 10.6 %collective-permute-start.8 = (bf16[512,128]{1,0:T(8,128)(2,1)S(1)}, bf16[512,128]{1,0:T(8,128)(2,1)S(1)}, u32[]{:S(2)}, u32[]{:S(2)}) collective-permute-start(bf16[512,128]{1,0:T(8,128)(2,1)S(1)} %bitcast.54), channel_id=1, source_target_pairs={{0,3},{1,0},{2,1},{3,2},{4,7},{5,4},{6,5},{7,6},{8,11},{9,8},{10,9... | collective-permute-start | bytes 393224 | tf_op jit(solution)/shard_map/ppermute | solution.py:259
  174.4 11.5 %collective-permute-start.7 = (bf16[512,128]{1,0:T(8,128)(2,1)S(1)}, bf16[512,128]{1,0:T(8,128)(2,1)S(1)}, u32[]{:S(2)}, u32[]{:S(2)}) collective-permute-start(bf16[512,128]{1,0:T(8,128)(2,1)S(1)} %bitcast.55), channel_id=1, source_target_pairs={{0,2},{1,3},{2,0},{3,1},{4,6},{5,7},{6,4},{7,5},{8,10},{9,11},{10,... | collective-permute-start | bytes 393224 | tf_op jit(solution)/shard_map/ppermute | solution.py:259
  175.0 10.6 %collective-permute-start.6 = (bf16[512,128]{1,0:T(8,128)(2,1)S(1)}, bf16[512,128]{1,0:T(8,128)(2,1)S(1)}, u32[]{:S(2)}, u32[]{:S(2)}) collective-permute-start(bf16[512,128]{1,0:T(8,128)(2,1)S(1)} %bitcast.56), channel_id=1, source_target_pairs={{0,1},{1,2},{2,3},{3,0},{4,5},{5,6},{6,7},{7,4},{8,9},{9,10},{10,1... | collective-permute-start | bytes 393224 | tf_op jit(solution)/shard_map/ppermute | solution.py:259
  179.5 8.0 %collective-permute-start.5 = (bf16[512,128]{1,0:T(8,128)(2,1)S(1)}, bf16[512,128]{1,0:T(8,128)(2,1)S(1)}, u32[]{:S(2)}, u32[]{:S(2)}) collective-permute-start(bf16[512,128]{1,0:T(8,128)(2,1)S(1)} %bitcast.50), channel_id=1, source_target_pairs={{0,3},{1,0},{2,1},{3,2},{4,7},{5,4},{6,5},{7,6},{8,11},{9,8},{10,9... | collective-permute-start | bytes 393224 | tf_op jit(solution)/shard_map/ppermute | solution.py:259
  182.2 9.1 %collective-permute-start.4 = (bf16[512,128]{1,0:T(8,128)(2,1)S(1)}, bf16[512,128]{1,0:T(8,128)(2,1)S(1)}, u32[]{:S(2)}, u32[]{:S(2)}) collective-permute-start(bf16[512,128]{1,0:T(8,128)(2,1)S(1)} %bitcast.51), channel_id=1, source_target_pairs={{0,2},{1,3},{2,0},{3,1},{4,6},{5,7},{6,4},{7,5},{8,10},{9,11},{10,... | collective-permute-start | bytes 393224 | tf_op jit(solution)/shard_map/ppermute | solution.py:259
  184.1 7.0 %collective-permute-start.3 = (bf16[512,128]{1,0:T(8,128)(2,1)S(1)}, bf16[512,128]{1,0:T(8,128)(2,1)S(1)}, u32[]{:S(2)}, u32[]{:S(2)}) collective-permute-start(bf16[512,128]{1,0:T(8,128)(2,1)S(1)} %bitcast.53), channel_id=1, source_target_pairs={{0,1},{1,2},{2,3},{3,0},{4,5},{5,6},{6,7},{7,4},{8,9},{9,10},{10,1... | collective-permute-start | bytes 393224 | tf_op jit(solution)/shard_map/ppermute | solution.py:259

commit v19 on v16

--- a/solution.py
+++ b/solution.py
@@ -234,11 +234,10 @@
             piece, w_part, (((1,), (1,)), ((), ())), preferred_element_type=jnp.float32
         )
 
-    halves = 2
-    per_half = nblocks // halves
+    first = (nblocks * 5) // 8
     outs = []
-    for part in range(halves):
-        lo, hi = part * per_half, (part + 1) * per_half
+    for lo, hi in ((0, first), (first, nblocks)):
+        per_half = hi - lo
         attn_half = attend(
             query_stack[lo:hi],
             own_kv[lo:hi],

time: 193 us -> 194 us (level)
  waiting for transfers between devices: 74.5 us -> 79.1 us
  local copies, waits for them, and re-layouts: 12.8 us -> 10.5 us
    all_to_all x1, waiting for transfers between devices: 39.2 us -> 44.9 us  [body(): lax.all_to_all(payload.reshape(devices, capacity * quarter, model), 'node...]
    another operation x2, local copies, waits for them, and re-layouts: 3.69 us -> 0.6 us  [body(): jnp.stack([w_key_all, w_value_all], axis=2).reshape(model, heads * 2 * feat)]
    all_to_all x1, waiting for transfers between devices: 20.6 us -> 18.5 us  [body(): got = lax.all_to_all(send, 'heads', 0, 0, tiled=True)]
  transfers between devices with their start and end apart: 9 -> 9, of which waited for: 5 -> 4; matrix products, arithmetic and copies ran while one was open for 11% -> 10% of each run, Pallas kernels for 2% -> 2%
where the time goes in v19:
time: 194 us; the launch traced here: 193 us
  waiting for transfers between devices  79.1 us (41%)
  blocking collectives  41.5 us (21%)
  starting transfers between devices  30.9 us (16%)
  Pallas kernels  17.9 us (9%)
  local copies, waits for them, and re-layouts  10.5 us (5%)
  other arithmetic  8.3 us (4%)
  matrix products  4.85 us (2%)
    all_to_all x1, waiting for transfers between devices, body(): lax.all_to_all(payload.reshape(devices, capacity * quarter, model), 'node...  44.9 us
    all_to_all x1, waiting for transfers between devices, body(): got = lax.all_to_all(send, 'heads', 0, 0, tiled=True)  18.5 us
    all_gather x1, blocking collectives, body(): lax.all_gather(w_key_b, 'heads', axis=1, tiled=True)  14 us
    all_gather x1, blocking collectives, body(): lax.all_gather(w_value_b, 'heads', axis=1, tiled=True)  13.9 us
    all_gather x1, blocking collectives, body(): w_out_t = lax.all_gather(w_out.T, 'heads', axis=1, tiled=True)  13.5 us
    all_to_all x1, starting transfers between devices, body(): lax.all_to_all(request.reshape(devices, capacity), 'nodes', split_axis=0,...  12 us
    all_to_all x1, waiting for transfers between devices, body(): lax.all_to_all(request.reshape(devices, capacity), 'nodes', split_axis=0,...  8.51 us
    ppermute x6, starting transfers between devices, body(): lax.ppermute(attn_half, 'heads', [(j, (j + k) % heads_n) for j in range(h...  7.81 us
  transfers between devices with their start and end apart: 9, of which 4 were waited for; matrix products, arithmetic and copies ran while one was open for 10% of the time, Pallas kernels for 2%

profile of v19, /device:TPU:2, one launch (start us, length us, event | category | flops | bytes accessed | tf_op | source)
XLA Modules:
  0.0 193.5 jit_solution(4669764593000087078)
XLA Ops:
  0.0 0.7 select_add_fusion
  0.7 0.1 copy.45
  0.8 0.1 reshape.138
  0.9 0.8 copy.44
  1.7 0.1 reshape.129
  1.7 0.1 fusion.19
  1.8 0.1 reduce_window_sum.11
  1.9 0.2 select_reduce_fusion.1
  2.1 0.5 broadcast_clamp_fusion
  2.6 0.1 select_reduce_fusion
  2.7 0.8 sub.33
  3.4 12.0 %all-to-all-start = ((s32[64,1,2]{2,1,0:T(1,128)}), s32[64,1,2]{2,1,0:T(1,128)S(1)}, u32[]{:S(2)}, u32[]{:S(2)}) async-start(s32[64,1,2]{2,1,0:T(1,128)} %bitcast.5), calls=%async_computation | async-start | bytes 65536 | tf_op jit(solution)/shard_map/all_to_all | solution.py:197
  15.5 8.5 %all-to-all-done = s32[64,1,2]{2,1,0:T(1,128)S(1)} async-done(((s32[64,1,2]{2,1,0:T(1,128)}), s32[64,1,2]{2,1,0:T(1,128)S(1)}, u32[]{:S(2)}, u32[]{:S(2)}) %all-to-all-start) | async-done | bytes 544 | tf_op jit(solution)/shard_map/all_to_all | solution.py:197
  24.0 0.1 add_reduce_fusion
  24.1 0.7 add.130.pick_ref
  24.8 4.1 %shard_map.91 = bf16[128,32,512]{2,1,0:T(8,128)(2,1)} custom-call(s32[128]{0:T(128)} %add.130.pick_ref, bf16[32,32,512]{2,1,0:T(8,128)(2,1)} %bitcast.52), custom_call_target="tpu_custom_call" | custom-call | tf_op jit(solution)/shard_map/pallas_call | solution.py:108
  28.9 6.6 %all-to-all-start.1 = ((bf16[64,64,512]{2,1,0:T(8,128)(2,1)}), bf16[64,64,512]{2,1,0:T(8,128)(2,1)}, u32[]{:S(2)}, u32[]{:S(2)}) async-start(bf16[64,64,512]{2,1,0:T(8,128)(2,1)} %bitcast.51), calls=%async_computation.1 | async-start | bytes 8388608 | tf_op jit(solution)/shard_map/all_to_all | solution.py:212
  35.5 0.0 copy-start.5
  35.6 0.1 slice.42.slot_ref
  35.7 0.1 slice.43
  35.8 0.1 copy.49
  35.9 0.1 slice.44.live_ref
  36.0 0.1 copy.40
  36.0 0.1 slice.38.live_ref
  36.1 0.5 bitcast_reduce_fusion
  36.7 0.5 convolution_convert_fusion
  37.3 0.2 copy.43
  37.5 0.1 copy.50
  37.6 14.0 %all_gather.10 = bf16[512,512]{1,0:T(8,128)(2,1)S(1)} all-gather(bf16[512,128]{1,0:T(8,128)(2,1)S(1)} %copy-done.4), channel_id=1, replica_groups=mesh['nodes'=64,'heads'=4] {'heads'}, dimensions={1}, use_global_device_ids=true | all-gather | bytes 655360 | tf_op jit(solution)/shard_map/all_gather | solution.py:209
  51.6 0.3 stack_reshape.8
  51.9 13.9 %all_gather.11 = bf16[512,512]{1,0:T(8,128)(2,1)S(1)} all-gather(bf16[512,128]{1,0:T(8,128)(2,1)S(1)} %copy-done.5), channel_id=1, replica_groups=mesh['nodes'=64,'heads'=4] {'heads'}, dimensions={1}, use_global_device_ids=true | all-gather | bytes 655360 | tf_op jit(solution)/shard_map/all_gather | solution.py:210
  65.9 0.3 stack_reshape.9
  66.2 3.2 %pad_maximum_fusion = bf16[512,4,2,128]{3,2,1,0:T(2,128)(2,1)} fusion(bf16[512,4,1,128]{3,2,1,0:T(2,128)(2,1)S(1)} %stack_reshape.9, bf16[512,4,1,128]{3,2,1,0:T(2,128)(2,1)S(1)} %stack_reshape.8), kind=kLoop, calls=%fused_computation.9 | loop fusion | flops 2097152 | bytes 2097152 | tf_op jit(solution)/shard_map/stack | solution.py:211
  69.4 2.6 %reshape.133.w_ref = bf16[512,1024]{1,0:T(8,128)(2,1)} reshape(bf16[512,4,2,128]{3,2,1,0:T(2,128)(2,1)} %pad_maximum_fusion) | data formatting | bytes 2097152 | tf_op jit(solution)/shard_map/reshape | solution.py:211
  72.0 13.5 %all_gather.9 = bf16[512,512]{0,1:T(8,128)(2,1)} all-gather(bf16[512,128]{0,1:T(8,128)(2,1)S(1)} %bitcast.57), channel_id=1, replica_groups=mesh['nodes'=64,'heads'=4] {'heads'}, dimensions={1}, use_global_device_ids=true | all-gather | bytes 655360 | tf_op jit(solution)/shard_map/all_gather | solution.py:208
  85.5 44.9 %all-to-all-done.1 = bf16[64,64,512]{2,1,0:T(8,128)(2,1)} async-done(((bf16[64,64,512]{2,1,0:T(8,128)(2,1)}), bf16[64,64,512]{2,1,0:T(8,128)(2,1)}, u32[]{:S(2)}, u32[]{:S(2)}) %all-to-all-start.1) | async-done | bytes 4194336 | tf_op jit(solution)/shard_map/all_to_all | solution.py:212
  130.4 6.6 %shard_map.92 = bf16[4,1024,256]{2,1,0:T(8,128)(2,1)} custom-call(s32[32]{0:T(128)} %get-tuple-element.19.slot_ref, bf16[128,32,512]{2,1,0:T(8,128)(2,1)} %bitcast.8.recv_ref, bf16[512,1024]{1,0:T(8,128)(2,1)} %reshape.133.w_ref), custom_call_target="tpu_custom_call" | custom-call | tf_op jit(solution)/shard_map/pallas_call | solution.py:164
  137.1 4.5 %all-to-all-start.2 = ((bf16[4,32,32,256]{3,2,1,0:T(8,128)(2,1)}), bf16[4,32,32,256]{3,2,1,0:T(8,128)(2,1)S(1)}, u32[]{:S(2)}, u32[]{:S(2)}) async-start(bf16[4,32,32,256]{3,2,1,0:T(8,128)(2,1)} %bitcast.53), calls=%async_computation.2 | async-start | bytes 4194304 | tf_op jit(solution)/shard_map/all_to_all | solution.py:225
  141.5 2.5 %fusion.20 = (f32[1024,128]{1,0:T(8,128)S(1)}, f32[1024,128]{1,0:T(8,128)}) fusion(bf16[1024,512]{1,0:T(8,128)(2,1)} %param.9, bf16[512,128]{1,0:T(8,128)(2,1)S(1)} %copy-done), kind=kOutput, calls=%fused_computation.57 | convolution fusion | flops 134348800 | bytes 2228224 | tf_op jit(solution)/shard_map/dot_general | solution.py:180
  144.0 1.0 copy.41
  145.0 1.1 bitcast_reduce_fusion.1
  146.2 0.9 copy.51
  147.1 2.1 %copy.42 = f32[8,128,128]{2,1,0:T(8,128)} copy(f32[8,128,128]{1,0,2:T(8,128)} %bitcast.56) | data formatting | bytes 1048576 | tf_op jit(solution)/shard_map/mul | solution.py:14
  149.1 1.3 broadcast_select_fusion.1
  150.5 18.5 %all-to-all-done.2.recv_ref = bf16[4,32,32,256]{3,2,1,0:T(8,128)(2,1)S(1)} async-done(((bf16[4,32,32,256]{3,2,1,0:T(8,128)(2,1)}), bf16[4,32,32,256]{3,2,1,0:T(8,128)(2,1)S(1)}, u32[]{:S(2)}, u32[]{:S(2)}) %all-to-all-start.2) | async-done | bytes 2097184 | tf_op jit(solution)/shard_map/all_to_all | solution.py:225
  169.0 3.0 %shard_map.94 = bf16[3,128,128]{2,1,0:T(8,128)(2,1)S(1)} custom-call(s32[12]{0:T(128)S(1)} %slice.42.slot_ref, s32[12]{0:T(128)S(1)} %slice.44.live_ref, f32[2]{0:T(128)S(1)} %copy-done.1, bf16[3,256,128]{2,1,0:T(8,128)(2,1)S(1)} %pad_maximum_fusion.3.q_ref, bf16[3,128,256]{2,1,0:T(8,128)(2,1)S(1)} %bitcast.41, ...), custom_call_target="tpu_custom_call" | custom-call | tf_op jit(solution)/shard_map/pallas_call | solution.py:83
  172.0 1.2 collective-permute-start.5
  173.3 1.5 collective-permute-start.4
  174.7 4.2 %shard_map.93 = bf16[5,128,128]{2,1,0:T(8,128)(2,1)S(1)} custom-call(s32[20]{0:T(128)S(1)} %bitcast.50, s32[20]{0:T(128)S(1)} %slice.38.live_ref, f32[2]{0:T(128)S(1)} %copy-done.1, bf16[5,256,128]{2,1,0:T(8,128)(2,1)S(1)} %fusion.6.q_ref, bf16[5,128,256]{2,1,0:T(8,128)(2,1)S(1)} %bitcast.40, bf16[4,32,32,256]{3,2,1,0:T(8,128)(2,1)S(1)} %all-to-all-done.2.recv_ref), custom_call_target="tpu_custom_call" | custom-call | tf_op jit(solution)/shard_map/pallas_call | solution.py:83
  179.0 3.3 %collective-permute-start.2 = (bf16[640,128]{1,0:T(8,128)(2,1)S(1)}, bf16[640,128]{1,0:T(8,128)(2,1)S(1)}, u32[]{:S(2)}, u32[]{:S(2)}) collective-permute-start(bf16[640,128]{1,0:T(8,128)(2,1)S(1)} %bitcast.42), channel_id=1, source_target_pairs={{0,3},{1,0},{2,1},{3,2},{4,7},{5,4},{6,5},{7,6},{8,11},{9,8},{10,9... | collective-permute-start | bytes 491528 | tf_op jit(solution)/shard_map/ppermute | solution.py:251
  182.3 0.8 collective-permute-start.1
  183.1 0.2 fusion.9
  183.3 0.2 fusion.7
  183.5 0.0 collective-permute-done.3
  183.5 0.9 collective-permute-start
  184.4 0.2 convolution_add_fusion.3
  184.6 0.2 fusion.11
  184.8 0.0 collective-permute-done.4
  184.8 0.2 fusion.3
  185.0 7.2 %collective-permute-done = bf16[640,128]{1,0:T(8,128)(2,1)S(1)} collective-permute-done((bf16[640,128]{1,0:T(8,128)(2,1)S(1)}, bf16[640,128]{1,0:T(8,128)(2,1)S(1)}, u32[]{:S(2)}, u32[]{:S(2)}) %collective-permute-start) | collective-permute-done | bytes 163872 | tf_op jit(solution)/shard_map/ppermute | solution.py:251
  192.1 0.2 convolution_add_fusion.1
  192.3 0.2 fusion.13
  192.5 0.2 fusion.1
  192.7 0.7 pad_maximum_fusion.1
  (34 shorter events, 0.3 us)
Async XLA Ops:
  0.0 141.5 %copy-start = (bf16[512,128]{1,0:T(8,128)(2,1)S(1)}, bf16[512,128]{1,0:T(8,128)(2,1)}, u32[]{:S(2)}) copy-start(bf16[512,128]{1,0:T(8,128)(2,1)} %param.10) | copy-start | bytes 393220
  3.4 20.5 %all-to-all-start = ((s32[64,1,2]{2,1,0:T(1,128)}), s32[64,1,2]{2,1,0:T(1,128)S(1)}, u32[]{:S(2)}, u32[]{:S(2)}) async-start(s32[64,1,2]{2,1,0:T(1,128)} %bitcast.5), calls=%async_computation | async-start | bytes 65536 | tf_op jit(solution)/shard_map/all_to_all | solution.py:197
  28.9 6.8 %copy-start.7 = (s32[8,4]{0,1:T(4,128)S(1)}, s32[8,4]{0,1:T(4,128)}, u32[]{:S(2)}) copy-start(s32[8,4]{0,1:T(4,128)} %param.17) | copy-start | bytes 388
  28.9 7.2 %copy-start.2 = (bf16[1024,512]{1,0:T(8,128)(2,1)S(1)}, bf16[1024,512]{1,0:T(8,128)(2,1)}, u32[]{:S(2)}) copy-start(bf16[1024,512]{1,0:T(8,128)(2,1)} %param.9) | copy-start | bytes 3145732
  28.9 7.2 %copy-start.4 = (bf16[512,128]{1,0:T(8,128)(2,1)S(1)}, bf16[512,128]{1,0:T(8,128)(2,1)}, u32[]{:S(2)}) copy-start(bf16[512,128]{1,0:T(8,128)(2,1)} %param.11) | copy-start | bytes 393220
  28.9 101.5 %all-to-all-start.1 = ((bf16[64,64,512]{2,1,0:T(8,128)(2,1)}), bf16[64,64,512]{2,1,0:T(8,128)(2,1)}, u32[]{:S(2)}, u32[]{:S(2)}) async-start(bf16[64,64,512]{2,1,0:T(8,128)(2,1)} %bitcast.51), calls=%async_computation.1 | async-start | bytes 8388608 | tf_op jit(solution)/shard_map/all_to_all | solution.py:212
  35.5 1.2 copy-start.5
  66.2 5.8 %copy-start.6 = (bf16[128,512]{1,0:T(8,128)(2,1)S(1)}, bf16[128,512]{1,0:T(8,128)(2,1)}, u32[]{:S(2)}) copy-start(bf16[128,512]{1,0:T(8,128)(2,1)} %param.13) | copy-start | bytes 393220
  137.1 32.0 %all-to-all-start.2 = ((bf16[4,32,32,256]{3,2,1,0:T(8,128)(2,1)}), bf16[4,32,32,256]{3,2,1,0:T(8,128)(2,1)S(1)}, u32[]{:S(2)}, u32[]{:S(2)}) async-start(bf16[4,32,32,256]{3,2,1,0:T(8,128)(2,1)} %bitcast.53), calls=%async_computation.2 | async-start | bytes 4194304 | tf_op jit(solution)/shard_map/all_to_all | solution.py:225
  149.1 19.9 %copy-start.1 = (f32[2]{0:T(128)S(1)}, f32[2]{0:T(128)}, u32[]{:S(2)}) copy-start(f32[2]{0:T(128)} %scale_ref.3) | copy-start | bytes 28
  172.0 11.1 %copy-start.3 = (bf16[512,512]{0,1:T(8,128)(2,1)S(1)}, bf16[512,512]{0,1:T(8,128)(2,1)}, u32[]{:S(2)}) copy-start(bf16[512,512]{0,1:T(8,128)(2,1)} %all_gather.9) | copy-start | bytes 1572868
  172.0 12.6 %collective-permute-start.5 = (bf16[384,128]{1,0:T(8,128)(2,1)S(1)}, bf16[384,128]{1,0:T(8,128)(2,1)S(1)}, u32[]{:S(2)}, u32[]{:S(2)}) collective-permute-start(bf16[384,128]{1,0:T(8,128)(2,1)S(1)} %bitcast.46), channel_id=1, source_target_pairs={{0,3},{1,0},{2,1},{3,2},{4,7},{5,4},{6,5},{7,6},{8,11},{9,8},{10,9... | collective-permute-start | bytes 294920 | tf_op jit(solution)/shard_map/ppermute | solution.py:251
  173.3 11.5 %collective-permute-start.4 = (bf16[384,128]{1,0:T(8,128)(2,1)S(1)}, bf16[384,128]{1,0:T(8,128)(2,1)S(1)}, u32[]{:S(2)}, u32[]{:S(2)}) collective-permute-start(bf16[384,128]{1,0:T(8,128)(2,1)S(1)} %bitcast.47), channel_id=1, source_target_pairs={{0,2},{1,3},{2,0},{3,1},{4,6},{5,7},{6,4},{7,5},{8,10},{9,11},{10,... | collective-permute-start | bytes 294920 | tf_op jit(solution)/shard_map/ppermute | solution.py:251
  174.7 8.7 %collective-permute-start.3 = (bf16[384,128]{1,0:T(8,128)(2,1)S(1)}, bf16[384,128]{1,0:T(8,128)(2,1)S(1)}, u32[]{:S(2)}, u32[]{:S(2)}) collective-permute-start(bf16[384,128]{1,0:T(8,128)(2,1)S(1)} %bitcast.48), channel_id=1, source_target_pairs={{0,1},{1,2},{2,3},{3,0},{4,5},{5,6},{6,7},{7,4},{8,9},{9,10},{10,1... | collective-permute-start | bytes 294920 | tf_op jit(solution)/shard_map/ppermute | solution.py:251
  179.0 13.4 %collective-permute-start.2 = (bf16[640,128]{1,0:T(8,128)(2,1)S(1)}, bf16[640,128]{1,0:T(8,128)(2,1)S(1)}, u32[]{:S(2)}, u32[]{:S(2)}) collective-permute-start(bf16[640,128]{1,0:T(8,128)(2,1)S(1)} %bitcast.42), channel_id=1, source_target_pairs={{0,3},{1,0},{2,1},{3,2},{4,7},{5,4},{6,5},{7,6},{8,11},{9,8},{10,9... | collective-permute-start | bytes 491528 | tf_op jit(solution)/shard_map/ppermute | solution.py:251
  182.3 10.3 %collective-permute-start.1 = (bf16[640,128]{1,0:T(8,128)(2,1)S(1)}, bf16[640,128]{1,0:T(8,128)(2,1)S(1)}, u32[]{:S(2)}, u32[]{:S(2)}) collective-permute-start(bf16[640,128]{1,0:T(8,128)(2,1)S(1)} %bitcast.43), channel_id=1, source_target_pairs={{0,2},{1,3},{2,0},{3,1},{4,6},{5,7},{6,4},{7,5},{8,10},{9,11},{10,... | collective-permute-start | bytes 491528 | tf_op jit(solution)/shard_map/ppermute | solution.py:251
  183.5 8.6 %collective-permute-start = (bf16[640,128]{1,0:T(8,128)(2,1)S(1)}, bf16[640,128]{1,0:T(8,128)(2,1)S(1)}, u32[]{:S(2)}, u32[]{:S(2)}) collective-permute-start(bf16[640,128]{1,0:T(8,128)(2,1)S(1)} %bitcast.45), channel_id=1, source_target_pairs={{0,1},{1,2},{2,3},{3,0},{4,5},{5,6},{6,7},{7,4},{8,9},{9,10},{10,1... | collective-permute-start | bytes 491528 | tf_op jit(solution)/shard_map/ppermute | solution.py:251
